TPU v7x, 32 devices: a whole 2x2x4 slice. The times are simulated.
32 devices in a mesh: groups: 2 (over y), freq: 4 (over z), src: 2 (over x), vp: 2 (over core).
Axes of the slice: x: 2, y: 2, z: 4, core: 2. Of those that a mesh axis runs over, the one named last changes fastest.
Arguments:
- focus_direct: bfloat16 [4, 2, 192, 8192], P('freq', None, ('groups', 'vp'), 'src'), parts along dimension 2, may hold values from -6 to 6
- u_factors: bfloat16 [4, 32, 2, 32, 2048], P('freq', 'src'), may hold values from -0.1875 to 0.1875
- v_factors: bfloat16 [4, 8, 2, 32, 8192], P('freq', None, None, None, 'src'), may hold values from -0.375 to 0.375
- tile_ranks: int32 [4, 8, 32], P('freq', None, 'src'), may hold values from 16 to 32
- onset_rec: int32 [192, 2048], P(('groups', 'vp'), 'src'), parts along dimension 0, may hold values from 64 to 191
- onset_src: int32 [192, 8192], P(('groups', 'vp'), 'src'), parts along dimension 0, may hold values from 64 to 191
Outputs:
- focus_plus: bfloat16 [4, 2, 192, 8192], P('freq', None, ('groups', 'vp'), 'src'), parts along dimension 2
- focus_minus: bfloat16 [4, 2, 192, 2048], P('freq', None, ('groups', 'vp'), 'src'), parts along dimension 2
There are 2 independent parts, one for each index of `groups`. A program takes and returns all parts, laid end to end along the dimension named above; an argument that names none is the same for every part. Nothing has to cross between parts.
All inputs are finite; a program needn't handle non-finite values.
Results may differ from a plain program's by a relative error of at most 0.018.
Values may be sent and summed in bfloat16 or wider, within the bound.
No kernel may reach another device: no remote copies, remote signals or barrier semaphores. Data moves between devices by JAX's collectives and lax.ppermute only.
A program may use at most 128 MiB of HBM per device.

v0:
```python
import math

import jax
import jax.numpy as jnp
from jax import lax
from jax.experimental import pallas as pl
from jax.sharding import PartitionSpec as P

TILE = 256
RANK = 32
NT = 256
FLO = 8
ITERS = 2
GATHER_MAX = 4


def make_tables(count):
    index = FLO + jnp.arange(count, dtype=jnp.int32)
    sample = jnp.arange(NT, dtype=jnp.int32)
    phase = (index[:, None] * sample[None, :] % NT).astype(jnp.float32) * (2.0 * math.pi / NT)
    cosine = jnp.cos(phase)
    sine = jnp.sin(phase)
    inverse = jnp.stack([cosine, -sine]) * (2.0 / NT)
    forward = jnp.stack([cosine, -sine])
    return (inverse, forward)


def gather_kernel(table_ref, onset_ref, out_ref):
    rows = onset_ref.shape[1]
    width = onset_ref.shape[2]
    size = out_ref.shape[0]
    sample = lax.broadcasted_iota(jnp.int32, (NT, width), 0)
    for row in range(rows):
        place = jnp.clip(onset_ref[0, row : row + 1, :], 0, NT) - 1
        pick = (sample == place).astype(jnp.bfloat16)
        parts = jnp.dot(table_ref[...], pick, preferred_element_type=jnp.float32)
        out_ref[:, 0, row, :] = (parts[:size] + parts[size : 2 * size]) + parts[2 * size :]


def window_gather(count, onset):
    if count > GATHER_MAX:
        return onset
    inverse, forward = make_tables(count)
    terms = jnp.einsum("cft,dgt->tgdfc", forward, inverse, precision=lax.Precision.HIGHEST)
    size = 4 * count * count
    table = jnp.cumsum(terms.reshape(NT, size), axis=0)
    high = table.astype(jnp.bfloat16)
    rest = table - high.astype(jnp.float32)
    middle = rest.astype(jnp.bfloat16)
    low = (rest - middle.astype(jnp.float32)).astype(jnp.bfloat16)
    stacked = jnp.concatenate([high, middle, low], axis=1).T
    blocks, points, width = onset.shape
    rows = 8
    return pl.pallas_call(
        gather_kernel,
        grid=(blocks, points // rows),
        in_specs=[
            pl.BlockSpec((3 * size, NT), lambda b, r: (0, 0)),
            pl.BlockSpec((1, rows, width), lambda b, r: (b, r, 0)),
        ],
        out_specs=pl.BlockSpec((size, 1, rows, width), lambda b, r: (0, b, r, 0)),
        out_shape=jax.ShapeDtypeStruct((size, blocks, points, width), jnp.float32),
    )(stacked, onset)


def window_kernel(matrix_ref, spectrum_ref, out_ref):
    count = spectrum_ref.shape[0]
    comps = 2 * count
    source = [spectrum_ref[q // 2, 0, q % 2].astype(jnp.float32) for q in range(comps)]
    for target in range(comps):
        total = matrix_ref[target, 0] * source[0]
        for q in range(1, comps):
            total = total + matrix_ref[q * comps + target, 0] * source[q]
        out_ref[target // 2, 0, target % 2] = total.astype(out_ref.dtype)


def window(spectrum, picked):
    count = spectrum.shape[0]
    if count > GATHER_MAX:
        inverse, forward = make_tables(count)
        signal = jnp.einsum(
            "fbcvm,cft->bvmt", spectrum.astype(jnp.float32), inverse, precision=lax.Precision.HIGHEST
        )
        keep = lax.broadcasted_iota(jnp.int32, signal.shape, 3) < picked[..., None]
        signal = jnp.where(keep, signal, jnp.zeros_like(signal))
        result = jnp.einsum("bvmt,cft->fbcvm", signal, forward, precision=lax.Precision.HIGHEST)
        return result.astype(jnp.bfloat16)
    _, blocks, comps, points, width = spectrum.shape
    size = picked.shape[0]
    return pl.pallas_call(
        window_kernel,
        grid=(blocks,),
        in_specs=[
            pl.BlockSpec((size, 1, points, width), lambda b: (0, b, 0, 0)),
            pl.BlockSpec((count, 1, comps, points, width), lambda b: (0, b, 0, 0, 0)),
        ],
        out_specs=pl.BlockSpec((count, 1, comps, points, width), lambda b: (0, b, 0, 0, 0)),
        out_shape=jax.ShapeDtypeStruct(spectrum.shape, jnp.bfloat16),
    )(picked, spectrum)


def piece_count(tiles, parts):
    return parts // math.gcd(tiles, parts)


def to_pieces(x, parts):
    tiles, comps, points, width = x.shape
    k = piece_count(tiles, parts)
    if k == 1:
        return x
    x = x.reshape(tiles, comps, points, k, width // k)
    return jnp.transpose(x, (0, 3, 1, 2, 4)).reshape(tiles * k, comps, points, width // k)


def from_pieces(x, tiles):
    count, comps, points, width = x.shape
    k = count // tiles
    if k == 1:
        return x
    x = x.reshape(tiles, k, comps, points, width)
    return jnp.transpose(x, (0, 2, 3, 1, 4)).reshape(tiles, comps, points, k * width)


def onset_pieces(onset, tiles, parts, place):
    points = onset.shape[0]
    k = piece_count(tiles, parts)
    blocks = tiles * k
    each = blocks // parts
    split = onset.reshape(points, blocks, TILE // k)
    split = jnp.transpose(split, (1, 0, 2))
    return lax.dynamic_slice_in_dim(split, place * each, each, 0)


def exchange(x, parts):
    tiles = x.shape[0]
    pieces = to_pieces(x, parts)
    got = lax.all_to_all(pieces, "freq", split_axis=0, concat_axis=0, tiled=True)
    return got.reshape((parts, got.shape[0] // parts) + got.shape[1:])


def exchange_back(y, tiles):
    flat = y.reshape((y.shape[0] * y.shape[1],) + y.shape[2:])
    got = lax.all_to_all(flat, "freq", split_axis=0, concat_axis=0, tiled=True)
    return from_pieces(got, tiles)


def coefficients(v_tiles, mask, plus):
    form = "irjt,jvt->ivjr"
    p_re = plus[:, 0]
    p_im = plus[:, 1]
    z_real = jnp.einsum(
        form, v_tiles[:, 0], p_re, preferred_element_type=jnp.float32
    ) + jnp.einsum(form, v_tiles[:, 1], p_im, preferred_element_type=jnp.float32)
    z_imag = jnp.einsum(
        form, v_tiles[:, 0], p_im, preferred_element_type=jnp.float32
    ) - jnp.einsum(form, v_tiles[:, 1], p_re, preferred_element_type=jnp.float32)
    z_real = jnp.where(mask, z_real, 0.0).astype(jnp.bfloat16)
    z_imag = jnp.where(mask, z_imag, 0.0).astype(jnp.bfloat16)
    return z_real, z_imag


def expand_rows(u_tiles, z_real, z_imag):
    other = "jrit,ivjr->ivt"
    y_real = jnp.einsum(
        other, u_tiles[:, 0], z_real, preferred_element_type=jnp.float32
    ) - jnp.einsum(other, u_tiles[:, 1], z_imag, preferred_element_type=jnp.float32)
    y_imag = jnp.einsum(
        other, u_tiles[:, 0], z_imag, preferred_element_type=jnp.float32
    ) + jnp.einsum(other, u_tiles[:, 1], z_real, preferred_element_type=jnp.float32)
    return jnp.stack([y_real, y_imag], axis=1)


def adjoint_local(u_tiles, v_tiles, mask, minus):
    form = "jrit,ivt->ivjr"
    m_re = minus[:, 0]
    m_im = minus[:, 1]
    w_real = jnp.einsum(
        form, u_tiles[:, 0], m_re, preferred_element_type=jnp.float32
    ) + jnp.einsum(form, u_tiles[:, 1], m_im, preferred_element_type=jnp.float32)
    w_imag = jnp.einsum(
        form, u_tiles[:, 0], m_im, preferred_element_type=jnp.float32
    ) - jnp.einsum(form, u_tiles[:, 1], m_re, preferred_element_type=jnp.float32)
    w_real = jnp.where(mask, w_real, 0.0).astype(jnp.bfloat16)
    w_imag = jnp.where(mask, w_imag, 0.0).astype(jnp.bfloat16)
    other = "irjt,ivjr->jvt"
    x_real = jnp.einsum(
        other, v_tiles[:, 0], w_real, preferred_element_type=jnp.float32
    ) - jnp.einsum(other, v_tiles[:, 1], w_imag, preferred_element_type=jnp.float32)
    x_imag = jnp.einsum(
        other, v_tiles[:, 0], w_imag, preferred_element_type=jnp.float32
    ) + jnp.einsum(other, v_tiles[:, 1], w_real, preferred_element_type=jnp.float32)
    return jnp.stack([x_real, x_imag], axis=1)


def reduce_src(partial):
    count = lax.axis_size("src")
    if count != 2:
        return lax.psum_scatter(
            partial.astype(jnp.bfloat16), "src", scatter_dimension=0, tiled=True
        )
    place = lax.axis_index("src")
    half = partial.shape[0] // 2
    mine = lax.dynamic_slice_in_dim(partial, place * half, half, 0)
    other = lax.dynamic_slice_in_dim(partial, (1 - place) * half, half, 0)
    got = lax.ppermute(other.astype(jnp.bfloat16), "src", perm=[(0, 1), (1, 0)])
    return (mine.astype(jnp.bfloat16).astype(jnp.float32) + got.astype(jnp.float32)).astype(jnp.bfloat16)


def tile_major(x):
    comps, points, width = x.shape
    return jnp.transpose(x.reshape(comps, points, width // TILE, TILE), (2, 0, 1, 3))


def tile_minor(x):
    tiles, comps, points, width = x.shape
    return jnp.transpose(x, (1, 2, 0, 3)).reshape(comps, points, tiles * width)


def per_device(focus_direct, u_factors, v_factors, tile_ranks, onset_rec, onset_src):
    parts = lax.axis_size("freq")
    place = lax.axis_index("freq")
    u_fac = u_factors[0]
    v_fac = v_factors[0]
    col_tiles = u_fac.shape[0]
    row_tiles = v_fac.shape[0]
    u_tiles = u_fac.reshape(col_tiles, 2, RANK, row_tiles, TILE)
    v_tiles = v_fac.reshape(row_tiles, 2, RANK, col_tiles, TILE)
    rank_index = jnp.arange(RANK, dtype=jnp.int32)
    mask = (rank_index[None, None, :] < tile_ranks[0][:, :, None])[:, None]
    rec_tiles = onset_rec.shape[1] // TILE
    rec_picked = window_gather(parts, onset_pieces(onset_rec, rec_tiles, parts, place))
    src_picked = window_gather(parts, onset_pieces(onset_src, col_tiles, parts, place))
    direct = tile_major(focus_direct[0])
    direct_f32 = direct.astype(jnp.float32)
    plus = direct
    minus = None
    for sweep in range(ITERS):
        z_real, z_imag = coefficients(v_tiles, mask, plus)
        partial_terms = expand_rows(u_tiles, z_real, z_imag)
        summed = reduce_src(partial_terms)
        traces = exchange(summed, parts)
        windowed = window(traces, rec_picked)
        minus = exchange_back(windowed, rec_tiles)
        minus_all = lax.all_gather(minus, "src", axis=0, tiled=True)
        adjoint = adjoint_local(u_tiles, v_tiles, mask, minus_all)
        source_traces = exchange(adjoint.astype(jnp.bfloat16), parts)
        src_windowed = window(source_traces, src_picked)
        returned = exchange_back(src_windowed, col_tiles).astype(jnp.float32)
        plus = (direct_f32 + returned).astype(jnp.bfloat16)
    return (tile_minor(plus)[None], tile_minor(minus)[None])


def solution(mesh):
    placed = (
        P("freq", None, ("groups", "vp"), "src"),
        P("freq", "src", None, None, None),
        P("freq", None, None, None, "src"),
        P("freq", None, "src"),
        P(("groups", "vp"), "src"),
        P(("groups", "vp"), "src"),
    )
    return jax.shard_map(
        per_device,
        mesh=mesh,
        in_specs=placed,
        out_specs=(
            P("freq", None, ("groups", "vp"), "src"),
            P("freq", None, ("groups", "vp"), "src"),
        ),
        check_vma=False,
    )
```

profile of v0, /device:TPU:0, one launch (start us, length us, event | category | flops | bytes accessed | tf_op | source)
XLA Modules:
  0.0 239.8 jit_solution(2109554453354944567)
XLA Ops:
  0.6 1.3 copy.161
  2.2 3.6 %copy.163 = bf16[64,8,16,256]{3,2,1,0:T(8,128)(2,1)S(1)} copy(bf16[64,8,16,256]{3,1,2,0:T(8,128)(2,1)} %bitcast.481) | data formatting | bytes 8388608
  6.9 2.1 fusion.123
  9.0 2.1 fusion.126
  11.8 2.0 fusion.125
  13.9 2.0 fusion.124
  16.1 3.7 %copy.164 = bf16[128,8,8,256]{3,2,1,0:T(8,128)(2,1)S(1)} copy(bf16[128,8,8,256]{3,1,2,0:T(8,128)(2,1)} %bitcast.482) | data formatting | bytes 8388608
  19.8 3.2 %slice_bitcast_fusion.25 = (bf16[16,32,8,256]{3,2,1,0:T(8,128)(2,1)}, bf16[16,32,8,256]{3,2,1,0:T(8,128)(2,1)}, bf16[16,1,32,8,256]{4,3,2,1,0:T(8,128)(2,1)S(1)}, bf16[16,1,32,8,256]{4,3,2,1,0:T(8,128)(2,1)S(1)}) fusion(bf16[16,2,32,8,256]{4,3,2,1,0:T(8,128)(2,1)S(1)} %bitcast.456), kind=kLoop, calls=%fused_computation.160 | loop fusion | bytes 12582912 | tf_op jit(solution)/shard_map/squeeze | solution.py:165
  23.0 1.6 copy-done.17
  24.5 1.7 copy-done.18
  26.3 1.2 fusion.3
  27.5 0.8 fusion.99
  28.3 0.8 fusion.98
  29.2 0.9 fusion.111
  30.1 0.9 fusion.113
  31.6 2.9 %collective-permute-start = (bf16[4,2,48,256]{3,2,1,0:T(8,128)(2,1)}, bf16[4,2,48,256]{3,2,1,0:T(8,128)(2,1)}, u32[]{:S(2)}, u32[]{:S(2)}) collective-permute-start(bf16[4,2,48,256]{3,2,1,0:T(8,128)(2,1)} %fusion.120), channel_id=1, source_target_pairs={{0,2},{2,0},{1,3},{3,1},{4,6},{6,4},{5,7},{7,5},{8,10},{10,8},{9,1... | collective-permute-start | bytes 589832 | tf_op jit(solution)/shard_map/ppermute | solution.py:205
  36.3 1.0 reshape.161
  38.7 1.0 collective-permute-done
  39.8 1.7 add_convert_fusion.1
  41.4 5.1 %all-to-all-start = ((bf16[4,2,48,256]{3,2,1,0:T(8,128)(2,1)}), bf16[4,2,48,256]{3,2,1,0:T(8,128)(2,1)S(1)}, u32[]{:S(2)}, u32[]{:S(2)}) async-start(bf16[4,2,48,256]{3,2,1,0:T(8,128)(2,1)} %add_convert_fusion.1), calls=%async_computation | async-start | bytes 393216 | tf_op jit(solution)/shard_map/all_to_all | solution.py:137
  48.0 5.4 %shard_map.78.matrix_ref = f32[64,1,48,256]{3,2,1,0:T(8,128)} custom-call(bf16[192,256]{1,0:T(8,128)(2,1)} %maximum_bitcast_fusion.table_ref, s32[1,48,256]{2,1,0:T(8,128)} %bitcast.495), custom_call_target="tpu_custom_call" | custom-call | tf_op jit(solution)/shard_map/pallas_call | solution.py:54
  54.1 2.8 %shard_map.79 = bf16[4,1,2,48,256]{4,3,2,1,0:T(8,128)(2,1)} custom-call(f32[64,1,48,256]{3,2,1,0:T(8,128)} %shard_map.78.matrix_ref, bf16[4,1,2,48,256]{4,3,2,1,0:T(8,128)(2,1)} %bitcast.488), custom_call_target="tpu_custom_call" | custom-call | tf_op jit(solution)/shard_map/pallas_call | solution.py:90
  56.9 5.1 %all-to-all-start.1 = ((bf16[4,2,48,256]{3,2,1,0:T(8,128)(2,1)}), bf16[4,2,48,256]{3,2,1,0:T(8,128)(2,1)S(1)}, u32[]{:S(2)}, u32[]{:S(2)}) async-start(bf16[4,2,48,256]{3,2,1,0:T(8,128)(2,1)} %bitcast.489), calls=%async_computation.1 | async-start | bytes 393216 | tf_op jit(solution)/shard_map/all_to_all | solution.py:143
  62.0 3.6 %copy.114 = bf16[16,32,8,256]{3,1,0,2:T(8,128)(2,1)} copy(bf16[16,32,8,256]{3,2,1,0:T(8,128)(2,1)} %get-tuple-element.2) | data formatting | bytes 4194304 | tf_op jit(solution)/shard_map/squeeze | solution.py:165
  65.6 1.9 copy.116
  68.3 6.3 %all_gather.6 = bf16[8,2,48,256]{3,2,1,0:T(8,128)(2,1)S(1)} all-gather(bf16[4,2,48,256]{3,2,1,0:T(8,128)(2,1)S(1)} %all-to-all-done.1), channel_id=1, replica_groups=mesh['groups'=2,'freq'=4,'src'=2,'vp'=2] {'src'}, dimensions={0}, use_global_device_ids=true | all-gather | bytes 589824 | tf_op jit(solution)/shard_map/all_gather | solution.py:244
  74.6 2.4 %fusion.133 = f32[8,48,512]{1,2,0:S(1)} fusion(bf16[8,256,512]{1,2,0:T(8,128)(2,1)} %bitcast.448, bf16[8,2,48,256]{3,2,1,0:T(8,128)(2,1)S(1)} %all_gather.6), kind=kOutput, calls=%fused_computation.127 | convolution fusion | flops 100663296 | bytes 4390912
  77.7 0.9 copy-done.13
  80.0 1.2 fusion.27
  81.6 0.9 fusion.44
  82.4 0.9 fusion.47
  83.3 0.9 fusion.89
  84.2 0.8 fusion.86
  85.1 1.0 copy.123
  86.1 4.3 %all-to-all-start.2 = ((bf16[16,2,48,256]{3,2,1,0:T(8,128)(2,1)}), bf16[16,2,48,256]{3,2,1,0:T(8,128)(2,1)}, u32[]{:S(2)}, u32[]{:S(2)}) async-start(bf16[16,2,48,256]{3,2,1,0:T(8,128)(2,1)} %copy.123), calls=%async_computation.2 | async-start | bytes 1572864 | tf_op jit(solution)/shard_map/all_to_all | solution.py:137
  90.4 2.3 copy.162
  92.6 1.0 constant_dynamic-slice_fusion.1
  94.4 17.1 %shard_map.77.matrix_ref = f32[64,4,48,256]{3,2,1,0:T(8,128)} custom-call(bf16[192,256]{1,0:T(8,128)(2,1)} %maximum_bitcast_fusion.table_ref, s32[4,48,256]{2,1,0:T(8,128)} %bitcast.494), custom_call_target="tpu_custom_call" | custom-call | tf_op jit(solution)/shard_map/pallas_call | solution.py:54
  111.5 6.3 %shard_map.80 = bf16[4,4,2,48,256]{4,3,2,1,0:T(8,128)(2,1)} custom-call(f32[64,4,48,256]{3,2,1,0:T(8,128)} %shard_map.77.matrix_ref, bf16[4,4,2,48,256]{4,3,2,1,0:T(8,128)(2,1)} %bitcast.62.spectrum_ref), custom_call_target="tpu_custom_call" | custom-call | tf_op jit(solution)/shard_map/pallas_call | solution.py:90
  117.8 21.7 %all_to_all.40 = bf16[16,2,48,256]{3,2,1,0:T(8,128)(2,1)S(1)} all-to-all(bf16[16,2,48,256]{3,2,1,0:T(8,128)(2,1)} %bitcast.485), channel_id=1, replica_groups=mesh['groups'=2,'freq'=4,'src'=2,'vp'=2] {'freq'}, dimensions={0} | all-to-all | bytes 1572864 | tf_op jit(solution)/shard_map/all_to_all | solution.py:143
  141.2 0.9 copy-done.4
  143.5 1.3 fusion.1
  145.1 0.8 fusion.101
  146.0 0.9 fusion.100
  147.5 0.9 fusion.107
  148.4 0.9 fusion.109
  149.3 1.5 collective-permute-start.1
  150.8 4.2 %collective-permute-done.1 = bf16[4,2,48,256]{3,2,1,0:T(8,128)(2,1)S(1)} collective-permute-done((bf16[4,2,48,256]{3,2,1,0:T(8,128)(2,1)S(1)}, bf16[4,2,48,256]{3,2,1,0:T(8,128)(2,1)S(1)}, u32[]{:S(2)}, u32[]{:S(2)}) %collective-permute-start.1) | collective-permute-done | bytes 196640 | tf_op jit(solution)/shard_map/ppermute | solution.py:205
  155.1 9.9 %all_to_all.41 = bf16[4,2,48,256]{3,2,1,0:T(8,128)(2,1)} all-to-all(bf16[4,2,48,256]{3,2,1,0:T(8,128)(2,1)S(1)} %add_convert_fusion), channel_id=1, replica_groups=mesh['groups'=2,'freq'=4,'src'=2,'vp'=2] {'freq'}, dimensions={0} | all-to-all | bytes 393216 | tf_op jit(solution)/shard_map/all_to_all | solution.py:137
  165.0 2.8 %shard_map.81 = bf16[4,1,2,48,256]{4,3,2,1,0:T(8,128)(2,1)} custom-call(f32[64,1,48,256]{3,2,1,0:T(8,128)} %shard_map.78.matrix_ref, bf16[4,1,2,48,256]{4,3,2,1,0:T(8,128)(2,1)} %bitcast.490), custom_call_target="tpu_custom_call" | custom-call | tf_op jit(solution)/shard_map/pallas_call | solution.py:90
  167.8 10.1 %all_to_all.42 = bf16[4,2,48,256]{3,2,1,0:T(8,128)(2,1)S(1)} all-to-all(bf16[4,2,48,256]{3,2,1,0:T(8,128)(2,1)} %bitcast.491), channel_id=1, replica_groups=mesh['groups'=2,'freq'=4,'src'=2,'vp'=2] {'freq'}, dimensions={0} | all-to-all | bytes 393216 | tf_op jit(solution)/shard_map/all_to_all | solution.py:143
  177.9 6.6 %all_gather.7 = bf16[8,2,48,256]{3,2,1,0:T(8,128)(2,1)S(1)} all-gather(bf16[4,2,48,256]{3,2,1,0:T(8,128)(2,1)S(1)} %all_to_all.42), channel_id=1, replica_groups=mesh['groups'=2,'freq'=4,'src'=2,'vp'=2] {'src'}, dimensions={0}, use_global_device_ids=true | all-gather | bytes 589824 | tf_op jit(solution)/shard_map/all_gather | solution.py:244
  184.5 2.4 %fusion.137 = f32[8,48,512]{1,2,0:S(1)} fusion(bf16[8,256,512]{1,2,0:T(8,128)(2,1)} %bitcast.449, bf16[8,2,48,256]{3,2,1,0:T(8,128)(2,1)S(1)} %all_gather.7), kind=kOutput, calls=%fused_computation.131 | convolution fusion | flops 100663296 | bytes 4390912
  187.7 0.9 copy-done.14
  189.9 1.2 fusion.23
  191.5 0.9 fusion.38
  192.4 0.9 fusion.41
  193.2 0.9 fusion.95
  194.1 0.8 fusion.92
  195.1 17.1 %all_to_all.43 = bf16[16,2,48,256]{3,2,1,0:T(8,128)(2,1)} all-to-all(bf16[16,2,48,256]{3,2,1,0:T(8,128)(2,1)S(1)} %copy.135), channel_id=1, replica_groups=mesh['groups'=2,'freq'=4,'src'=2,'vp'=2] {'freq'}, dimensions={0} | all-to-all | bytes 1572864 | tf_op jit(solution)/shard_map/all_to_all | solution.py:137
  212.2 6.3 %shard_map.82 = bf16[4,4,2,48,256]{4,3,2,1,0:T(8,128)(2,1)} custom-call(f32[64,4,48,256]{3,2,1,0:T(8,128)} %shard_map.77.matrix_ref, bf16[4,4,2,48,256]{4,3,2,1,0:T(8,128)(2,1)} %bitcast.484), custom_call_target="tpu_custom_call" | custom-call | tf_op jit(solution)/shard_map/pallas_call | solution.py:90
  218.5 3.5 %all-to-all-start.7 = ((bf16[16,2,48,256]{3,2,1,0:T(8,128)(2,1)}), bf16[16,2,48,256]{3,2,1,0:T(8,128)(2,1)S(1)}, u32[]{:S(2)}, u32[]{:S(2)}) async-start(bf16[16,2,48,256]{3,2,1,0:T(8,128)(2,1)} %bitcast.483), calls=%async_computation.7 | async-start | bytes 1572864 | tf_op jit(solution)/shard_map/all_to_all | solution.py:143
  222.9 15.0 %all-to-all-done.7 = bf16[16,2,48,256]{3,2,1,0:T(8,128)(2,1)S(1)} async-done(((bf16[16,2,48,256]{3,2,1,0:T(8,128)(2,1)}), bf16[16,2,48,256]{3,2,1,0:T(8,128)(2,1)S(1)}, u32[]{:S(2)}, u32[]{:S(2)}) %all-to-all-start.7) | async-done | bytes 786464 | tf_op jit(solution)/shard_map/all_to_all | solution.py:143
  238.6 1.2 broadcast_in_dim_reshape.6
  (87 shorter events, 20.6 us)
Async XLA Ops:
  6.2 4.9 %copy-start = (bf16[8,1,32,16,256]{4,3,2,1,0:T(8,128)(2,1)}, bf16[8,1,32,16,256]{4,3,2,1,0:T(8,128)(2,1)S(1)}, u32[]{:S(2)}) copy-start(bf16[8,1,32,16,256]{4,3,2,1,0:T(8,128)(2,1)S(1)} %get-tuple-element.7) | copy-start | bytes 6291460
  6.9 2.1 copy-start.3
  11.8 2.1 copy-start.5
  13.9 2.1 copy-start.21
  19.8 3.2 %copy-start.15 = (f32[16,48,256]{1,2,0:S(1)}, f32[16,48,256]{1,2,0}, u32[]{:S(2)}) copy-start(f32[16,48,256]{1,2,0} %fusion.123) | copy-start | bytes 2359300
  19.8 3.2 %copy-start.16 = (f32[16,48,256]{1,2,0:S(1)}, f32[16,48,256]{1,2,0}, u32[]{:S(2)}) copy-start(f32[16,48,256]{1,2,0} %fusion.126) | copy-start | bytes 2359300
  19.8 4.8 %copy-start.17 = (f32[16,48,256]{1,2,0:S(1)}, f32[16,48,256]{1,2,0}, u32[]{:S(2)}) copy-start(f32[16,48,256]{1,2,0} %fusion.125) | copy-start | bytes 2359300
  19.8 6.5 %copy-start.18 = (f32[16,48,256]{1,2,0:S(1)}, f32[16,48,256]{1,2,0}, u32[]{:S(2)}) copy-start(f32[16,48,256]{1,2,0} %fusion.124) | copy-start | bytes 2359300
  23.0 5.4 %copy-start.9 = (bf16[16,1,32,8,256]{4,3,2,1,0:T(8,128)(2,1)}, bf16[16,1,32,8,256]{4,3,2,1,0:T(8,128)(2,1)S(1)}, u32[]{:S(2)}) copy-start(bf16[16,1,32,8,256]{4,3,2,1,0:T(8,128)(2,1)S(1)} %get-tuple-element.5) | copy-start | bytes 6291460
  23.0 7.1 %copy-start.7 = (bf16[16,1,32,8,256]{4,3,2,1,0:T(8,128)(2,1)}, bf16[16,1,32,8,256]{4,3,2,1,0:T(8,128)(2,1)S(1)}, u32[]{:S(2)}) copy-start(bf16[16,1,32,8,256]{4,3,2,1,0:T(8,128)(2,1)S(1)} %get-tuple-element.4) | copy-start | bytes 6291460
  31.6 8.2 %collective-permute-start = (bf16[4,2,48,256]{3,2,1,0:T(8,128)(2,1)}, bf16[4,2,48,256]{3,2,1,0:T(8,128)(2,1)}, u32[]{:S(2)}, u32[]{:S(2)}) collective-permute-start(bf16[4,2,48,256]{3,2,1,0:T(8,128)(2,1)} %fusion.120), channel_id=1, source_target_pairs={{0,2},{2,0},{1,3},{3,1},{4,6},{6,4},{5,7},{7,5},{8,10},{10,8},{9,1... | collective-permute-start | bytes 589832 | tf_op jit(solution)/shard_map/ppermute | solution.py:205
  41.4 12.0 %all-to-all-start = ((bf16[4,2,48,256]{3,2,1,0:T(8,128)(2,1)}), bf16[4,2,48,256]{3,2,1,0:T(8,128)(2,1)S(1)}, u32[]{:S(2)}, u32[]{:S(2)}) async-start(bf16[4,2,48,256]{3,2,1,0:T(8,128)(2,1)} %add_convert_fusion.1), calls=%async_computation | async-start | bytes 393216 | tf_op jit(solution)/shard_map/all_to_all | solution.py:137
  53.4 0.7 copy-start.20
  56.9 11.3 %all-to-all-start.1 = ((bf16[4,2,48,256]{3,2,1,0:T(8,128)(2,1)}), bf16[4,2,48,256]{3,2,1,0:T(8,128)(2,1)S(1)}, u32[]{:S(2)}, u32[]{:S(2)}) async-start(bf16[4,2,48,256]{3,2,1,0:T(8,128)(2,1)} %bitcast.489), calls=%async_computation.1 | async-start | bytes 393216 | tf_op jit(solution)/shard_map/all_to_all | solution.py:143
  62.0 3.6 %copy-start.19 = (bf16[16,32,8,256]{3,2,1,0:T(8,128)(2,1)S(1)}, bf16[16,32,8,256]{3,2,1,0:T(8,128)(2,1)}, u32[]{:S(2)}) copy-start(bf16[16,32,8,256]{3,2,1,0:T(8,128)(2,1)} %get-tuple-element.3) | copy-start | bytes 6291460
  74.6 2.4 %copy-start.11 = (bf16[16,32,8,256]{3,1,0,2:T(8,128)(2,1)S(1)}, bf16[16,32,8,256]{3,1,0,2:T(8,128)(2,1)}, u32[]{:S(2)}) copy-start(bf16[16,32,8,256]{3,1,0,2:T(8,128)(2,1)} %copy.114) | copy-start | bytes 6291460
  77.0 1.6 copy-start.13
  80.0 1.6 copy-start.1
  86.1 25.5 %all-to-all-start.2 = ((bf16[16,2,48,256]{3,2,1,0:T(8,128)(2,1)}), bf16[16,2,48,256]{3,2,1,0:T(8,128)(2,1)}, u32[]{:S(2)}, u32[]{:S(2)}) async-start(bf16[16,2,48,256]{3,2,1,0:T(8,128)(2,1)} %copy.123), calls=%async_computation.2 | async-start | bytes 1572864 | tf_op jit(solution)/shard_map/all_to_all | solution.py:137
  117.8 22.0 %copy-start.6 = (bf16[8,1,32,16,256]{4,2,0,3,1:T(8,128)(2,1)S(1)}, bf16[8,1,32,16,256]{4,2,0,3,1:T(8,128)(2,1)}, u32[]{:S(2)}) copy-start(bf16[8,1,32,16,256]{4,2,0,3,1:T(8,128)(2,1)} %copy-done.5) | copy-start | bytes 6291460
  140.5 1.6 copy-start.4
  143.5 1.6 copy-start.10
  145.9 1.6 copy-start.8
  149.3 5.7 %collective-permute-start.1 = (bf16[4,2,48,256]{3,2,1,0:T(8,128)(2,1)S(1)}, bf16[4,2,48,256]{3,2,1,0:T(8,128)(2,1)S(1)}, u32[]{:S(2)}, u32[]{:S(2)}) collective-permute-start(bf16[4,2,48,256]{3,2,1,0:T(8,128)(2,1)S(1)} %fusion.116), channel_id=1, source_target_pairs={{0,2},{2,0},{1,3},{3,1},{4,6},{6,4},{5,7},{7,5},{8,10},{10,8},{9,1... | collective-permute-start | bytes 589832 | tf_op jit(solution)/shard_map/ppermute | solution.py:205
  184.5 2.4 %copy-start.12 = (bf16[16,32,8,256]{3,1,0,2:T(8,128)(2,1)S(1)}, bf16[16,32,8,256]{3,1,0,2:T(8,128)(2,1)}, u32[]{:S(2)}) copy-start(bf16[16,32,8,256]{3,1,0,2:T(8,128)(2,1)} %copy.114) | copy-start | bytes 6291460
  187.0 1.6 copy-start.14
  189.9 1.6 copy-start.2
  218.5 19.5 %all-to-all-start.7 = ((bf16[16,2,48,256]{3,2,1,0:T(8,128)(2,1)}), bf16[16,2,48,256]{3,2,1,0:T(8,128)(2,1)S(1)}, u32[]{:S(2)}, u32[]{:S(2)}) async-start(bf16[16,2,48,256]{3,2,1,0:T(8,128)(2,1)} %bitcast.483), calls=%async_computation.7 | async-start | bytes 1572864 | tf_op jit(solution)/shard_map/all_to_all | solution.py:143
where the time goes:
time: 242 us; the launch traced here: 240 us
  blocking collectives  71.6 us (30%)
  Pallas kernels  40.8 us (17%)
  local copies, waits for them, and re-layouts  38 us (16%)
  matrix products  33.6 us (14%)
  starting transfers between devices  22.5 us (9%)
  waiting for transfers between devices  21.1 us (9%)
  other arithmetic  11.1 us (5%)
    all_to_all x2, blocking collectives, exchange_back(): got = lax.all_to_all(flat, 'freq', split_axis=0, concat_axis=0, tiled=True)  31.8 us
    all_to_all x2, blocking collectives, exchange(): lax.all_to_all(pieces, 'freq', split_axis=0, concat_axis=0, tiled=True)  26.9 us
    pallas_call x2, Pallas kernels, window_gather(): pl.pallas_call(gather_kernel, grid=(blocks, points // rows), in_specs=[pl...  22.6 us
    unnamed x52, local copies, waits for them, and re-layouts  22.2 us
    unnamed x16, matrix products  19.9 us
    pallas_call x4, Pallas kernels, window(): pl.pallas_call(window_kernel, grid=(blocks,), in_specs=[pl.BlockSpec((siz...  18.2 us
    all_to_all x2, waiting for transfers between devices, exchange_back(): got = lax.all_to_all(flat, 'freq', split_axis=0, concat_axis=0, tiled=True)  15.8 us
    all_gather x2, blocking collectives, per_device(): minus_all = lax.all_gather(minus, 'src', axis=0, tiled=True)  12.9 us
  transfers between devices with their start and end apart: 6, of which 4 were waited for; matrix products, arithmetic and copies ran while one was open for 7% of the time, Pallas kernels for 9%

commit v1 on v0

--- a/solution.py
+++ b/solution.py
@@ -34,7 +34,7 @@
         place = jnp.clip(onset_ref[0, row : row + 1, :], 0, NT) - 1
         pick = (sample == place).astype(jnp.bfloat16)
         parts = jnp.dot(table_ref[...], pick, preferred_element_type=jnp.float32)
-        out_ref[:, 0, row, :] = (parts[:size] + parts[size : 2 * size]) + parts[2 * size :]
+        out_ref[:, 0, row, :] = parts[:size] + parts[size:]
 
 
 def window_gather(count, onset):
@@ -46,16 +46,15 @@
     table = jnp.cumsum(terms.reshape(NT, size), axis=0)
     high = table.astype(jnp.bfloat16)
     rest = table - high.astype(jnp.float32)
-    middle = rest.astype(jnp.bfloat16)
-    low = (rest - middle.astype(jnp.float32)).astype(jnp.bfloat16)
-    stacked = jnp.concatenate([high, middle, low], axis=1).T
+    low = rest.astype(jnp.bfloat16)
+    stacked = jnp.concatenate([high, low], axis=1).T
     blocks, points, width = onset.shape
     rows = 8
     return pl.pallas_call(
         gather_kernel,
         grid=(blocks, points // rows),
         in_specs=[
-            pl.BlockSpec((3 * size, NT), lambda b, r: (0, 0)),
+            pl.BlockSpec((2 * size, NT), lambda b, r: (0, 0)),
             pl.BlockSpec((1, rows, width), lambda b, r: (b, r, 0)),
         ],
         out_specs=pl.BlockSpec((size, 1, rows, width), lambda b, r: (0, b, r, 0)),

time: 242 us -> 242 us (level)
  no operation moved by 1% of the time
where the time goes in v1:
time: 242 us; the launch traced here: 239 us
  blocking collectives  71.6 us (30%)
  Pallas kernels  40 us (17%)
  local copies, waits for them, and re-layouts  37.9 us (16%)
  matrix products  33.6 us (14%)
  starting transfers between devices  22.7 us (9%)
  waiting for transfers between devices  21.1 us (9%)
  other arithmetic  11.1 us (5%)
    all_to_all x2, blocking collectives, exchange_back(): got = lax.all_to_all(flat, 'freq', split_axis=0, concat_axis=0, tiled=True)  31.8 us
    all_to_all x2, blocking collectives, exchange(): lax.all_to_all(pieces, 'freq', split_axis=0, concat_axis=0, tiled=True)  26.9 us
    unnamed x52, local copies, waits for them, and re-layouts  22.2 us
    pallas_call x2, Pallas kernels, window_gather(): pl.pallas_call(gather_kernel, grid=(blocks, points // rows), in_specs=[pl...  21.8 us
    unnamed x16, matrix products  19.9 us
    pallas_call x4, Pallas kernels, window(): pl.pallas_call(window_kernel, grid=(blocks,), in_specs=[pl.BlockSpec((siz...  18.2 us
    all_to_all x2, waiting for transfers between devices, exchange_back(): got = lax.all_to_all(flat, 'freq', split_axis=0, concat_axis=0, tiled=True)  15.9 us
    all_gather x2, blocking collectives, per_device(): minus_all = lax.all_gather(minus, 'src', axis=0, tiled=True)  12.9 us
  transfers between devices with their start and end apart: 6, of which 4 were waited for; matrix products, arithmetic and copies ran while one was open for 7% of the time, Pallas kernels for 9%

profile of v1, /device:TPU:0, one launch (start us, length us, event | category | flops | bytes accessed | tf_op | source)
XLA Modules:
  0.0 239.1 jit_solution(1396094471038442662)
XLA Ops:
  0.6 1.3 copy.161
  2.2 3.6 %copy.163 = bf16[64,8,16,256]{3,2,1,0:T(8,128)(2,1)S(1)} copy(bf16[64,8,16,256]{3,1,2,0:T(8,128)(2,1)} %bitcast.469) | data formatting | bytes 8388608
  6.9 2.1 fusion.123
  9.0 2.1 fusion.126
  11.8 2.0 fusion.125
  13.9 2.1 fusion.124
  16.1 3.7 %copy.164 = bf16[128,8,8,256]{3,2,1,0:T(8,128)(2,1)S(1)} copy(bf16[128,8,8,256]{3,1,2,0:T(8,128)(2,1)} %bitcast.470) | data formatting | bytes 8388608
  19.8 3.2 %slice_bitcast_fusion.25 = (bf16[16,32,8,256]{3,2,1,0:T(8,128)(2,1)}, bf16[16,32,8,256]{3,2,1,0:T(8,128)(2,1)}, bf16[16,1,32,8,256]{4,3,2,1,0:T(8,128)(2,1)S(1)}, bf16[16,1,32,8,256]{4,3,2,1,0:T(8,128)(2,1)S(1)}) fusion(bf16[16,2,32,8,256]{4,3,2,1,0:T(8,128)(2,1)S(1)} %bitcast.444), kind=kLoop, calls=%fused_computation.159 | loop fusion | bytes 12582912 | tf_op jit(solution)/shard_map/squeeze | solution.py:164
  23.0 1.6 copy-done.17
  24.5 1.7 copy-done.18
  26.3 1.2 fusion.3
  27.5 0.8 fusion.99
  28.3 0.8 fusion.98
  29.2 0.9 fusion.111
  30.1 0.9 fusion.113
  31.6 2.9 %collective-permute-start = (bf16[4,2,48,256]{3,2,1,0:T(8,128)(2,1)}, bf16[4,2,48,256]{3,2,1,0:T(8,128)(2,1)}, u32[]{:S(2)}, u32[]{:S(2)}) collective-permute-start(bf16[4,2,48,256]{3,2,1,0:T(8,128)(2,1)} %fusion.120), channel_id=1, source_target_pairs={{0,2},{2,0},{1,3},{3,1},{4,6},{6,4},{5,7},{7,5},{8,10},{10,8},{9,1... | collective-permute-start | bytes 589832 | tf_op jit(solution)/shard_map/ppermute | solution.py:204
  36.2 1.0 reshape.161
  38.7 1.1 collective-permute-done
  39.8 1.7 add_convert_fusion.1
  41.4 5.1 %all-to-all-start = ((bf16[4,2,48,256]{3,2,1,0:T(8,128)(2,1)}), bf16[4,2,48,256]{3,2,1,0:T(8,128)(2,1)S(1)}, u32[]{:S(2)}, u32[]{:S(2)}) async-start(bf16[4,2,48,256]{3,2,1,0:T(8,128)(2,1)} %add_convert_fusion.1), calls=%async_computation | async-start | bytes 393216 | tf_op jit(solution)/shard_map/all_to_all | solution.py:136
  47.9 5.2 %shard_map.78.matrix_ref = f32[64,1,48,256]{3,2,1,0:T(8,128)} custom-call(bf16[128,256]{1,0:T(8,128)(2,1)} %maximum_bitcast_fusion.table_ref, s32[1,48,256]{2,1,0:T(8,128)} %bitcast.483), custom_call_target="tpu_custom_call" | custom-call | tf_op jit(solution)/shard_map/pallas_call | solution.py:53
  53.8 2.8 %shard_map.79 = bf16[4,1,2,48,256]{4,3,2,1,0:T(8,128)(2,1)} custom-call(f32[64,1,48,256]{3,2,1,0:T(8,128)} %shard_map.78.matrix_ref, bf16[4,1,2,48,256]{4,3,2,1,0:T(8,128)(2,1)} %bitcast.476), custom_call_target="tpu_custom_call" | custom-call | tf_op jit(solution)/shard_map/pallas_call | solution.py:89
  56.6 5.1 %all-to-all-start.1 = ((bf16[4,2,48,256]{3,2,1,0:T(8,128)(2,1)}), bf16[4,2,48,256]{3,2,1,0:T(8,128)(2,1)S(1)}, u32[]{:S(2)}, u32[]{:S(2)}) async-start(bf16[4,2,48,256]{3,2,1,0:T(8,128)(2,1)} %bitcast.477), calls=%async_computation.1 | async-start | bytes 393216 | tf_op jit(solution)/shard_map/all_to_all | solution.py:142
  61.7 3.5 %copy.114 = bf16[16,32,8,256]{3,1,0,2:T(8,128)(2,1)} copy(bf16[16,32,8,256]{3,2,1,0:T(8,128)(2,1)} %get-tuple-element.2) | data formatting | bytes 4194304 | tf_op jit(solution)/shard_map/squeeze | solution.py:164
  65.3 1.9 copy.116
  68.0 6.3 %all_gather.6 = bf16[8,2,48,256]{3,2,1,0:T(8,128)(2,1)S(1)} all-gather(bf16[4,2,48,256]{3,2,1,0:T(8,128)(2,1)S(1)} %all-to-all-done.1), channel_id=1, replica_groups=mesh['groups'=2,'freq'=4,'src'=2,'vp'=2] {'src'}, dimensions={0}, use_global_device_ids=true | all-gather | bytes 589824 | tf_op jit(solution)/shard_map/all_gather | solution.py:243
  74.3 2.4 %fusion.133 = f32[8,48,512]{1,2,0:S(1)} fusion(bf16[8,256,512]{1,2,0:T(8,128)(2,1)} %bitcast.436, bf16[8,2,48,256]{3,2,1,0:T(8,128)(2,1)S(1)} %all_gather.6), kind=kOutput, calls=%fused_computation.127 | convolution fusion | flops 100663296 | bytes 4390912
  77.4 0.9 copy-done.13
  79.7 1.2 fusion.27
  81.3 0.9 fusion.44
  82.1 0.9 fusion.47
  83.0 0.9 fusion.89
  83.9 0.8 fusion.86
  84.8 1.0 copy.123
  85.8 4.5 %all-to-all-start.2 = ((bf16[16,2,48,256]{3,2,1,0:T(8,128)(2,1)}), bf16[16,2,48,256]{3,2,1,0:T(8,128)(2,1)}, u32[]{:S(2)}, u32[]{:S(2)}) async-start(bf16[16,2,48,256]{3,2,1,0:T(8,128)(2,1)} %copy.123), calls=%async_computation.2 | async-start | bytes 1572864 | tf_op jit(solution)/shard_map/all_to_all | solution.py:136
  90.3 2.3 copy.162
  92.5 1.0 constant_dynamic-slice_fusion.1
  94.3 16.6 %shard_map.77.matrix_ref = f32[64,4,48,256]{3,2,1,0:T(8,128)} custom-call(bf16[128,256]{1,0:T(8,128)(2,1)} %maximum_bitcast_fusion.table_ref, s32[4,48,256]{2,1,0:T(8,128)} %bitcast.482), custom_call_target="tpu_custom_call" | custom-call | tf_op jit(solution)/shard_map/pallas_call | solution.py:53
  110.8 6.3 %shard_map.80 = bf16[4,4,2,48,256]{4,3,2,1,0:T(8,128)(2,1)} custom-call(f32[64,4,48,256]{3,2,1,0:T(8,128)} %shard_map.77.matrix_ref, bf16[4,4,2,48,256]{4,3,2,1,0:T(8,128)(2,1)} %bitcast.62.spectrum_ref), custom_call_target="tpu_custom_call" | custom-call | tf_op jit(solution)/shard_map/pallas_call | solution.py:89
  117.1 21.6 %all_to_all.40 = bf16[16,2,48,256]{3,2,1,0:T(8,128)(2,1)S(1)} all-to-all(bf16[16,2,48,256]{3,2,1,0:T(8,128)(2,1)} %bitcast.473), channel_id=1, replica_groups=mesh['groups'=2,'freq'=4,'src'=2,'vp'=2] {'freq'}, dimensions={0} | all-to-all | bytes 1572864 | tf_op jit(solution)/shard_map/all_to_all | solution.py:142
  140.5 0.9 copy-done.4
  142.8 1.3 fusion.1
  144.4 0.8 fusion.101
  145.3 0.9 fusion.100
  146.8 0.9 fusion.107
  147.7 0.9 fusion.109
  148.6 1.6 collective-permute-start.1
  150.2 4.2 %collective-permute-done.1 = bf16[4,2,48,256]{3,2,1,0:T(8,128)(2,1)S(1)} collective-permute-done((bf16[4,2,48,256]{3,2,1,0:T(8,128)(2,1)S(1)}, bf16[4,2,48,256]{3,2,1,0:T(8,128)(2,1)S(1)}, u32[]{:S(2)}, u32[]{:S(2)}) %collective-permute-start.1) | collective-permute-done | bytes 196640 | tf_op jit(solution)/shard_map/ppermute | solution.py:204
  154.4 9.9 %all_to_all.41 = bf16[4,2,48,256]{3,2,1,0:T(8,128)(2,1)} all-to-all(bf16[4,2,48,256]{3,2,1,0:T(8,128)(2,1)S(1)} %add_convert_fusion), channel_id=1, replica_groups=mesh['groups'=2,'freq'=4,'src'=2,'vp'=2] {'freq'}, dimensions={0} | all-to-all | bytes 393216 | tf_op jit(solution)/shard_map/all_to_all | solution.py:136
  164.3 2.8 %shard_map.81 = bf16[4,1,2,48,256]{4,3,2,1,0:T(8,128)(2,1)} custom-call(f32[64,1,48,256]{3,2,1,0:T(8,128)} %shard_map.78.matrix_ref, bf16[4,1,2,48,256]{4,3,2,1,0:T(8,128)(2,1)} %bitcast.478), custom_call_target="tpu_custom_call" | custom-call | tf_op jit(solution)/shard_map/pallas_call | solution.py:89
  167.1 10.1 %all_to_all.42 = bf16[4,2,48,256]{3,2,1,0:T(8,128)(2,1)S(1)} all-to-all(bf16[4,2,48,256]{3,2,1,0:T(8,128)(2,1)} %bitcast.479), channel_id=1, replica_groups=mesh['groups'=2,'freq'=4,'src'=2,'vp'=2] {'freq'}, dimensions={0} | all-to-all | bytes 393216 | tf_op jit(solution)/shard_map/all_to_all | solution.py:142
  177.2 6.6 %all_gather.7 = bf16[8,2,48,256]{3,2,1,0:T(8,128)(2,1)S(1)} all-gather(bf16[4,2,48,256]{3,2,1,0:T(8,128)(2,1)S(1)} %all_to_all.42), channel_id=1, replica_groups=mesh['groups'=2,'freq'=4,'src'=2,'vp'=2] {'src'}, dimensions={0}, use_global_device_ids=true | all-gather | bytes 589824 | tf_op jit(solution)/shard_map/all_gather | solution.py:243
  183.8 2.4 %fusion.137 = f32[8,48,512]{1,2,0:S(1)} fusion(bf16[8,256,512]{1,2,0:T(8,128)(2,1)} %bitcast.437, bf16[8,2,48,256]{3,2,1,0:T(8,128)(2,1)S(1)} %all_gather.7), kind=kOutput, calls=%fused_computation.131 | convolution fusion | flops 100663296 | bytes 4390912
  187.0 0.9 copy-done.14
  189.2 1.2 fusion.23
  190.8 0.9 fusion.38
  191.7 0.9 fusion.41
  192.5 0.9 fusion.95
  193.4 0.8 fusion.92
  194.4 17.1 %all_to_all.43 = bf16[16,2,48,256]{3,2,1,0:T(8,128)(2,1)} all-to-all(bf16[16,2,48,256]{3,2,1,0:T(8,128)(2,1)S(1)} %copy.135), channel_id=1, replica_groups=mesh['groups'=2,'freq'=4,'src'=2,'vp'=2] {'freq'}, dimensions={0} | all-to-all | bytes 1572864 | tf_op jit(solution)/shard_map/all_to_all | solution.py:136
  211.5 6.3 %shard_map.82 = bf16[4,4,2,48,256]{4,3,2,1,0:T(8,128)(2,1)} custom-call(f32[64,4,48,256]{3,2,1,0:T(8,128)} %shard_map.77.matrix_ref, bf16[4,4,2,48,256]{4,3,2,1,0:T(8,128)(2,1)} %bitcast.472), custom_call_target="tpu_custom_call" | custom-call | tf_op jit(solution)/shard_map/pallas_call | solution.py:89
  217.8 3.5 %all-to-all-start.7 = ((bf16[16,2,48,256]{3,2,1,0:T(8,128)(2,1)}), bf16[16,2,48,256]{3,2,1,0:T(8,128)(2,1)S(1)}, u32[]{:S(2)}, u32[]{:S(2)}) async-start(bf16[16,2,48,256]{3,2,1,0:T(8,128)(2,1)} %bitcast.471), calls=%async_computation.7 | async-start | bytes 1572864 | tf_op jit(solution)/shard_map/all_to_all | solution.py:142
  222.2 15.0 %all-to-all-done.7 = bf16[16,2,48,256]{3,2,1,0:T(8,128)(2,1)S(1)} async-done(((bf16[16,2,48,256]{3,2,1,0:T(8,128)(2,1)}), bf16[16,2,48,256]{3,2,1,0:T(8,128)(2,1)S(1)}, u32[]{:S(2)}, u32[]{:S(2)}) %all-to-all-start.7) | async-done | bytes 786464 | tf_op jit(solution)/shard_map/all_to_all | solution.py:142
  237.9 1.2 broadcast_in_dim_reshape.6
  (87 shorter events, 20.5 us)
Async XLA Ops:
  6.2 4.9 %copy-start = (bf16[8,1,32,16,256]{4,3,2,1,0:T(8,128)(2,1)}, bf16[8,1,32,16,256]{4,3,2,1,0:T(8,128)(2,1)S(1)}, u32[]{:S(2)}) copy-start(bf16[8,1,32,16,256]{4,3,2,1,0:T(8,128)(2,1)S(1)} %get-tuple-element.7) | copy-start | bytes 6291460
  6.9 2.1 copy-start.3
  11.8 2.0 copy-start.5
  13.9 2.1 copy-start.21
  19.8 3.2 %copy-start.15 = (f32[16,48,256]{1,2,0:S(1)}, f32[16,48,256]{1,2,0}, u32[]{:S(2)}) copy-start(f32[16,48,256]{1,2,0} %fusion.123) | copy-start | bytes 2359300
  19.8 3.2 %copy-start.16 = (f32[16,48,256]{1,2,0:S(1)}, f32[16,48,256]{1,2,0}, u32[]{:S(2)}) copy-start(f32[16,48,256]{1,2,0} %fusion.126) | copy-start | bytes 2359300
  19.8 4.8 %copy-start.17 = (f32[16,48,256]{1,2,0:S(1)}, f32[16,48,256]{1,2,0}, u32[]{:S(2)}) copy-start(f32[16,48,256]{1,2,0} %fusion.125) | copy-start | bytes 2359300
  19.8 6.5 %copy-start.18 = (f32[16,48,256]{1,2,0:S(1)}, f32[16,48,256]{1,2,0}, u32[]{:S(2)}) copy-start(f32[16,48,256]{1,2,0} %fusion.124) | copy-start | bytes 2359300
  23.0 5.4 %copy-start.9 = (bf16[16,1,32,8,256]{4,3,2,1,0:T(8,128)(2,1)}, bf16[16,1,32,8,256]{4,3,2,1,0:T(8,128)(2,1)S(1)}, u32[]{:S(2)}) copy-start(bf16[16,1,32,8,256]{4,3,2,1,0:T(8,128)(2,1)S(1)} %get-tuple-element.5) | copy-start | bytes 6291460
  23.0 7.1 %copy-start.7 = (bf16[16,1,32,8,256]{4,3,2,1,0:T(8,128)(2,1)}, bf16[16,1,32,8,256]{4,3,2,1,0:T(8,128)(2,1)S(1)}, u32[]{:S(2)}) copy-start(bf16[16,1,32,8,256]{4,3,2,1,0:T(8,128)(2,1)S(1)} %get-tuple-element.4) | copy-start | bytes 6291460
  31.6 8.1 %collective-permute-start = (bf16[4,2,48,256]{3,2,1,0:T(8,128)(2,1)}, bf16[4,2,48,256]{3,2,1,0:T(8,128)(2,1)}, u32[]{:S(2)}, u32[]{:S(2)}) collective-permute-start(bf16[4,2,48,256]{3,2,1,0:T(8,128)(2,1)} %fusion.120), channel_id=1, source_target_pairs={{0,2},{2,0},{1,3},{3,1},{4,6},{6,4},{5,7},{7,5},{8,10},{10,8},{9,1... | collective-permute-start | bytes 589832 | tf_op jit(solution)/shard_map/ppermute | solution.py:204
  41.4 11.7 %all-to-all-start = ((bf16[4,2,48,256]{3,2,1,0:T(8,128)(2,1)}), bf16[4,2,48,256]{3,2,1,0:T(8,128)(2,1)S(1)}, u32[]{:S(2)}, u32[]{:S(2)}) async-start(bf16[4,2,48,256]{3,2,1,0:T(8,128)(2,1)} %add_convert_fusion.1), calls=%async_computation | async-start | bytes 393216 | tf_op jit(solution)/shard_map/all_to_all | solution.py:136
  53.1 0.7 copy-start.20
  56.6 11.3 %all-to-all-start.1 = ((bf16[4,2,48,256]{3,2,1,0:T(8,128)(2,1)}), bf16[4,2,48,256]{3,2,1,0:T(8,128)(2,1)S(1)}, u32[]{:S(2)}, u32[]{:S(2)}) async-start(bf16[4,2,48,256]{3,2,1,0:T(8,128)(2,1)} %bitcast.477), calls=%async_computation.1 | async-start | bytes 393216 | tf_op jit(solution)/shard_map/all_to_all | solution.py:142
  61.7 3.6 %copy-start.19 = (bf16[16,32,8,256]{3,2,1,0:T(8,128)(2,1)S(1)}, bf16[16,32,8,256]{3,2,1,0:T(8,128)(2,1)}, u32[]{:S(2)}) copy-start(bf16[16,32,8,256]{3,2,1,0:T(8,128)(2,1)} %get-tuple-element.3) | copy-start | bytes 6291460
  74.3 2.4 %copy-start.11 = (bf16[16,32,8,256]{3,1,0,2:T(8,128)(2,1)S(1)}, bf16[16,32,8,256]{3,1,0,2:T(8,128)(2,1)}, u32[]{:S(2)}) copy-start(bf16[16,32,8,256]{3,1,0,2:T(8,128)(2,1)} %copy.114) | copy-start | bytes 6291460
  76.7 1.6 copy-start.13
  79.7 1.6 copy-start.1
  85.8 25.1 %all-to-all-start.2 = ((bf16[16,2,48,256]{3,2,1,0:T(8,128)(2,1)}), bf16[16,2,48,256]{3,2,1,0:T(8,128)(2,1)}, u32[]{:S(2)}, u32[]{:S(2)}) async-start(bf16[16,2,48,256]{3,2,1,0:T(8,128)(2,1)} %copy.123), calls=%async_computation.2 | async-start | bytes 1572864 | tf_op jit(solution)/shard_map/all_to_all | solution.py:136
  117.1 22.0 %copy-start.6 = (bf16[8,1,32,16,256]{4,2,0,3,1:T(8,128)(2,1)S(1)}, bf16[8,1,32,16,256]{4,2,0,3,1:T(8,128)(2,1)}, u32[]{:S(2)}) copy-start(bf16[8,1,32,16,256]{4,2,0,3,1:T(8,128)(2,1)} %copy-done.5) | copy-start | bytes 6291460
  139.8 1.6 copy-start.4
  142.8 1.6 copy-start.10
  145.2 1.6 copy-start.8
  148.6 5.7 %collective-permute-start.1 = (bf16[4,2,48,256]{3,2,1,0:T(8,128)(2,1)S(1)}, bf16[4,2,48,256]{3,2,1,0:T(8,128)(2,1)S(1)}, u32[]{:S(2)}, u32[]{:S(2)}) collective-permute-start(bf16[4,2,48,256]{3,2,1,0:T(8,128)(2,1)S(1)} %fusion.116), channel_id=1, source_target_pairs={{0,2},{2,0},{1,3},{3,1},{4,6},{6,4},{5,7},{7,5},{8,10},{10,8},{9,1... | collective-permute-start | bytes 589832 | tf_op jit(solution)/shard_map/ppermute | solution.py:204
  183.8 2.4 %copy-start.12 = (bf16[16,32,8,256]{3,1,0,2:T(8,128)(2,1)S(1)}, bf16[16,32,8,256]{3,1,0,2:T(8,128)(2,1)}, u32[]{:S(2)}) copy-start(bf16[16,32,8,256]{3,1,0,2:T(8,128)(2,1)} %copy.114) | copy-start | bytes 6291460
  186.3 1.6 copy-start.14
  189.2 1.6 copy-start.2
  217.8 19.5 %all-to-all-start.7 = ((bf16[16,2,48,256]{3,2,1,0:T(8,128)(2,1)}), bf16[16,2,48,256]{3,2,1,0:T(8,128)(2,1)S(1)}, u32[]{:S(2)}, u32[]{:S(2)}) async-start(bf16[16,2,48,256]{3,2,1,0:T(8,128)(2,1)} %bitcast.471), calls=%async_computation.7 | async-start | bytes 1572864 | tf_op jit(solution)/shard_map/all_to_all | solution.py:142

commit v2 on v1

--- a/solution.py
+++ b/solution.py
@@ -231,9 +231,9 @@
     src_picked = window_gather(parts, onset_pieces(onset_src, col_tiles, parts, place))
     direct = tile_major(focus_direct[0])
     direct_f32 = direct.astype(jnp.float32)
-    plus = direct
-    minus = None
-    for sweep in range(ITERS):
+
+    def sweep(_, state):
+        plus, _ = state
         z_real, z_imag = coefficients(v_tiles, mask, plus)
         partial_terms = expand_rows(u_tiles, z_real, z_imag)
         summed = reduce_src(partial_terms)
@@ -245,7 +245,10 @@
         source_traces = exchange(adjoint.astype(jnp.bfloat16), parts)
         src_windowed = window(source_traces, src_picked)
         returned = exchange_back(src_windowed, col_tiles).astype(jnp.float32)
-        plus = (direct_f32 + returned).astype(jnp.bfloat16)
+        return ((direct_f32 + returned).astype(jnp.bfloat16), minus)
+
+    start = jnp.zeros((rec_tiles,) + direct.shape[1:], jnp.bfloat16)
+    plus, minus = lax.fori_loop(0, ITERS, sweep, (direct, start))
     return (tile_minor(plus)[None], tile_minor(minus)[None])
 
 

time: 242 us -> 252 us (1.041)
  waiting for transfers between devices: 21.1 us -> 49 us
  matrix products: 33.6 us -> 18.6 us
  starting transfers between devices: 22.7 us -> 18.4 us
    all_to_all x2 -> x4, blocking collectives: 26.9 us -> 60.1 us  [exchange(): lax.all_to_all(pieces, 'freq', split_axis=0, concat_axis=0, tiled=True)]
    all_to_all x2 -> x0, blocking collectives: 31.8 us -> none  [exchange_back(): got = lax.all_to_all(flat, 'freq', split_axis=0, concat_axis=0, tiled=True)]
    all_to_all x2 -> x4, waiting for transfers between devices: 15.9 us -> 39.3 us  [exchange_back(): got = lax.all_to_all(flat, 'freq', split_axis=0, concat_axis=0, tiled=True)]
    unnamed x16 -> x0, matrix products: 19.9 us -> none
    while x0 -> x16, matrix products: none -> 11 us
    all_to_all x2 -> x0, starting transfers between devices: 9.63 us -> none  [exchange(): lax.all_to_all(pieces, 'freq', split_axis=0, concat_axis=0, tiled=True)]
    unnamed x52 -> x23, local copies, waits for them, and re-layouts: 22.2 us -> 16.1 us
    while x0 -> x24, local copies, waits for them, and re-layouts: none -> 5.64 us
  transfers between devices with their start and end apart: 6 -> 6, of which waited for: 4 -> 6; matrix products, arithmetic and copies ran while one was open for 7% -> 4% of each run, Pallas kernels for 9% -> 0%
where the time goes in v2:
time: 252 us; the launch traced here: 250 us
  blocking collectives  72.7 us (29%)
  waiting for transfers between devices  49 us (19%)
  local copies, waits for them, and re-layouts  39.4 us (16%)
  Pallas kernels  38.1 us (15%)
  matrix products  18.6 us (7%)
  starting transfers between devices  18.4 us (7%)
  other arithmetic  12.2 us (5%)
    all_to_all x4, blocking collectives, exchange(): lax.all_to_all(pieces, 'freq', split_axis=0, concat_axis=0, tiled=True)  60.1 us
    all_to_all x4, waiting for transfers between devices, exchange_back(): got = lax.all_to_all(flat, 'freq', split_axis=0, concat_axis=0, tiled=True)  39.3 us
    pallas_call x2, Pallas kernels, window_gather(): pl.pallas_call(gather_kernel, grid=(blocks, points // rows), in_specs=[pl...  21.9 us
    pallas_call x4, Pallas kernels, window(): pl.pallas_call(window_kernel, grid=(blocks,), in_specs=[pl.BlockSpec((siz...  16.3 us
    unnamed x23, local copies, waits for them, and re-layouts  16.1 us
    all_to_all x4, starting transfers between devices, exchange_back(): got = lax.all_to_all(flat, 'freq', split_axis=0, concat_axis=0, tiled=True)  14 us
    all_gather x2, blocking collectives, sweep(): minus_all = lax.all_gather(minus, 'src', axis=0, tiled=True)  12.7 us
    while x16, matrix products  11 us
  transfers between devices with their start and end apart: 6, of which 6 were waited for; matrix products, arithmetic and copies ran while one was open for 4% of the time, Pallas kernels for 0%

profile of v2, /device:TPU:0, one launch (start us, length us, event | category | flops | bytes accessed | tf_op | source)
XLA Modules:
  0.0 249.8 jit_solution(10187739289152759815)
XLA Ops:
  2.6 1.4 copy.111
  4.0 0.7 copy.143
  4.7 16.6 %shard_map.78 = f32[64,4,48,256]{3,2,1,0:T(8,128)} custom-call(bf16[128,256]{1,0:T(8,128)(2,1)} %maximum_bitcast_fusion.table_ref, s32[4,48,256]{2,1,0:T(8,128)} %bitcast.398), custom_call_target="tpu_custom_call" | custom-call | tf_op jit(solution)/shard_map/pallas_call | solution.py:53
  22.1 5.2 %shard_map.77 = f32[64,1,48,256]{3,2,1,0:T(8,128)} custom-call(bf16[128,256]{1,0:T(8,128)(2,1)} %maximum_bitcast_fusion.table_ref, s32[1,48,256]{2,1,0:T(8,128)} %bitcast.399), custom_call_target="tpu_custom_call" | custom-call | tf_op jit(solution)/shard_map/pallas_call | solution.py:53
  27.8 2.1 copy.94
  30.5 1.4 copy.109
  32.0 3.5 %copy.92 = bf16[8,2,32,16,256]{4,2,0,3,1:T(8,128)(2,1)} copy(bf16[8,2,32,16,256]{4,3,2,1,0:T(8,128)(2,1)S(1)} %bitcast.389) | data formatting | bytes 8388608
  35.5 1.5 copy.110
  37.0 3.3 %copy.93 = bf16[16,2,32,8,256]{4,2,3,0,1:T(8,128)(2,1)} copy(bf16[16,2,32,8,256]{4,3,2,1,0:T(8,128)(2,1)S(1)} %bitcast.390) | data formatting | bytes 8388608
  41.0 206.1 %while.13 = (s32[]{:T(128)}, bf16[16,2,48,256]{3,2,1,0:T(8,128)(2,1)S(1)}, bf16[4,2,48,256]{3,2,1,0:T(8,128)(2,1)}, bf16[8,2,32,16,256]{4,2,0,3,1:T(8,128)(2,1)}...) while((s32[]{:T(128)}, ...), condition=%wide.region_3.4_spmd.clone, body=%wide.region_2.3_spmd.clone.sunk | while | flops 1616318464 | bytes 175584288 | solution.py:251
  41.0 2.7 %fusion.165 = (bf16[8,1,32,16,256]{4,2,0,3,1:T(8,128)(2,1)S(1)}, bf16[8,1,32,16,256]{4,2,0,3,1:T(8,128)(2,1)S(1)}) fusion(bf16[8,2,32,16,256]{4,2,0,3,1:T(8,128)(2,1)} %get-tuple-element.239), kind=kLoop, calls=%fused_computation.95.clone.1 | loop fusion | bytes 8388608 | tf_op jit(solution)/shard_map/while/body/eval_jaxpr/slice | solution.py:152
  43.7 0.7 fusion.166
  44.4 0.7 fusion.169
  45.8 0.7 fusion.170
  46.5 0.8 fusion.168
  47.3 1.3 fusion.171
  48.6 0.9 copy-done
  51.4 0.7 fusion.174
  52.1 2.9 %collective-permute-start = (bf16[4,2,48,256]{3,2,1,0:T(8,128)(2,1)}, bf16[4,2,48,256]{3,2,1,0:T(8,128)(2,1)}, u32[]{:S(2)}, u32[]{:S(2)}) collective-permute-start(bf16[4,2,48,256]{3,2,1,0:T(8,128)(2,1)} %fusion.174), channel_id=1, source_target_pairs={{0,2},{2,0},{1,3},{3,1},{4,6},{6,4},{5,7},{7,5},{8,10},{10,8},{9,1... | collective-permute-start | bytes 589832 | tf_op jit(solution)/shard_map/while/body/eval_jaxpr/ppermute | solution.py:204
  55.1 5.2 %collective-permute-done = bf16[4,2,48,256]{3,2,1,0:T(8,128)(2,1)} collective-permute-done((bf16[4,2,48,256]{3,2,1,0:T(8,128)(2,1)}, bf16[4,2,48,256]{3,2,1,0:T(8,128)(2,1)}, u32[]{:S(2)}, u32[]{:S(2)}) %collective-permute-start) | collective-permute-done | bytes 196640 | tf_op jit(solution)/shard_map/while/body/eval_jaxpr/ppermute | solution.py:204
  60.3 1.0 add_convert_fusion.4
  61.3 11.8 %all_to_all.28 = bf16[4,2,48,256]{3,2,1,0:T(8,128)(2,1)} all-to-all(bf16[4,2,48,256]{3,2,1,0:T(8,128)(2,1)S(1)} %add_convert_fusion.4), channel_id=1, replica_groups=mesh['groups'=2,'freq'=4,'src'=2,'vp'=2] {'freq'}, dimensions={0} | all-to-all | bytes 393216 | tf_op jit(solution)/shard_map/while/body/eval_jaxpr/all_to_all | solution.py:136
  73.1 1.9 eval_jaxpr.2
  75.0 3.4 %all-to-all-start.1 = ((bf16[4,2,48,256]{3,2,1,0:T(8,128)(2,1)}), bf16[4,2,48,256]{3,2,1,0:T(8,128)(2,1)S(1)}, u32[]{:S(2)}, u32[]{:S(2)}) async-start(bf16[4,2,48,256]{3,2,1,0:T(8,128)(2,1)} %bitcast.387), calls=%async_computation.1 | async-start | bytes 393216 | tf_op jit(solution)/shard_map/while/body/eval_jaxpr/all_to_all | solution.py:142
  78.3 2.7 %slice_bitcast_fusion.43 = (bf16[16,32,8,256]{3,1,2,0:T(8,128)(2,1)S(1)}, bf16[16,32,8,256]{3,1,2,0:T(8,128)(2,1)S(1)}) fusion(bf16[16,2,32,8,256]{4,2,3,0,1:T(8,128)(2,1)} %get-tuple-element.240), kind=kLoop, calls=%fused_computation.20.clone.3 | loop fusion | bytes 8388608 | tf_op jit(solution)/shard_map/while/body/eval_jaxpr/squeeze | solution.py:164
  81.3 1.6 copy.160
  82.9 1.7 all-to-all-done.1
  84.6 6.3 %all_gather.5 = bf16[8,2,48,256]{3,2,1,0:T(8,128)(2,1)S(1)} all-gather(bf16[4,2,48,256]{3,2,1,0:T(8,128)(2,1)S(1)} %all-to-all-done.1), channel_id=1, replica_groups=mesh['groups'=2,'freq'=4,'src'=2,'vp'=2] {'src'}, dimensions={0}, use_global_device_ids=true | all-gather | bytes 589824 | tf_op jit(solution)/shard_map/while/body/eval_jaxpr/all_gather | solution.py:243
  90.9 0.7 fusion.178
  92.3 0.9 copy-done.2
  94.6 1.2 fusion.179
  95.7 1.0 copy-done.1
  98.8 19.7 %all_to_all.29 = bf16[16,2,48,256]{3,2,1,0:T(8,128)(2,1)} all-to-all(bf16[16,2,48,256]{3,2,1,0:T(8,128)(2,1)S(1)} %copy.162), channel_id=1, replica_groups=mesh['groups'=2,'freq'=4,'src'=2,'vp'=2] {'freq'}, dimensions={0} | all-to-all | bytes 1572864 | tf_op jit(solution)/shard_map/while/body/eval_jaxpr/all_to_all | solution.py:136
  118.5 6.3 %eval_jaxpr.3 = bf16[4,4,2,48,256]{4,3,2,1,0:T(8,128)(2,1)} custom-call(f32[64,4,48,256]{3,2,1,0:T(8,128)} %get-tuple-element.242.matrix_ref, bf16[4,4,2,48,256]{4,3,2,1,0:T(8,128)(2,1)} %bitcast.386), custom_call_target="tpu_custom_call" | custom-call | tf_op jit(solution)/shard_map/while/body/eval_jaxpr/pallas_call | solution.py:89
  124.8 3.6 %all-to-all-start.3 = ((bf16[16,2,48,256]{3,2,1,0:T(8,128)(2,1)}), bf16[16,2,48,256]{3,2,1,0:T(8,128)(2,1)S(1)}, u32[]{:S(2)}, u32[]{:S(2)}) async-start(bf16[16,2,48,256]{3,2,1,0:T(8,128)(2,1)} %bitcast.385), calls=%async_computation.3 | async-start | bytes 1572864 | tf_op jit(solution)/shard_map/while/body/eval_jaxpr/all_to_all | solution.py:142
  128.4 18.2 %all-to-all-done.3 = bf16[16,2,48,256]{3,2,1,0:T(8,128)(2,1)S(1)} async-done(((bf16[16,2,48,256]{3,2,1,0:T(8,128)(2,1)}), bf16[16,2,48,256]{3,2,1,0:T(8,128)(2,1)S(1)}, u32[]{:S(2)}, u32[]{:S(2)}) %all-to-all-start.3) | async-done | bytes 786464 | tf_op jit(solution)/shard_map/while/body/eval_jaxpr/all_to_all | solution.py:142
  146.9 2.7 %fusion.165 = (bf16[8,1,32,16,256]{4,2,0,3,1:T(8,128)(2,1)S(1)}, bf16[8,1,32,16,256]{4,2,0,3,1:T(8,128)(2,1)S(1)}) fusion(bf16[8,2,32,16,256]{4,2,0,3,1:T(8,128)(2,1)} %get-tuple-element.239), kind=kLoop, calls=%fused_computation.95.clone.1 | loop fusion | bytes 8388608 | tf_op jit(solution)/shard_map/while/body/eval_jaxpr/slice | solution.py:152
  149.6 0.7 fusion.166
  150.3 0.7 fusion.169
  151.0 0.7 fusion.167
  151.7 0.7 fusion.170
  152.4 0.8 fusion.168
  153.1 1.3 fusion.171
  154.4 0.9 copy-done
  157.3 0.7 fusion.174
  158.0 1.5 collective-permute-start
  159.5 4.5 %collective-permute-done = bf16[4,2,48,256]{3,2,1,0:T(8,128)(2,1)} collective-permute-done((bf16[4,2,48,256]{3,2,1,0:T(8,128)(2,1)}, bf16[4,2,48,256]{3,2,1,0:T(8,128)(2,1)}, u32[]{:S(2)}, u32[]{:S(2)}) %collective-permute-start) | collective-permute-done | bytes 196640 | tf_op jit(solution)/shard_map/while/body/eval_jaxpr/ppermute | solution.py:204
  164.0 1.0 add_convert_fusion.4
  165.0 9.8 %all_to_all.28 = bf16[4,2,48,256]{3,2,1,0:T(8,128)(2,1)} all-to-all(bf16[4,2,48,256]{3,2,1,0:T(8,128)(2,1)S(1)} %add_convert_fusion.4), channel_id=1, replica_groups=mesh['groups'=2,'freq'=4,'src'=2,'vp'=2] {'freq'}, dimensions={0} | all-to-all | bytes 393216 | tf_op jit(solution)/shard_map/while/body/eval_jaxpr/all_to_all | solution.py:136
  174.8 1.9 eval_jaxpr.2
  176.7 3.4 %all-to-all-start.1 = ((bf16[4,2,48,256]{3,2,1,0:T(8,128)(2,1)}), bf16[4,2,48,256]{3,2,1,0:T(8,128)(2,1)S(1)}, u32[]{:S(2)}, u32[]{:S(2)}) async-start(bf16[4,2,48,256]{3,2,1,0:T(8,128)(2,1)} %bitcast.387), calls=%async_computation.1 | async-start | bytes 393216 | tf_op jit(solution)/shard_map/while/body/eval_jaxpr/all_to_all | solution.py:142
  180.1 2.7 %slice_bitcast_fusion.43 = (bf16[16,32,8,256]{3,1,2,0:T(8,128)(2,1)S(1)}, bf16[16,32,8,256]{3,1,2,0:T(8,128)(2,1)S(1)}) fusion(bf16[16,2,32,8,256]{4,2,3,0,1:T(8,128)(2,1)} %get-tuple-element.240), kind=kLoop, calls=%fused_computation.20.clone.3 | loop fusion | bytes 8388608 | tf_op jit(solution)/shard_map/while/body/eval_jaxpr/squeeze | solution.py:164
  183.0 1.6 copy.160
  184.6 1.7 all-to-all-done.1
  186.3 6.3 %all_gather.5 = bf16[8,2,48,256]{3,2,1,0:T(8,128)(2,1)S(1)} all-gather(bf16[4,2,48,256]{3,2,1,0:T(8,128)(2,1)S(1)} %all-to-all-done.1), channel_id=1, replica_groups=mesh['groups'=2,'freq'=4,'src'=2,'vp'=2] {'src'}, dimensions={0}, use_global_device_ids=true | all-gather | bytes 589824 | tf_op jit(solution)/shard_map/while/body/eval_jaxpr/all_gather | solution.py:243
  194.0 0.9 copy-done.2
  196.3 1.2 fusion.179
  197.5 1.0 copy-done.1
  200.5 18.7 %all_to_all.29 = bf16[16,2,48,256]{3,2,1,0:T(8,128)(2,1)} all-to-all(bf16[16,2,48,256]{3,2,1,0:T(8,128)(2,1)S(1)} %copy.162), channel_id=1, replica_groups=mesh['groups'=2,'freq'=4,'src'=2,'vp'=2] {'freq'}, dimensions={0} | all-to-all | bytes 1572864 | tf_op jit(solution)/shard_map/while/body/eval_jaxpr/all_to_all | solution.py:136
  219.2 6.3 %eval_jaxpr.3 = bf16[4,4,2,48,256]{4,3,2,1,0:T(8,128)(2,1)} custom-call(f32[64,4,48,256]{3,2,1,0:T(8,128)} %get-tuple-element.242.matrix_ref, bf16[4,4,2,48,256]{4,3,2,1,0:T(8,128)(2,1)} %bitcast.386), custom_call_target="tpu_custom_call" | custom-call | tf_op jit(solution)/shard_map/while/body/eval_jaxpr/pallas_call | solution.py:89
  225.5 3.6 %all-to-all-start.3 = ((bf16[16,2,48,256]{3,2,1,0:T(8,128)(2,1)}), bf16[16,2,48,256]{3,2,1,0:T(8,128)(2,1)S(1)}, u32[]{:S(2)}, u32[]{:S(2)}) async-start(bf16[16,2,48,256]{3,2,1,0:T(8,128)(2,1)} %bitcast.385), calls=%async_computation.3 | async-start | bytes 1572864 | tf_op jit(solution)/shard_map/while/body/eval_jaxpr/all_to_all | solution.py:142
  229.1 17.7 %all-to-all-done.3 = bf16[16,2,48,256]{3,2,1,0:T(8,128)(2,1)S(1)} async-done(((bf16[16,2,48,256]{3,2,1,0:T(8,128)(2,1)}), bf16[16,2,48,256]{3,2,1,0:T(8,128)(2,1)S(1)}, u32[]{:S(2)}, u32[]{:S(2)}) %all-to-all-start.3) | async-done | bytes 786464 | tf_op jit(solution)/shard_map/while/body/eval_jaxpr/all_to_all | solution.py:142
  247.6 1.2 broadcast_in_dim_reshape.6
  249.0 0.8 broadcast_in_dim_reshape.7
  (88 shorter events, 19.3 us)
Async XLA Ops:
  4.7 16.6 %copy-start.10 = (s32[48,1024]{1,0:T(8,128)S(1)}, s32[48,1024]{1,0:T(8,128)}, u32[]{:S(2)}) copy-start(s32[48,1024]{1,0:T(8,128)} %param.12) | copy-start | bytes 589828
  21.3 6.0 %copy-start.9 = (bf16[1,2,48,4096]{3,2,1,0:T(8,128)(2,1)S(1)}, bf16[1,2,48,4096]{3,2,1,0:T(8,128)(2,1)}, u32[]{:S(2)}) copy-start(bf16[1,2,48,4096]{3,2,1,0:T(8,128)(2,1)} %param.8) | copy-start | bytes 2359300
  27.8 2.8 %copy-start.7 = (bf16[1,8,2,32,4096]{4,3,2,1,0:T(8,128)(2,1)S(1)}, bf16[1,8,2,32,4096]{4,3,2,1,0:T(8,128)(2,1)}, u32[]{:S(2)}) copy-start(bf16[1,8,2,32,4096]{4,3,2,1,0:T(8,128)(2,1)} %param.10) | copy-start | bytes 12582916
  32.0 3.5 %copy-start.8 = (bf16[1,16,2,32,2048]{4,3,2,1,0:T(8,128)(2,1)S(1)}, bf16[1,16,2,32,2048]{4,3,2,1,0:T(8,128)(2,1)}, u32[]{:S(2)}) copy-start(bf16[1,16,2,32,2048]{4,3,2,1,0:T(8,128)(2,1)} %param.9) | copy-start | bytes 12582916
  37.0 3.4 %copy-start.11 = (s32[1,8,16]{2,1,0:T(8,128)S(1)}, s32[1,8,16]{2,1,0:T(8,128)}, u32[]{:S(2)}) copy-start(s32[1,8,16]{2,1,0:T(8,128)} %param.11) | copy-start | bytes 1540
  47.3 2.2 copy-start
  50.9 22.2 %copy-start.3 = (f32[64,1,48,256]{3,2,1,0:T(8,128)S(1)}, f32[64,1,48,256]{3,2,1,0:T(8,128)}, u32[]{:S(2)}) copy-start(f32[64,1,48,256]{3,2,1,0:T(8,128)} %get-tuple-element.241.matrix_ref) | copy-start | bytes 9437188 | tf_op jit(solution)/shard_map/while
  52.1 8.1 %collective-permute-start = (bf16[4,2,48,256]{3,2,1,0:T(8,128)(2,1)}, bf16[4,2,48,256]{3,2,1,0:T(8,128)(2,1)}, u32[]{:S(2)}, u32[]{:S(2)}) collective-permute-start(bf16[4,2,48,256]{3,2,1,0:T(8,128)(2,1)} %fusion.174), channel_id=1, source_target_pairs={{0,2},{2,0},{1,3},{3,1},{4,6},{6,4},{5,7},{7,5},{8,10},{10,8},{9,1... | collective-permute-start | bytes 589832 | tf_op jit(solution)/shard_map/while/body/eval_jaxpr/ppermute | solution.py:204
  75.0 9.6 %all-to-all-start.1 = ((bf16[4,2,48,256]{3,2,1,0:T(8,128)(2,1)}), bf16[4,2,48,256]{3,2,1,0:T(8,128)(2,1)S(1)}, u32[]{:S(2)}, u32[]{:S(2)}) async-start(bf16[4,2,48,256]{3,2,1,0:T(8,128)(2,1)} %bitcast.387), calls=%async_computation.1 | async-start | bytes 393216 | tf_op jit(solution)/shard_map/while/body/eval_jaxpr/all_to_all | solution.py:142
  84.5 7.0 %copy-start.5 = (bf16[4,2,48,256]{3,2,1,0:T(8,128)(2,1)}, bf16[4,2,48,256]{3,2,1,0:T(8,128)(2,1)S(1)}, u32[]{:S(2)}) copy-start(bf16[4,2,48,256]{3,2,1,0:T(8,128)(2,1)S(1)} %all-to-all-done.1) | copy-start | bytes 589828 | tf_op jit(solution)/shard_map/while
  91.6 1.6 copy-start.2
  94.5 2.2 copy-start.1
  124.8 21.9 %copy-start.4 = (f32[16,2,48,256]{3,2,1,0:T(8,128)S(1)}, f32[16,2,48,256]{3,2,1,0:T(8,128)}, u32[]{:S(2)}) copy-start(f32[16,2,48,256]{3,2,1,0:T(8,128)} %get-tuple-element.243) | copy-start | bytes 4718596 | tf_op jit(solution)/shard_map/while
  124.8 21.9 %all-to-all-start.3 = ((bf16[16,2,48,256]{3,2,1,0:T(8,128)(2,1)}), bf16[16,2,48,256]{3,2,1,0:T(8,128)(2,1)S(1)}, u32[]{:S(2)}, u32[]{:S(2)}) async-start(bf16[16,2,48,256]{3,2,1,0:T(8,128)(2,1)} %bitcast.385), calls=%async_computation.3 | async-start | bytes 1572864 | tf_op jit(solution)/shard_map/while/body/eval_jaxpr/all_to_all | solution.py:142
  153.1 2.2 copy-start
  156.8 18.1 %copy-start.3 = (f32[64,1,48,256]{3,2,1,0:T(8,128)S(1)}, f32[64,1,48,256]{3,2,1,0:T(8,128)}, u32[]{:S(2)}) copy-start(f32[64,1,48,256]{3,2,1,0:T(8,128)} %get-tuple-element.241.matrix_ref) | copy-start | bytes 9437188 | tf_op jit(solution)/shard_map/while
  158.0 6.0 %collective-permute-start = (bf16[4,2,48,256]{3,2,1,0:T(8,128)(2,1)}, bf16[4,2,48,256]{3,2,1,0:T(8,128)(2,1)}, u32[]{:S(2)}, u32[]{:S(2)}) collective-permute-start(bf16[4,2,48,256]{3,2,1,0:T(8,128)(2,1)} %fusion.174), channel_id=1, source_target_pairs={{0,2},{2,0},{1,3},{3,1},{4,6},{6,4},{5,7},{7,5},{8,10},{10,8},{9,1... | collective-permute-start | bytes 589832 | tf_op jit(solution)/shard_map/while/body/eval_jaxpr/ppermute | solution.py:204
  176.7 9.6 %all-to-all-start.1 = ((bf16[4,2,48,256]{3,2,1,0:T(8,128)(2,1)}), bf16[4,2,48,256]{3,2,1,0:T(8,128)(2,1)S(1)}, u32[]{:S(2)}, u32[]{:S(2)}) async-start(bf16[4,2,48,256]{3,2,1,0:T(8,128)(2,1)} %bitcast.387), calls=%async_computation.1 | async-start | bytes 393216 | tf_op jit(solution)/shard_map/while/body/eval_jaxpr/all_to_all | solution.py:142
  186.3 7.0 %copy-start.5 = (bf16[4,2,48,256]{3,2,1,0:T(8,128)(2,1)}, bf16[4,2,48,256]{3,2,1,0:T(8,128)(2,1)S(1)}, u32[]{:S(2)}) copy-start(bf16[4,2,48,256]{3,2,1,0:T(8,128)(2,1)S(1)} %all-to-all-done.1) | copy-start | bytes 589828 | tf_op jit(solution)/shard_map/while
  193.3 1.6 copy-start.2
  196.3 2.2 copy-start.1
  225.5 21.4 %copy-start.4 = (f32[16,2,48,256]{3,2,1,0:T(8,128)S(1)}, f32[16,2,48,256]{3,2,1,0:T(8,128)}, u32[]{:S(2)}) copy-start(f32[16,2,48,256]{3,2,1,0:T(8,128)} %get-tuple-element.243) | copy-start | bytes 4718596 | tf_op jit(solution)/shard_map/while
  225.5 21.4 %all-to-all-start.3 = ((bf16[16,2,48,256]{3,2,1,0:T(8,128)(2,1)}), bf16[16,2,48,256]{3,2,1,0:T(8,128)(2,1)S(1)}, u32[]{:S(2)}, u32[]{:S(2)}) async-start(bf16[16,2,48,256]{3,2,1,0:T(8,128)(2,1)} %bitcast.385), calls=%async_computation.3 | async-start | bytes 1572864 | tf_op jit(solution)/shard_map/while/body/eval_jaxpr/all_to_all | solution.py:142
  247.1 1.7 copy-start.6

commit v3 on v1

--- a/solution.py
+++ b/solution.py
@@ -28,13 +28,12 @@
 def gather_kernel(table_ref, onset_ref, out_ref):
     rows = onset_ref.shape[1]
     width = onset_ref.shape[2]
-    size = out_ref.shape[0]
     sample = lax.broadcasted_iota(jnp.int32, (NT, width), 0)
     for row in range(rows):
         place = jnp.clip(onset_ref[0, row : row + 1, :], 0, NT) - 1
         pick = (sample == place).astype(jnp.bfloat16)
         parts = jnp.dot(table_ref[...], pick, preferred_element_type=jnp.float32)
-        out_ref[:, 0, row, :] = parts[:size] + parts[size:]
+        out_ref[:, 0, row, :] = parts.astype(out_ref.dtype)
 
 
 def window_gather(count, onset):
@@ -44,21 +43,18 @@
     terms = jnp.einsum("cft,dgt->tgdfc", forward, inverse, precision=lax.Precision.HIGHEST)
     size = 4 * count * count
     table = jnp.cumsum(terms.reshape(NT, size), axis=0)
-    high = table.astype(jnp.bfloat16)
-    rest = table - high.astype(jnp.float32)
-    low = rest.astype(jnp.bfloat16)
-    stacked = jnp.concatenate([high, low], axis=1).T
+    stacked = table.astype(jnp.bfloat16).T
     blocks, points, width = onset.shape
     rows = 8
     return pl.pallas_call(
         gather_kernel,
         grid=(blocks, points // rows),
         in_specs=[
-            pl.BlockSpec((2 * size, NT), lambda b, r: (0, 0)),
+            pl.BlockSpec((size, NT), lambda b, r: (0, 0)),
             pl.BlockSpec((1, rows, width), lambda b, r: (b, r, 0)),
         ],
         out_specs=pl.BlockSpec((size, 1, rows, width), lambda b, r: (0, b, r, 0)),
-        out_shape=jax.ShapeDtypeStruct((size, blocks, points, width), jnp.float32),
+        out_shape=jax.ShapeDtypeStruct((size, blocks, points, width), jnp.bfloat16),
     )(stacked, onset)
 
 
@@ -67,9 +63,9 @@
     comps = 2 * count
     source = [spectrum_ref[q // 2, 0, q % 2].astype(jnp.float32) for q in range(comps)]
     for target in range(comps):
-        total = matrix_ref[target, 0] * source[0]
+        total = matrix_ref[target, 0].astype(jnp.float32) * source[0]
         for q in range(1, comps):
-            total = total + matrix_ref[q * comps + target, 0] * source[q]
+            total = total + matrix_ref[q * comps + target, 0].astype(jnp.float32) * source[q]
         out_ref[target // 2, 0, target % 2] = total.astype(out_ref.dtype)
 
 
@@ -86,14 +82,15 @@
         return result.astype(jnp.bfloat16)
     _, blocks, comps, points, width = spectrum.shape
     size = picked.shape[0]
+    rows = 16 if points % 16 == 0 else points
     return pl.pallas_call(
         window_kernel,
-        grid=(blocks,),
+        grid=(blocks, points // rows),
         in_specs=[
-            pl.BlockSpec((size, 1, points, width), lambda b: (0, b, 0, 0)),
-            pl.BlockSpec((count, 1, comps, points, width), lambda b: (0, b, 0, 0, 0)),
+            pl.BlockSpec((size, 1, rows, width), lambda b, r: (0, b, r, 0)),
+            pl.BlockSpec((count, 1, comps, rows, width), lambda b, r: (0, b, 0, r, 0)),
         ],
-        out_specs=pl.BlockSpec((count, 1, comps, points, width), lambda b: (0, b, 0, 0, 0)),
+        out_specs=pl.BlockSpec((count, 1, comps, rows, width), lambda b, r: (0, b, 0, r, 0)),
         out_shape=jax.ShapeDtypeStruct(spectrum.shape, jnp.bfloat16),
     )(picked, spectrum)
 

time: 242 us -> 247 us (1.021)
  Pallas kernels: 40 us -> 44.6 us
    pallas_call x4, Pallas kernels: 18.2 us -> 22.2 us  [window(): pl.pallas_call(window_kernel, grid=(blocks, points // rows), in_specs=[pl...]
  transfers between devices with their start and end apart: 6 -> 6, of which waited for: 4 -> 4; matrix products, arithmetic and copies ran while one was open for 7% -> 6% of each run, Pallas kernels for 9% -> 9%
where the time goes in v3:
time: 247 us; the launch traced here: 244 us
  blocking collectives  71.4 us (29%)
  Pallas kernels  44.6 us (18%)
  local copies, waits for them, and re-layouts  37.9 us (15%)
  matrix products  33.5 us (14%)
  starting transfers between devices  22.6 us (9%)
  waiting for transfers between devices  22.6 us (9%)
  other arithmetic  10.3 us (4%)
    all_to_all x2, blocking collectives, exchange_back(): got = lax.all_to_all(flat, 'freq', split_axis=0, concat_axis=0, tiled=True)  31.6 us
    all_to_all x2, blocking collectives, exchange(): lax.all_to_all(pieces, 'freq', split_axis=0, concat_axis=0, tiled=True)  26.9 us
    pallas_call x2, Pallas kernels, window_gather(): pl.pallas_call(gather_kernel, grid=(blocks, points // rows), in_specs=[pl...  22.5 us
    unnamed x52, local copies, waits for them, and re-layouts  22.2 us
    pallas_call x4, Pallas kernels, window(): pl.pallas_call(window_kernel, grid=(blocks, points // rows), in_specs=[pl...  22.2 us
    unnamed x16, matrix products  19.8 us
    all_to_all x2, waiting for transfers between devices, exchange_back(): got = lax.all_to_all(flat, 'freq', split_axis=0, concat_axis=0, tiled=True)  15.9 us
    all_gather x2, blocking collectives, per_device(): minus_all = lax.all_gather(minus, 'src', axis=0, tiled=True)  12.9 us
  transfers between devices with their start and end apart: 6, of which 4 were waited for; matrix products, arithmetic and copies ran while one was open for 6% of the time, Pallas kernels for 9%

profile of v3, /device:TPU:0, one launch (start us, length us, event | category | flops | bytes accessed | tf_op | source)
XLA Modules:
  0.0 244.0 jit_solution(17086164021994723437)
XLA Ops:
  0.6 1.3 copy.161
  2.2 3.6 %copy.163 = bf16[64,8,16,256]{3,2,1,0:T(8,128)(2,1)S(1)} copy(bf16[64,8,16,256]{3,1,2,0:T(8,128)(2,1)} %bitcast.448) | data formatting | bytes 8388608
  6.9 2.0 fusion.123
  8.9 2.1 fusion.126
  11.8 2.1 fusion.125
  13.8 2.0 fusion.124
  16.0 3.7 %copy.164 = bf16[128,8,8,256]{3,2,1,0:T(8,128)(2,1)S(1)} copy(bf16[128,8,8,256]{3,1,2,0:T(8,128)(2,1)} %bitcast.449) | data formatting | bytes 8388608
  19.7 3.2 %slice_bitcast_fusion.25 = (bf16[16,32,8,256]{3,2,1,0:T(8,128)(2,1)}, bf16[16,32,8,256]{3,2,1,0:T(8,128)(2,1)}, bf16[16,1,32,8,256]{4,3,2,1,0:T(8,128)(2,1)S(1)}, bf16[16,1,32,8,256]{4,3,2,1,0:T(8,128)(2,1)S(1)}) fusion(bf16[16,2,32,8,256]{4,3,2,1,0:T(8,128)(2,1)S(1)} %bitcast.423), kind=kLoop, calls=%fused_computation.156 | loop fusion | bytes 12582912 | tf_op jit(solution)/shard_map/squeeze | solution.py:161
  22.9 1.6 copy-done.17
  24.5 1.7 copy-done.18
  26.2 1.2 fusion.3
  27.4 0.8 fusion.99
  28.2 0.8 fusion.98
  29.1 0.9 fusion.111
  30.0 0.9 fusion.113
  31.6 2.9 %collective-permute-start = (bf16[4,2,48,256]{3,2,1,0:T(8,128)(2,1)}, bf16[4,2,48,256]{3,2,1,0:T(8,128)(2,1)}, u32[]{:S(2)}, u32[]{:S(2)}) collective-permute-start(bf16[4,2,48,256]{3,2,1,0:T(8,128)(2,1)} %fusion.120), channel_id=1, source_target_pairs={{0,2},{2,0},{1,3},{3,1},{4,6},{6,4},{5,7},{7,5},{8,10},{10,8},{9,1... | collective-permute-start | bytes 589832 | tf_op jit(solution)/shard_map/ppermute | solution.py:201
  36.2 1.0 reshape.162
  37.2 2.5 %collective-permute-done = bf16[4,2,48,256]{3,2,1,0:T(8,128)(2,1)} collective-permute-done((bf16[4,2,48,256]{3,2,1,0:T(8,128)(2,1)}, bf16[4,2,48,256]{3,2,1,0:T(8,128)(2,1)}, u32[]{:S(2)}, u32[]{:S(2)}) %collective-permute-start) | collective-permute-done | bytes 196640 | tf_op jit(solution)/shard_map/ppermute | solution.py:201
  39.7 1.7 add_convert_fusion.1
  41.3 5.1 %all-to-all-start = ((bf16[4,2,48,256]{3,2,1,0:T(8,128)(2,1)}), bf16[4,2,48,256]{3,2,1,0:T(8,128)(2,1)S(1)}, u32[]{:S(2)}, u32[]{:S(2)}) async-start(bf16[4,2,48,256]{3,2,1,0:T(8,128)(2,1)} %add_convert_fusion.1), calls=%async_computation | async-start | bytes 393216 | tf_op jit(solution)/shard_map/all_to_all | solution.py:133
  47.1 1.3 copy_bitcast_fusion.46.table_ref
  48.5 5.3 %shard_map.78.matrix_ref = bf16[64,1,48,256]{3,2,1,0:T(8,128)(2,1)} custom-call(bf16[64,256]{1,0:T(8,128)(2,1)} %copy_bitcast_fusion.46.table_ref, s32[1,48,256]{2,1,0:T(8,128)} %bitcast.462), custom_call_target="tpu_custom_call" | custom-call | tf_op jit(solution)/shard_map/pallas_call | solution.py:49
  54.5 2.9 %shard_map.79 = bf16[4,1,2,48,256]{4,3,2,1,0:T(8,128)(2,1)} custom-call(bf16[64,1,48,256]{3,2,1,0:T(8,128)(2,1)} %shard_map.78.matrix_ref, bf16[4,1,2,48,256]{4,3,2,1,0:T(8,128)(2,1)} %bitcast.458), custom_call_target="tpu_custom_call" | custom-call | tf_op jit(solution)/shard_map/pallas_call | solution.py:86
  57.4 5.1 %all-to-all-start.1 = ((bf16[4,2,48,256]{3,2,1,0:T(8,128)(2,1)}), bf16[4,2,48,256]{3,2,1,0:T(8,128)(2,1)S(1)}, u32[]{:S(2)}, u32[]{:S(2)}) async-start(bf16[4,2,48,256]{3,2,1,0:T(8,128)(2,1)} %bitcast.459), calls=%async_computation.1 | async-start | bytes 393216 | tf_op jit(solution)/shard_map/all_to_all | solution.py:139
  62.5 3.6 %copy.114 = bf16[16,32,8,256]{3,1,0,2:T(8,128)(2,1)} copy(bf16[16,32,8,256]{3,2,1,0:T(8,128)(2,1)} %get-tuple-element.2) | data formatting | bytes 4194304 | tf_op jit(solution)/shard_map/squeeze | solution.py:161
  66.0 1.8 copy.116
  67.8 0.9 all-to-all-done.1
  68.7 6.3 %all_gather.6 = bf16[8,2,48,256]{3,2,1,0:T(8,128)(2,1)S(1)} all-gather(bf16[4,2,48,256]{3,2,1,0:T(8,128)(2,1)S(1)} %all-to-all-done.1), channel_id=1, replica_groups=mesh['groups'=2,'freq'=4,'src'=2,'vp'=2] {'src'}, dimensions={0}, use_global_device_ids=true | all-gather | bytes 589824 | tf_op jit(solution)/shard_map/all_gather | solution.py:240
  75.0 2.4 fusion.133
  78.2 0.9 copy-done.13
  80.5 1.2 fusion.27
  82.0 0.9 fusion.44
  82.9 0.9 fusion.47
  83.8 0.9 fusion.89
  84.6 0.8 fusion.86
  85.5 1.0 copy.123
  86.5 4.4 %all-to-all-start.2 = ((bf16[16,2,48,256]{3,2,1,0:T(8,128)(2,1)}), bf16[16,2,48,256]{3,2,1,0:T(8,128)(2,1)}, u32[]{:S(2)}, u32[]{:S(2)}) async-start(bf16[16,2,48,256]{3,2,1,0:T(8,128)(2,1)} %copy.123), calls=%async_computation.2 | async-start | bytes 1572864 | tf_op jit(solution)/shard_map/all_to_all | solution.py:133
  90.9 2.3 copy.162
  93.2 1.0 constant_dynamic-slice_fusion.1
  94.9 17.2 %shard_map.77.matrix_ref = bf16[64,4,48,256]{3,2,1,0:T(8,128)(2,1)} custom-call(bf16[64,256]{1,0:T(8,128)(2,1)} %copy_bitcast_fusion.46.table_ref, s32[4,48,256]{2,1,0:T(8,128)} %bitcast.455), custom_call_target="tpu_custom_call" | custom-call | tf_op jit(solution)/shard_map/pallas_call | solution.py:49
  112.1 8.2 %shard_map.80 = bf16[4,4,2,48,256]{4,3,2,1,0:T(8,128)(2,1)} custom-call(bf16[64,4,48,256]{3,2,1,0:T(8,128)(2,1)} %shard_map.77.matrix_ref, bf16[4,4,2,48,256]{4,3,2,1,0:T(8,128)(2,1)} %bitcast.60.spectrum_ref), custom_call_target="tpu_custom_call" | custom-call | tf_op jit(solution)/shard_map/pallas_call | solution.py:86
  120.3 21.4 %all_to_all.40 = bf16[16,2,48,256]{3,2,1,0:T(8,128)(2,1)S(1)} all-to-all(bf16[16,2,48,256]{3,2,1,0:T(8,128)(2,1)} %bitcast.452), channel_id=1, replica_groups=mesh['groups'=2,'freq'=4,'src'=2,'vp'=2] {'freq'}, dimensions={0} | all-to-all | bytes 1572864 | tf_op jit(solution)/shard_map/all_to_all | solution.py:139
  143.5 0.9 copy-done.4
  145.7 1.3 fusion.1
  148.2 0.9 fusion.100
  149.8 0.9 fusion.107
  150.6 0.9 fusion.109
  151.6 1.6 collective-permute-start.1
  153.1 4.2 %collective-permute-done.1 = bf16[4,2,48,256]{3,2,1,0:T(8,128)(2,1)S(1)} collective-permute-done((bf16[4,2,48,256]{3,2,1,0:T(8,128)(2,1)S(1)}, bf16[4,2,48,256]{3,2,1,0:T(8,128)(2,1)S(1)}, u32[]{:S(2)}, u32[]{:S(2)}) %collective-permute-start.1) | collective-permute-done | bytes 196640 | tf_op jit(solution)/shard_map/ppermute | solution.py:201
  157.4 9.9 %all_to_all.41 = bf16[4,2,48,256]{3,2,1,0:T(8,128)(2,1)} all-to-all(bf16[4,2,48,256]{3,2,1,0:T(8,128)(2,1)S(1)} %add_convert_fusion), channel_id=1, replica_groups=mesh['groups'=2,'freq'=4,'src'=2,'vp'=2] {'freq'}, dimensions={0} | all-to-all | bytes 393216 | tf_op jit(solution)/shard_map/all_to_all | solution.py:133
  167.2 2.9 %shard_map.81 = bf16[4,1,2,48,256]{4,3,2,1,0:T(8,128)(2,1)} custom-call(bf16[64,1,48,256]{3,2,1,0:T(8,128)(2,1)} %shard_map.78.matrix_ref, bf16[4,1,2,48,256]{4,3,2,1,0:T(8,128)(2,1)} %bitcast.460), custom_call_target="tpu_custom_call" | custom-call | tf_op jit(solution)/shard_map/pallas_call | solution.py:86
  170.1 10.1 %all_to_all.42 = bf16[4,2,48,256]{3,2,1,0:T(8,128)(2,1)S(1)} all-to-all(bf16[4,2,48,256]{3,2,1,0:T(8,128)(2,1)} %bitcast.461), channel_id=1, replica_groups=mesh['groups'=2,'freq'=4,'src'=2,'vp'=2] {'freq'}, dimensions={0} | all-to-all | bytes 393216 | tf_op jit(solution)/shard_map/all_to_all | solution.py:139
  180.2 6.6 %all_gather.7 = bf16[8,2,48,256]{3,2,1,0:T(8,128)(2,1)S(1)} all-gather(bf16[4,2,48,256]{3,2,1,0:T(8,128)(2,1)S(1)} %all_to_all.42), channel_id=1, replica_groups=mesh['groups'=2,'freq'=4,'src'=2,'vp'=2] {'src'}, dimensions={0}, use_global_device_ids=true | all-gather | bytes 589824 | tf_op jit(solution)/shard_map/all_gather | solution.py:240
  186.8 2.4 fusion.137
  190.0 0.9 copy-done.14
  192.3 1.2 fusion.23
  193.9 0.9 fusion.38
  194.7 0.9 fusion.41
  195.6 0.9 fusion.95
  197.4 17.1 %all_to_all.43 = bf16[16,2,48,256]{3,2,1,0:T(8,128)(2,1)} all-to-all(bf16[16,2,48,256]{3,2,1,0:T(8,128)(2,1)S(1)} %copy.135), channel_id=1, replica_groups=mesh['groups'=2,'freq'=4,'src'=2,'vp'=2] {'freq'}, dimensions={0} | all-to-all | bytes 1572864 | tf_op jit(solution)/shard_map/all_to_all | solution.py:133
  214.5 8.2 %shard_map.82 = bf16[4,4,2,48,256]{4,3,2,1,0:T(8,128)(2,1)} custom-call(bf16[64,4,48,256]{3,2,1,0:T(8,128)(2,1)} %shard_map.77.matrix_ref, bf16[4,4,2,48,256]{4,3,2,1,0:T(8,128)(2,1)} %bitcast.451), custom_call_target="tpu_custom_call" | custom-call | tf_op jit(solution)/shard_map/pallas_call | solution.py:86
  222.7 3.5 %all-to-all-start.7 = ((bf16[16,2,48,256]{3,2,1,0:T(8,128)(2,1)}), bf16[16,2,48,256]{3,2,1,0:T(8,128)(2,1)S(1)}, u32[]{:S(2)}, u32[]{:S(2)}) async-start(bf16[16,2,48,256]{3,2,1,0:T(8,128)(2,1)} %bitcast.450), calls=%async_computation.7 | async-start | bytes 1572864 | tf_op jit(solution)/shard_map/all_to_all | solution.py:139
  227.1 15.0 %all-to-all-done.7 = bf16[16,2,48,256]{3,2,1,0:T(8,128)(2,1)S(1)} async-done(((bf16[16,2,48,256]{3,2,1,0:T(8,128)(2,1)}), bf16[16,2,48,256]{3,2,1,0:T(8,128)(2,1)S(1)}, u32[]{:S(2)}, u32[]{:S(2)}) %all-to-all-start.7) | async-done | bytes 786464 | tf_op jit(solution)/shard_map/all_to_all | solution.py:139
  242.8 1.2 broadcast_in_dim_reshape.6
  (85 shorter events, 19.3 us)
Async XLA Ops:
  6.2 4.8 %copy-start = (bf16[8,1,32,16,256]{4,3,2,1,0:T(8,128)(2,1)}, bf16[8,1,32,16,256]{4,3,2,1,0:T(8,128)(2,1)S(1)}, u32[]{:S(2)}) copy-start(bf16[8,1,32,16,256]{4,3,2,1,0:T(8,128)(2,1)S(1)} %get-tuple-element.7) | copy-start | bytes 6291460
  6.9 2.0 copy-start.3
  11.8 2.1 copy-start.5
  13.8 2.0 copy-start.21
  19.7 3.2 %copy-start.15 = (f32[16,48,256]{1,2,0:S(1)}, f32[16,48,256]{1,2,0}, u32[]{:S(2)}) copy-start(f32[16,48,256]{1,2,0} %fusion.123) | copy-start | bytes 2359300
  19.7 3.2 %copy-start.16 = (f32[16,48,256]{1,2,0:S(1)}, f32[16,48,256]{1,2,0}, u32[]{:S(2)}) copy-start(f32[16,48,256]{1,2,0} %fusion.126) | copy-start | bytes 2359300
  19.7 4.8 %copy-start.17 = (f32[16,48,256]{1,2,0:S(1)}, f32[16,48,256]{1,2,0}, u32[]{:S(2)}) copy-start(f32[16,48,256]{1,2,0} %fusion.125) | copy-start | bytes 2359300
  19.7 6.5 %copy-start.18 = (f32[16,48,256]{1,2,0:S(1)}, f32[16,48,256]{1,2,0}, u32[]{:S(2)}) copy-start(f32[16,48,256]{1,2,0} %fusion.124) | copy-start | bytes 2359300
  22.9 5.4 %copy-start.9 = (bf16[16,1,32,8,256]{4,3,2,1,0:T(8,128)(2,1)}, bf16[16,1,32,8,256]{4,3,2,1,0:T(8,128)(2,1)S(1)}, u32[]{:S(2)}) copy-start(bf16[16,1,32,8,256]{4,3,2,1,0:T(8,128)(2,1)S(1)} %get-tuple-element.5) | copy-start | bytes 6291460
  22.9 7.1 %copy-start.7 = (bf16[16,1,32,8,256]{4,3,2,1,0:T(8,128)(2,1)}, bf16[16,1,32,8,256]{4,3,2,1,0:T(8,128)(2,1)S(1)}, u32[]{:S(2)}) copy-start(bf16[16,1,32,8,256]{4,3,2,1,0:T(8,128)(2,1)S(1)} %get-tuple-element.4) | copy-start | bytes 6291460
  31.6 8.1 %collective-permute-start = (bf16[4,2,48,256]{3,2,1,0:T(8,128)(2,1)}, bf16[4,2,48,256]{3,2,1,0:T(8,128)(2,1)}, u32[]{:S(2)}, u32[]{:S(2)}) collective-permute-start(bf16[4,2,48,256]{3,2,1,0:T(8,128)(2,1)} %fusion.120), channel_id=1, source_target_pairs={{0,2},{2,0},{1,3},{3,1},{4,6},{6,4},{5,7},{7,5},{8,10},{10,8},{9,1... | collective-permute-start | bytes 589832 | tf_op jit(solution)/shard_map/ppermute | solution.py:201
  41.3 12.4 %all-to-all-start = ((bf16[4,2,48,256]{3,2,1,0:T(8,128)(2,1)}), bf16[4,2,48,256]{3,2,1,0:T(8,128)(2,1)S(1)}, u32[]{:S(2)}, u32[]{:S(2)}) async-start(bf16[4,2,48,256]{3,2,1,0:T(8,128)(2,1)} %add_convert_fusion.1), calls=%async_computation | async-start | bytes 393216 | tf_op jit(solution)/shard_map/all_to_all | solution.py:133
  53.8 0.7 copy-start.20
  57.4 11.3 %all-to-all-start.1 = ((bf16[4,2,48,256]{3,2,1,0:T(8,128)(2,1)}), bf16[4,2,48,256]{3,2,1,0:T(8,128)(2,1)S(1)}, u32[]{:S(2)}, u32[]{:S(2)}) async-start(bf16[4,2,48,256]{3,2,1,0:T(8,128)(2,1)} %bitcast.459), calls=%async_computation.1 | async-start | bytes 393216 | tf_op jit(solution)/shard_map/all_to_all | solution.py:139
  62.5 3.6 %copy-start.19 = (bf16[16,32,8,256]{3,2,1,0:T(8,128)(2,1)S(1)}, bf16[16,32,8,256]{3,2,1,0:T(8,128)(2,1)}, u32[]{:S(2)}) copy-start(bf16[16,32,8,256]{3,2,1,0:T(8,128)(2,1)} %get-tuple-element.3) | copy-start | bytes 6291460
  75.0 2.4 copy-start.11
  77.5 1.6 copy-start.13
  80.4 1.6 copy-start.1
  86.5 25.6 %all-to-all-start.2 = ((bf16[16,2,48,256]{3,2,1,0:T(8,128)(2,1)}), bf16[16,2,48,256]{3,2,1,0:T(8,128)(2,1)}, u32[]{:S(2)}, u32[]{:S(2)}) async-start(bf16[16,2,48,256]{3,2,1,0:T(8,128)(2,1)} %copy.123), calls=%async_computation.2 | async-start | bytes 1572864 | tf_op jit(solution)/shard_map/all_to_all | solution.py:133
  120.3 21.8 %copy-start.6 = (bf16[8,1,32,16,256]{4,2,0,3,1:T(8,128)(2,1)S(1)}, bf16[8,1,32,16,256]{4,2,0,3,1:T(8,128)(2,1)}, u32[]{:S(2)}) copy-start(bf16[8,1,32,16,256]{4,2,0,3,1:T(8,128)(2,1)} %copy-done.5) | copy-start | bytes 6291460
  142.8 1.6 copy-start.4
  145.7 1.6 copy-start.10
  148.2 1.6 copy-start.8
  151.6 5.7 %collective-permute-start.1 = (bf16[4,2,48,256]{3,2,1,0:T(8,128)(2,1)S(1)}, bf16[4,2,48,256]{3,2,1,0:T(8,128)(2,1)S(1)}, u32[]{:S(2)}, u32[]{:S(2)}) collective-permute-start(bf16[4,2,48,256]{3,2,1,0:T(8,128)(2,1)S(1)} %fusion.116), channel_id=1, source_target_pairs={{0,2},{2,0},{1,3},{3,1},{4,6},{6,4},{5,7},{7,5},{8,10},{10,8},{9,1... | collective-permute-start | bytes 589832 | tf_op jit(solution)/shard_map/ppermute | solution.py:201
  186.8 2.4 copy-start.12
  189.3 1.6 copy-start.14
  192.3 1.6 copy-start.2
  222.7 19.5 %all-to-all-start.7 = ((bf16[16,2,48,256]{3,2,1,0:T(8,128)(2,1)}), bf16[16,2,48,256]{3,2,1,0:T(8,128)(2,1)S(1)}, u32[]{:S(2)}, u32[]{:S(2)}) async-start(bf16[16,2,48,256]{3,2,1,0:T(8,128)(2,1)} %bitcast.450), calls=%async_computation.7 | async-start | bytes 1572864 | tf_op jit(solution)/shard_map/all_to_all | solution.py:139

commit v4 on v1

--- a/solution.py
+++ b/solution.py
@@ -86,14 +86,15 @@
         return result.astype(jnp.bfloat16)
     _, blocks, comps, points, width = spectrum.shape
     size = picked.shape[0]
+    rows = 24 if points % 24 == 0 else points
     return pl.pallas_call(
         window_kernel,
-        grid=(blocks,),
+        grid=(blocks, points // rows),
         in_specs=[
-            pl.BlockSpec((size, 1, points, width), lambda b: (0, b, 0, 0)),
-            pl.BlockSpec((count, 1, comps, points, width), lambda b: (0, b, 0, 0, 0)),
+            pl.BlockSpec((size, 1, rows, width), lambda b, r: (0, b, r, 0)),
+            pl.BlockSpec((count, 1, comps, rows, width), lambda b, r: (0, b, 0, r, 0)),
         ],
-        out_specs=pl.BlockSpec((count, 1, comps, points, width), lambda b: (0, b, 0, 0, 0)),
+        out_specs=pl.BlockSpec((count, 1, comps, rows, width), lambda b, r: (0, b, 0, r, 0)),
         out_shape=jax.ShapeDtypeStruct(spectrum.shape, jnp.bfloat16),
     )(picked, spectrum)
 

time: 242 us -> 244 us (level)
  Pallas kernels: 40 us -> 42.9 us
    pallas_call x4, Pallas kernels: 18.2 us -> 21.1 us  [window(): pl.pallas_call(window_kernel, grid=(blocks, points // rows), in_specs=[pl...]
where the time goes in v4:
time: 244 us; the launch traced here: 242 us
  blocking collectives  71.2 us (29%)
  Pallas kernels  42.9 us (18%)
  local copies, waits for them, and re-layouts  37.6 us (15%)
  matrix products  33.6 us (14%)
  starting transfers between devices  22.6 us (9%)
  waiting for transfers between devices  21.1 us (9%)
  other arithmetic  11.3 us (5%)
    all_to_all x2, blocking collectives, exchange_back(): got = lax.all_to_all(flat, 'freq', split_axis=0, concat_axis=0, tiled=True)  31.6 us
    all_to_all x2, blocking collectives, exchange(): lax.all_to_all(pieces, 'freq', split_axis=0, concat_axis=0, tiled=True)  26.9 us
    unnamed x52, local copies, waits for them, and re-layouts  22 us
    pallas_call x2, Pallas kernels, window_gather(): pl.pallas_call(gather_kernel, grid=(blocks, points // rows), in_specs=[pl...  21.8 us
    pallas_call x4, Pallas kernels, window(): pl.pallas_call(window_kernel, grid=(blocks, points // rows), in_specs=[pl...  21.1 us
    unnamed x16, matrix products  19.9 us
    all_to_all x2, waiting for transfers between devices, exchange_back(): got = lax.all_to_all(flat, 'freq', split_axis=0, concat_axis=0, tiled=True)  15.9 us
    all_gather x2, blocking collectives, per_device(): minus_all = lax.all_gather(minus, 'src', axis=0, tiled=True)  12.7 us
  transfers between devices with their start and end apart: 6, of which 4 were waited for; matrix products, arithmetic and copies ran while one was open for 7% of the time, Pallas kernels for 9%

profile of v4, /device:TPU:0, one launch (start us, length us, event | category | flops | bytes accessed | tf_op | source)
XLA Modules:
  0.0 241.6 jit_solution(3587715074872775243)
XLA Ops:
  0.6 1.3 copy.161
  2.2 3.6 %copy.163 = bf16[64,8,16,256]{3,2,1,0:T(8,128)(2,1)S(1)} copy(bf16[64,8,16,256]{3,1,2,0:T(8,128)(2,1)} %bitcast.469) | data formatting | bytes 8388608
  6.9 2.1 fusion.123
  9.0 2.1 fusion.126
  11.8 2.0 fusion.125
  13.9 2.1 fusion.124
  16.1 3.7 %copy.164 = bf16[128,8,8,256]{3,2,1,0:T(8,128)(2,1)S(1)} copy(bf16[128,8,8,256]{3,1,2,0:T(8,128)(2,1)} %bitcast.470) | data formatting | bytes 8388608
  19.8 3.2 %slice_bitcast_fusion.25 = (bf16[16,32,8,256]{3,2,1,0:T(8,128)(2,1)}, bf16[16,32,8,256]{3,2,1,0:T(8,128)(2,1)}, bf16[16,1,32,8,256]{4,3,2,1,0:T(8,128)(2,1)S(1)}, bf16[16,1,32,8,256]{4,3,2,1,0:T(8,128)(2,1)S(1)}) fusion(bf16[16,2,32,8,256]{4,3,2,1,0:T(8,128)(2,1)S(1)} %bitcast.444), kind=kLoop, calls=%fused_computation.159 | loop fusion | bytes 12582912 | tf_op jit(solution)/shard_map/squeeze | solution.py:165
  23.0 1.6 copy-done.17
  24.5 1.7 copy-done.18
  26.3 1.2 fusion.3
  27.5 0.8 fusion.99
  28.3 0.8 fusion.98
  29.2 0.9 fusion.111
  30.1 0.9 fusion.113
  31.6 2.9 %collective-permute-start = (bf16[4,2,48,256]{3,2,1,0:T(8,128)(2,1)}, bf16[4,2,48,256]{3,2,1,0:T(8,128)(2,1)}, u32[]{:S(2)}, u32[]{:S(2)}) collective-permute-start(bf16[4,2,48,256]{3,2,1,0:T(8,128)(2,1)} %fusion.120), channel_id=1, source_target_pairs={{0,2},{2,0},{1,3},{3,1},{4,6},{6,4},{5,7},{7,5},{8,10},{10,8},{9,1... | collective-permute-start | bytes 589832 | tf_op jit(solution)/shard_map/ppermute | solution.py:205
  36.2 1.0 reshape.161
  38.7 1.1 collective-permute-done
  39.8 1.7 add_convert_fusion.1
  41.4 5.1 %all-to-all-start = ((bf16[4,2,48,256]{3,2,1,0:T(8,128)(2,1)}), bf16[4,2,48,256]{3,2,1,0:T(8,128)(2,1)S(1)}, u32[]{:S(2)}, u32[]{:S(2)}) async-start(bf16[4,2,48,256]{3,2,1,0:T(8,128)(2,1)} %add_convert_fusion.1), calls=%async_computation | async-start | bytes 393216 | tf_op jit(solution)/shard_map/all_to_all | solution.py:137
  47.9 5.2 %shard_map.78.matrix_ref = f32[64,1,48,256]{3,2,1,0:T(8,128)} custom-call(bf16[128,256]{1,0:T(8,128)(2,1)} %maximum_bitcast_fusion.table_ref, s32[1,48,256]{2,1,0:T(8,128)} %bitcast.483), custom_call_target="tpu_custom_call" | custom-call | tf_op jit(solution)/shard_map/pallas_call | solution.py:53
  53.8 2.7 %shard_map.79 = bf16[4,1,2,48,256]{4,3,2,1,0:T(8,128)(2,1)} custom-call(f32[64,1,48,256]{3,2,1,0:T(8,128)} %shard_map.78.matrix_ref, bf16[4,1,2,48,256]{4,3,2,1,0:T(8,128)(2,1)} %bitcast.476), custom_call_target="tpu_custom_call" | custom-call | tf_op jit(solution)/shard_map/pallas_call | solution.py:90
  56.5 5.1 %all-to-all-start.1 = ((bf16[4,2,48,256]{3,2,1,0:T(8,128)(2,1)}), bf16[4,2,48,256]{3,2,1,0:T(8,128)(2,1)S(1)}, u32[]{:S(2)}, u32[]{:S(2)}) async-start(bf16[4,2,48,256]{3,2,1,0:T(8,128)(2,1)} %bitcast.477), calls=%async_computation.1 | async-start | bytes 393216 | tf_op jit(solution)/shard_map/all_to_all | solution.py:143
  61.6 3.5 %copy.114 = bf16[16,32,8,256]{3,1,0,2:T(8,128)(2,1)} copy(bf16[16,32,8,256]{3,2,1,0:T(8,128)(2,1)} %get-tuple-element.2) | data formatting | bytes 4194304 | tf_op jit(solution)/shard_map/squeeze | solution.py:165
  65.1 1.9 copy.116
  67.8 6.3 %all_gather.6 = bf16[8,2,48,256]{3,2,1,0:T(8,128)(2,1)S(1)} all-gather(bf16[4,2,48,256]{3,2,1,0:T(8,128)(2,1)S(1)} %all-to-all-done.1), channel_id=1, replica_groups=mesh['groups'=2,'freq'=4,'src'=2,'vp'=2] {'src'}, dimensions={0}, use_global_device_ids=true | all-gather | bytes 589824 | tf_op jit(solution)/shard_map/all_gather | solution.py:244
  74.2 2.4 %fusion.133 = f32[8,48,512]{1,2,0:S(1)} fusion(bf16[8,256,512]{1,2,0:T(8,128)(2,1)} %bitcast.436, bf16[8,2,48,256]{3,2,1,0:T(8,128)(2,1)S(1)} %all_gather.6), kind=kOutput, calls=%fused_computation.127 | convolution fusion | flops 100663296 | bytes 4390912
  77.3 0.9 copy-done.13
  79.6 1.2 fusion.27
  81.1 0.9 fusion.44
  82.0 0.9 fusion.47
  82.9 0.9 fusion.89
  83.7 0.8 fusion.86
  84.7 1.0 copy.123
  85.6 4.4 %all-to-all-start.2 = ((bf16[16,2,48,256]{3,2,1,0:T(8,128)(2,1)}), bf16[16,2,48,256]{3,2,1,0:T(8,128)(2,1)}, u32[]{:S(2)}, u32[]{:S(2)}) async-start(bf16[16,2,48,256]{3,2,1,0:T(8,128)(2,1)} %copy.123), calls=%async_computation.2 | async-start | bytes 1572864 | tf_op jit(solution)/shard_map/all_to_all | solution.py:137
  90.0 2.3 copy.162
  92.3 1.0 constant_dynamic-slice_fusion.1
  94.1 16.6 %shard_map.77.matrix_ref = f32[64,4,48,256]{3,2,1,0:T(8,128)} custom-call(bf16[128,256]{1,0:T(8,128)(2,1)} %maximum_bitcast_fusion.table_ref, s32[4,48,256]{2,1,0:T(8,128)} %bitcast.482), custom_call_target="tpu_custom_call" | custom-call | tf_op jit(solution)/shard_map/pallas_call | solution.py:53
  110.6 7.9 %shard_map.80 = bf16[4,4,2,48,256]{4,3,2,1,0:T(8,128)(2,1)} custom-call(f32[64,4,48,256]{3,2,1,0:T(8,128)} %shard_map.77.matrix_ref, bf16[4,4,2,48,256]{4,3,2,1,0:T(8,128)(2,1)} %bitcast.62.spectrum_ref), custom_call_target="tpu_custom_call" | custom-call | tf_op jit(solution)/shard_map/pallas_call | solution.py:90
  118.5 21.5 %all_to_all.40 = bf16[16,2,48,256]{3,2,1,0:T(8,128)(2,1)S(1)} all-to-all(bf16[16,2,48,256]{3,2,1,0:T(8,128)(2,1)} %bitcast.473), channel_id=1, replica_groups=mesh['groups'=2,'freq'=4,'src'=2,'vp'=2] {'freq'}, dimensions={0} | all-to-all | bytes 1572864 | tf_op jit(solution)/shard_map/all_to_all | solution.py:143
  141.8 0.9 copy-done.4
  144.0 1.3 fusion.1
  145.6 0.8 fusion.101
  146.5 0.9 fusion.100
  148.1 0.9 fusion.107
  148.9 0.9 fusion.109
  149.9 1.6 collective-permute-start.1
  151.4 4.2 %collective-permute-done.1 = bf16[4,2,48,256]{3,2,1,0:T(8,128)(2,1)S(1)} collective-permute-done((bf16[4,2,48,256]{3,2,1,0:T(8,128)(2,1)S(1)}, bf16[4,2,48,256]{3,2,1,0:T(8,128)(2,1)S(1)}, u32[]{:S(2)}, u32[]{:S(2)}) %collective-permute-start.1) | collective-permute-done | bytes 196640 | tf_op jit(solution)/shard_map/ppermute | solution.py:205
  155.7 9.9 %all_to_all.41 = bf16[4,2,48,256]{3,2,1,0:T(8,128)(2,1)} all-to-all(bf16[4,2,48,256]{3,2,1,0:T(8,128)(2,1)S(1)} %add_convert_fusion), channel_id=1, replica_groups=mesh['groups'=2,'freq'=4,'src'=2,'vp'=2] {'freq'}, dimensions={0} | all-to-all | bytes 393216 | tf_op jit(solution)/shard_map/all_to_all | solution.py:137
  165.5 2.7 %shard_map.81 = bf16[4,1,2,48,256]{4,3,2,1,0:T(8,128)(2,1)} custom-call(f32[64,1,48,256]{3,2,1,0:T(8,128)} %shard_map.78.matrix_ref, bf16[4,1,2,48,256]{4,3,2,1,0:T(8,128)(2,1)} %bitcast.478), custom_call_target="tpu_custom_call" | custom-call | tf_op jit(solution)/shard_map/pallas_call | solution.py:90
  168.2 10.1 %all_to_all.42 = bf16[4,2,48,256]{3,2,1,0:T(8,128)(2,1)S(1)} all-to-all(bf16[4,2,48,256]{3,2,1,0:T(8,128)(2,1)} %bitcast.479), channel_id=1, replica_groups=mesh['groups'=2,'freq'=4,'src'=2,'vp'=2] {'freq'}, dimensions={0} | all-to-all | bytes 393216 | tf_op jit(solution)/shard_map/all_to_all | solution.py:143
  178.3 6.3 %all_gather.7 = bf16[8,2,48,256]{3,2,1,0:T(8,128)(2,1)S(1)} all-gather(bf16[4,2,48,256]{3,2,1,0:T(8,128)(2,1)S(1)} %all_to_all.42), channel_id=1, replica_groups=mesh['groups'=2,'freq'=4,'src'=2,'vp'=2] {'src'}, dimensions={0}, use_global_device_ids=true | all-gather | bytes 589824 | tf_op jit(solution)/shard_map/all_gather | solution.py:244
  184.7 2.4 %fusion.137 = f32[8,48,512]{1,2,0:S(1)} fusion(bf16[8,256,512]{1,2,0:T(8,128)(2,1)} %bitcast.437, bf16[8,2,48,256]{3,2,1,0:T(8,128)(2,1)S(1)} %all_gather.7), kind=kOutput, calls=%fused_computation.131 | convolution fusion | flops 100663296 | bytes 4390912
  187.8 0.9 copy-done.14
  190.1 1.4 fusion.23
  191.7 0.9 fusion.38
  192.5 0.9 fusion.41
  193.4 0.9 fusion.95
  194.2 0.8 fusion.92
  195.3 17.1 %all_to_all.43 = bf16[16,2,48,256]{3,2,1,0:T(8,128)(2,1)} all-to-all(bf16[16,2,48,256]{3,2,1,0:T(8,128)(2,1)S(1)} %copy.135), channel_id=1, replica_groups=mesh['groups'=2,'freq'=4,'src'=2,'vp'=2] {'freq'}, dimensions={0} | all-to-all | bytes 1572864 | tf_op jit(solution)/shard_map/all_to_all | solution.py:137
  212.3 7.9 %shard_map.82 = bf16[4,4,2,48,256]{4,3,2,1,0:T(8,128)(2,1)} custom-call(f32[64,4,48,256]{3,2,1,0:T(8,128)} %shard_map.77.matrix_ref, bf16[4,4,2,48,256]{4,3,2,1,0:T(8,128)(2,1)} %bitcast.472), custom_call_target="tpu_custom_call" | custom-call | tf_op jit(solution)/shard_map/pallas_call | solution.py:90
  220.2 3.5 %all-to-all-start.7 = ((bf16[16,2,48,256]{3,2,1,0:T(8,128)(2,1)}), bf16[16,2,48,256]{3,2,1,0:T(8,128)(2,1)S(1)}, u32[]{:S(2)}, u32[]{:S(2)}) async-start(bf16[16,2,48,256]{3,2,1,0:T(8,128)(2,1)} %bitcast.471), calls=%async_computation.7 | async-start | bytes 1572864 | tf_op jit(solution)/shard_map/all_to_all | solution.py:143
  224.7 15.0 %all-to-all-done.7 = bf16[16,2,48,256]{3,2,1,0:T(8,128)(2,1)S(1)} async-done(((bf16[16,2,48,256]{3,2,1,0:T(8,128)(2,1)}), bf16[16,2,48,256]{3,2,1,0:T(8,128)(2,1)S(1)}, u32[]{:S(2)}, u32[]{:S(2)}) %all-to-all-start.7) | async-done | bytes 786464 | tf_op jit(solution)/shard_map/all_to_all | solution.py:143
  240.3 1.2 broadcast_in_dim_reshape.6
  (87 shorter events, 20.3 us)
Async XLA Ops:
  6.2 4.9 %copy-start = (bf16[8,1,32,16,256]{4,3,2,1,0:T(8,128)(2,1)}, bf16[8,1,32,16,256]{4,3,2,1,0:T(8,128)(2,1)S(1)}, u32[]{:S(2)}) copy-start(bf16[8,1,32,16,256]{4,3,2,1,0:T(8,128)(2,1)S(1)} %get-tuple-element.7) | copy-start | bytes 6291460
  6.9 2.1 copy-start.3
  11.8 2.0 copy-start.5
  13.9 2.1 copy-start.21
  19.8 3.2 %copy-start.15 = (f32[16,48,256]{1,2,0:S(1)}, f32[16,48,256]{1,2,0}, u32[]{:S(2)}) copy-start(f32[16,48,256]{1,2,0} %fusion.123) | copy-start | bytes 2359300
  19.8 3.2 %copy-start.16 = (f32[16,48,256]{1,2,0:S(1)}, f32[16,48,256]{1,2,0}, u32[]{:S(2)}) copy-start(f32[16,48,256]{1,2,0} %fusion.126) | copy-start | bytes 2359300
  19.8 4.8 %copy-start.17 = (f32[16,48,256]{1,2,0:S(1)}, f32[16,48,256]{1,2,0}, u32[]{:S(2)}) copy-start(f32[16,48,256]{1,2,0} %fusion.125) | copy-start | bytes 2359300
  19.8 6.5 %copy-start.18 = (f32[16,48,256]{1,2,0:S(1)}, f32[16,48,256]{1,2,0}, u32[]{:S(2)}) copy-start(f32[16,48,256]{1,2,0} %fusion.124) | copy-start | bytes 2359300
  23.0 5.4 %copy-start.9 = (bf16[16,1,32,8,256]{4,3,2,1,0:T(8,128)(2,1)}, bf16[16,1,32,8,256]{4,3,2,1,0:T(8,128)(2,1)S(1)}, u32[]{:S(2)}) copy-start(bf16[16,1,32,8,256]{4,3,2,1,0:T(8,128)(2,1)S(1)} %get-tuple-element.5) | copy-start | bytes 6291460
  23.0 7.1 %copy-start.7 = (bf16[16,1,32,8,256]{4,3,2,1,0:T(8,128)(2,1)}, bf16[16,1,32,8,256]{4,3,2,1,0:T(8,128)(2,1)S(1)}, u32[]{:S(2)}) copy-start(bf16[16,1,32,8,256]{4,3,2,1,0:T(8,128)(2,1)S(1)} %get-tuple-element.4) | copy-start | bytes 6291460
  31.6 8.1 %collective-permute-start = (bf16[4,2,48,256]{3,2,1,0:T(8,128)(2,1)}, bf16[4,2,48,256]{3,2,1,0:T(8,128)(2,1)}, u32[]{:S(2)}, u32[]{:S(2)}) collective-permute-start(bf16[4,2,48,256]{3,2,1,0:T(8,128)(2,1)} %fusion.120), channel_id=1, source_target_pairs={{0,2},{2,0},{1,3},{3,1},{4,6},{6,4},{5,7},{7,5},{8,10},{10,8},{9,1... | collective-permute-start | bytes 589832 | tf_op jit(solution)/shard_map/ppermute | solution.py:205
  41.4 11.7 %all-to-all-start = ((bf16[4,2,48,256]{3,2,1,0:T(8,128)(2,1)}), bf16[4,2,48,256]{3,2,1,0:T(8,128)(2,1)S(1)}, u32[]{:S(2)}, u32[]{:S(2)}) async-start(bf16[4,2,48,256]{3,2,1,0:T(8,128)(2,1)} %add_convert_fusion.1), calls=%async_computation | async-start | bytes 393216 | tf_op jit(solution)/shard_map/all_to_all | solution.py:137
  53.1 0.7 copy-start.20
  56.5 11.3 %all-to-all-start.1 = ((bf16[4,2,48,256]{3,2,1,0:T(8,128)(2,1)}), bf16[4,2,48,256]{3,2,1,0:T(8,128)(2,1)S(1)}, u32[]{:S(2)}, u32[]{:S(2)}) async-start(bf16[4,2,48,256]{3,2,1,0:T(8,128)(2,1)} %bitcast.477), calls=%async_computation.1 | async-start | bytes 393216 | tf_op jit(solution)/shard_map/all_to_all | solution.py:143
  61.6 3.6 %copy-start.19 = (bf16[16,32,8,256]{3,2,1,0:T(8,128)(2,1)S(1)}, bf16[16,32,8,256]{3,2,1,0:T(8,128)(2,1)}, u32[]{:S(2)}) copy-start(bf16[16,32,8,256]{3,2,1,0:T(8,128)(2,1)} %get-tuple-element.3) | copy-start | bytes 6291460
  74.2 2.4 %copy-start.11 = (bf16[16,32,8,256]{3,1,0,2:T(8,128)(2,1)S(1)}, bf16[16,32,8,256]{3,1,0,2:T(8,128)(2,1)}, u32[]{:S(2)}) copy-start(bf16[16,32,8,256]{3,1,0,2:T(8,128)(2,1)} %copy.114) | copy-start | bytes 6291460
  76.6 1.6 copy-start.13
  79.5 1.6 copy-start.1
  85.6 25.0 %all-to-all-start.2 = ((bf16[16,2,48,256]{3,2,1,0:T(8,128)(2,1)}), bf16[16,2,48,256]{3,2,1,0:T(8,128)(2,1)}, u32[]{:S(2)}, u32[]{:S(2)}) async-start(bf16[16,2,48,256]{3,2,1,0:T(8,128)(2,1)} %copy.123), calls=%async_computation.2 | async-start | bytes 1572864 | tf_op jit(solution)/shard_map/all_to_all | solution.py:137
  118.5 21.8 %copy-start.6 = (bf16[8,1,32,16,256]{4,2,0,3,1:T(8,128)(2,1)S(1)}, bf16[8,1,32,16,256]{4,2,0,3,1:T(8,128)(2,1)}, u32[]{:S(2)}) copy-start(bf16[8,1,32,16,256]{4,2,0,3,1:T(8,128)(2,1)} %copy-done.5) | copy-start | bytes 6291460
  141.1 1.6 copy-start.4
  144.0 1.6 copy-start.10
  146.5 1.6 copy-start.8
  149.9 5.7 %collective-permute-start.1 = (bf16[4,2,48,256]{3,2,1,0:T(8,128)(2,1)S(1)}, bf16[4,2,48,256]{3,2,1,0:T(8,128)(2,1)S(1)}, u32[]{:S(2)}, u32[]{:S(2)}) collective-permute-start(bf16[4,2,48,256]{3,2,1,0:T(8,128)(2,1)S(1)} %fusion.116), channel_id=1, source_target_pairs={{0,2},{2,0},{1,3},{3,1},{4,6},{6,4},{5,7},{7,5},{8,10},{10,8},{9,1... | collective-permute-start | bytes 589832 | tf_op jit(solution)/shard_map/ppermute | solution.py:205
  184.7 2.4 %copy-start.12 = (bf16[16,32,8,256]{3,1,0,2:T(8,128)(2,1)S(1)}, bf16[16,32,8,256]{3,1,0,2:T(8,128)(2,1)}, u32[]{:S(2)}) copy-start(bf16[16,32,8,256]{3,1,0,2:T(8,128)(2,1)} %copy.114) | copy-start | bytes 6291460
  187.1 1.6 copy-start.14
  190.1 1.6 copy-start.2
  220.2 19.5 %all-to-all-start.7 = ((bf16[16,2,48,256]{3,2,1,0:T(8,128)(2,1)}), bf16[16,2,48,256]{3,2,1,0:T(8,128)(2,1)S(1)}, u32[]{:S(2)}, u32[]{:S(2)}) async-start(bf16[16,2,48,256]{3,2,1,0:T(8,128)(2,1)} %bitcast.471), calls=%async_computation.7 | async-start | bytes 1572864 | tf_op jit(solution)/shard_map/all_to_all | solution.py:143

commit v5 on v1

--- a/solution.py
+++ b/solution.py
@@ -229,7 +229,7 @@
     rec_tiles = onset_rec.shape[1] // TILE
     rec_picked = window_gather(parts, onset_pieces(onset_rec, rec_tiles, parts, place))
     src_picked = window_gather(parts, onset_pieces(onset_src, col_tiles, parts, place))
-    direct = tile_major(focus_direct[0])
+    direct = lax.optimization_barrier(tile_major(focus_direct[0]))
     direct_f32 = direct.astype(jnp.float32)
     plus = direct
     minus = None

time: 242 us -> 241 us (level)
  no operation moved by 1% of the time
where the time goes in v5:
time: 241 us; the launch traced here: 239 us
  blocking collectives  71.7 us (30%)
  Pallas kernels  40 us (17%)
  local copies, waits for them, and re-layouts  37.9 us (16%)
  matrix products  33.6 us (14%)
  starting transfers between devices  22.7 us (9%)
  waiting for transfers between devices  21.1 us (9%)
  other arithmetic  10.8 us (4%)
    all_to_all x2, blocking collectives, exchange_back(): got = lax.all_to_all(flat, 'freq', split_axis=0, concat_axis=0, tiled=True)  31.8 us
    all_to_all x2, blocking collectives, exchange(): lax.all_to_all(pieces, 'freq', split_axis=0, concat_axis=0, tiled=True)  26.9 us
    unnamed x52, local copies, waits for them, and re-layouts  22.2 us
    pallas_call x2, Pallas kernels, window_gather(): pl.pallas_call(gather_kernel, grid=(blocks, points // rows), in_specs=[pl...  21.8 us
    unnamed x16, matrix products  19.9 us
    pallas_call x4, Pallas kernels, window(): pl.pallas_call(window_kernel, grid=(blocks,), in_specs=[pl.BlockSpec((siz...  18.2 us
    all_to_all x2, waiting for transfers between devices, exchange_back(): got = lax.all_to_all(flat, 'freq', split_axis=0, concat_axis=0, tiled=True)  15.9 us
    all_gather x2, blocking collectives, per_device(): minus_all = lax.all_gather(minus, 'src', axis=0, tiled=True)  12.9 us
  transfers between devices with their start and end apart: 6, of which 4 were waited for; matrix products, arithmetic and copies ran while one was open for 7% of the time, Pallas kernels for 9%

profile of v5, /device:TPU:0, one launch (start us, length us, event | category | flops | bytes accessed | tf_op | source)
XLA Modules:
  0.0 238.9 jit_solution(8054457013788304120)
XLA Ops:
  0.6 1.3 copy.161
  2.2 3.6 %copy.163 = bf16[64,8,16,256]{3,2,1,0:T(8,128)(2,1)S(1)} copy(bf16[64,8,16,256]{3,1,2,0:T(8,128)(2,1)} %bitcast.464) | data formatting | bytes 8388608
  6.9 2.1 fusion.123
  9.0 2.1 fusion.126
  11.8 2.0 fusion.125
  13.9 2.1 fusion.124
  16.1 3.7 %copy.164 = bf16[128,8,8,256]{3,2,1,0:T(8,128)(2,1)S(1)} copy(bf16[128,8,8,256]{3,1,2,0:T(8,128)(2,1)} %bitcast.465) | data formatting | bytes 8388608
  19.8 3.2 %slice_bitcast_fusion.25 = (bf16[16,32,8,256]{3,2,1,0:T(8,128)(2,1)}, bf16[16,32,8,256]{3,2,1,0:T(8,128)(2,1)}, bf16[16,1,32,8,256]{4,3,2,1,0:T(8,128)(2,1)S(1)}, bf16[16,1,32,8,256]{4,3,2,1,0:T(8,128)(2,1)S(1)}) fusion(bf16[16,2,32,8,256]{4,3,2,1,0:T(8,128)(2,1)S(1)} %bitcast.446), kind=kLoop, calls=%fused_computation.159 | loop fusion | bytes 12582912 | tf_op jit(solution)/shard_map/squeeze | solution.py:164
  23.0 1.6 copy-done.17
  24.6 1.7 copy-done.18
  26.3 1.2 fusion.3
  27.5 0.8 fusion.99
  28.3 0.8 fusion.98
  29.2 0.9 fusion.111
  30.1 0.9 fusion.113
  31.6 2.9 %collective-permute-start = (bf16[4,2,48,256]{3,2,1,0:T(8,128)(2,1)}, bf16[4,2,48,256]{3,2,1,0:T(8,128)(2,1)}, u32[]{:S(2)}, u32[]{:S(2)}) collective-permute-start(bf16[4,2,48,256]{3,2,1,0:T(8,128)(2,1)} %fusion.120), channel_id=1, source_target_pairs={{0,2},{2,0},{1,3},{3,1},{4,6},{6,4},{5,7},{7,5},{8,10},{10,8},{9,1... | collective-permute-start | bytes 589832 | tf_op jit(solution)/shard_map/ppermute | solution.py:204
  36.3 1.0 reshape.161
  38.7 1.1 collective-permute-done
  39.8 1.7 add_convert_fusion.1
  41.4 5.1 %all-to-all-start = ((bf16[4,2,48,256]{3,2,1,0:T(8,128)(2,1)}), bf16[4,2,48,256]{3,2,1,0:T(8,128)(2,1)S(1)}, u32[]{:S(2)}, u32[]{:S(2)}) async-start(bf16[4,2,48,256]{3,2,1,0:T(8,128)(2,1)} %add_convert_fusion.1), calls=%async_computation | async-start | bytes 393216 | tf_op jit(solution)/shard_map/all_to_all | solution.py:136
  48.0 5.2 %shard_map.78.matrix_ref = f32[64,1,48,256]{3,2,1,0:T(8,128)} custom-call(bf16[128,256]{1,0:T(8,128)(2,1)} %maximum_bitcast_fusion.table_ref, s32[1,48,256]{2,1,0:T(8,128)} %bitcast.479), custom_call_target="tpu_custom_call" | custom-call | tf_op jit(solution)/shard_map/pallas_call | solution.py:53
  53.8 2.8 %shard_map.79 = bf16[4,1,2,48,256]{4,3,2,1,0:T(8,128)(2,1)} custom-call(f32[64,1,48,256]{3,2,1,0:T(8,128)} %shard_map.78.matrix_ref, bf16[4,1,2,48,256]{4,3,2,1,0:T(8,128)(2,1)} %bitcast.472), custom_call_target="tpu_custom_call" | custom-call | tf_op jit(solution)/shard_map/pallas_call | solution.py:89
  56.6 5.1 %all-to-all-start.1 = ((bf16[4,2,48,256]{3,2,1,0:T(8,128)(2,1)}), bf16[4,2,48,256]{3,2,1,0:T(8,128)(2,1)S(1)}, u32[]{:S(2)}, u32[]{:S(2)}) async-start(bf16[4,2,48,256]{3,2,1,0:T(8,128)(2,1)} %bitcast.473), calls=%async_computation.1 | async-start | bytes 393216 | tf_op jit(solution)/shard_map/all_to_all | solution.py:142
  61.7 3.5 %copy.114 = bf16[16,32,8,256]{3,1,0,2:T(8,128)(2,1)} copy(bf16[16,32,8,256]{3,2,1,0:T(8,128)(2,1)} %get-tuple-element.2) | data formatting | bytes 4194304 | tf_op jit(solution)/shard_map/squeeze | solution.py:164
  65.3 1.9 copy.116
  68.0 6.3 %all_gather.6 = bf16[8,2,48,256]{3,2,1,0:T(8,128)(2,1)S(1)} all-gather(bf16[4,2,48,256]{3,2,1,0:T(8,128)(2,1)S(1)} %all-to-all-done.1), channel_id=1, replica_groups=mesh['groups'=2,'freq'=4,'src'=2,'vp'=2] {'src'}, dimensions={0}, use_global_device_ids=true | all-gather | bytes 589824 | tf_op jit(solution)/shard_map/all_gather | solution.py:243
  74.3 2.4 %fusion.133 = f32[8,48,512]{1,2,0:S(1)} fusion(bf16[8,256,512]{1,2,0:T(8,128)(2,1)} %bitcast.432, bf16[8,2,48,256]{3,2,1,0:T(8,128)(2,1)S(1)} %all_gather.6), kind=kOutput, calls=%fused_computation.127 | convolution fusion | flops 100663296 | bytes 4390912
  77.4 0.9 copy-done.13
  79.7 1.2 fusion.27
  81.3 0.9 fusion.44
  82.2 0.9 fusion.47
  83.0 0.9 fusion.89
  83.9 0.8 fusion.86
  84.8 1.0 copy.123
  85.8 4.5 %all-to-all-start.2 = ((bf16[16,2,48,256]{3,2,1,0:T(8,128)(2,1)}), bf16[16,2,48,256]{3,2,1,0:T(8,128)(2,1)}, u32[]{:S(2)}, u32[]{:S(2)}) async-start(bf16[16,2,48,256]{3,2,1,0:T(8,128)(2,1)} %copy.123), calls=%async_computation.2 | async-start | bytes 1572864 | tf_op jit(solution)/shard_map/all_to_all | solution.py:136
  90.3 2.3 copy.162
  92.5 1.0 constant_dynamic-slice_fusion.1
  94.3 16.6 %shard_map.77.matrix_ref = f32[64,4,48,256]{3,2,1,0:T(8,128)} custom-call(bf16[128,256]{1,0:T(8,128)(2,1)} %maximum_bitcast_fusion.table_ref, s32[4,48,256]{2,1,0:T(8,128)} %bitcast.478), custom_call_target="tpu_custom_call" | custom-call | tf_op jit(solution)/shard_map/pallas_call | solution.py:53
  110.9 6.3 %shard_map.80 = bf16[4,4,2,48,256]{4,3,2,1,0:T(8,128)(2,1)} custom-call(f32[64,4,48,256]{3,2,1,0:T(8,128)} %shard_map.77.matrix_ref, bf16[4,4,2,48,256]{4,3,2,1,0:T(8,128)(2,1)} %bitcast.62.spectrum_ref), custom_call_target="tpu_custom_call" | custom-call | tf_op jit(solution)/shard_map/pallas_call | solution.py:89
  117.2 21.7 %all_to_all.40 = bf16[16,2,48,256]{3,2,1,0:T(8,128)(2,1)S(1)} all-to-all(bf16[16,2,48,256]{3,2,1,0:T(8,128)(2,1)} %bitcast.468), channel_id=1, replica_groups=mesh['groups'=2,'freq'=4,'src'=2,'vp'=2] {'freq'}, dimensions={0} | all-to-all | bytes 1572864 | tf_op jit(solution)/shard_map/all_to_all | solution.py:142
  140.4 0.9 copy-done.4
  142.7 1.3 fusion.1
  144.3 0.8 fusion.101
  145.2 0.9 fusion.100
  146.7 0.9 fusion.107
  147.6 0.9 fusion.109
  148.5 1.5 collective-permute-start.1
  150.1 4.2 %collective-permute-done.1 = bf16[4,2,48,256]{3,2,1,0:T(8,128)(2,1)S(1)} collective-permute-done((bf16[4,2,48,256]{3,2,1,0:T(8,128)(2,1)S(1)}, bf16[4,2,48,256]{3,2,1,0:T(8,128)(2,1)S(1)}, u32[]{:S(2)}, u32[]{:S(2)}) %collective-permute-start.1) | collective-permute-done | bytes 196640 | tf_op jit(solution)/shard_map/ppermute | solution.py:204
  154.3 9.9 %all_to_all.41 = bf16[4,2,48,256]{3,2,1,0:T(8,128)(2,1)} all-to-all(bf16[4,2,48,256]{3,2,1,0:T(8,128)(2,1)S(1)} %add_convert_fusion), channel_id=1, replica_groups=mesh['groups'=2,'freq'=4,'src'=2,'vp'=2] {'freq'}, dimensions={0} | all-to-all | bytes 393216 | tf_op jit(solution)/shard_map/all_to_all | solution.py:136
  164.2 2.8 %shard_map.81 = bf16[4,1,2,48,256]{4,3,2,1,0:T(8,128)(2,1)} custom-call(f32[64,1,48,256]{3,2,1,0:T(8,128)} %shard_map.78.matrix_ref, bf16[4,1,2,48,256]{4,3,2,1,0:T(8,128)(2,1)} %bitcast.474), custom_call_target="tpu_custom_call" | custom-call | tf_op jit(solution)/shard_map/pallas_call | solution.py:89
  167.0 10.1 %all_to_all.42 = bf16[4,2,48,256]{3,2,1,0:T(8,128)(2,1)S(1)} all-to-all(bf16[4,2,48,256]{3,2,1,0:T(8,128)(2,1)} %bitcast.475), channel_id=1, replica_groups=mesh['groups'=2,'freq'=4,'src'=2,'vp'=2] {'freq'}, dimensions={0} | all-to-all | bytes 393216 | tf_op jit(solution)/shard_map/all_to_all | solution.py:142
  177.1 6.6 %all_gather.7 = bf16[8,2,48,256]{3,2,1,0:T(8,128)(2,1)S(1)} all-gather(bf16[4,2,48,256]{3,2,1,0:T(8,128)(2,1)S(1)} %all_to_all.42), channel_id=1, replica_groups=mesh['groups'=2,'freq'=4,'src'=2,'vp'=2] {'src'}, dimensions={0}, use_global_device_ids=true | all-gather | bytes 589824 | tf_op jit(solution)/shard_map/all_gather | solution.py:243
  183.7 2.4 %fusion.137 = f32[8,48,512]{1,2,0:S(1)} fusion(bf16[8,256,512]{1,2,0:T(8,128)(2,1)} %bitcast.433, bf16[8,2,48,256]{3,2,1,0:T(8,128)(2,1)S(1)} %all_gather.7), kind=kOutput, calls=%fused_computation.131 | convolution fusion | flops 100663296 | bytes 4390912
  186.9 0.9 copy-done.14
  189.1 1.2 fusion.23
  190.7 0.9 fusion.38
  191.6 0.9 fusion.41
  192.4 0.9 fusion.95
  193.3 0.8 fusion.92
  194.3 17.1 %all_to_all.43 = bf16[16,2,48,256]{3,2,1,0:T(8,128)(2,1)} all-to-all(bf16[16,2,48,256]{3,2,1,0:T(8,128)(2,1)S(1)} %copy.135), channel_id=1, replica_groups=mesh['groups'=2,'freq'=4,'src'=2,'vp'=2] {'freq'}, dimensions={0} | all-to-all | bytes 1572864 | tf_op jit(solution)/shard_map/all_to_all | solution.py:136
  211.4 6.3 %shard_map.82 = bf16[4,4,2,48,256]{4,3,2,1,0:T(8,128)(2,1)} custom-call(f32[64,4,48,256]{3,2,1,0:T(8,128)} %shard_map.77.matrix_ref, bf16[4,4,2,48,256]{4,3,2,1,0:T(8,128)(2,1)} %bitcast.467), custom_call_target="tpu_custom_call" | custom-call | tf_op jit(solution)/shard_map/pallas_call | solution.py:89
  217.7 3.5 %all-to-all-start.7 = ((bf16[16,2,48,256]{3,2,1,0:T(8,128)(2,1)}), bf16[16,2,48,256]{3,2,1,0:T(8,128)(2,1)S(1)}, u32[]{:S(2)}, u32[]{:S(2)}) async-start(bf16[16,2,48,256]{3,2,1,0:T(8,128)(2,1)} %bitcast.466), calls=%async_computation.7 | async-start | bytes 1572864 | tf_op jit(solution)/shard_map/all_to_all | solution.py:142
  222.2 15.0 %all-to-all-done.7 = bf16[16,2,48,256]{3,2,1,0:T(8,128)(2,1)S(1)} async-done(((bf16[16,2,48,256]{3,2,1,0:T(8,128)(2,1)}), bf16[16,2,48,256]{3,2,1,0:T(8,128)(2,1)S(1)}, u32[]{:S(2)}, u32[]{:S(2)}) %all-to-all-start.7) | async-done | bytes 786464 | tf_op jit(solution)/shard_map/all_to_all | solution.py:142
  237.6 1.2 broadcast_in_dim_reshape.6
  (87 shorter events, 20.3 us)
Async XLA Ops:
  6.2 4.9 %copy-start = (bf16[8,1,32,16,256]{4,3,2,1,0:T(8,128)(2,1)}, bf16[8,1,32,16,256]{4,3,2,1,0:T(8,128)(2,1)S(1)}, u32[]{:S(2)}) copy-start(bf16[8,1,32,16,256]{4,3,2,1,0:T(8,128)(2,1)S(1)} %get-tuple-element.7) | copy-start | bytes 6291460
  6.9 2.1 copy-start.3
  11.8 2.1 copy-start.5
  13.9 2.1 copy-start.21
  19.8 3.2 %copy-start.15 = (f32[16,48,256]{1,2,0:S(1)}, f32[16,48,256]{1,2,0}, u32[]{:S(2)}) copy-start(f32[16,48,256]{1,2,0} %fusion.123) | copy-start | bytes 2359300
  19.8 3.2 %copy-start.16 = (f32[16,48,256]{1,2,0:S(1)}, f32[16,48,256]{1,2,0}, u32[]{:S(2)}) copy-start(f32[16,48,256]{1,2,0} %fusion.126) | copy-start | bytes 2359300
  19.8 4.8 %copy-start.17 = (f32[16,48,256]{1,2,0:S(1)}, f32[16,48,256]{1,2,0}, u32[]{:S(2)}) copy-start(f32[16,48,256]{1,2,0} %fusion.125) | copy-start | bytes 2359300
  19.8 6.5 %copy-start.18 = (f32[16,48,256]{1,2,0:S(1)}, f32[16,48,256]{1,2,0}, u32[]{:S(2)}) copy-start(f32[16,48,256]{1,2,0} %fusion.124) | copy-start | bytes 2359300
  23.0 5.4 %copy-start.9 = (bf16[16,1,32,8,256]{4,3,2,1,0:T(8,128)(2,1)}, bf16[16,1,32,8,256]{4,3,2,1,0:T(8,128)(2,1)S(1)}, u32[]{:S(2)}) copy-start(bf16[16,1,32,8,256]{4,3,2,1,0:T(8,128)(2,1)S(1)} %get-tuple-element.5) | copy-start | bytes 6291460
  23.0 7.1 %copy-start.7 = (bf16[16,1,32,8,256]{4,3,2,1,0:T(8,128)(2,1)}, bf16[16,1,32,8,256]{4,3,2,1,0:T(8,128)(2,1)S(1)}, u32[]{:S(2)}) copy-start(bf16[16,1,32,8,256]{4,3,2,1,0:T(8,128)(2,1)S(1)} %get-tuple-element.4) | copy-start | bytes 6291460
  31.6 8.2 %collective-permute-start = (bf16[4,2,48,256]{3,2,1,0:T(8,128)(2,1)}, bf16[4,2,48,256]{3,2,1,0:T(8,128)(2,1)}, u32[]{:S(2)}, u32[]{:S(2)}) collective-permute-start(bf16[4,2,48,256]{3,2,1,0:T(8,128)(2,1)} %fusion.120), channel_id=1, source_target_pairs={{0,2},{2,0},{1,3},{3,1},{4,6},{6,4},{5,7},{7,5},{8,10},{10,8},{9,1... | collective-permute-start | bytes 589832 | tf_op jit(solution)/shard_map/ppermute | solution.py:204
  41.4 11.7 %all-to-all-start = ((bf16[4,2,48,256]{3,2,1,0:T(8,128)(2,1)}), bf16[4,2,48,256]{3,2,1,0:T(8,128)(2,1)S(1)}, u32[]{:S(2)}, u32[]{:S(2)}) async-start(bf16[4,2,48,256]{3,2,1,0:T(8,128)(2,1)} %add_convert_fusion.1), calls=%async_computation | async-start | bytes 393216 | tf_op jit(solution)/shard_map/all_to_all | solution.py:136
  53.1 0.7 copy-start.20
  56.6 11.3 %all-to-all-start.1 = ((bf16[4,2,48,256]{3,2,1,0:T(8,128)(2,1)}), bf16[4,2,48,256]{3,2,1,0:T(8,128)(2,1)S(1)}, u32[]{:S(2)}, u32[]{:S(2)}) async-start(bf16[4,2,48,256]{3,2,1,0:T(8,128)(2,1)} %bitcast.473), calls=%async_computation.1 | async-start | bytes 393216 | tf_op jit(solution)/shard_map/all_to_all | solution.py:142
  61.7 3.6 %copy-start.19 = (bf16[16,32,8,256]{3,2,1,0:T(8,128)(2,1)S(1)}, bf16[16,32,8,256]{3,2,1,0:T(8,128)(2,1)}, u32[]{:S(2)}) copy-start(bf16[16,32,8,256]{3,2,1,0:T(8,128)(2,1)} %get-tuple-element.3) | copy-start | bytes 6291460
  74.3 2.4 %copy-start.11 = (bf16[16,32,8,256]{3,1,0,2:T(8,128)(2,1)S(1)}, bf16[16,32,8,256]{3,1,0,2:T(8,128)(2,1)}, u32[]{:S(2)}) copy-start(bf16[16,32,8,256]{3,1,0,2:T(8,128)(2,1)} %copy.114) | copy-start | bytes 6291460
  76.7 1.6 copy-start.13
  79.7 1.6 copy-start.1
  85.8 25.1 %all-to-all-start.2 = ((bf16[16,2,48,256]{3,2,1,0:T(8,128)(2,1)}), bf16[16,2,48,256]{3,2,1,0:T(8,128)(2,1)}, u32[]{:S(2)}, u32[]{:S(2)}) async-start(bf16[16,2,48,256]{3,2,1,0:T(8,128)(2,1)} %copy.123), calls=%async_computation.2 | async-start | bytes 1572864 | tf_op jit(solution)/shard_map/all_to_all | solution.py:136
  117.2 21.9 %copy-start.6 = (bf16[8,1,32,16,256]{4,2,0,3,1:T(8,128)(2,1)S(1)}, bf16[8,1,32,16,256]{4,2,0,3,1:T(8,128)(2,1)}, u32[]{:S(2)}) copy-start(bf16[8,1,32,16,256]{4,2,0,3,1:T(8,128)(2,1)} %copy-done.5) | copy-start | bytes 6291460
  139.7 1.6 copy-start.4
  142.7 1.6 copy-start.10
  145.2 1.6 copy-start.8
  148.5 5.7 %collective-permute-start.1 = (bf16[4,2,48,256]{3,2,1,0:T(8,128)(2,1)S(1)}, bf16[4,2,48,256]{3,2,1,0:T(8,128)(2,1)S(1)}, u32[]{:S(2)}, u32[]{:S(2)}) collective-permute-start(bf16[4,2,48,256]{3,2,1,0:T(8,128)(2,1)S(1)} %fusion.116), channel_id=1, source_target_pairs={{0,2},{2,0},{1,3},{3,1},{4,6},{6,4},{5,7},{7,5},{8,10},{10,8},{9,1... | collective-permute-start | bytes 589832 | tf_op jit(solution)/shard_map/ppermute | solution.py:204
  183.7 2.4 %copy-start.12 = (bf16[16,32,8,256]{3,1,0,2:T(8,128)(2,1)S(1)}, bf16[16,32,8,256]{3,1,0,2:T(8,128)(2,1)}, u32[]{:S(2)}) copy-start(bf16[16,32,8,256]{3,1,0,2:T(8,128)(2,1)} %copy.114) | copy-start | bytes 6291460
  186.2 1.6 copy-start.14
  189.1 1.6 copy-start.2
  217.7 19.5 %all-to-all-start.7 = ((bf16[16,2,48,256]{3,2,1,0:T(8,128)(2,1)}), bf16[16,2,48,256]{3,2,1,0:T(8,128)(2,1)S(1)}, u32[]{:S(2)}, u32[]{:S(2)}) async-start(bf16[16,2,48,256]{3,2,1,0:T(8,128)(2,1)} %bitcast.466), calls=%async_computation.7 | async-start | bytes 1572864 | tf_op jit(solution)/shard_map/all_to_all | solution.py:142

commit v6 on v1

--- a/solution.py
+++ b/solution.py
@@ -37,13 +37,18 @@
         out_ref[:, 0, row, :] = parts[:size] + parts[size:]
 
 
-def window_gather(count, onset):
+def window_gather(count, onset, target=None):
     if count > GATHER_MAX:
         return onset
     inverse, forward = make_tables(count)
     terms = jnp.einsum("cft,dgt->tgdfc", forward, inverse, precision=lax.Precision.HIGHEST)
     size = 4 * count * count
     table = jnp.cumsum(terms.reshape(NT, size), axis=0)
+    if target is not None:
+        table = table.reshape(NT, 2 * count, count, 2)
+        table = lax.dynamic_index_in_dim(table, target, 2, keepdims=False)
+        size = 4 * count
+        table = table.reshape(NT, size)
     high = table.astype(jnp.bfloat16)
     rest = table - high.astype(jnp.float32)
     low = rest.astype(jnp.bfloat16)
@@ -71,6 +76,32 @@
         for q in range(1, comps):
             total = total + matrix_ref[q * comps + target, 0] * source[q]
         out_ref[target // 2, 0, target % 2] = total.astype(out_ref.dtype)
+
+
+def own_window_kernel(matrix_ref, spectrum_ref, out_ref):
+    count = spectrum_ref.shape[0]
+    comps = 2 * count
+    source = [spectrum_ref[q // 2, 0, q % 2].astype(jnp.float32) for q in range(comps)]
+    for target in range(2):
+        total = matrix_ref[target, 0] * source[0]
+        for q in range(1, comps):
+            total = total + matrix_ref[q * 2 + target, 0] * source[q]
+        out_ref[0, target] = total.astype(out_ref.dtype)
+
+
+def own_window(spectrum, picked):
+    _, blocks, comps, points, width = spectrum.shape
+    size = picked.shape[0]
+    return pl.pallas_call(
+        own_window_kernel,
+        grid=(blocks,),
+        in_specs=[
+            pl.BlockSpec((size, 1, points, width), lambda b: (0, b, 0, 0)),
+            pl.BlockSpec((spectrum.shape[0], 1, comps, points, width), lambda b: (0, b, 0, 0, 0)),
+        ],
+        out_specs=pl.BlockSpec((1, comps, points, width), lambda b: (b, 0, 0, 0)),
+        out_shape=jax.ShapeDtypeStruct((blocks, comps, points, width), jnp.bfloat16),
+    )(picked, spectrum)
 
 
 def window(spectrum, picked):
@@ -227,7 +258,11 @@
     rank_index = jnp.arange(RANK, dtype=jnp.int32)
     mask = (rank_index[None, None, :] < tile_ranks[0][:, :, None])[:, None]
     rec_tiles = onset_rec.shape[1] // TILE
-    rec_picked = window_gather(parts, onset_pieces(onset_rec, rec_tiles, parts, place))
+    own_rec = parts <= GATHER_MAX
+    if own_rec:
+        rec_picked = window_gather(parts, onset_pieces(onset_rec, rec_tiles, 1, 0), place)
+    else:
+        rec_picked = window_gather(parts, onset_pieces(onset_rec, rec_tiles, parts, place))
     src_picked = window_gather(parts, onset_pieces(onset_src, col_tiles, parts, place))
     direct = tile_major(focus_direct[0])
     direct_f32 = direct.astype(jnp.float32)
@@ -237,9 +272,13 @@
         z_real, z_imag = coefficients(v_tiles, mask, plus)
         partial_terms = expand_rows(u_tiles, z_real, z_imag)
         summed = reduce_src(partial_terms)
-        traces = exchange(summed, parts)
-        windowed = window(traces, rec_picked)
-        minus = exchange_back(windowed, rec_tiles)
+        if own_rec:
+            traces = lax.all_gather(summed, "freq", axis=0, tiled=False)
+            minus = own_window(traces, rec_picked)
+        else:
+            traces = exchange(summed, parts)
+            windowed = window(traces, rec_picked)
+            minus = exchange_back(windowed, rec_tiles)
         minus_all = lax.all_gather(minus, "src", axis=0, tiled=True)
         adjoint = adjoint_local(u_tiles, v_tiles, mask, minus_all)
         source_traces = exchange(adjoint.astype(jnp.bfloat16), parts)

time: 242 us -> 253 us (1.045)
  blocking collectives: 71.6 us -> 86.5 us
  Pallas kernels: 40 us -> 51.3 us
  starting transfers between devices: 22.7 us -> 11.5 us
  waiting for transfers between devices: 21.1 us -> 17.2 us
    all_gather x0 -> x2, blocking collectives: none -> 37.2 us  [per_device(): traces = lax.all_gather(summed, 'freq', axis=0, tiled=False)]
    all_to_all x2 -> x1, blocking collectives: 31.8 us -> 20 us  [exchange_back(): got = lax.all_to_all(flat, 'freq', split_axis=0, concat_axis=0, tiled=True)]
    all_to_all x2 -> x1, blocking collectives: 26.9 us -> 16.2 us  [exchange(): lax.all_to_all(pieces, 'freq', split_axis=0, concat_axis=0, tiled=True)]
    pallas_call x2, Pallas kernels: 21.8 us -> 31 us  [window_gather(): pl.pallas_call(gather_kernel, grid=(blocks, points // rows), in_specs=[pl...]
    pallas_call x0 -> x2, Pallas kernels: none -> 7.6 us  [own_window(): pl.pallas_call(own_window_kernel, grid=(blocks,), in_specs=[pl.BlockSpec(...]
    pallas_call x4 -> x2, Pallas kernels: 18.2 us -> 12.6 us  [window(): pl.pallas_call(window_kernel, grid=(blocks,), in_specs=[pl.BlockSpec((siz...]
    all_to_all x2 -> x1, starting transfers between devices: 9.63 us -> 4.42 us  [exchange(): lax.all_to_all(pieces, 'freq', split_axis=0, concat_axis=0, tiled=True)]
    all_to_all x2 -> x1, starting transfers between devices: 8.57 us -> 3.49 us  [exchange_back(): got = lax.all_to_all(flat, 'freq', split_axis=0, concat_axis=0, tiled=True)]
  transfers between devices with their start and end apart: 6 -> 4, of which waited for: 4 -> 2; matrix products, arithmetic and copies ran while one was open for 7% -> 6% of each run, Pallas kernels for 9% -> 12%
where the time goes in v6:
time: 253 us; the launch traced here: 250 us
  blocking collectives  86.5 us (34%)
  Pallas kernels  51.3 us (20%)
  local copies, waits for them, and re-layouts  38.3 us (15%)
  matrix products  33.6 us (13%)
  waiting for transfers between devices  17.2 us (7%)
  starting transfers between devices  11.5 us (5%)
  other arithmetic  10 us (4%)
    all_gather x2, blocking collectives, per_device(): traces = lax.all_gather(summed, 'freq', axis=0, tiled=False)  37.2 us
    pallas_call x2, Pallas kernels, window_gather(): pl.pallas_call(gather_kernel, grid=(blocks, points // rows), in_specs=[pl...  31 us
    unnamed x52, local copies, waits for them, and re-layouts  20.7 us
    all_to_all x1, blocking collectives, exchange_back(): got = lax.all_to_all(flat, 'freq', split_axis=0, concat_axis=0, tiled=True)  20 us
    unnamed x16, matrix products  19.9 us
    all_to_all x1, blocking collectives, exchange(): lax.all_to_all(pieces, 'freq', split_axis=0, concat_axis=0, tiled=True)  16.2 us
    all_gather x2, blocking collectives, per_device(): minus_all = lax.all_gather(minus, 'src', axis=0, tiled=True)  13.1 us
    pallas_call x2, Pallas kernels, window(): pl.pallas_call(window_kernel, grid=(blocks,), in_specs=[pl.BlockSpec((siz...  12.6 us
  transfers between devices with their start and end apart: 4, of which 2 were waited for; matrix products, arithmetic and copies ran while one was open for 6% of the time, Pallas kernels for 12%

profile of v6, /device:TPU:0, one launch (start us, length us, event | category | flops | bytes accessed | tf_op | source)
XLA Modules:
  0.0 249.6 jit_solution(17838105700836861344)
XLA Ops:
  0.6 1.3 copy.173
  2.2 3.6 %copy.175 = bf16[64,8,16,256]{3,2,1,0:T(8,128)(2,1)S(1)} copy(bf16[64,8,16,256]{3,1,2,0:T(8,128)(2,1)} %bitcast.476) | data formatting | bytes 8388608
  6.9 2.1 fusion.123
  9.0 2.0 fusion.126
  11.0 0.8 copy.160
  11.8 2.0 fusion.125
  13.9 2.1 fusion.124
  16.1 3.7 %copy.176 = bf16[128,8,8,256]{3,2,1,0:T(8,128)(2,1)S(1)} copy(bf16[128,8,8,256]{3,1,2,0:T(8,128)(2,1)} %bitcast.477) | data formatting | bytes 8388608
  19.8 3.2 %slice_bitcast_fusion.25 = (bf16[16,32,8,256]{3,2,1,0:T(8,128)(2,1)}, bf16[16,32,8,256]{3,2,1,0:T(8,128)(2,1)}, bf16[16,1,32,8,256]{4,3,2,1,0:T(8,128)(2,1)S(1)}, bf16[16,1,32,8,256]{4,3,2,1,0:T(8,128)(2,1)S(1)}) fusion(bf16[16,2,32,8,256]{4,3,2,1,0:T(8,128)(2,1)S(1)} %bitcast.451), kind=kLoop, calls=%fused_computation.160 | loop fusion | bytes 12582912 | tf_op jit(solution)/shard_map/squeeze | solution.py:195
  23.0 1.6 copy-done.17
  24.5 1.7 copy-done.18
  26.3 1.2 fusion.3
  27.5 0.8 fusion.99
  28.3 0.8 fusion.98
  29.2 0.9 fusion.111
  30.1 0.9 fusion.113
  31.6 3.0 %collective-permute-start = (bf16[4,2,48,256]{3,2,0,1:T(8,128)(2,1)}, bf16[4,2,48,256]{3,2,0,1:T(8,128)(2,1)}, u32[]{:S(2)}, u32[]{:S(2)}) collective-permute-start(bf16[4,2,48,256]{3,2,0,1:T(8,128)(2,1)} %fusion.120), channel_id=1, source_target_pairs={{0,2},{2,0},{1,3},{3,1},{4,6},{6,4},{5,7},{7,5},{8,10},{10,8},{9,1... | collective-permute-start | bytes 589832 | tf_op jit(solution)/shard_map/ppermute | solution.py:235
  35.9 1.6 copy.293
  37.5 3.5 %copy.124 = bf16[16,32,8,256]{3,1,0,2:T(8,128)(2,1)} copy(bf16[16,32,8,256]{3,2,1,0:T(8,128)(2,1)} %get-tuple-element.4) | data formatting | bytes 4194304 | tf_op jit(solution)/shard_map/squeeze | solution.py:195
  41.1 1.9 copy.126
  43.6 14.5 %shard_map.78.matrix_ref = f32[16,4,48,256]{3,2,1,0:T(8,128)} custom-call(bf16[32,256]{1,0:T(8,128)(2,1)} %maximum_bitcast_fusion.1.table_ref, s32[4,48,256]{2,1,0:T(8,128)} %bitcast.485), custom_call_target="tpu_custom_call" | custom-call | tf_op jit(solution)/shard_map/pallas_call | solution.py:58
  58.0 1.0 add_convert_fusion.1
  59.0 19.9 %all-gather = bf16[16,2,48,256]{3,2,0,1:T(8,128)(2,1)S(1)} all-gather(bf16[4,2,48,256]{3,2,0,1:T(8,128)(2,1)S(1)} %add_convert_fusion.1), channel_id=2, replica_groups=mesh['groups'=2,'freq'=4,'src'=2,'vp'=2] {'freq'}, dimensions={0}, use_global_device_ids=true | all-gather | bytes 983040 | tf_op jit(solution)/shard_map/all_gather | solution.py:276
  78.9 1.0 copy.122
  79.9 3.8 %shard_map.79 = bf16[4,2,48,256]{3,2,1,0:T(8,128)(2,1)} custom-call(f32[16,4,48,256]{3,2,1,0:T(8,128)} %shard_map.78.matrix_ref, bf16[4,4,2,48,256]{4,3,2,1,0:T(8,128)(2,1)} %bitcast.482), custom_call_target="tpu_custom_call" | custom-call | tf_op jit(solution)/shard_map/pallas_call | solution.py:95
  83.7 6.5 %all_gather.20 = bf16[8,2,48,256]{3,2,1,0:T(8,128)(2,1)S(1)} all-gather(bf16[4,2,48,256]{3,2,1,0:T(8,128)(2,1)} %shard_map.79), channel_id=1, replica_groups=mesh['groups'=2,'freq'=4,'src'=2,'vp'=2] {'src'}, dimensions={0}, use_global_device_ids=true | all-gather | bytes 589824 | tf_op jit(solution)/shard_map/all_gather | solution.py:282
  90.2 2.4 fusion.133
  93.4 0.9 copy-done.13
  95.6 1.2 fusion.27
  97.2 0.9 fusion.44
  98.1 0.9 fusion.47
  98.9 0.9 fusion.89
  99.8 0.8 fusion.86
  100.7 1.0 copy.133
  101.7 4.4 %all-to-all-start = ((bf16[16,2,48,256]{3,2,1,0:T(8,128)(2,1)}), bf16[16,2,48,256]{3,2,1,0:T(8,128)(2,1)}, u32[]{:S(2)}, u32[]{:S(2)}) async-start(bf16[16,2,48,256]{3,2,1,0:T(8,128)(2,1)} %copy.133), calls=%async_computation | async-start | bytes 1572864 | tf_op jit(solution)/shard_map/all_to_all | solution.py:167
  106.1 2.3 copy.174
  108.4 1.0 constant_dynamic-slice_fusion
  110.9 16.6 %shard_map.77.matrix_ref = f32[64,4,48,256]{3,2,1,0:T(8,128)} custom-call(bf16[128,256]{1,0:T(8,128)(2,1)} %maximum_bitcast_fusion.table_ref, s32[4,48,256]{2,1,0:T(8,128)} %bitcast.488), custom_call_target="tpu_custom_call" | custom-call | tf_op jit(solution)/shard_map/pallas_call | solution.py:58
  127.5 6.3 %shard_map.80 = bf16[4,4,2,48,256]{4,3,2,1,0:T(8,128)(2,1)} custom-call(f32[64,4,48,256]{3,2,1,0:T(8,128)} %shard_map.77.matrix_ref, bf16[4,4,2,48,256]{4,3,2,1,0:T(8,128)(2,1)} %bitcast.62.spectrum_ref), custom_call_target="tpu_custom_call" | custom-call | tf_op jit(solution)/shard_map/pallas_call | solution.py:120
  133.8 20.0 %all_to_all.20 = bf16[16,2,48,256]{3,2,1,0:T(8,128)(2,1)S(1)} all-to-all(bf16[16,2,48,256]{3,2,1,0:T(8,128)(2,1)} %bitcast.480), channel_id=1, replica_groups=mesh['groups'=2,'freq'=4,'src'=2,'vp'=2] {'freq'}, dimensions={0} | all-to-all | bytes 1572864 | tf_op jit(solution)/shard_map/all_to_all | solution.py:173
  155.5 0.9 copy-done.4
  157.8 1.3 fusion.1
  159.4 0.8 fusion.101
  160.2 0.9 fusion.100
  161.8 0.9 fusion.107
  162.7 0.9 fusion.109
  164.2 5.1 %collective-permute-done.1 = bf16[4,2,48,256]{3,2,0,1:T(8,128)(2,1)S(1)} collective-permute-done((bf16[4,2,48,256]{3,2,0,1:T(8,128)(2,1)S(1)}, bf16[4,2,48,256]{3,2,0,1:T(8,128)(2,1)S(1)}, u32[]{:S(2)}, u32[]{:S(2)}) %collective-permute-start.1) | collective-permute-done | bytes 196640 | tf_op jit(solution)/shard_map/ppermute | solution.py:235
  169.4 17.3 %all-gather.1 = bf16[16,2,48,256]{3,2,0,1:T(8,128)(2,1)S(1)} all-gather(bf16[4,2,48,256]{3,2,0,1:T(8,128)(2,1)S(1)} %add_convert_fusion), channel_id=3, replica_groups=mesh['groups'=2,'freq'=4,'src'=2,'vp'=2] {'freq'}, dimensions={0}, use_global_device_ids=true | all-gather | bytes 983040 | tf_op jit(solution)/shard_map/all_gather | solution.py:276
  186.8 1.0 copy.135
  187.7 3.8 %shard_map.81 = bf16[4,2,48,256]{3,2,1,0:T(8,128)(2,1)} custom-call(f32[16,4,48,256]{3,2,1,0:T(8,128)} %shard_map.78.matrix_ref, bf16[4,4,2,48,256]{4,3,2,1,0:T(8,128)(2,1)} %bitcast.481), custom_call_target="tpu_custom_call" | custom-call | tf_op jit(solution)/shard_map/pallas_call | solution.py:95
  191.5 6.5 %all_gather.23 = bf16[8,2,48,256]{3,2,1,0:T(8,128)(2,1)S(1)} all-gather(bf16[4,2,48,256]{3,2,1,0:T(8,128)(2,1)} %shard_map.81), channel_id=1, replica_groups=mesh['groups'=2,'freq'=4,'src'=2,'vp'=2] {'src'}, dimensions={0}, use_global_device_ids=true | all-gather | bytes 589824 | tf_op jit(solution)/shard_map/all_gather | solution.py:282
  198.1 2.4 fusion.137
  201.2 0.9 copy-done.14
  203.5 1.4 fusion.23
  205.1 0.9 fusion.38
  205.9 0.9 fusion.41
  206.8 0.9 fusion.95
  207.7 0.8 fusion.92
  208.7 16.2 %all_to_all.21 = bf16[16,2,48,256]{3,2,1,0:T(8,128)(2,1)} all-to-all(bf16[16,2,48,256]{3,2,1,0:T(8,128)(2,1)S(1)} %copy.146), channel_id=1, replica_groups=mesh['groups'=2,'freq'=4,'src'=2,'vp'=2] {'freq'}, dimensions={0} | all-to-all | bytes 1572864 | tf_op jit(solution)/shard_map/all_to_all | solution.py:167
  224.9 6.3 %shard_map.82 = bf16[4,4,2,48,256]{4,3,2,1,0:T(8,128)(2,1)} custom-call(f32[64,4,48,256]{3,2,1,0:T(8,128)} %shard_map.77.matrix_ref, bf16[4,4,2,48,256]{4,3,2,1,0:T(8,128)(2,1)} %bitcast.479), custom_call_target="tpu_custom_call" | custom-call | tf_op jit(solution)/shard_map/pallas_call | solution.py:120
  231.2 3.5 %all-to-all-start.3 = ((bf16[16,2,48,256]{3,2,1,0:T(8,128)(2,1)}), bf16[16,2,48,256]{3,2,1,0:T(8,128)(2,1)S(1)}, u32[]{:S(2)}, u32[]{:S(2)}) async-start(bf16[16,2,48,256]{3,2,1,0:T(8,128)(2,1)} %bitcast.478), calls=%async_computation.3 | async-start | bytes 1572864 | tf_op jit(solution)/shard_map/all_to_all | solution.py:173
  234.9 0.8 broadcast_in_dim_reshape.7
  235.7 12.1 %all-to-all-done.3 = bf16[16,2,48,256]{3,2,1,0:T(8,128)(2,1)S(1)} async-done(((bf16[16,2,48,256]{3,2,1,0:T(8,128)(2,1)}), bf16[16,2,48,256]{3,2,1,0:T(8,128)(2,1)S(1)}, u32[]{:S(2)}, u32[]{:S(2)}) %all-to-all-start.3) | async-done | bytes 786464 | tf_op jit(solution)/shard_map/all_to_all | solution.py:173
  248.4 1.2 broadcast_in_dim_reshape.6
  (89 shorter events, 16.1 us)
Async XLA Ops:
  6.2 4.9 %copy-start = (bf16[8,1,32,16,256]{4,3,2,1,0:T(8,128)(2,1)}, bf16[8,1,32,16,256]{4,3,2,1,0:T(8,128)(2,1)S(1)}, u32[]{:S(2)}) copy-start(bf16[8,1,32,16,256]{4,3,2,1,0:T(8,128)(2,1)S(1)} %get-tuple-element.9) | copy-start | bytes 6291460
  6.9 2.1 copy-start.3
  11.8 2.1 copy-start.5
  13.9 2.1 copy-start.21
  19.8 3.2 %copy-start.15 = (f32[16,48,256]{1,2,0:S(1)}, f32[16,48,256]{1,2,0}, u32[]{:S(2)}) copy-start(f32[16,48,256]{1,2,0} %fusion.123) | copy-start | bytes 2359300
  19.8 3.2 %copy-start.16 = (f32[16,48,256]{1,2,0:S(1)}, f32[16,48,256]{1,2,0}, u32[]{:S(2)}) copy-start(f32[16,48,256]{1,2,0} %fusion.126) | copy-start | bytes 2359300
  19.8 4.8 %copy-start.17 = (f32[16,48,256]{1,2,0:S(1)}, f32[16,48,256]{1,2,0}, u32[]{:S(2)}) copy-start(f32[16,48,256]{1,2,0} %fusion.125) | copy-start | bytes 2359300
  19.8 6.5 %copy-start.18 = (f32[16,48,256]{1,2,0:S(1)}, f32[16,48,256]{1,2,0}, u32[]{:S(2)}) copy-start(f32[16,48,256]{1,2,0} %fusion.124) | copy-start | bytes 2359300
  23.0 5.4 %copy-start.9 = (bf16[16,1,32,8,256]{4,3,2,1,0:T(8,128)(2,1)}, bf16[16,1,32,8,256]{4,3,2,1,0:T(8,128)(2,1)S(1)}, u32[]{:S(2)}) copy-start(bf16[16,1,32,8,256]{4,3,2,1,0:T(8,128)(2,1)S(1)} %get-tuple-element.7) | copy-start | bytes 6291460
  23.0 7.1 %copy-start.7 = (bf16[16,1,32,8,256]{4,3,2,1,0:T(8,128)(2,1)}, bf16[16,1,32,8,256]{4,3,2,1,0:T(8,128)(2,1)S(1)}, u32[]{:S(2)}) copy-start(bf16[16,1,32,8,256]{4,3,2,1,0:T(8,128)(2,1)S(1)} %get-tuple-element.6) | copy-start | bytes 6291460
  31.6 26.4 %collective-permute-start = (bf16[4,2,48,256]{3,2,0,1:T(8,128)(2,1)}, bf16[4,2,48,256]{3,2,0,1:T(8,128)(2,1)}, u32[]{:S(2)}, u32[]{:S(2)}) collective-permute-start(bf16[4,2,48,256]{3,2,0,1:T(8,128)(2,1)} %fusion.120), channel_id=1, source_target_pairs={{0,2},{2,0},{1,3},{3,1},{4,6},{6,4},{5,7},{7,5},{8,10},{10,8},{9,1... | collective-permute-start | bytes 589832 | tf_op jit(solution)/shard_map/ppermute | solution.py:235
  37.5 3.5 %copy-start.19 = (bf16[16,32,8,256]{3,2,1,0:T(8,128)(2,1)S(1)}, bf16[16,32,8,256]{3,2,1,0:T(8,128)(2,1)}, u32[]{:S(2)}) copy-start(bf16[16,32,8,256]{3,2,1,0:T(8,128)(2,1)} %get-tuple-element.5) | copy-start | bytes 6291460
  90.2 2.4 copy-start.11
  92.7 1.6 copy-start.13
  95.6 1.6 copy-start.1
  101.7 25.8 %all-to-all-start = ((bf16[16,2,48,256]{3,2,1,0:T(8,128)(2,1)}), bf16[16,2,48,256]{3,2,1,0:T(8,128)(2,1)}, u32[]{:S(2)}, u32[]{:S(2)}) async-start(bf16[16,2,48,256]{3,2,1,0:T(8,128)(2,1)} %copy.133), calls=%async_computation | async-start | bytes 1572864 | tf_op jit(solution)/shard_map/all_to_all | solution.py:167
  133.8 20.3 %copy-start.6 = (bf16[8,1,32,16,256]{4,2,0,3,1:T(8,128)(2,1)S(1)}, bf16[8,1,32,16,256]{4,2,0,3,1:T(8,128)(2,1)}, u32[]{:S(2)}) copy-start(bf16[8,1,32,16,256]{4,2,0,3,1:T(8,128)(2,1)} %copy-done.5) | copy-start | bytes 6291460
  154.8 1.6 copy-start.4
  157.8 1.6 copy-start.10
  160.2 1.6 copy-start.8
  163.6 5.7 %collective-permute-start.1 = (bf16[4,2,48,256]{3,2,0,1:T(8,128)(2,1)S(1)}, bf16[4,2,48,256]{3,2,0,1:T(8,128)(2,1)S(1)}, u32[]{:S(2)}, u32[]{:S(2)}) collective-permute-start(bf16[4,2,48,256]{3,2,0,1:T(8,128)(2,1)S(1)} %fusion.116), channel_id=1, source_target_pairs={{0,2},{2,0},{1,3},{3,1},{4,6},{6,4},{5,7},{7,5},{8,10},{10,8},{9,1... | collective-permute-start | bytes 589832 | tf_op jit(solution)/shard_map/ppermute | solution.py:235
  198.1 2.4 copy-start.12
  200.5 1.6 copy-start.14
  203.5 1.6 copy-start.2
  224.9 9.8 %copy-start.20 = (bf16[4,2,48,256]{3,2,1,0:T(8,128)(2,1)S(1)}, bf16[4,2,48,256]{3,2,1,0:T(8,128)(2,1)}, u32[]{:S(2)}) copy-start(bf16[4,2,48,256]{3,2,1,0:T(8,128)(2,1)} %shard_map.81) | copy-start | bytes 589828
  231.2 16.6 %all-to-all-start.3 = ((bf16[16,2,48,256]{3,2,1,0:T(8,128)(2,1)}), bf16[16,2,48,256]{3,2,1,0:T(8,128)(2,1)S(1)}, u32[]{:S(2)}, u32[]{:S(2)}) async-start(bf16[16,2,48,256]{3,2,1,0:T(8,128)(2,1)} %bitcast.478), calls=%async_computation.3 | async-start | bytes 1572864 | tf_op jit(solution)/shard_map/all_to_all | solution.py:173

commit v7 on v1

--- a/solution.py
+++ b/solution.py
@@ -205,6 +205,25 @@
     return (mine.astype(jnp.bfloat16).astype(jnp.float32) + got.astype(jnp.float32)).astype(jnp.bfloat16)
 
 
+def expand_reduce(u_tiles, z_real, z_imag):
+    count = lax.axis_size("src")
+    if count != 2:
+        return reduce_src(expand_rows(u_tiles, z_real, z_imag))
+    place = lax.axis_index("src")
+    half = z_real.shape[0] // 2
+
+    def rows(start):
+        u_part = lax.dynamic_slice_in_dim(u_tiles, start, half, 3)
+        re_part = lax.dynamic_slice_in_dim(z_real, start, half, 0)
+        im_part = lax.dynamic_slice_in_dim(z_imag, start, half, 0)
+        return expand_rows(u_part, re_part, im_part)
+
+    other = rows((1 - place) * half).astype(jnp.bfloat16)
+    got = lax.ppermute(other, "src", perm=[(0, 1), (1, 0)])
+    mine = rows(place * half)
+    return (mine.astype(jnp.bfloat16).astype(jnp.float32) + got.astype(jnp.float32)).astype(jnp.bfloat16)
+
+
 def tile_major(x):
     comps, points, width = x.shape
     return jnp.transpose(x.reshape(comps, points, width // TILE, TILE), (2, 0, 1, 3))
@@ -235,8 +254,7 @@
     minus = None
     for sweep in range(ITERS):
         z_real, z_imag = coefficients(v_tiles, mask, plus)
-        partial_terms = expand_rows(u_tiles, z_real, z_imag)
-        summed = reduce_src(partial_terms)
+        summed = expand_reduce(u_tiles, z_real, z_imag)
         traces = exchange(summed, parts)
         windowed = window(traces, rec_picked)
         minus = exchange_back(windowed, rec_tiles)

time: 242 us -> 250 us (1.033)
  local copies, waits for them, and re-layouts: 37.9 us -> 43.8 us
  matrix products: 33.6 us -> 36.2 us
    slice x1 -> x3, local copies, waits for them, and re-layouts: 0.17 us -> 10.2 us  [the longest x1 7.34 us: expand_rows(): u_tiles[:, 1]]
    squeeze x3 -> x0, local copies, waits for them, and re-layouts: 8.58 us -> none  [the longest x2 6.71 us: expand_rows(): u_tiles[:, 0]]
    unnamed x52 -> x66, local copies, waits for them, and re-layouts: 22.2 us -> 25.7 us
  transfers between devices with their start and end apart: 6 -> 6, of which waited for: 4 -> 4; matrix products, arithmetic and copies ran while one was open for 7% -> 9% of each run, Pallas kernels for 9% -> 9%
where the time goes in v7:
time: 250 us; the launch traced here: 247 us
  blocking collectives  72.2 us (29%)
  local copies, waits for them, and re-layouts  43.8 us (18%)
  Pallas kernels  39.9 us (16%)
  matrix products  36.2 us (14%)
  waiting for transfers between devices  21.6 us (9%)
  starting transfers between devices  20.7 us (8%)
  other arithmetic  11.3 us (5%)
    all_to_all x2, blocking collectives, exchange_back(): got = lax.all_to_all(flat, 'freq', split_axis=0, concat_axis=0, tiled=True)  32.4 us
    all_to_all x2, blocking collectives, exchange(): lax.all_to_all(pieces, 'freq', split_axis=0, concat_axis=0, tiled=True)  27.2 us
    unnamed x66, local copies, waits for them, and re-layouts  25.7 us
    pallas_call x2, Pallas kernels, window_gather(): pl.pallas_call(gather_kernel, grid=(blocks, points // rows), in_specs=[pl...  21.7 us
    unnamed x16, matrix products  19.9 us
    pallas_call x4, Pallas kernels, window(): pl.pallas_call(window_kernel, grid=(blocks,), in_specs=[pl.BlockSpec((siz...  18.2 us
    all_to_all x2, waiting for transfers between devices, exchange_back(): got = lax.all_to_all(flat, 'freq', split_axis=0, concat_axis=0, tiled=True)  15.7 us
    all_gather x2, blocking collectives, per_device(): minus_all = lax.all_gather(minus, 'src', axis=0, tiled=True)  12.7 us
  transfers between devices with their start and end apart: 6, of which 4 were waited for; matrix products, arithmetic and copies ran while one was open for 9% of the time, Pallas kernels for 9%

profile of v7, /device:TPU:0, one launch (start us, length us, event | category | flops | bytes accessed | tf_op | source)
XLA Modules:
  0.0 247.1 jit_solution(11077650731752171039)
XLA Ops:
  0.6 1.3 copy.171
  2.9 3.6 %copy.173 = bf16[64,8,16,256]{3,2,1,0:T(8,128)(2,1)S(1)} copy(bf16[64,8,16,256]{3,1,2,0:T(8,128)(2,1)} %bitcast.498) | data formatting | bytes 8388608
  6.9 0.7 copy.156
  7.6 2.1 fusion.131
  9.7 2.1 fusion.134
  11.7 0.8 copy.155
  12.5 2.0 fusion.133
  14.5 2.1 fusion.132
  16.8 5.6 %copy.174 = bf16[128,8,8,256]{3,2,1,0:T(8,128)(2,1)} copy(bf16[128,8,8,256]{3,1,2,0:T(8,128)(2,1)} %bitcast.499) | data formatting | bytes 8388608
  22.4 7.3 %constant_dynamic-slice_fusion.3 = (bf16[16,1,32,4,256]{4,3,2,1,0:T(4,128)(2,1)S(1)}, bf16[16,1,32,4,256]{4,3,2,1,0:T(4,128)(2,1)S(1)}, bf16[16,1,32,4,256]{4,3,2,1,0:T(4,128)(2,1)}, bf16[16,1,32,4,256]{4,3,2,1,0:T(4,128)(2,1)S(1)}) fusion(bf16[16,2,32,8,256]{4,3,2,1,0:T(8,128)(2,1)} %bitcast.472, s32[]{:T(128)S(6)} %add.124, s32[]{:T(128)S(6)} %select_n.73, ...), kind=kLoop, calls=%fused_computation.192 | loop fusion | bytes 8388620 | tf_op jit(solution)/shard_map/slice | solution.py:165
  29.8 1.4 fusion.3
  33.6 2.9 %collective-permute-start = (bf16[4,2,48,256]{3,2,1,0:T(8,128)(2,1)}, bf16[4,2,48,256]{3,2,1,0:T(8,128)(2,1)}, u32[]{:S(2)}, u32[]{:S(2)}) collective-permute-start(bf16[4,2,48,256]{3,2,1,0:T(8,128)(2,1)} %pad_maximum_fusion.2), channel_id=1, source_target_pairs={{0,2},{2,0},{1,3},{3,1},{4,6},{6,4},{5,7},{7,5},{8,10},{10,8},{9,1... | collective-permute-start | bytes 589832 | tf_op jit(solution)/shard_map/ppermute | solution.py:222
  36.5 2.5 %convolution_bitcast_fusion.15 = f32[4,48,256]{2,1,0:T(8,128)} fusion(bf16[16,1,32,4,256]{4,3,2,1,0:T(4,128)(2,1)} %get-tuple-element.6, bf16[8,48,16,32]{1,3,0,2:T(8,128)(2,1)} %copy-done.19, s32[]{:T(128)S(6)} %select_n.73), kind=kOutput, calls=%fused_computation.83 | convolution fusion | flops 50331648 | bytes 1769476 | tf_op jit(solution)/shard_map/jrit,ivjr->ivt/dot_general | solution.py:163
  39.0 1.3 convolution_bitcast_fusion.13
  41.5 1.7 reshape.161
  43.2 1.5 fusion.113
  44.7 1.0 constant_dynamic-slice_fusion.4
  46.7 1.7 add_convert_fusion.1
  48.3 4.9 %all-to-all-start = ((bf16[4,2,48,256]{3,2,1,0:T(8,128)(2,1)}), bf16[4,2,48,256]{3,2,1,0:T(8,128)(2,1)S(1)}, u32[]{:S(2)}, u32[]{:S(2)}) async-start(bf16[4,2,48,256]{3,2,1,0:T(8,128)(2,1)} %add_convert_fusion.1), calls=%async_computation | async-start | bytes 393216 | tf_op jit(solution)/shard_map/all_to_all | solution.py:136
  53.9 5.2 %shard_map.78.matrix_ref = f32[64,1,48,256]{3,2,1,0:T(8,128)} custom-call(bf16[128,256]{1,0:T(8,128)(2,1)} %maximum_bitcast_fusion.table_ref, s32[1,48,256]{2,1,0:T(8,128)} %bitcast.512), custom_call_target="tpu_custom_call" | custom-call | tf_op jit(solution)/shard_map/pallas_call | solution.py:53
  59.1 1.4 all-to-all-done
  61.2 2.8 %shard_map.79 = bf16[4,1,2,48,256]{4,3,2,1,0:T(8,128)(2,1)} custom-call(f32[64,1,48,256]{3,2,1,0:T(8,128)} %shard_map.78.matrix_ref, bf16[4,1,2,48,256]{4,3,2,1,0:T(8,128)(2,1)} %bitcast.505), custom_call_target="tpu_custom_call" | custom-call | tf_op jit(solution)/shard_map/pallas_call | solution.py:89
  64.0 3.7 %all-to-all-start.1 = ((bf16[4,2,48,256]{3,2,1,0:T(8,128)(2,1)}), bf16[4,2,48,256]{3,2,1,0:T(8,128)(2,1)S(1)}, u32[]{:S(2)}, u32[]{:S(2)}) async-start(bf16[4,2,48,256]{3,2,1,0:T(8,128)(2,1)} %bitcast.506), calls=%async_computation.1 | async-start | bytes 393216 | tf_op jit(solution)/shard_map/all_to_all | solution.py:142
  67.7 2.7 %fusion.179 = (bf16[16,1,32,8,256]{4,3,2,1,0:T(8,128)(2,1)S(1)}, bf16[16,1,32,8,256]{4,3,2,1,0:T(8,128)(2,1)S(1)}) fusion(bf16[16,2,32,8,256]{4,3,2,1,0:T(8,128)(2,1)} %bitcast.473), kind=kLoop, calls=%fused_computation.206 | loop fusion | bytes 8388608 | tf_op jit(solution)/shard_map/slice | solution.py:177
  70.4 1.9 copy.164
  72.2 1.8 copy.166
  74.2 6.3 %all_gather.6 = bf16[8,2,48,256]{3,2,1,0:T(8,128)(2,1)S(1)} all-gather(bf16[4,2,48,256]{3,2,1,0:T(8,128)(2,1)S(1)} %all-to-all-done.1), channel_id=1, replica_groups=mesh['groups'=2,'freq'=4,'src'=2,'vp'=2] {'src'}, dimensions={0}, use_global_device_ids=true | all-gather | bytes 589824 | tf_op jit(solution)/shard_map/all_gather | solution.py:261
  80.5 2.4 fusion.141
  83.6 0.9 copy-done.9
  85.9 1.2 fusion.27
  87.5 0.9 fusion.36
  88.4 0.9 fusion.39
  89.2 0.9 fusion.81
  90.1 0.8 fusion.78
  91.0 1.0 copy.133
  92.0 5.0 %all-to-all-start.2 = ((bf16[16,2,48,256]{3,2,1,0:T(8,128)(2,1)}), bf16[16,2,48,256]{3,2,1,0:T(8,128)(2,1)}, u32[]{:S(2)}, u32[]{:S(2)}) async-start(bf16[16,2,48,256]{3,2,1,0:T(8,128)(2,1)} %copy.133), calls=%async_computation.2 | async-start | bytes 1572864 | tf_op jit(solution)/shard_map/all_to_all | solution.py:136
  96.9 2.3 copy.172
  99.2 1.0 constant_dynamic-slice_fusion.5
  100.2 0.7 copy.266
  100.9 16.5 %shard_map.77.matrix_ref = f32[64,4,48,256]{3,2,1,0:T(8,128)} custom-call(bf16[128,256]{1,0:T(8,128)(2,1)} %maximum_bitcast_fusion.table_ref, s32[4,48,256]{2,1,0:T(8,128)} %bitcast.511), custom_call_target="tpu_custom_call" | custom-call | tf_op jit(solution)/shard_map/pallas_call | solution.py:53
  117.5 6.3 %shard_map.80 = bf16[4,4,2,48,256]{4,3,2,1,0:T(8,128)(2,1)} custom-call(f32[64,4,48,256]{3,2,1,0:T(8,128)} %shard_map.77.matrix_ref, bf16[4,4,2,48,256]{4,3,2,1,0:T(8,128)(2,1)} %bitcast.72.spectrum_ref), custom_call_target="tpu_custom_call" | custom-call | tf_op jit(solution)/shard_map/pallas_call | solution.py:89
  123.8 22.2 %all_to_all.40 = bf16[16,2,48,256]{3,2,1,0:T(8,128)(2,1)S(1)} all-to-all(bf16[16,2,48,256]{3,2,1,0:T(8,128)(2,1)} %bitcast.502), channel_id=1, replica_groups=mesh['groups'=2,'freq'=4,'src'=2,'vp'=2] {'freq'}, dimensions={0} | all-to-all | bytes 1572864 | tf_op jit(solution)/shard_map/all_to_all | solution.py:142
  146.0 1.4 fusion.28
  148.8 0.9 copy-done.4
  151.1 1.3 fusion.1
  152.7 0.9 copy-done.12
  157.1 4.5 %collective-permute-done.1 = bf16[4,2,48,256]{3,2,1,0:T(8,128)(2,1)S(1)} collective-permute-done((bf16[4,2,48,256]{3,2,1,0:T(8,128)(2,1)S(1)}, bf16[4,2,48,256]{3,2,1,0:T(8,128)(2,1)S(1)}, u32[]{:S(2)}, u32[]{:S(2)}) %collective-permute-start.1) | collective-permute-done | bytes 196640 | tf_op jit(solution)/shard_map/ppermute | solution.py:222
  161.7 9.9 %all_to_all.41 = bf16[4,2,48,256]{3,2,1,0:T(8,128)(2,1)} all-to-all(bf16[4,2,48,256]{3,2,1,0:T(8,128)(2,1)S(1)} %add_convert_fusion), channel_id=1, replica_groups=mesh['groups'=2,'freq'=4,'src'=2,'vp'=2] {'freq'}, dimensions={0} | all-to-all | bytes 393216 | tf_op jit(solution)/shard_map/all_to_all | solution.py:136
  171.5 2.8 %shard_map.81 = bf16[4,1,2,48,256]{4,3,2,1,0:T(8,128)(2,1)} custom-call(f32[64,1,48,256]{3,2,1,0:T(8,128)} %shard_map.78.matrix_ref, bf16[4,1,2,48,256]{4,3,2,1,0:T(8,128)(2,1)} %bitcast.507), custom_call_target="tpu_custom_call" | custom-call | tf_op jit(solution)/shard_map/pallas_call | solution.py:89
  174.3 10.1 %all_to_all.42 = bf16[4,2,48,256]{3,2,1,0:T(8,128)(2,1)S(1)} all-to-all(bf16[4,2,48,256]{3,2,1,0:T(8,128)(2,1)} %bitcast.508), channel_id=1, replica_groups=mesh['groups'=2,'freq'=4,'src'=2,'vp'=2] {'freq'}, dimensions={0} | all-to-all | bytes 393216 | tf_op jit(solution)/shard_map/all_to_all | solution.py:142
  184.5 6.3 %all_gather.7 = bf16[8,2,48,256]{3,2,1,0:T(8,128)(2,1)S(1)} all-gather(bf16[4,2,48,256]{3,2,1,0:T(8,128)(2,1)S(1)} %all_to_all.42), channel_id=1, replica_groups=mesh['groups'=2,'freq'=4,'src'=2,'vp'=2] {'src'}, dimensions={0}, use_global_device_ids=true | all-gather | bytes 589824 | tf_op jit(solution)/shard_map/all_gather | solution.py:261
  190.8 2.4 fusion.145
  193.9 0.9 copy-done.10
  196.2 1.4 fusion.23
  197.8 0.9 fusion.30
  198.6 0.9 fusion.33
  199.5 0.9 fusion.87
  200.4 0.8 fusion.84
  201.4 17.4 %all_to_all.43 = bf16[16,2,48,256]{3,2,1,0:T(8,128)(2,1)} all-to-all(bf16[16,2,48,256]{3,2,1,0:T(8,128)(2,1)S(1)} %copy.141), channel_id=1, replica_groups=mesh['groups'=2,'freq'=4,'src'=2,'vp'=2] {'freq'}, dimensions={0} | all-to-all | bytes 1572864 | tf_op jit(solution)/shard_map/all_to_all | solution.py:136
  218.7 6.3 %shard_map.82 = bf16[4,4,2,48,256]{4,3,2,1,0:T(8,128)(2,1)} custom-call(f32[64,4,48,256]{3,2,1,0:T(8,128)} %shard_map.77.matrix_ref, bf16[4,4,2,48,256]{4,3,2,1,0:T(8,128)(2,1)} %bitcast.501), custom_call_target="tpu_custom_call" | custom-call | tf_op jit(solution)/shard_map/pallas_call | solution.py:89
  225.0 3.6 %all-to-all-start.7 = ((bf16[16,2,48,256]{3,2,1,0:T(8,128)(2,1)}), bf16[16,2,48,256]{3,2,1,0:T(8,128)(2,1)S(1)}, u32[]{:S(2)}, u32[]{:S(2)}) async-start(bf16[16,2,48,256]{3,2,1,0:T(8,128)(2,1)} %bitcast.500), calls=%async_computation.7 | async-start | bytes 1572864 | tf_op jit(solution)/shard_map/all_to_all | solution.py:142
  228.8 0.8 broadcast_in_dim_reshape.7
  229.6 15.6 %all-to-all-done.7 = bf16[16,2,48,256]{3,2,1,0:T(8,128)(2,1)S(1)} async-done(((bf16[16,2,48,256]{3,2,1,0:T(8,128)(2,1)}), bf16[16,2,48,256]{3,2,1,0:T(8,128)(2,1)S(1)}, u32[]{:S(2)}, u32[]{:S(2)}) %all-to-all-start.7) | async-done | bytes 786464 | tf_op jit(solution)/shard_map/all_to_all | solution.py:142
  245.8 1.2 broadcast_in_dim_reshape.6
  (108 shorter events, 19.5 us)
Async XLA Ops:
  1.9 0.9 copy-start.17
  6.8 4.9 %copy-start = (bf16[8,1,32,16,256]{4,3,2,1,0:T(8,128)(2,1)}, bf16[8,1,32,16,256]{4,3,2,1,0:T(8,128)(2,1)S(1)}, u32[]{:S(2)}) copy-start(bf16[8,1,32,16,256]{4,3,2,1,0:T(8,128)(2,1)S(1)} %get-tuple-element.9) | copy-start | bytes 6291460
  7.6 2.1 copy-start.3
  12.5 2.1 copy-start.5
  14.5 2.1 copy-start.27
  22.4 7.4 %copy-start.22 = (f32[16,48,256]{1,2,0:S(1)}, f32[16,48,256]{1,2,0}, u32[]{:S(2)}) copy-start(f32[16,48,256]{1,2,0} %fusion.131) | copy-start | bytes 2359300
  22.4 7.4 %copy-start.23 = (f32[16,48,256]{1,2,0:S(1)}, f32[16,48,256]{1,2,0}, u32[]{:S(2)}) copy-start(f32[16,48,256]{1,2,0} %fusion.134) | copy-start | bytes 2359300
  22.4 7.4 %copy-start.24 = (f32[16,48,256]{1,2,0:S(1)}, f32[16,48,256]{1,2,0}, u32[]{:S(2)}) copy-start(f32[16,48,256]{1,2,0} %fusion.133) | copy-start | bytes 2359300
  22.4 7.4 %copy-start.25 = (f32[16,48,256]{1,2,0:S(1)}, f32[16,48,256]{1,2,0}, u32[]{:S(2)}) copy-start(f32[16,48,256]{1,2,0} %fusion.132) | copy-start | bytes 2359300
  29.8 1.8 copy-start.15
  29.8 2.5 %copy-start.13 = (bf16[16,1,32,4,256]{4,3,2,1,0:T(4,128)(2,1)}, bf16[16,1,32,4,256]{4,3,2,1,0:T(4,128)(2,1)S(1)}, u32[]{:S(2)}) copy-start(bf16[16,1,32,4,256]{4,3,2,1,0:T(4,128)(2,1)S(1)} %get-tuple-element.7) | copy-start | bytes 3145732
  31.2 1.0 copy-start.19
  31.3 1.3 copy-start.21
  33.6 13.1 %collective-permute-start = (bf16[4,2,48,256]{3,2,1,0:T(8,128)(2,1)}, bf16[4,2,48,256]{3,2,1,0:T(8,128)(2,1)}, u32[]{:S(2)}, u32[]{:S(2)}) collective-permute-start(bf16[4,2,48,256]{3,2,1,0:T(8,128)(2,1)} %pad_maximum_fusion.2), channel_id=1, source_target_pairs={{0,2},{2,0},{1,3},{3,1},{4,6},{6,4},{5,7},{7,5},{8,10},{10,8},{9,1... | collective-permute-start | bytes 589832 | tf_op jit(solution)/shard_map/ppermute | solution.py:222
  36.5 2.5 %copy-start.11 = (bf16[16,1,32,4,256]{4,3,2,1,0:T(4,128)(2,1)S(1)}, bf16[16,1,32,4,256]{4,3,2,1,0:T(4,128)(2,1)}, u32[]{:S(2)}) copy-start(bf16[16,1,32,4,256]{4,3,2,1,0:T(4,128)(2,1)} %get-tuple-element.6) | copy-start | bytes 3145732
  43.2 3.1 %copy-start.20 = (bf16[8,48,16,32]{1,3,0,2:T(8,128)(2,1)S(1)}, bf16[8,48,16,32]{1,3,0,2:T(8,128)(2,1)}, u32[]{:S(2)}) copy-start(bf16[8,48,16,32]{1,3,0,2:T(8,128)(2,1)} %copy-done.19) | copy-start | bytes 1179652
  48.3 12.2 %all-to-all-start = ((bf16[4,2,48,256]{3,2,1,0:T(8,128)(2,1)}), bf16[4,2,48,256]{3,2,1,0:T(8,128)(2,1)S(1)}, u32[]{:S(2)}, u32[]{:S(2)}) async-start(bf16[4,2,48,256]{3,2,1,0:T(8,128)(2,1)} %add_convert_fusion.1), calls=%async_computation | async-start | bytes 393216 | tf_op jit(solution)/shard_map/all_to_all | solution.py:136
  60.5 0.7 copy-start.26
  64.0 10.2 %all-to-all-start.1 = ((bf16[4,2,48,256]{3,2,1,0:T(8,128)(2,1)}), bf16[4,2,48,256]{3,2,1,0:T(8,128)(2,1)S(1)}, u32[]{:S(2)}, u32[]{:S(2)}) async-start(bf16[4,2,48,256]{3,2,1,0:T(8,128)(2,1)} %bitcast.506), calls=%async_computation.1 | async-start | bytes 393216 | tf_op jit(solution)/shard_map/all_to_all | solution.py:142
  80.5 2.4 copy-start.7
  82.9 1.6 copy-start.9
  85.9 1.6 copy-start.1
  92.0 25.5 %all-to-all-start.2 = ((bf16[16,2,48,256]{3,2,1,0:T(8,128)(2,1)}), bf16[16,2,48,256]{3,2,1,0:T(8,128)(2,1)}, u32[]{:S(2)}, u32[]{:S(2)}) async-start(bf16[16,2,48,256]{3,2,1,0:T(8,128)(2,1)} %copy.133), calls=%async_computation.2 | async-start | bytes 1572864 | tf_op jit(solution)/shard_map/all_to_all | solution.py:136
  123.8 23.7 %copy-start.6 = (bf16[8,1,32,16,256]{4,2,0,3,1:T(8,128)(2,1)S(1)}, bf16[8,1,32,16,256]{4,2,0,3,1:T(8,128)(2,1)}, u32[]{:S(2)}) copy-start(bf16[8,1,32,16,256]{4,2,0,3,1:T(8,128)(2,1)} %copy-done.5) | copy-start | bytes 6291460
  148.1 1.6 copy-start.4
  151.1 1.3 copy-start.16
  152.4 1.2 copy-start.12
  153.6 1.2 copy-start.14
  155.9 5.7 %collective-permute-start.1 = (bf16[4,2,48,256]{3,2,1,0:T(8,128)(2,1)S(1)}, bf16[4,2,48,256]{3,2,1,0:T(8,128)(2,1)S(1)}, u32[]{:S(2)}, u32[]{:S(2)}) collective-permute-start(bf16[4,2,48,256]{3,2,1,0:T(8,128)(2,1)S(1)} %pad_maximum_fusion.3), channel_id=1, source_target_pairs={{0,2},{2,0},{1,3},{3,1},{4,6},{6,4},{5,7},{7,5},{8,10},{10,8},{9,1... | collective-permute-start | bytes 589832 | tf_op jit(solution)/shard_map/ppermute | solution.py:222
  190.8 2.4 copy-start.8
  193.2 1.6 copy-start.10
  196.2 1.6 copy-start.2
  225.0 20.2 %copy-start.18 = (bf16[12,8,16,256]{3,2,1,0:T(8,128)(2,1)S(1)}, bf16[12,8,16,256]{3,2,1,0:T(8,128)(2,1)}, u32[]{:S(2)}) copy-start(bf16[12,8,16,256]{3,2,1,0:T(8,128)(2,1)} %copy-done.17) | copy-start | bytes 2359300
  225.0 20.2 %all-to-all-start.7 = ((bf16[16,2,48,256]{3,2,1,0:T(8,128)(2,1)}), bf16[16,2,48,256]{3,2,1,0:T(8,128)(2,1)S(1)}, u32[]{:S(2)}, u32[]{:S(2)}) async-start(bf16[16,2,48,256]{3,2,1,0:T(8,128)(2,1)} %bitcast.500), calls=%async_computation.7 | async-start | bytes 1572864 | tf_op jit(solution)/shard_map/all_to_all | solution.py:142

commit v8 on v1

--- a/solution.py
+++ b/solution.py
@@ -144,51 +144,26 @@
 
 
 def coefficients(v_tiles, mask, plus):
-    form = "irjt,jvt->ivjr"
-    p_re = plus[:, 0]
-    p_im = plus[:, 1]
-    z_real = jnp.einsum(
-        form, v_tiles[:, 0], p_re, preferred_element_type=jnp.float32
-    ) + jnp.einsum(form, v_tiles[:, 1], p_im, preferred_element_type=jnp.float32)
-    z_imag = jnp.einsum(
-        form, v_tiles[:, 0], p_im, preferred_element_type=jnp.float32
-    ) - jnp.einsum(form, v_tiles[:, 1], p_re, preferred_element_type=jnp.float32)
-    z_real = jnp.where(mask, z_real, 0.0).astype(jnp.bfloat16)
-    z_imag = jnp.where(mask, z_imag, 0.0).astype(jnp.bfloat16)
-    return z_real, z_imag
+    turned = jnp.stack([plus[:, 1], -plus[:, 0]], axis=1)
+    both = jnp.stack([plus, turned])
+    z = jnp.einsum("icrjt,ojcvt->oivjr", v_tiles, both, preferred_element_type=jnp.float32)
+    z = jnp.where(mask[None], z, 0.0).astype(jnp.bfloat16)
+    return z[0], z[1]
 
 
 def expand_rows(u_tiles, z_real, z_imag):
-    other = "jrit,ivjr->ivt"
-    y_real = jnp.einsum(
-        other, u_tiles[:, 0], z_real, preferred_element_type=jnp.float32
-    ) - jnp.einsum(other, u_tiles[:, 1], z_imag, preferred_element_type=jnp.float32)
-    y_imag = jnp.einsum(
-        other, u_tiles[:, 0], z_imag, preferred_element_type=jnp.float32
-    ) + jnp.einsum(other, u_tiles[:, 1], z_real, preferred_element_type=jnp.float32)
-    return jnp.stack([y_real, y_imag], axis=1)
+    both = jnp.stack([jnp.stack([z_real, -z_imag]), jnp.stack([z_imag, z_real])])
+    return jnp.einsum("jcrit,ocivjr->iovt", u_tiles, both, preferred_element_type=jnp.float32)
 
 
 def adjoint_local(u_tiles, v_tiles, mask, minus):
-    form = "jrit,ivt->ivjr"
-    m_re = minus[:, 0]
-    m_im = minus[:, 1]
-    w_real = jnp.einsum(
-        form, u_tiles[:, 0], m_re, preferred_element_type=jnp.float32
-    ) + jnp.einsum(form, u_tiles[:, 1], m_im, preferred_element_type=jnp.float32)
-    w_imag = jnp.einsum(
-        form, u_tiles[:, 0], m_im, preferred_element_type=jnp.float32
-    ) - jnp.einsum(form, u_tiles[:, 1], m_re, preferred_element_type=jnp.float32)
-    w_real = jnp.where(mask, w_real, 0.0).astype(jnp.bfloat16)
-    w_imag = jnp.where(mask, w_imag, 0.0).astype(jnp.bfloat16)
-    other = "irjt,ivjr->jvt"
-    x_real = jnp.einsum(
-        other, v_tiles[:, 0], w_real, preferred_element_type=jnp.float32
-    ) - jnp.einsum(other, v_tiles[:, 1], w_imag, preferred_element_type=jnp.float32)
-    x_imag = jnp.einsum(
-        other, v_tiles[:, 0], w_imag, preferred_element_type=jnp.float32
-    ) + jnp.einsum(other, v_tiles[:, 1], w_real, preferred_element_type=jnp.float32)
-    return jnp.stack([x_real, x_imag], axis=1)
+    turned = jnp.stack([minus[:, 1], -minus[:, 0]], axis=1)
+    both = jnp.stack([minus, turned])
+    w = jnp.einsum("jcrit,oicvt->oivjr", u_tiles, both, preferred_element_type=jnp.float32)
+    w = jnp.where(mask[None], w, 0.0).astype(jnp.bfloat16)
+    w_real, w_imag = w[0], w[1]
+    parts = jnp.stack([jnp.stack([w_real, -w_imag]), jnp.stack([w_imag, w_real])])
+    return jnp.einsum("icrjt,ocivjr->jovt", v_tiles, parts, preferred_element_type=jnp.float32)
 
 
 def reduce_src(partial):

time: 242 us -> 220 us (0.909)
  local copies, waits for them, and re-layouts: 37.9 us -> 21.4 us
  matrix products: 33.6 us -> 25.5 us
  waiting for transfers between devices: 21.1 us -> 27.4 us
    unnamed x16 -> x0, matrix products: 19.9 us -> none
    dot_general x16 -> x8, matrix products: 13.7 us -> 25.5 us  [the longest x2 7.33 us: adjoint_local(): jnp.einsum('jcrit,oicvt->oivjr', u_tiles, both, preferred_element_type=jn...]
    squeeze x3 -> x0, local copies, waits for them, and re-layouts: 8.58 us -> none  [the longest x2 6.71 us: expand_rows(): u_tiles[:, 0]]
    unnamed x52 -> x32, local copies, waits for them, and re-layouts: 22.2 us -> 16.1 us
    convert_element_type x6 -> x0, other arithmetic: 5.51 us -> none  [the longest x2 2.46 us: coefficients(): z_real = jnp.where(mask, z_real, 0.0).astype(jnp.bfloat16)]
    another operation x4 -> x10, other arithmetic: 0.8 us -> 5.95 us  [the longest x2 3.32 us: expand_rows(): jnp.stack([jnp.stack([z_real, -z_imag]), jnp.stack([z_imag, z_real])])]
    all_to_all x2, waiting for transfers between devices: 15.9 us -> 19.7 us  [exchange_back(): got = lax.all_to_all(flat, 'freq', split_axis=0, concat_axis=0, tiled=True)]
    another operation x5 -> x3, local copies, waits for them, and re-layouts: 2.72 us -> 0.11 us
  transfers between devices with their start and end apart: 6 -> 6, of which waited for: 4 -> 5; matrix products, arithmetic and copies ran while one was open for 7% -> 2% of each run, Pallas kernels for 9% -> 10%
where the time goes in v8:
time: 220 us; the launch traced here: 218 us
  blocking collectives  70.6 us (32%)
  Pallas kernels  39.9 us (18%)
  waiting for transfers between devices  27.4 us (12%)
  matrix products  25.5 us (12%)
  local copies, waits for them, and re-layouts  21.4 us (10%)
  starting transfers between devices  21.2 us (10%)
  other arithmetic  10.6 us (5%)
    all_to_all x2, blocking collectives, exchange_back(): got = lax.all_to_all(flat, 'freq', split_axis=0, concat_axis=0, tiled=True)  31 us
    all_to_all x2, blocking collectives, exchange(): lax.all_to_all(pieces, 'freq', split_axis=0, concat_axis=0, tiled=True)  26.5 us
    pallas_call x2, Pallas kernels, window_gather(): pl.pallas_call(gather_kernel, grid=(blocks, points // rows), in_specs=[pl...  21.7 us
    all_to_all x2, waiting for transfers between devices, exchange_back(): got = lax.all_to_all(flat, 'freq', split_axis=0, concat_axis=0, tiled=True)  19.7 us
    pallas_call x4, Pallas kernels, window(): pl.pallas_call(window_kernel, grid=(blocks,), in_specs=[pl.BlockSpec((siz...  18.2 us
    unnamed x32, local copies, waits for them, and re-layouts  16.1 us
    all_gather x2, blocking collectives, per_device(): minus_all = lax.all_gather(minus, 'src', axis=0, tiled=True)  13.1 us
    all_to_all x2, starting transfers between devices, exchange(): lax.all_to_all(pieces, 'freq', split_axis=0, concat_axis=0, tiled=True)  8.61 us
  transfers between devices with their start and end apart: 6, of which 5 were waited for; matrix products, arithmetic and copies ran while one was open for 2% of the time, Pallas kernels for 10%

profile of v8, /device:TPU:0, one launch (start us, length us, event | category | flops | bytes accessed | tf_op | source)
XLA Modules:
  0.0 217.8 jit_solution(11908682503147698358)
XLA Ops:
  0.6 0.8 copy.113
  1.5 1.5 copy.188
  3.0 0.2 copy.263
  3.3 0.6 copy-done
  3.9 3.5 %copy.191 = bf16[128,8,8,256]{3,2,1,0:T(8,128)(2,1)} copy(bf16[128,8,8,256]{3,1,2,0:T(8,128)(2,1)S(1)} %bitcast.196) | data formatting | bytes 8388608
  7.4 1.4 copy.190
  8.9 3.4 %fusion.1 = bf16[2,8,48,16,32]{2,4,1,0,3:T(8,128)(2,1)S(1)} fusion(pred[8,16,32]{2,0,1:T(8,128)(4,1)S(1)} %iota_compare_fusion, bf16[8,2,32,16,256,1]{4,3,2,1,0,5:T(8,128)(2,1)S(1)} %bitcast.198, bf16[1,16,2,48,256]{4,3,2,0,1:T(8,128)(2,1)S(1)} %maximum_bitcast_fusion.13, bf16[1,16,2,48,256]{4,3,2,0,1:T(8,128)(2,1)S(1)} %bitcast.211), kind=kOutput, calls=%fused_computation.7 | convolution fusion | flops 406585344 | bytes 6557696 | tf_op jit(solution)/shard_map/icrjt,ojcvt->oivjr/dot_general | solution.py:149
  12.3 1.3 slice_negate_fusion.7
  13.5 2.5 %maximum_bitcast_fusion = (bf16[1,2,8,48,16,32]{3,5,2,1,4,0:T(8,128)(2,1)S(1)}, bf16[1,2,8,48,16,32]{3,5,2,1,4,0:T(8,128)(2,1)S(1)}) fusion(bf16[1,8,48,16,32]{2,4,1,0,3:T(8,128)(2,1)S(1)} %get-tuple-element.11, bf16[1,8,48,16,32]{2,4,1,0,3:T(8,128)(2,1)} %get-tuple-element.13, bf16[1,8,48,16,32]{2,4,1,0,3:T(8,128)(2,1)S(1)} %get-tuple-element.12), kind=kLoop, calls=%fused_computation.34 | loop fusion | flops 786432 | bytes 2752512 | tf_op jit(solution)/shard_map/stack | solution.py:155
  16.0 0.3 copy-done.6
  16.3 2.3 %fusion.41 = bf16[8,2,48,256]{3,2,0,1:T(8,128)(2,1)S(1)} fusion(bf16[16,2,32,8,256,1]{4,3,2,1,0,5:T(8,128)(2,1)S(1)} %bitcast.204, bf16[1,2,8,48,16,32]{3,5,2,1,4,0:T(8,128)(2,1)S(1)} %get-tuple-element.21, bf16[1,2,8,48,16,32]{3,5,2,1,4,0:T(8,128)(2,1)S(1)} %get-tuple-element.20), kind=kOutput, calls=%fused_computation.53 | convolution fusion | flops 403439616 | bytes 6160384 | tf_op jit(solution)/shard_map/jcrit,ocivjr->iovt/dot_general | solution.py:156
  18.7 3.0 %collective-permute-start = (bf16[4,2,48,256]{3,2,1,0:T(8,128)(2,1)S(1)}, bf16[4,2,48,256]{3,2,1,0:T(8,128)(2,1)S(1)}, u32[]{:S(2)}, u32[]{:S(2)}) collective-permute-start(bf16[4,2,48,256]{3,2,1,0:T(8,128)(2,1)S(1)} %copy.260), channel_id=1, source_target_pairs={{0,2},{2,0},{1,3},{3,1},{4,6},{6,4},{5,7},{7,5},{8,10},{10,8},{9,1... | collective-permute-start | bytes 589832 | tf_op jit(solution)/shard_map/ppermute | solution.py:179
  22.0 0.6 reduce-window.6
  23.0 0.6 copy.265
  23.7 2.9 %collective-permute-done = bf16[4,2,48,256]{3,2,1,0:T(8,128)(2,1)S(1)} collective-permute-done((bf16[4,2,48,256]{3,2,1,0:T(8,128)(2,1)S(1)}, bf16[4,2,48,256]{3,2,1,0:T(8,128)(2,1)S(1)}, u32[]{:S(2)}, u32[]{:S(2)}) %collective-permute-start) | collective-permute-done | bytes 196640 | tf_op jit(solution)/shard_map/ppermute | solution.py:179
  26.6 0.7 add_convert_fusion.1
  27.3 5.1 %all-to-all-start = ((bf16[4,2,48,256]{3,2,1,0:T(8,128)(2,1)}), bf16[4,2,48,256]{3,2,1,0:T(8,128)(2,1)S(1)}, u32[]{:S(2)}, u32[]{:S(2)}) async-start(bf16[4,2,48,256]{3,2,1,0:T(8,128)(2,1)} %add_convert_fusion.1), calls=%async_computation | async-start | bytes 393216 | tf_op jit(solution)/shard_map/all_to_all | solution.py:136
  32.5 0.6 maximum_bitcast_fusion.21.table_ref
  33.1 5.2 %shard_map.78.matrix_ref = f32[64,1,48,256]{3,2,1,0:T(8,128)} custom-call(bf16[128,256]{1,0:T(8,128)(2,1)} %maximum_bitcast_fusion.21.table_ref, s32[1,48,256]{2,1,0:T(8,128)} %bitcast.226), custom_call_target="tpu_custom_call" | custom-call | tf_op jit(solution)/shard_map/pallas_call | solution.py:53
  38.3 0.5 all-to-all-done
  38.9 0.7 copy-done.9
  39.6 2.8 %shard_map.79 = bf16[4,1,2,48,256]{4,3,2,1,0:T(8,128)(2,1)} custom-call(f32[64,1,48,256]{3,2,1,0:T(8,128)} %shard_map.78.matrix_ref, bf16[4,1,2,48,256]{4,3,2,1,0:T(8,128)(2,1)} %bitcast.219), custom_call_target="tpu_custom_call" | custom-call | tf_op jit(solution)/shard_map/pallas_call | solution.py:89
  42.4 4.6 %all-to-all-start.1 = ((bf16[4,2,48,256]{3,2,1,0:T(8,128)(2,1)}), bf16[4,2,48,256]{3,2,1,0:T(8,128)(2,1)S(1)}, u32[]{:S(2)}, u32[]{:S(2)}) async-start(bf16[4,2,48,256]{3,2,1,0:T(8,128)(2,1)} %bitcast.220), calls=%async_computation.1 | async-start | bytes 393216 | tf_op jit(solution)/shard_map/all_to_all | solution.py:142
  47.0 6.2 %all-to-all-done.1 = bf16[4,2,48,256]{3,2,1,0:T(8,128)(2,1)S(1)} async-done(((bf16[4,2,48,256]{3,2,1,0:T(8,128)(2,1)}), bf16[4,2,48,256]{3,2,1,0:T(8,128)(2,1)S(1)}, u32[]{:S(2)}, u32[]{:S(2)}) %all-to-all-start.1) | async-done | bytes 196640 | tf_op jit(solution)/shard_map/all_to_all | solution.py:142
  53.2 6.5 %all_gather.6 = bf16[8,2,48,256]{3,2,1,0:T(8,128)(2,1)S(1)} all-gather(bf16[4,2,48,256]{3,2,1,0:T(8,128)(2,1)S(1)} %all-to-all-done.1), channel_id=1, replica_groups=mesh['groups'=2,'freq'=4,'src'=2,'vp'=2] {'src'}, dimensions={0}, use_global_device_ids=true | all-gather | bytes 589824 | tf_op jit(solution)/shard_map/all_gather | solution.py:218
  59.8 3.7 %fusion.24 = bf16[2,8,48,16,32]{2,4,3,0,1:T(8,128)(2,1)S(1)} fusion(pred[8,16,32]{2,1,0:T(8,128)(4,1)S(1)} %copy.114, bf16[16,2,32,8,256,1]{4,3,2,1,0,5:T(8,128)(2,1)} %bitcast.202, bf16[1,8,2,48,256]{4,3,2,0,1:T(8,128)(2,1)S(1)} %maximum_bitcast_fusion.19, bf16[1,8,2,48,256]{4,3,2,0,1:T(8,128)(2,1)S(1)} %bitcast.217), kind=kOutput, calls=%fused_computation.32 | convolution fusion | flops 405012480 | bytes 5771264 | tf_op jit(solution)/shard_map/jcrit,oicvt->oivjr/dot_general | solution.py:162
  63.5 0.3 slice_negate_fusion.6
  63.7 0.9 maximum_bitcast_fusion.2
  64.6 1.3 copy-done.3
  65.9 3.5 %fusion.5 = bf16[16,2,48,256,1,1]{3,2,4,1,0,5:T(8,128)(2,1)S(1)} fusion(bf16[8,2,32,16,256,1]{4,3,2,1,0,5:T(8,128)(2,1)S(1)} %bitcast.199, bf16[1,2,8,48,16,32]{3,5,4,1,2,0:T(8,128)(2,1)S(1)} %get-tuple-element.19, bf16[1,2,8,48,16,32]{3,5,4,1,2,0:T(8,128)(2,1)S(1)} %get-tuple-element.18), kind=kOutput, calls=%fused_computation.12 | convolution fusion | flops 403439616 | bytes 6553600 | tf_op jit(solution)/shard_map/icrjt,ocivjr->jovt/dot_general | solution.py:166
  69.5 1.0 copy.125
  70.4 3.5 %all-to-all-start.2 = ((bf16[16,2,48,256]{3,2,1,0:T(8,128)(2,1)}), bf16[16,2,48,256]{3,2,1,0:T(8,128)(2,1)S(1)}, u32[]{:S(2)}, u32[]{:S(2)}) async-start(bf16[16,2,48,256]{3,2,1,0:T(8,128)(2,1)} %copy.125), calls=%async_computation.2 | async-start | bytes 1572864 | tf_op jit(solution)/shard_map/all_to_all | solution.py:136
  74.0 0.2 copy.189
  74.3 0.7 copy.264
  75.0 16.5 %shard_map.77.matrix_ref = f32[64,4,48,256]{3,2,1,0:T(8,128)} custom-call(bf16[128,256]{1,0:T(8,128)(2,1)} %maximum_bitcast_fusion.21.table_ref, s32[4,48,256]{2,1,0:T(8,128)} %bitcast.225), custom_call_target="tpu_custom_call" | custom-call | tf_op jit(solution)/shard_map/pallas_call | solution.py:53
  91.5 0.9 copy-done.8
  92.4 6.3 %shard_map.80 = bf16[4,4,2,48,256]{4,3,2,1,0:T(8,128)(2,1)} custom-call(f32[64,4,48,256]{3,2,1,0:T(8,128)} %shard_map.77.matrix_ref, bf16[4,4,2,48,256]{4,3,2,1,0:T(8,128)(2,1)} %bitcast.206), custom_call_target="tpu_custom_call" | custom-call | tf_op jit(solution)/shard_map/pallas_call | solution.py:89
  98.7 20.9 %all_to_all.40 = bf16[16,2,48,256]{3,2,1,0:T(8,128)(2,1)S(1)} all-to-all(bf16[16,2,48,256]{3,2,1,0:T(8,128)(2,1)} %bitcast.209), channel_id=1, replica_groups=mesh['groups'=2,'freq'=4,'src'=2,'vp'=2] {'freq'}, dimensions={0} | all-to-all | bytes 1572864 | tf_op jit(solution)/shard_map/all_to_all | solution.py:142
  119.5 0.3 fusion.26
  120.0 1.7 copy-done.4
  121.7 3.3 %fusion = bf16[2,8,48,16,32]{2,4,1,0,3:T(8,128)(2,1)S(1)} fusion(pred[8,16,32]{2,0,1:T(8,128)(4,1)S(1)} %iota_compare_fusion, bf16[8,2,32,16,256,1]{4,3,2,1,0,5:T(8,128)(2,1)S(1)} %bitcast.200, bf16[1,16,2,48,256]{4,3,2,1,0:T(8,128)(2,1)S(1)} %maximum_bitcast_fusion.16, bf16[1,16,2,48,256]{4,3,2,1,0:T(8,128)(2,1)S(1)} %bitcast.214), kind=kOutput, calls=%fused_computation.5 | convolution fusion | flops 404226048 | bytes 6557696 | tf_op jit(solution)/shard_map/icrjt,ojcvt->oivjr/dot_general | solution.py:149
  125.1 0.3 slice_negate_fusion.5
  125.3 0.8 maximum_bitcast_fusion.4
  126.2 1.4 copy-done.7
  127.5 2.3 %fusion.46 = bf16[8,2,48,256]{3,2,0,1:T(8,128)(2,1)S(1)} fusion(bf16[16,2,32,8,256,1]{4,3,2,1,0,5:T(8,128)(2,1)S(1)} %bitcast.205, bf16[1,2,8,48,16,32]{3,5,2,1,4,0:T(8,128)(2,1)S(1)} %get-tuple-element.17, bf16[1,2,8,48,16,32]{3,5,2,1,4,0:T(8,128)(2,1)S(1)} %get-tuple-element.16), kind=kOutput, calls=%fused_computation.54 | convolution fusion | flops 403439616 | bytes 6160384 | tf_op jit(solution)/shard_map/jcrit,ocivjr->iovt/dot_general | solution.py:156
  129.9 1.6 collective-permute-start.1
  131.4 4.2 %collective-permute-done.1 = bf16[4,2,48,256]{3,2,1,0:T(8,128)(2,1)S(1)} collective-permute-done((bf16[4,2,48,256]{3,2,1,0:T(8,128)(2,1)S(1)}, bf16[4,2,48,256]{3,2,1,0:T(8,128)(2,1)S(1)}, u32[]{:S(2)}, u32[]{:S(2)}) %collective-permute-start.1) | collective-permute-done | bytes 196640 | tf_op jit(solution)/shard_map/ppermute | solution.py:179
  135.7 9.8 %all_to_all.41 = bf16[4,2,48,256]{3,2,1,0:T(8,128)(2,1)} all-to-all(bf16[4,2,48,256]{3,2,1,0:T(8,128)(2,1)S(1)} %add_convert_fusion), channel_id=1, replica_groups=mesh['groups'=2,'freq'=4,'src'=2,'vp'=2] {'freq'}, dimensions={0} | all-to-all | bytes 393216 | tf_op jit(solution)/shard_map/all_to_all | solution.py:136
  145.5 2.8 %shard_map.81 = bf16[4,1,2,48,256]{4,3,2,1,0:T(8,128)(2,1)} custom-call(f32[64,1,48,256]{3,2,1,0:T(8,128)} %shard_map.78.matrix_ref, bf16[4,1,2,48,256]{4,3,2,1,0:T(8,128)(2,1)} %bitcast.221), custom_call_target="tpu_custom_call" | custom-call | tf_op jit(solution)/shard_map/pallas_call | solution.py:89
  148.3 10.1 %all_to_all.42 = bf16[4,2,48,256]{3,2,1,0:T(8,128)(2,1)S(1)} all-to-all(bf16[4,2,48,256]{3,2,1,0:T(8,128)(2,1)} %bitcast.222), channel_id=1, replica_groups=mesh['groups'=2,'freq'=4,'src'=2,'vp'=2] {'freq'}, dimensions={0} | all-to-all | bytes 393216 | tf_op jit(solution)/shard_map/all_to_all | solution.py:142
  158.5 6.6 %all_gather.7 = bf16[8,2,48,256]{3,2,1,0:T(8,128)(2,1)S(1)} all-gather(bf16[4,2,48,256]{3,2,1,0:T(8,128)(2,1)S(1)} %all_to_all.42), channel_id=1, replica_groups=mesh['groups'=2,'freq'=4,'src'=2,'vp'=2] {'src'}, dimensions={0}, use_global_device_ids=true | all-gather | bytes 589824 | tf_op jit(solution)/shard_map/all_gather | solution.py:218
  165.1 3.7 %fusion.25 = bf16[2,8,48,16,32]{2,4,3,0,1:T(8,128)(2,1)S(1)} fusion(pred[8,16,32]{2,1,0:T(8,128)(4,1)S(1)} %copy.114, bf16[16,2,32,8,256,1]{4,3,2,1,0,5:T(8,128)(2,1)} %bitcast.203, bf16[1,8,2,48,256]{4,3,2,0,1:T(8,128)(2,1)S(1)} %maximum_bitcast_fusion.20, bf16[1,8,2,48,256]{4,3,2,0,1:T(8,128)(2,1)S(1)} %bitcast.216), kind=kOutput, calls=%fused_computation.33 | convolution fusion | flops 405012480 | bytes 5771264 | tf_op jit(solution)/shard_map/jcrit,oicvt->oivjr/dot_general | solution.py:162
  168.8 0.3 slice_negate_fusion.4
  169.1 0.9 maximum_bitcast_fusion.6
  169.9 1.3 copy-done.5
  171.2 3.5 %fusion.2 = bf16[16,2,48,256,1,1]{3,2,4,1,0,5:T(8,128)(2,1)S(1)} fusion(bf16[8,2,32,16,256,1]{4,3,2,1,0,5:T(8,128)(2,1)S(1)} %bitcast.201, bf16[1,2,8,48,16,32]{3,5,4,1,2,0:T(8,128)(2,1)S(1)} %get-tuple-element.15, bf16[1,2,8,48,16,32]{3,5,4,1,2,0:T(8,128)(2,1)S(1)} %get-tuple-element.14), kind=kOutput, calls=%fused_computation.8 | convolution fusion | flops 403439616 | bytes 6553600 | tf_op jit(solution)/shard_map/icrjt,ocivjr->jovt/dot_general | solution.py:166
  174.9 16.7 %all_to_all.43 = bf16[16,2,48,256]{3,2,1,0:T(8,128)(2,1)} all-to-all(bf16[16,2,48,256]{3,2,1,0:T(8,128)(2,1)S(1)} %copy.135), channel_id=1, replica_groups=mesh['groups'=2,'freq'=4,'src'=2,'vp'=2] {'freq'}, dimensions={0} | all-to-all | bytes 1572864 | tf_op jit(solution)/shard_map/all_to_all | solution.py:136
  191.5 6.3 %shard_map.82 = bf16[4,4,2,48,256]{4,3,2,1,0:T(8,128)(2,1)} custom-call(f32[64,4,48,256]{3,2,1,0:T(8,128)} %shard_map.77.matrix_ref, bf16[4,4,2,48,256]{4,3,2,1,0:T(8,128)(2,1)} %bitcast.208), custom_call_target="tpu_custom_call" | custom-call | tf_op jit(solution)/shard_map/pallas_call | solution.py:89
  197.8 3.5 %all-to-all-start.7 = ((bf16[16,2,48,256]{3,2,1,0:T(8,128)(2,1)}), bf16[16,2,48,256]{3,2,1,0:T(8,128)(2,1)S(1)}, u32[]{:S(2)}, u32[]{:S(2)}) async-start(bf16[16,2,48,256]{3,2,1,0:T(8,128)(2,1)} %bitcast.207), calls=%async_computation.7 | async-start | bytes 1572864 | tf_op jit(solution)/shard_map/all_to_all | solution.py:142
  201.5 0.8 broadcast_in_dim_reshape.7
  202.3 13.5 %all-to-all-done.7 = bf16[16,2,48,256]{3,2,1,0:T(8,128)(2,1)S(1)} async-done(((bf16[16,2,48,256]{3,2,1,0:T(8,128)(2,1)}), bf16[16,2,48,256]{3,2,1,0:T(8,128)(2,1)S(1)}, u32[]{:S(2)}, u32[]{:S(2)}) %all-to-all-start.7) | async-done | bytes 786464 | tf_op jit(solution)/shard_map/all_to_all | solution.py:142
  215.8 0.3 fusion.51
  216.1 0.4 copy.136
  216.5 1.2 broadcast_in_dim_reshape.6
  (52 shorter events, 1.8 us)
Async XLA Ops:
  1.5 2.4 %copy-start = (bf16[1,16,2,32,2048]{4,3,2,1,0:T(8,128)(2,1)S(1)}, bf16[1,16,2,32,2048]{4,3,2,1,0:T(8,128)(2,1)}, u32[]{:S(2)}) copy-start(bf16[1,16,2,32,2048]{4,3,2,1,0:T(8,128)(2,1)} %param.7) | copy-start | bytes 12582916
  3.9 3.5 %copy-start.1 = (bf16[1,8,2,32,4096]{4,3,2,1,0:T(8,128)(2,1)S(1)}, bf16[1,8,2,32,4096]{4,3,2,1,0:T(8,128)(2,1)}, u32[]{:S(2)}) copy-start(bf16[1,8,2,32,4096]{4,3,2,1,0:T(8,128)(2,1)} %param.8) | copy-start | bytes 12582916
  8.8 3.5 %copy-start.2 = (bf16[64,8,16,256]{3,2,1,0:T(8,128)(2,1)}, bf16[64,8,16,256]{3,2,1,0:T(8,128)(2,1)S(1)}, u32[]{:S(2)}) copy-start(bf16[64,8,16,256]{3,2,1,0:T(8,128)(2,1)S(1)} %copy.190) | copy-start | bytes 12582916
  13.5 2.8 %copy-start.6 = (bf16[128,8,8,256]{3,2,1,0:T(8,128)(2,1)S(1)}, bf16[128,8,8,256]{3,2,1,0:T(8,128)(2,1)}, u32[]{:S(2)}) copy-start(bf16[128,8,8,256]{3,2,1,0:T(8,128)(2,1)} %copy.191) | copy-start | bytes 12582916
  16.3 6.5 %copy-start.11 = (s32[48,1024]{1,0:T(8,128)S(1)}, s32[48,1024]{1,0:T(8,128)}, u32[]{:S(2)}) copy-start(s32[48,1024]{1,0:T(8,128)} %param.10) | copy-start | bytes 589828
  18.7 7.9 %collective-permute-start = (bf16[4,2,48,256]{3,2,1,0:T(8,128)(2,1)S(1)}, bf16[4,2,48,256]{3,2,1,0:T(8,128)(2,1)S(1)}, u32[]{:S(2)}, u32[]{:S(2)}) collective-permute-start(bf16[4,2,48,256]{3,2,1,0:T(8,128)(2,1)S(1)} %copy.260), channel_id=1, source_target_pairs={{0,2},{2,0},{1,3},{3,1},{4,6},{6,4},{5,7},{7,5},{8,10},{10,8},{9,1... | collective-permute-start | bytes 589832 | tf_op jit(solution)/shard_map/ppermute | solution.py:179
  27.3 11.6 %all-to-all-start = ((bf16[4,2,48,256]{3,2,1,0:T(8,128)(2,1)}), bf16[4,2,48,256]{3,2,1,0:T(8,128)(2,1)S(1)}, u32[]{:S(2)}, u32[]{:S(2)}) async-start(bf16[4,2,48,256]{3,2,1,0:T(8,128)(2,1)} %add_convert_fusion.1), calls=%async_computation | async-start | bytes 393216 | tf_op jit(solution)/shard_map/all_to_all | solution.py:136
  38.9 0.7 copy-start.9
  42.4 10.8 %all-to-all-start.1 = ((bf16[4,2,48,256]{3,2,1,0:T(8,128)(2,1)}), bf16[4,2,48,256]{3,2,1,0:T(8,128)(2,1)S(1)}, u32[]{:S(2)}, u32[]{:S(2)}) async-start(bf16[4,2,48,256]{3,2,1,0:T(8,128)(2,1)} %bitcast.220), calls=%async_computation.1 | async-start | bytes 393216 | tf_op jit(solution)/shard_map/all_to_all | solution.py:142
  63.7 2.2 %copy-start.3 = (bf16[64,8,16,256]{3,2,1,0:T(8,128)(2,1)S(1)}, bf16[64,8,16,256]{3,2,1,0:T(8,128)(2,1)}, u32[]{:S(2)}) copy-start(bf16[64,8,16,256]{3,2,1,0:T(8,128)(2,1)} %copy-done.2) | copy-start | bytes 12582916
  69.4 4.5 %copy-start.10 = (s32[48,4096]{1,0:T(8,128)S(1)}, s32[48,4096]{1,0:T(8,128)}, u32[]{:S(2)}) copy-start(s32[48,4096]{1,0:T(8,128)} %param.11) | copy-start | bytes 2359300
  70.4 21.1 %all-to-all-start.2 = ((bf16[16,2,48,256]{3,2,1,0:T(8,128)(2,1)}), bf16[16,2,48,256]{3,2,1,0:T(8,128)(2,1)S(1)}, u32[]{:S(2)}, u32[]{:S(2)}) async-start(bf16[16,2,48,256]{3,2,1,0:T(8,128)(2,1)} %copy.125), calls=%async_computation.2 | async-start | bytes 1572864 | tf_op jit(solution)/shard_map/all_to_all | solution.py:136
  91.5 0.9 copy-start.8
  119.5 2.2 %copy-start.4 = (bf16[64,8,16,256]{3,2,1,0:T(8,128)(2,1)S(1)}, bf16[64,8,16,256]{3,2,1,0:T(8,128)(2,1)}, u32[]{:S(2)}) copy-start(bf16[64,8,16,256]{3,2,1,0:T(8,128)(2,1)} %copy-done.2) | copy-start | bytes 12582916
  125.3 2.2 %copy-start.7 = (bf16[128,8,8,256]{3,2,1,0:T(8,128)(2,1)S(1)}, bf16[128,8,8,256]{3,2,1,0:T(8,128)(2,1)}, u32[]{:S(2)}) copy-start(bf16[128,8,8,256]{3,2,1,0:T(8,128)(2,1)} %copy.191) | copy-start | bytes 12582916
  129.9 5.7 %collective-permute-start.1 = (bf16[4,2,48,256]{3,2,1,0:T(8,128)(2,1)S(1)}, bf16[4,2,48,256]{3,2,1,0:T(8,128)(2,1)S(1)}, u32[]{:S(2)}, u32[]{:S(2)}) collective-permute-start(bf16[4,2,48,256]{3,2,1,0:T(8,128)(2,1)S(1)} %copy.259), channel_id=1, source_target_pairs={{0,2},{2,0},{1,3},{3,1},{4,6},{6,4},{5,7},{7,5},{8,10},{10,8},{9,1... | collective-permute-start | bytes 589832 | tf_op jit(solution)/shard_map/ppermute | solution.py:179
  169.0 2.2 %copy-start.5 = (bf16[64,8,16,256]{3,2,1,0:T(8,128)(2,1)S(1)}, bf16[64,8,16,256]{3,2,1,0:T(8,128)(2,1)}, u32[]{:S(2)}) copy-start(bf16[64,8,16,256]{3,2,1,0:T(8,128)(2,1)} %copy-done.2) | copy-start | bytes 12582916
  197.8 17.9 %all-to-all-start.7 = ((bf16[16,2,48,256]{3,2,1,0:T(8,128)(2,1)}), bf16[16,2,48,256]{3,2,1,0:T(8,128)(2,1)S(1)}, u32[]{:S(2)}, u32[]{:S(2)}) async-start(bf16[16,2,48,256]{3,2,1,0:T(8,128)(2,1)} %bitcast.207), calls=%async_computation.7 | async-start | bytes 1572864 | tf_op jit(solution)/shard_map/all_to_all | solution.py:142

commit v9 on v8

--- a/solution.py
+++ b/solution.py
@@ -28,13 +28,12 @@
 def gather_kernel(table_ref, onset_ref, out_ref):
     rows = onset_ref.shape[1]
     width = onset_ref.shape[2]
-    size = out_ref.shape[0]
     sample = lax.broadcasted_iota(jnp.int32, (NT, width), 0)
     for row in range(rows):
         place = jnp.clip(onset_ref[0, row : row + 1, :], 0, NT) - 1
         pick = (sample == place).astype(jnp.bfloat16)
         parts = jnp.dot(table_ref[...], pick, preferred_element_type=jnp.float32)
-        out_ref[:, 0, row, :] = parts[:size] + parts[size:]
+        out_ref[:, 0, row, :] = parts.astype(out_ref.dtype)
 
 
 def window_gather(count, onset):
@@ -44,21 +43,18 @@
     terms = jnp.einsum("cft,dgt->tgdfc", forward, inverse, precision=lax.Precision.HIGHEST)
     size = 4 * count * count
     table = jnp.cumsum(terms.reshape(NT, size), axis=0)
-    high = table.astype(jnp.bfloat16)
-    rest = table - high.astype(jnp.float32)
-    low = rest.astype(jnp.bfloat16)
-    stacked = jnp.concatenate([high, low], axis=1).T
+    stacked = table.astype(jnp.bfloat16).T
     blocks, points, width = onset.shape
     rows = 8
     return pl.pallas_call(
         gather_kernel,
         grid=(blocks, points // rows),
         in_specs=[
-            pl.BlockSpec((2 * size, NT), lambda b, r: (0, 0)),
+            pl.BlockSpec((size, NT), lambda b, r: (0, 0)),
             pl.BlockSpec((1, rows, width), lambda b, r: (b, r, 0)),
         ],
         out_specs=pl.BlockSpec((size, 1, rows, width), lambda b, r: (0, b, r, 0)),
-        out_shape=jax.ShapeDtypeStruct((size, blocks, points, width), jnp.float32),
+        out_shape=jax.ShapeDtypeStruct((size, blocks, points, width), jnp.bfloat16),
     )(stacked, onset)
 
 
@@ -67,9 +63,9 @@
     comps = 2 * count
     source = [spectrum_ref[q // 2, 0, q % 2].astype(jnp.float32) for q in range(comps)]
     for target in range(comps):
-        total = matrix_ref[target, 0] * source[0]
+        total = matrix_ref[target, 0].astype(jnp.float32) * source[0]
         for q in range(1, comps):
-            total = total + matrix_ref[q * comps + target, 0] * source[q]
+            total = total + matrix_ref[q * comps + target, 0].astype(jnp.float32) * source[q]
         out_ref[target // 2, 0, target % 2] = total.astype(out_ref.dtype)
 
 

time: 220 us -> 217 us (0.986)
  Pallas kernels: 39.9 us -> 36.3 us
    pallas_call x4, Pallas kernels: 18.2 us -> 13.8 us  [window(): pl.pallas_call(window_kernel, grid=(blocks,), in_specs=[pl.BlockSpec((siz...]
  transfers between devices with their start and end apart: 6 -> 6, of which waited for: 5 -> 4; matrix products, arithmetic and copies ran while one was open for 2% -> 2% of each run, Pallas kernels for 10% -> 10%
where the time goes in v9:
time: 217 us; the launch traced here: 214 us
  blocking collectives  70.6 us (33%)
  Pallas kernels  36.3 us (17%)
  waiting for transfers between devices  26.9 us (12%)
  matrix products  25.5 us (12%)
  starting transfers between devices  21.7 us (10%)
  local copies, waits for them, and re-layouts  21.5 us (10%)
  other arithmetic  10.5 us (5%)
    all_to_all x2, blocking collectives, exchange_back(): got = lax.all_to_all(flat, 'freq', split_axis=0, concat_axis=0, tiled=True)  31 us
    all_to_all x2, blocking collectives, exchange(): lax.all_to_all(pieces, 'freq', split_axis=0, concat_axis=0, tiled=True)  26.5 us
    pallas_call x2, Pallas kernels, window_gather(): pl.pallas_call(gather_kernel, grid=(blocks, points // rows), in_specs=[pl...  22.5 us
    all_to_all x2, waiting for transfers between devices, exchange_back(): got = lax.all_to_all(flat, 'freq', split_axis=0, concat_axis=0, tiled=True)  19 us
    unnamed x32, local copies, waits for them, and re-layouts  16.2 us
    pallas_call x4, Pallas kernels, window(): pl.pallas_call(window_kernel, grid=(blocks,), in_specs=[pl.BlockSpec((siz...  13.8 us
    all_gather x2, blocking collectives, per_device(): minus_all = lax.all_gather(minus, 'src', axis=0, tiled=True)  13.1 us
    all_to_all x2, starting transfers between devices, exchange(): lax.all_to_all(pieces, 'freq', split_axis=0, concat_axis=0, tiled=True)  8.62 us
  transfers between devices with their start and end apart: 6, of which 4 were waited for; matrix products, arithmetic and copies ran while one was open for 2% of the time, Pallas kernels for 10%

profile of v9, /device:TPU:0, one launch (start us, length us, event | category | flops | bytes accessed | tf_op | source)
XLA Modules:
  0.0 214.2 jit_solution(838166952678458739)
XLA Ops:
  0.6 0.8 copy.113
  1.5 1.5 copy.188
  3.0 0.2 copy.260
  3.3 0.6 copy-done
  3.9 3.6 %copy.191 = bf16[128,8,8,256]{3,2,1,0:T(8,128)(2,1)} copy(bf16[128,8,8,256]{3,1,2,0:T(8,128)(2,1)S(1)} %bitcast.175) | data formatting | bytes 8388608
  7.5 1.4 copy.190
  9.0 3.4 %fusion.1 = bf16[2,8,48,16,32]{2,4,1,0,3:T(8,128)(2,1)S(1)} fusion(pred[8,16,32]{2,0,1:T(8,128)(4,1)S(1)} %iota_compare_fusion, bf16[8,2,32,16,256,1]{4,3,2,1,0,5:T(8,128)(2,1)S(1)} %bitcast.177, bf16[1,16,2,48,256]{4,3,2,0,1:T(8,128)(2,1)S(1)} %maximum_bitcast_fusion.13, bf16[1,16,2,48,256]{4,3,2,0,1:T(8,128)(2,1)S(1)} %bitcast.186), kind=kOutput, calls=%fused_computation.7 | convolution fusion | flops 406585344 | bytes 6557696 | tf_op jit(solution)/shard_map/icrjt,ojcvt->oivjr/dot_general | solution.py:145
  12.4 1.3 slice_negate_fusion.7
  13.6 2.5 %maximum_bitcast_fusion = (bf16[1,2,8,48,16,32]{3,5,2,1,4,0:T(8,128)(2,1)S(1)}, bf16[1,2,8,48,16,32]{3,5,2,1,4,0:T(8,128)(2,1)S(1)}) fusion(bf16[1,8,48,16,32]{2,4,1,0,3:T(8,128)(2,1)S(1)} %get-tuple-element.11, bf16[1,8,48,16,32]{2,4,1,0,3:T(8,128)(2,1)} %get-tuple-element.13, bf16[1,8,48,16,32]{2,4,1,0,3:T(8,128)(2,1)S(1)} %get-tuple-element.12), kind=kLoop, calls=%fused_computation.34 | loop fusion | flops 786432 | bytes 2752512 | tf_op jit(solution)/shard_map/stack | solution.py:151
  16.1 0.3 copy-done.6
  16.4 2.3 %fusion.41 = bf16[8,2,48,256]{3,2,0,1:T(8,128)(2,1)S(1)} fusion(bf16[16,2,32,8,256,1]{4,3,2,1,0,5:T(8,128)(2,1)S(1)} %bitcast.183, bf16[1,2,8,48,16,32]{3,5,2,1,4,0:T(8,128)(2,1)S(1)} %get-tuple-element.21, bf16[1,2,8,48,16,32]{3,5,2,1,4,0:T(8,128)(2,1)S(1)} %get-tuple-element.20), kind=kOutput, calls=%fused_computation.53 | convolution fusion | flops 403439616 | bytes 6160384 | tf_op jit(solution)/shard_map/jcrit,ocivjr->iovt/dot_general | solution.py:152
  18.8 3.0 %collective-permute-start = (bf16[4,2,48,256]{3,2,1,0:T(8,128)(2,1)S(1)}, bf16[4,2,48,256]{3,2,1,0:T(8,128)(2,1)S(1)}, u32[]{:S(2)}, u32[]{:S(2)}) collective-permute-start(bf16[4,2,48,256]{3,2,1,0:T(8,128)(2,1)S(1)} %copy.257), channel_id=1, source_target_pairs={{0,2},{2,0},{1,3},{3,1},{4,6},{6,4},{5,7},{7,5},{8,10},{10,8},{9,1... | collective-permute-start | bytes 589832 | tf_op jit(solution)/shard_map/ppermute | solution.py:175
  22.1 0.6 reduce-window.6
  22.7 0.2 slice_reduce_fusion
  23.0 3.7 %collective-permute-done = bf16[4,2,48,256]{3,2,1,0:T(8,128)(2,1)S(1)} collective-permute-done((bf16[4,2,48,256]{3,2,1,0:T(8,128)(2,1)S(1)}, bf16[4,2,48,256]{3,2,1,0:T(8,128)(2,1)S(1)}, u32[]{:S(2)}, u32[]{:S(2)}) %collective-permute-start) | collective-permute-done | bytes 196640 | tf_op jit(solution)/shard_map/ppermute | solution.py:175
  26.7 0.7 add_convert_fusion.1
  27.4 5.1 %all-to-all-start = ((bf16[4,2,48,256]{3,2,1,0:T(8,128)(2,1)}), bf16[4,2,48,256]{3,2,1,0:T(8,128)(2,1)S(1)}, u32[]{:S(2)}, u32[]{:S(2)}) async-start(bf16[4,2,48,256]{3,2,1,0:T(8,128)(2,1)} %add_convert_fusion.1), calls=%async_computation | async-start | bytes 393216 | tf_op jit(solution)/shard_map/all_to_all | solution.py:132
  32.6 0.6 copy.262
  33.2 0.7 copy_bitcast_fusion.5.table_ref
  33.9 5.3 %shard_map.78.matrix_ref = bf16[64,1,48,256]{3,2,1,0:T(8,128)(2,1)} custom-call(bf16[64,256]{1,0:T(8,128)(2,1)} %copy_bitcast_fusion.5.table_ref, s32[1,48,256]{2,1,0:T(8,128)} %bitcast.205), custom_call_target="tpu_custom_call" | custom-call | tf_op jit(solution)/shard_map/pallas_call | solution.py:49
  39.2 0.7 copy-done.10
  39.9 2.3 %shard_map.79 = bf16[4,1,2,48,256]{4,3,2,1,0:T(8,128)(2,1)} custom-call(bf16[64,1,48,256]{3,2,1,0:T(8,128)(2,1)} %shard_map.78.matrix_ref, bf16[4,1,2,48,256]{4,3,2,1,0:T(8,128)(2,1)} %bitcast.201), custom_call_target="tpu_custom_call" | custom-call | tf_op jit(solution)/shard_map/pallas_call | solution.py:85
  42.1 5.1 %all-to-all-start.1 = ((bf16[4,2,48,256]{3,2,1,0:T(8,128)(2,1)}), bf16[4,2,48,256]{3,2,1,0:T(8,128)(2,1)S(1)}, u32[]{:S(2)}, u32[]{:S(2)}) async-start(bf16[4,2,48,256]{3,2,1,0:T(8,128)(2,1)} %bitcast.202), calls=%async_computation.1 | async-start | bytes 393216 | tf_op jit(solution)/shard_map/all_to_all | solution.py:138
  47.2 6.2 %all-to-all-done.1 = bf16[4,2,48,256]{3,2,1,0:T(8,128)(2,1)S(1)} async-done(((bf16[4,2,48,256]{3,2,1,0:T(8,128)(2,1)}), bf16[4,2,48,256]{3,2,1,0:T(8,128)(2,1)S(1)}, u32[]{:S(2)}, u32[]{:S(2)}) %all-to-all-start.1) | async-done | bytes 196640 | tf_op jit(solution)/shard_map/all_to_all | solution.py:138
  53.5 6.5 %all_gather.6 = bf16[8,2,48,256]{3,2,1,0:T(8,128)(2,1)S(1)} all-gather(bf16[4,2,48,256]{3,2,1,0:T(8,128)(2,1)S(1)} %all-to-all-done.1), channel_id=1, replica_groups=mesh['groups'=2,'freq'=4,'src'=2,'vp'=2] {'src'}, dimensions={0}, use_global_device_ids=true | all-gather | bytes 589824 | tf_op jit(solution)/shard_map/all_gather | solution.py:214
  60.0 3.7 %fusion.24 = bf16[2,8,48,16,32]{2,4,3,0,1:T(8,128)(2,1)S(1)} fusion(pred[8,16,32]{2,1,0:T(8,128)(4,1)S(1)} %copy.114, bf16[16,2,32,8,256,1]{4,3,2,1,0,5:T(8,128)(2,1)} %bitcast.181, bf16[1,8,2,48,256]{4,3,2,0,1:T(8,128)(2,1)S(1)} %maximum_bitcast_fusion.19, bf16[1,8,2,48,256]{4,3,2,0,1:T(8,128)(2,1)S(1)} %bitcast.196), kind=kOutput, calls=%fused_computation.32 | convolution fusion | flops 405012480 | bytes 5771264 | tf_op jit(solution)/shard_map/jcrit,oicvt->oivjr/dot_general | solution.py:158
  63.7 0.3 slice_negate_fusion.6
  64.0 0.9 maximum_bitcast_fusion.2
  64.9 1.3 copy-done.3
  66.2 3.5 %fusion.5 = bf16[16,2,48,256,1,1]{3,2,4,1,0,5:T(8,128)(2,1)S(1)} fusion(bf16[8,2,32,16,256,1]{4,3,2,1,0,5:T(8,128)(2,1)S(1)} %bitcast.178, bf16[1,2,8,48,16,32]{3,5,4,1,2,0:T(8,128)(2,1)S(1)} %get-tuple-element.19, bf16[1,2,8,48,16,32]{3,5,4,1,2,0:T(8,128)(2,1)S(1)} %get-tuple-element.18), kind=kOutput, calls=%fused_computation.12 | convolution fusion | flops 403439616 | bytes 6553600 | tf_op jit(solution)/shard_map/icrjt,ocivjr->jovt/dot_general | solution.py:162
  69.8 1.0 copy.125
  70.7 3.5 %all-to-all-start.2 = ((bf16[16,2,48,256]{3,2,1,0:T(8,128)(2,1)}), bf16[16,2,48,256]{3,2,1,0:T(8,128)(2,1)S(1)}, u32[]{:S(2)}, u32[]{:S(2)}) async-start(bf16[16,2,48,256]{3,2,1,0:T(8,128)(2,1)} %copy.125), calls=%async_computation.2 | async-start | bytes 1572864 | tf_op jit(solution)/shard_map/all_to_all | solution.py:132
  74.2 0.2 copy.189
  74.5 0.7 copy.261
  75.3 17.2 %shard_map.77.matrix_ref = bf16[64,4,48,256]{3,2,1,0:T(8,128)(2,1)} custom-call(bf16[64,256]{1,0:T(8,128)(2,1)} %copy_bitcast_fusion.5.table_ref, s32[4,48,256]{2,1,0:T(8,128)} %bitcast.198), custom_call_target="tpu_custom_call" | custom-call | tf_op jit(solution)/shard_map/pallas_call | solution.py:49
  92.5 0.9 copy-done.8
  93.3 4.7 %shard_map.80 = bf16[4,4,2,48,256]{4,3,2,1,0:T(8,128)(2,1)} custom-call(bf16[64,4,48,256]{3,2,1,0:T(8,128)(2,1)} %shard_map.77.matrix_ref, bf16[4,4,2,48,256]{4,3,2,1,0:T(8,128)(2,1)} %bitcast.190), custom_call_target="tpu_custom_call" | custom-call | tf_op jit(solution)/shard_map/pallas_call | solution.py:85
  98.0 20.9 %all_to_all.40 = bf16[16,2,48,256]{3,2,1,0:T(8,128)(2,1)S(1)} all-to-all(bf16[16,2,48,256]{3,2,1,0:T(8,128)(2,1)} %bitcast.193), channel_id=1, replica_groups=mesh['groups'=2,'freq'=4,'src'=2,'vp'=2] {'freq'}, dimensions={0} | all-to-all | bytes 1572864 | tf_op jit(solution)/shard_map/all_to_all | solution.py:138
  118.9 0.3 fusion.26
  119.3 1.7 copy-done.4
  121.1 3.3 %fusion = bf16[2,8,48,16,32]{2,4,1,0,3:T(8,128)(2,1)S(1)} fusion(pred[8,16,32]{2,0,1:T(8,128)(4,1)S(1)} %iota_compare_fusion, bf16[8,2,32,16,256,1]{4,3,2,1,0,5:T(8,128)(2,1)S(1)} %bitcast.179, bf16[1,16,2,48,256]{4,3,2,1,0:T(8,128)(2,1)S(1)} %maximum_bitcast_fusion.16, bf16[1,16,2,48,256]{4,3,2,1,0:T(8,128)(2,1)S(1)} %bitcast.189), kind=kOutput, calls=%fused_computation.5 | convolution fusion | flops 404226048 | bytes 6557696 | tf_op jit(solution)/shard_map/icrjt,ojcvt->oivjr/dot_general | solution.py:145
  124.4 0.3 slice_negate_fusion.5
  124.7 0.8 maximum_bitcast_fusion.4
  125.5 1.4 copy-done.7
  126.8 2.3 %fusion.46 = bf16[8,2,48,256]{3,2,0,1:T(8,128)(2,1)S(1)} fusion(bf16[16,2,32,8,256,1]{4,3,2,1,0,5:T(8,128)(2,1)S(1)} %bitcast.184, bf16[1,2,8,48,16,32]{3,5,2,1,4,0:T(8,128)(2,1)S(1)} %get-tuple-element.17, bf16[1,2,8,48,16,32]{3,5,2,1,4,0:T(8,128)(2,1)S(1)} %get-tuple-element.16), kind=kOutput, calls=%fused_computation.54 | convolution fusion | flops 403439616 | bytes 6160384 | tf_op jit(solution)/shard_map/jcrit,ocivjr->iovt/dot_general | solution.py:152
  129.2 1.5 collective-permute-start.1
  130.7 4.2 %collective-permute-done.1 = bf16[4,2,48,256]{3,2,1,0:T(8,128)(2,1)S(1)} collective-permute-done((bf16[4,2,48,256]{3,2,1,0:T(8,128)(2,1)S(1)}, bf16[4,2,48,256]{3,2,1,0:T(8,128)(2,1)S(1)}, u32[]{:S(2)}, u32[]{:S(2)}) %collective-permute-start.1) | collective-permute-done | bytes 196640 | tf_op jit(solution)/shard_map/ppermute | solution.py:175
  135.0 9.9 %all_to_all.41 = bf16[4,2,48,256]{3,2,1,0:T(8,128)(2,1)} all-to-all(bf16[4,2,48,256]{3,2,1,0:T(8,128)(2,1)S(1)} %add_convert_fusion), channel_id=1, replica_groups=mesh['groups'=2,'freq'=4,'src'=2,'vp'=2] {'freq'}, dimensions={0} | all-to-all | bytes 393216 | tf_op jit(solution)/shard_map/all_to_all | solution.py:132
  144.8 2.3 %shard_map.81 = bf16[4,1,2,48,256]{4,3,2,1,0:T(8,128)(2,1)} custom-call(bf16[64,1,48,256]{3,2,1,0:T(8,128)(2,1)} %shard_map.78.matrix_ref, bf16[4,1,2,48,256]{4,3,2,1,0:T(8,128)(2,1)} %bitcast.203), custom_call_target="tpu_custom_call" | custom-call | tf_op jit(solution)/shard_map/pallas_call | solution.py:85
  147.1 10.1 %all_to_all.42 = bf16[4,2,48,256]{3,2,1,0:T(8,128)(2,1)S(1)} all-to-all(bf16[4,2,48,256]{3,2,1,0:T(8,128)(2,1)} %bitcast.204), channel_id=1, replica_groups=mesh['groups'=2,'freq'=4,'src'=2,'vp'=2] {'freq'}, dimensions={0} | all-to-all | bytes 393216 | tf_op jit(solution)/shard_map/all_to_all | solution.py:138
  157.2 6.6 %all_gather.7 = bf16[8,2,48,256]{3,2,1,0:T(8,128)(2,1)S(1)} all-gather(bf16[4,2,48,256]{3,2,1,0:T(8,128)(2,1)S(1)} %all_to_all.42), channel_id=1, replica_groups=mesh['groups'=2,'freq'=4,'src'=2,'vp'=2] {'src'}, dimensions={0}, use_global_device_ids=true | all-gather | bytes 589824 | tf_op jit(solution)/shard_map/all_gather | solution.py:214
  163.9 3.7 %fusion.25 = bf16[2,8,48,16,32]{2,4,3,0,1:T(8,128)(2,1)S(1)} fusion(pred[8,16,32]{2,1,0:T(8,128)(4,1)S(1)} %copy.114, bf16[16,2,32,8,256,1]{4,3,2,1,0,5:T(8,128)(2,1)} %bitcast.182, bf16[1,8,2,48,256]{4,3,2,0,1:T(8,128)(2,1)S(1)} %maximum_bitcast_fusion.20, bf16[1,8,2,48,256]{4,3,2,0,1:T(8,128)(2,1)S(1)} %bitcast.195), kind=kOutput, calls=%fused_computation.33 | convolution fusion | flops 405012480 | bytes 5771264 | tf_op jit(solution)/shard_map/jcrit,oicvt->oivjr/dot_general | solution.py:158
  167.5 0.3 slice_negate_fusion.4
  167.8 0.9 maximum_bitcast_fusion.6
  168.7 1.3 copy-done.5
  170.0 3.5 %fusion.2 = bf16[16,2,48,256,1,1]{3,2,4,1,0,5:T(8,128)(2,1)S(1)} fusion(bf16[8,2,32,16,256,1]{4,3,2,1,0,5:T(8,128)(2,1)S(1)} %bitcast.180, bf16[1,2,8,48,16,32]{3,5,4,1,2,0:T(8,128)(2,1)S(1)} %get-tuple-element.15, bf16[1,2,8,48,16,32]{3,5,4,1,2,0:T(8,128)(2,1)S(1)} %get-tuple-element.14), kind=kOutput, calls=%fused_computation.8 | convolution fusion | flops 403439616 | bytes 6553600 | tf_op jit(solution)/shard_map/icrjt,ocivjr->jovt/dot_general | solution.py:162
  173.6 16.6 %all_to_all.43 = bf16[16,2,48,256]{3,2,1,0:T(8,128)(2,1)} all-to-all(bf16[16,2,48,256]{3,2,1,0:T(8,128)(2,1)S(1)} %copy.135), channel_id=1, replica_groups=mesh['groups'=2,'freq'=4,'src'=2,'vp'=2] {'freq'}, dimensions={0} | all-to-all | bytes 1572864 | tf_op jit(solution)/shard_map/all_to_all | solution.py:132
  190.3 4.7 %shard_map.82 = bf16[4,4,2,48,256]{4,3,2,1,0:T(8,128)(2,1)} custom-call(bf16[64,4,48,256]{3,2,1,0:T(8,128)(2,1)} %shard_map.77.matrix_ref, bf16[4,4,2,48,256]{4,3,2,1,0:T(8,128)(2,1)} %bitcast.192), custom_call_target="tpu_custom_call" | custom-call | tf_op jit(solution)/shard_map/pallas_call | solution.py:85
  194.9 3.5 %all-to-all-start.7 = ((bf16[16,2,48,256]{3,2,1,0:T(8,128)(2,1)}), bf16[16,2,48,256]{3,2,1,0:T(8,128)(2,1)S(1)}, u32[]{:S(2)}, u32[]{:S(2)}) async-start(bf16[16,2,48,256]{3,2,1,0:T(8,128)(2,1)} %bitcast.191), calls=%async_computation.7 | async-start | bytes 1572864 | tf_op jit(solution)/shard_map/all_to_all | solution.py:138
  198.6 0.8 broadcast_in_dim_reshape.7
  199.4 12.8 %all-to-all-done.7 = bf16[16,2,48,256]{3,2,1,0:T(8,128)(2,1)S(1)} async-done(((bf16[16,2,48,256]{3,2,1,0:T(8,128)(2,1)}), bf16[16,2,48,256]{3,2,1,0:T(8,128)(2,1)S(1)}, u32[]{:S(2)}, u32[]{:S(2)}) %all-to-all-start.7) | async-done | bytes 786464 | tf_op jit(solution)/shard_map/all_to_all | solution.py:138
  212.2 0.3 fusion.51
  212.5 0.4 copy.136
  212.9 1.2 broadcast_in_dim_reshape.6
  (50 shorter events, 1.5 us)
Async XLA Ops:
  1.5 2.4 %copy-start = (bf16[1,16,2,32,2048]{4,3,2,1,0:T(8,128)(2,1)S(1)}, bf16[1,16,2,32,2048]{4,3,2,1,0:T(8,128)(2,1)}, u32[]{:S(2)}) copy-start(bf16[1,16,2,32,2048]{4,3,2,1,0:T(8,128)(2,1)} %param.7) | copy-start | bytes 12582916
  3.9 3.6 %copy-start.1 = (bf16[1,8,2,32,4096]{4,3,2,1,0:T(8,128)(2,1)S(1)}, bf16[1,8,2,32,4096]{4,3,2,1,0:T(8,128)(2,1)}, u32[]{:S(2)}) copy-start(bf16[1,8,2,32,4096]{4,3,2,1,0:T(8,128)(2,1)} %param.8) | copy-start | bytes 12582916
  8.9 3.5 %copy-start.2 = (bf16[64,8,16,256]{3,2,1,0:T(8,128)(2,1)}, bf16[64,8,16,256]{3,2,1,0:T(8,128)(2,1)S(1)}, u32[]{:S(2)}) copy-start(bf16[64,8,16,256]{3,2,1,0:T(8,128)(2,1)S(1)} %copy.190) | copy-start | bytes 12582916
  13.6 2.8 %copy-start.6 = (bf16[128,8,8,256]{3,2,1,0:T(8,128)(2,1)S(1)}, bf16[128,8,8,256]{3,2,1,0:T(8,128)(2,1)}, u32[]{:S(2)}) copy-start(bf16[128,8,8,256]{3,2,1,0:T(8,128)(2,1)} %copy.191) | copy-start | bytes 12582916
  16.4 6.5 %copy-start.11 = (s32[48,1024]{1,0:T(8,128)S(1)}, s32[48,1024]{1,0:T(8,128)}, u32[]{:S(2)}) copy-start(s32[48,1024]{1,0:T(8,128)} %param.10) | copy-start | bytes 589828
  18.8 7.9 %collective-permute-start = (bf16[4,2,48,256]{3,2,1,0:T(8,128)(2,1)S(1)}, bf16[4,2,48,256]{3,2,1,0:T(8,128)(2,1)S(1)}, u32[]{:S(2)}, u32[]{:S(2)}) collective-permute-start(bf16[4,2,48,256]{3,2,1,0:T(8,128)(2,1)S(1)} %copy.257), channel_id=1, source_target_pairs={{0,2},{2,0},{1,3},{3,1},{4,6},{6,4},{5,7},{7,5},{8,10},{10,8},{9,1... | collective-permute-start | bytes 589832 | tf_op jit(solution)/shard_map/ppermute | solution.py:175
  27.4 11.8 %all-to-all-start = ((bf16[4,2,48,256]{3,2,1,0:T(8,128)(2,1)}), bf16[4,2,48,256]{3,2,1,0:T(8,128)(2,1)S(1)}, u32[]{:S(2)}, u32[]{:S(2)}) async-start(bf16[4,2,48,256]{3,2,1,0:T(8,128)(2,1)} %add_convert_fusion.1), calls=%async_computation | async-start | bytes 393216 | tf_op jit(solution)/shard_map/all_to_all | solution.py:132
  39.2 0.7 copy-start.10
  42.1 11.3 %all-to-all-start.1 = ((bf16[4,2,48,256]{3,2,1,0:T(8,128)(2,1)}), bf16[4,2,48,256]{3,2,1,0:T(8,128)(2,1)S(1)}, u32[]{:S(2)}, u32[]{:S(2)}) async-start(bf16[4,2,48,256]{3,2,1,0:T(8,128)(2,1)} %bitcast.202), calls=%async_computation.1 | async-start | bytes 393216 | tf_op jit(solution)/shard_map/all_to_all | solution.py:138
  64.0 2.2 %copy-start.3 = (bf16[64,8,16,256]{3,2,1,0:T(8,128)(2,1)S(1)}, bf16[64,8,16,256]{3,2,1,0:T(8,128)(2,1)}, u32[]{:S(2)}) copy-start(bf16[64,8,16,256]{3,2,1,0:T(8,128)(2,1)} %copy-done.2) | copy-start | bytes 12582916
  69.7 4.5 %copy-start.9 = (s32[48,4096]{1,0:T(8,128)S(1)}, s32[48,4096]{1,0:T(8,128)}, u32[]{:S(2)}) copy-start(s32[48,4096]{1,0:T(8,128)} %param.11) | copy-start | bytes 2359300
  70.7 21.7 %all-to-all-start.2 = ((bf16[16,2,48,256]{3,2,1,0:T(8,128)(2,1)}), bf16[16,2,48,256]{3,2,1,0:T(8,128)(2,1)S(1)}, u32[]{:S(2)}, u32[]{:S(2)}) async-start(bf16[16,2,48,256]{3,2,1,0:T(8,128)(2,1)} %copy.125), calls=%async_computation.2 | async-start | bytes 1572864 | tf_op jit(solution)/shard_map/all_to_all | solution.py:132
  92.5 0.9 copy-start.8
  118.9 2.2 %copy-start.4 = (bf16[64,8,16,256]{3,2,1,0:T(8,128)(2,1)S(1)}, bf16[64,8,16,256]{3,2,1,0:T(8,128)(2,1)}, u32[]{:S(2)}) copy-start(bf16[64,8,16,256]{3,2,1,0:T(8,128)(2,1)} %copy-done.2) | copy-start | bytes 12582916
  124.7 2.2 %copy-start.7 = (bf16[128,8,8,256]{3,2,1,0:T(8,128)(2,1)S(1)}, bf16[128,8,8,256]{3,2,1,0:T(8,128)(2,1)}, u32[]{:S(2)}) copy-start(bf16[128,8,8,256]{3,2,1,0:T(8,128)(2,1)} %copy.191) | copy-start | bytes 12582916
  129.2 5.7 %collective-permute-start.1 = (bf16[4,2,48,256]{3,2,1,0:T(8,128)(2,1)S(1)}, bf16[4,2,48,256]{3,2,1,0:T(8,128)(2,1)S(1)}, u32[]{:S(2)}, u32[]{:S(2)}) collective-permute-start(bf16[4,2,48,256]{3,2,1,0:T(8,128)(2,1)S(1)} %copy.256), channel_id=1, source_target_pairs={{0,2},{2,0},{1,3},{3,1},{4,6},{6,4},{5,7},{7,5},{8,10},{10,8},{9,1... | collective-permute-start | bytes 589832 | tf_op jit(solution)/shard_map/ppermute | solution.py:175
  167.8 2.2 %copy-start.5 = (bf16[64,8,16,256]{3,2,1,0:T(8,128)(2,1)S(1)}, bf16[64,8,16,256]{3,2,1,0:T(8,128)(2,1)}, u32[]{:S(2)}) copy-start(bf16[64,8,16,256]{3,2,1,0:T(8,128)(2,1)} %copy-done.2) | copy-start | bytes 12582916
  194.9 17.2 %all-to-all-start.7 = ((bf16[16,2,48,256]{3,2,1,0:T(8,128)(2,1)}), bf16[16,2,48,256]{3,2,1,0:T(8,128)(2,1)S(1)}, u32[]{:S(2)}, u32[]{:S(2)}) async-start(bf16[16,2,48,256]{3,2,1,0:T(8,128)(2,1)} %bitcast.191), calls=%async_computation.7 | async-start | bytes 1572864 | tf_op jit(solution)/shard_map/all_to_all | solution.py:138

commit v10 on v9

--- a/solution.py
+++ b/solution.py
@@ -61,12 +61,13 @@
 def window_kernel(matrix_ref, spectrum_ref, out_ref):
     count = spectrum_ref.shape[0]
     comps = 2 * count
-    source = [spectrum_ref[q // 2, 0, q % 2].astype(jnp.float32) for q in range(comps)]
-    for target in range(comps):
-        total = matrix_ref[target, 0].astype(jnp.float32) * source[0]
-        for q in range(1, comps):
-            total = total + matrix_ref[q * comps + target, 0].astype(jnp.float32) * source[q]
-        out_ref[target // 2, 0, target % 2] = total.astype(out_ref.dtype)
+    for block in range(spectrum_ref.shape[1]):
+        source = [spectrum_ref[q // 2, block, q % 2].astype(jnp.float32) for q in range(comps)]
+        for target in range(comps):
+            total = matrix_ref[target, block].astype(jnp.float32) * source[0]
+            for q in range(1, comps):
+                total = total + matrix_ref[q * comps + target, block].astype(jnp.float32) * source[q]
+            out_ref[target // 2, block, target % 2] = total.astype(out_ref.dtype)
 
 
 def window(spectrum, picked):
@@ -82,14 +83,15 @@
         return result.astype(jnp.bfloat16)
     _, blocks, comps, points, width = spectrum.shape
     size = picked.shape[0]
+    step = 2 if blocks % 2 == 0 else 1
     return pl.pallas_call(
         window_kernel,
-        grid=(blocks,),
+        grid=(blocks // step,),
         in_specs=[
-            pl.BlockSpec((size, 1, points, width), lambda b: (0, b, 0, 0)),
-            pl.BlockSpec((count, 1, comps, points, width), lambda b: (0, b, 0, 0, 0)),
+            pl.BlockSpec((size, step, points, width), lambda b: (0, b, 0, 0)),
+            pl.BlockSpec((count, step, comps, points, width), lambda b: (0, b, 0, 0, 0)),
         ],
-        out_specs=pl.BlockSpec((count, 1, comps, points, width), lambda b: (0, b, 0, 0, 0)),
+        out_specs=pl.BlockSpec((count, step, comps, points, width), lambda b: (0, b, 0, 0, 0)),
         out_shape=jax.ShapeDtypeStruct(spectrum.shape, jnp.bfloat16),
     )(picked, spectrum)
 

time: 217 us -> 216 us (level)
  transfers between devices with their start and end apart: 6 -> 6, of which waited for: 4 -> 4; matrix products, arithmetic and copies ran while one was open for 2% -> 2% of each run, Pallas kernels for 10% -> 11%
where the time goes in v10:
time: 216 us; the launch traced here: 214 us
  blocking collectives  70.6 us (33%)
  Pallas kernels  35.1 us (16%)
  waiting for transfers between devices  27.6 us (13%)
  matrix products  25.5 us (12%)
  starting transfers between devices  21.7 us (10%)
  local copies, waits for them, and re-layouts  21.5 us (10%)
  other arithmetic  10.5 us (5%)
    all_to_all x2, blocking collectives, exchange_back(): got = lax.all_to_all(flat, 'freq', split_axis=0, concat_axis=0, tiled=True)  31 us
    all_to_all x2, blocking collectives, exchange(): lax.all_to_all(pieces, 'freq', split_axis=0, concat_axis=0, tiled=True)  26.5 us
    pallas_call x2, Pallas kernels, window_gather(): pl.pallas_call(gather_kernel, grid=(blocks, points // rows), in_specs=[pl...  22.5 us
    all_to_all x2, waiting for transfers between devices, exchange_back(): got = lax.all_to_all(flat, 'freq', split_axis=0, concat_axis=0, tiled=True)  19.7 us
    unnamed x32, local copies, waits for them, and re-layouts  16.2 us
    all_gather x2, blocking collectives, per_device(): minus_all = lax.all_gather(minus, 'src', axis=0, tiled=True)  13.1 us
    pallas_call x4, Pallas kernels, window(): pl.pallas_call(window_kernel, grid=(blocks // step,), in_specs=[pl.BlockS...  12.6 us
    all_to_all x2, starting transfers between devices, exchange(): lax.all_to_all(pieces, 'freq', split_axis=0, concat_axis=0, tiled=True)  8.62 us
  transfers between devices with their start and end apart: 6, of which 4 were waited for; matrix products, arithmetic and copies ran while one was open for 2% of the time, Pallas kernels for 11%

profile of v10, /device:TPU:0, one launch (start us, length us, event | category | flops | bytes accessed | tf_op | source)
XLA Modules:
  0.0 213.7 jit_solution(15266346501454434389)
XLA Ops:
  0.6 0.8 copy.113
  1.5 1.5 copy.188
  3.0 0.2 copy.260
  3.3 0.6 copy-done
  3.9 3.6 %copy.191 = bf16[128,8,8,256]{3,2,1,0:T(8,128)(2,1)} copy(bf16[128,8,8,256]{3,1,2,0:T(8,128)(2,1)S(1)} %bitcast.175) | data formatting | bytes 8388608
  7.5 1.4 copy.190
  9.0 3.4 %fusion.1 = bf16[2,8,48,16,32]{2,4,1,0,3:T(8,128)(2,1)S(1)} fusion(pred[8,16,32]{2,0,1:T(8,128)(4,1)S(1)} %iota_compare_fusion, bf16[8,2,32,16,256,1]{4,3,2,1,0,5:T(8,128)(2,1)S(1)} %bitcast.177, bf16[1,16,2,48,256]{4,3,2,0,1:T(8,128)(2,1)S(1)} %maximum_bitcast_fusion.13, bf16[1,16,2,48,256]{4,3,2,0,1:T(8,128)(2,1)S(1)} %bitcast.186), kind=kOutput, calls=%fused_computation.7 | convolution fusion | flops 406585344 | bytes 6557696 | tf_op jit(solution)/shard_map/icrjt,ojcvt->oivjr/dot_general | solution.py:147
  12.4 1.3 slice_negate_fusion.7
  13.6 2.5 %maximum_bitcast_fusion = (bf16[1,2,8,48,16,32]{3,5,2,1,4,0:T(8,128)(2,1)S(1)}, bf16[1,2,8,48,16,32]{3,5,2,1,4,0:T(8,128)(2,1)S(1)}) fusion(bf16[1,8,48,16,32]{2,4,1,0,3:T(8,128)(2,1)S(1)} %get-tuple-element.11, bf16[1,8,48,16,32]{2,4,1,0,3:T(8,128)(2,1)} %get-tuple-element.13, bf16[1,8,48,16,32]{2,4,1,0,3:T(8,128)(2,1)S(1)} %get-tuple-element.12), kind=kLoop, calls=%fused_computation.34 | loop fusion | flops 786432 | bytes 2752512 | tf_op jit(solution)/shard_map/stack | solution.py:153
  16.1 0.3 copy-done.6
  16.4 2.3 %fusion.41 = bf16[8,2,48,256]{3,2,0,1:T(8,128)(2,1)S(1)} fusion(bf16[16,2,32,8,256,1]{4,3,2,1,0,5:T(8,128)(2,1)S(1)} %bitcast.183, bf16[1,2,8,48,16,32]{3,5,2,1,4,0:T(8,128)(2,1)S(1)} %get-tuple-element.21, bf16[1,2,8,48,16,32]{3,5,2,1,4,0:T(8,128)(2,1)S(1)} %get-tuple-element.20), kind=kOutput, calls=%fused_computation.53 | convolution fusion | flops 403439616 | bytes 6160384 | tf_op jit(solution)/shard_map/jcrit,ocivjr->iovt/dot_general | solution.py:154
  18.8 3.0 %collective-permute-start = (bf16[4,2,48,256]{3,2,1,0:T(8,128)(2,1)S(1)}, bf16[4,2,48,256]{3,2,1,0:T(8,128)(2,1)S(1)}, u32[]{:S(2)}, u32[]{:S(2)}) collective-permute-start(bf16[4,2,48,256]{3,2,1,0:T(8,128)(2,1)S(1)} %copy.257), channel_id=1, source_target_pairs={{0,2},{2,0},{1,3},{3,1},{4,6},{6,4},{5,7},{7,5},{8,10},{10,8},{9,1... | collective-permute-start | bytes 589832 | tf_op jit(solution)/shard_map/ppermute | solution.py:177
  22.1 0.6 reduce-window.6
  22.7 0.2 slice_reduce_fusion
  23.0 3.7 %collective-permute-done = bf16[4,2,48,256]{3,2,1,0:T(8,128)(2,1)S(1)} collective-permute-done((bf16[4,2,48,256]{3,2,1,0:T(8,128)(2,1)S(1)}, bf16[4,2,48,256]{3,2,1,0:T(8,128)(2,1)S(1)}, u32[]{:S(2)}, u32[]{:S(2)}) %collective-permute-start) | collective-permute-done | bytes 196640 | tf_op jit(solution)/shard_map/ppermute | solution.py:177
  26.7 0.7 add_convert_fusion.1
  27.4 5.1 %all-to-all-start = ((bf16[4,2,48,256]{3,2,1,0:T(8,128)(2,1)}), bf16[4,2,48,256]{3,2,1,0:T(8,128)(2,1)S(1)}, u32[]{:S(2)}, u32[]{:S(2)}) async-start(bf16[4,2,48,256]{3,2,1,0:T(8,128)(2,1)} %add_convert_fusion.1), calls=%async_computation | async-start | bytes 393216 | tf_op jit(solution)/shard_map/all_to_all | solution.py:134
  32.6 0.6 copy.262
  33.2 0.7 copy_bitcast_fusion.5.table_ref
  33.9 5.3 %shard_map.78.matrix_ref = bf16[64,1,48,256]{3,2,1,0:T(8,128)(2,1)} custom-call(bf16[64,256]{1,0:T(8,128)(2,1)} %copy_bitcast_fusion.5.table_ref, s32[1,48,256]{2,1,0:T(8,128)} %bitcast.205), custom_call_target="tpu_custom_call" | custom-call | tf_op jit(solution)/shard_map/pallas_call | solution.py:49
  39.2 0.7 copy-done.10
  39.9 2.3 %shard_map.79 = bf16[4,1,2,48,256]{4,3,2,1,0:T(8,128)(2,1)} custom-call(bf16[64,1,48,256]{3,2,1,0:T(8,128)(2,1)} %shard_map.78.matrix_ref, bf16[4,1,2,48,256]{4,3,2,1,0:T(8,128)(2,1)} %bitcast.201), custom_call_target="tpu_custom_call" | custom-call | tf_op jit(solution)/shard_map/pallas_call | solution.py:87
  42.1 5.1 %all-to-all-start.1 = ((bf16[4,2,48,256]{3,2,1,0:T(8,128)(2,1)}), bf16[4,2,48,256]{3,2,1,0:T(8,128)(2,1)S(1)}, u32[]{:S(2)}, u32[]{:S(2)}) async-start(bf16[4,2,48,256]{3,2,1,0:T(8,128)(2,1)} %bitcast.202), calls=%async_computation.1 | async-start | bytes 393216 | tf_op jit(solution)/shard_map/all_to_all | solution.py:140
  47.2 6.2 %all-to-all-done.1 = bf16[4,2,48,256]{3,2,1,0:T(8,128)(2,1)S(1)} async-done(((bf16[4,2,48,256]{3,2,1,0:T(8,128)(2,1)}), bf16[4,2,48,256]{3,2,1,0:T(8,128)(2,1)S(1)}, u32[]{:S(2)}, u32[]{:S(2)}) %all-to-all-start.1) | async-done | bytes 196640 | tf_op jit(solution)/shard_map/all_to_all | solution.py:140
  53.5 6.5 %all_gather.6 = bf16[8,2,48,256]{3,2,1,0:T(8,128)(2,1)S(1)} all-gather(bf16[4,2,48,256]{3,2,1,0:T(8,128)(2,1)S(1)} %all-to-all-done.1), channel_id=1, replica_groups=mesh['groups'=2,'freq'=4,'src'=2,'vp'=2] {'src'}, dimensions={0}, use_global_device_ids=true | all-gather | bytes 589824 | tf_op jit(solution)/shard_map/all_gather | solution.py:216
  60.0 3.7 %fusion.24 = bf16[2,8,48,16,32]{2,4,3,0,1:T(8,128)(2,1)S(1)} fusion(pred[8,16,32]{2,1,0:T(8,128)(4,1)S(1)} %copy.114, bf16[16,2,32,8,256,1]{4,3,2,1,0,5:T(8,128)(2,1)} %bitcast.181, bf16[1,8,2,48,256]{4,3,2,0,1:T(8,128)(2,1)S(1)} %maximum_bitcast_fusion.19, bf16[1,8,2,48,256]{4,3,2,0,1:T(8,128)(2,1)S(1)} %bitcast.196), kind=kOutput, calls=%fused_computation.32 | convolution fusion | flops 405012480 | bytes 5771264 | tf_op jit(solution)/shard_map/jcrit,oicvt->oivjr/dot_general | solution.py:160
  63.7 0.3 slice_negate_fusion.6
  64.0 0.9 maximum_bitcast_fusion.2
  64.9 1.3 copy-done.3
  66.2 3.5 %fusion.5 = bf16[16,2,48,256,1,1]{3,2,4,1,0,5:T(8,128)(2,1)S(1)} fusion(bf16[8,2,32,16,256,1]{4,3,2,1,0,5:T(8,128)(2,1)S(1)} %bitcast.178, bf16[1,2,8,48,16,32]{3,5,4,1,2,0:T(8,128)(2,1)S(1)} %get-tuple-element.19, bf16[1,2,8,48,16,32]{3,5,4,1,2,0:T(8,128)(2,1)S(1)} %get-tuple-element.18), kind=kOutput, calls=%fused_computation.12 | convolution fusion | flops 403439616 | bytes 6553600 | tf_op jit(solution)/shard_map/icrjt,ocivjr->jovt/dot_general | solution.py:164
  69.8 1.0 copy.125
  70.7 3.5 %all-to-all-start.2 = ((bf16[16,2,48,256]{3,2,1,0:T(8,128)(2,1)}), bf16[16,2,48,256]{3,2,1,0:T(8,128)(2,1)S(1)}, u32[]{:S(2)}, u32[]{:S(2)}) async-start(bf16[16,2,48,256]{3,2,1,0:T(8,128)(2,1)} %copy.125), calls=%async_computation.2 | async-start | bytes 1572864 | tf_op jit(solution)/shard_map/all_to_all | solution.py:134
  74.2 0.2 copy.189
  74.5 0.7 copy.261
  75.3 17.2 %shard_map.77.matrix_ref = bf16[64,4,48,256]{3,2,1,0:T(8,128)(2,1)} custom-call(bf16[64,256]{1,0:T(8,128)(2,1)} %copy_bitcast_fusion.5.table_ref, s32[4,48,256]{2,1,0:T(8,128)} %bitcast.198), custom_call_target="tpu_custom_call" | custom-call | tf_op jit(solution)/shard_map/pallas_call | solution.py:49
  92.5 0.9 copy-done.8
  93.3 4.1 %shard_map.80 = bf16[4,4,2,48,256]{4,3,2,1,0:T(8,128)(2,1)} custom-call(bf16[64,4,48,256]{3,2,1,0:T(8,128)(2,1)} %shard_map.77.matrix_ref, bf16[4,4,2,48,256]{4,3,2,1,0:T(8,128)(2,1)} %bitcast.190), custom_call_target="tpu_custom_call" | custom-call | tf_op jit(solution)/shard_map/pallas_call | solution.py:87
  97.4 20.9 %all_to_all.40 = bf16[16,2,48,256]{3,2,1,0:T(8,128)(2,1)S(1)} all-to-all(bf16[16,2,48,256]{3,2,1,0:T(8,128)(2,1)} %bitcast.193), channel_id=1, replica_groups=mesh['groups'=2,'freq'=4,'src'=2,'vp'=2] {'freq'}, dimensions={0} | all-to-all | bytes 1572864 | tf_op jit(solution)/shard_map/all_to_all | solution.py:140
  118.3 0.3 fusion.26
  118.7 1.7 copy-done.4
  120.5 3.3 %fusion = bf16[2,8,48,16,32]{2,4,1,0,3:T(8,128)(2,1)S(1)} fusion(pred[8,16,32]{2,0,1:T(8,128)(4,1)S(1)} %iota_compare_fusion, bf16[8,2,32,16,256,1]{4,3,2,1,0,5:T(8,128)(2,1)S(1)} %bitcast.179, bf16[1,16,2,48,256]{4,3,2,1,0:T(8,128)(2,1)S(1)} %maximum_bitcast_fusion.16, bf16[1,16,2,48,256]{4,3,2,1,0:T(8,128)(2,1)S(1)} %bitcast.189), kind=kOutput, calls=%fused_computation.5 | convolution fusion | flops 404226048 | bytes 6557696 | tf_op jit(solution)/shard_map/icrjt,ojcvt->oivjr/dot_general | solution.py:147
  123.8 0.3 slice_negate_fusion.5
  124.1 0.8 maximum_bitcast_fusion.4
  124.9 1.4 copy-done.7
  126.2 2.3 %fusion.46 = bf16[8,2,48,256]{3,2,0,1:T(8,128)(2,1)S(1)} fusion(bf16[16,2,32,8,256,1]{4,3,2,1,0,5:T(8,128)(2,1)S(1)} %bitcast.184, bf16[1,2,8,48,16,32]{3,5,2,1,4,0:T(8,128)(2,1)S(1)} %get-tuple-element.17, bf16[1,2,8,48,16,32]{3,5,2,1,4,0:T(8,128)(2,1)S(1)} %get-tuple-element.16), kind=kOutput, calls=%fused_computation.54 | convolution fusion | flops 403439616 | bytes 6160384 | tf_op jit(solution)/shard_map/jcrit,ocivjr->iovt/dot_general | solution.py:154
  128.6 1.5 collective-permute-start.1
  130.1 4.2 %collective-permute-done.1 = bf16[4,2,48,256]{3,2,1,0:T(8,128)(2,1)S(1)} collective-permute-done((bf16[4,2,48,256]{3,2,1,0:T(8,128)(2,1)S(1)}, bf16[4,2,48,256]{3,2,1,0:T(8,128)(2,1)S(1)}, u32[]{:S(2)}, u32[]{:S(2)}) %collective-permute-start.1) | collective-permute-done | bytes 196640 | tf_op jit(solution)/shard_map/ppermute | solution.py:177
  134.4 9.9 %all_to_all.41 = bf16[4,2,48,256]{3,2,1,0:T(8,128)(2,1)} all-to-all(bf16[4,2,48,256]{3,2,1,0:T(8,128)(2,1)S(1)} %add_convert_fusion), channel_id=1, replica_groups=mesh['groups'=2,'freq'=4,'src'=2,'vp'=2] {'freq'}, dimensions={0} | all-to-all | bytes 393216 | tf_op jit(solution)/shard_map/all_to_all | solution.py:134
  144.2 2.3 %shard_map.81 = bf16[4,1,2,48,256]{4,3,2,1,0:T(8,128)(2,1)} custom-call(bf16[64,1,48,256]{3,2,1,0:T(8,128)(2,1)} %shard_map.78.matrix_ref, bf16[4,1,2,48,256]{4,3,2,1,0:T(8,128)(2,1)} %bitcast.203), custom_call_target="tpu_custom_call" | custom-call | tf_op jit(solution)/shard_map/pallas_call | solution.py:87
  146.5 10.1 %all_to_all.42 = bf16[4,2,48,256]{3,2,1,0:T(8,128)(2,1)S(1)} all-to-all(bf16[4,2,48,256]{3,2,1,0:T(8,128)(2,1)} %bitcast.204), channel_id=1, replica_groups=mesh['groups'=2,'freq'=4,'src'=2,'vp'=2] {'freq'}, dimensions={0} | all-to-all | bytes 393216 | tf_op jit(solution)/shard_map/all_to_all | solution.py:140
  156.6 6.6 %all_gather.7 = bf16[8,2,48,256]{3,2,1,0:T(8,128)(2,1)S(1)} all-gather(bf16[4,2,48,256]{3,2,1,0:T(8,128)(2,1)S(1)} %all_to_all.42), channel_id=1, replica_groups=mesh['groups'=2,'freq'=4,'src'=2,'vp'=2] {'src'}, dimensions={0}, use_global_device_ids=true | all-gather | bytes 589824 | tf_op jit(solution)/shard_map/all_gather | solution.py:216
  163.3 3.7 %fusion.25 = bf16[2,8,48,16,32]{2,4,3,0,1:T(8,128)(2,1)S(1)} fusion(pred[8,16,32]{2,1,0:T(8,128)(4,1)S(1)} %copy.114, bf16[16,2,32,8,256,1]{4,3,2,1,0,5:T(8,128)(2,1)} %bitcast.182, bf16[1,8,2,48,256]{4,3,2,0,1:T(8,128)(2,1)S(1)} %maximum_bitcast_fusion.20, bf16[1,8,2,48,256]{4,3,2,0,1:T(8,128)(2,1)S(1)} %bitcast.195), kind=kOutput, calls=%fused_computation.33 | convolution fusion | flops 405012480 | bytes 5771264 | tf_op jit(solution)/shard_map/jcrit,oicvt->oivjr/dot_general | solution.py:160
  166.9 0.3 slice_negate_fusion.4
  167.2 0.9 maximum_bitcast_fusion.6
  168.1 1.3 copy-done.5
  169.4 3.5 %fusion.2 = bf16[16,2,48,256,1,1]{3,2,4,1,0,5:T(8,128)(2,1)S(1)} fusion(bf16[8,2,32,16,256,1]{4,3,2,1,0,5:T(8,128)(2,1)S(1)} %bitcast.180, bf16[1,2,8,48,16,32]{3,5,4,1,2,0:T(8,128)(2,1)S(1)} %get-tuple-element.15, bf16[1,2,8,48,16,32]{3,5,4,1,2,0:T(8,128)(2,1)S(1)} %get-tuple-element.14), kind=kOutput, calls=%fused_computation.8 | convolution fusion | flops 403439616 | bytes 6553600 | tf_op jit(solution)/shard_map/icrjt,ocivjr->jovt/dot_general | solution.py:164
  173.0 16.6 %all_to_all.43 = bf16[16,2,48,256]{3,2,1,0:T(8,128)(2,1)} all-to-all(bf16[16,2,48,256]{3,2,1,0:T(8,128)(2,1)S(1)} %copy.135), channel_id=1, replica_groups=mesh['groups'=2,'freq'=4,'src'=2,'vp'=2] {'freq'}, dimensions={0} | all-to-all | bytes 1572864 | tf_op jit(solution)/shard_map/all_to_all | solution.py:134
  189.7 4.1 %shard_map.82 = bf16[4,4,2,48,256]{4,3,2,1,0:T(8,128)(2,1)} custom-call(bf16[64,4,48,256]{3,2,1,0:T(8,128)(2,1)} %shard_map.77.matrix_ref, bf16[4,4,2,48,256]{4,3,2,1,0:T(8,128)(2,1)} %bitcast.192), custom_call_target="tpu_custom_call" | custom-call | tf_op jit(solution)/shard_map/pallas_call | solution.py:87
  193.7 3.5 %all-to-all-start.7 = ((bf16[16,2,48,256]{3,2,1,0:T(8,128)(2,1)}), bf16[16,2,48,256]{3,2,1,0:T(8,128)(2,1)S(1)}, u32[]{:S(2)}, u32[]{:S(2)}) async-start(bf16[16,2,48,256]{3,2,1,0:T(8,128)(2,1)} %bitcast.191), calls=%async_computation.7 | async-start | bytes 1572864 | tf_op jit(solution)/shard_map/all_to_all | solution.py:140
  197.4 0.8 broadcast_in_dim_reshape.7
  198.2 13.5 %all-to-all-done.7 = bf16[16,2,48,256]{3,2,1,0:T(8,128)(2,1)S(1)} async-done(((bf16[16,2,48,256]{3,2,1,0:T(8,128)(2,1)}), bf16[16,2,48,256]{3,2,1,0:T(8,128)(2,1)S(1)}, u32[]{:S(2)}, u32[]{:S(2)}) %all-to-all-start.7) | async-done | bytes 786464 | tf_op jit(solution)/shard_map/all_to_all | solution.py:140
  211.7 0.3 fusion.51
  212.0 0.4 copy.136
  212.4 1.2 broadcast_in_dim_reshape.6
  (50 shorter events, 1.5 us)
Async XLA Ops:
  1.5 2.4 %copy-start = (bf16[1,16,2,32,2048]{4,3,2,1,0:T(8,128)(2,1)S(1)}, bf16[1,16,2,32,2048]{4,3,2,1,0:T(8,128)(2,1)}, u32[]{:S(2)}) copy-start(bf16[1,16,2,32,2048]{4,3,2,1,0:T(8,128)(2,1)} %param.7) | copy-start | bytes 12582916
  3.9 3.6 %copy-start.1 = (bf16[1,8,2,32,4096]{4,3,2,1,0:T(8,128)(2,1)S(1)}, bf16[1,8,2,32,4096]{4,3,2,1,0:T(8,128)(2,1)}, u32[]{:S(2)}) copy-start(bf16[1,8,2,32,4096]{4,3,2,1,0:T(8,128)(2,1)} %param.8) | copy-start | bytes 12582916
  8.9 3.5 %copy-start.2 = (bf16[64,8,16,256]{3,2,1,0:T(8,128)(2,1)}, bf16[64,8,16,256]{3,2,1,0:T(8,128)(2,1)S(1)}, u32[]{:S(2)}) copy-start(bf16[64,8,16,256]{3,2,1,0:T(8,128)(2,1)S(1)} %copy.190) | copy-start | bytes 12582916
  13.6 2.8 %copy-start.6 = (bf16[128,8,8,256]{3,2,1,0:T(8,128)(2,1)S(1)}, bf16[128,8,8,256]{3,2,1,0:T(8,128)(2,1)}, u32[]{:S(2)}) copy-start(bf16[128,8,8,256]{3,2,1,0:T(8,128)(2,1)} %copy.191) | copy-start | bytes 12582916
  16.4 6.5 %copy-start.11 = (s32[48,1024]{1,0:T(8,128)S(1)}, s32[48,1024]{1,0:T(8,128)}, u32[]{:S(2)}) copy-start(s32[48,1024]{1,0:T(8,128)} %param.10) | copy-start | bytes 589828
  18.8 7.9 %collective-permute-start = (bf16[4,2,48,256]{3,2,1,0:T(8,128)(2,1)S(1)}, bf16[4,2,48,256]{3,2,1,0:T(8,128)(2,1)S(1)}, u32[]{:S(2)}, u32[]{:S(2)}) collective-permute-start(bf16[4,2,48,256]{3,2,1,0:T(8,128)(2,1)S(1)} %copy.257), channel_id=1, source_target_pairs={{0,2},{2,0},{1,3},{3,1},{4,6},{6,4},{5,7},{7,5},{8,10},{10,8},{9,1... | collective-permute-start | bytes 589832 | tf_op jit(solution)/shard_map/ppermute | solution.py:177
  27.4 11.8 %all-to-all-start = ((bf16[4,2,48,256]{3,2,1,0:T(8,128)(2,1)}), bf16[4,2,48,256]{3,2,1,0:T(8,128)(2,1)S(1)}, u32[]{:S(2)}, u32[]{:S(2)}) async-start(bf16[4,2,48,256]{3,2,1,0:T(8,128)(2,1)} %add_convert_fusion.1), calls=%async_computation | async-start | bytes 393216 | tf_op jit(solution)/shard_map/all_to_all | solution.py:134
  39.2 0.7 copy-start.10
  42.1 11.3 %all-to-all-start.1 = ((bf16[4,2,48,256]{3,2,1,0:T(8,128)(2,1)}), bf16[4,2,48,256]{3,2,1,0:T(8,128)(2,1)S(1)}, u32[]{:S(2)}, u32[]{:S(2)}) async-start(bf16[4,2,48,256]{3,2,1,0:T(8,128)(2,1)} %bitcast.202), calls=%async_computation.1 | async-start | bytes 393216 | tf_op jit(solution)/shard_map/all_to_all | solution.py:140
  64.0 2.2 %copy-start.3 = (bf16[64,8,16,256]{3,2,1,0:T(8,128)(2,1)S(1)}, bf16[64,8,16,256]{3,2,1,0:T(8,128)(2,1)}, u32[]{:S(2)}) copy-start(bf16[64,8,16,256]{3,2,1,0:T(8,128)(2,1)} %copy-done.2) | copy-start | bytes 12582916
  69.7 4.5 %copy-start.9 = (s32[48,4096]{1,0:T(8,128)S(1)}, s32[48,4096]{1,0:T(8,128)}, u32[]{:S(2)}) copy-start(s32[48,4096]{1,0:T(8,128)} %param.11) | copy-start | bytes 2359300
  70.7 21.7 %all-to-all-start.2 = ((bf16[16,2,48,256]{3,2,1,0:T(8,128)(2,1)}), bf16[16,2,48,256]{3,2,1,0:T(8,128)(2,1)S(1)}, u32[]{:S(2)}, u32[]{:S(2)}) async-start(bf16[16,2,48,256]{3,2,1,0:T(8,128)(2,1)} %copy.125), calls=%async_computation.2 | async-start | bytes 1572864 | tf_op jit(solution)/shard_map/all_to_all | solution.py:134
  92.5 0.9 copy-start.8
  118.3 2.2 %copy-start.4 = (bf16[64,8,16,256]{3,2,1,0:T(8,128)(2,1)S(1)}, bf16[64,8,16,256]{3,2,1,0:T(8,128)(2,1)}, u32[]{:S(2)}) copy-start(bf16[64,8,16,256]{3,2,1,0:T(8,128)(2,1)} %copy-done.2) | copy-start | bytes 12582916
  124.1 2.2 %copy-start.7 = (bf16[128,8,8,256]{3,2,1,0:T(8,128)(2,1)S(1)}, bf16[128,8,8,256]{3,2,1,0:T(8,128)(2,1)}, u32[]{:S(2)}) copy-start(bf16[128,8,8,256]{3,2,1,0:T(8,128)(2,1)} %copy.191) | copy-start | bytes 12582916
  128.6 5.7 %collective-permute-start.1 = (bf16[4,2,48,256]{3,2,1,0:T(8,128)(2,1)S(1)}, bf16[4,2,48,256]{3,2,1,0:T(8,128)(2,1)S(1)}, u32[]{:S(2)}, u32[]{:S(2)}) collective-permute-start(bf16[4,2,48,256]{3,2,1,0:T(8,128)(2,1)S(1)} %copy.256), channel_id=1, source_target_pairs={{0,2},{2,0},{1,3},{3,1},{4,6},{6,4},{5,7},{7,5},{8,10},{10,8},{9,1... | collective-permute-start | bytes 589832 | tf_op jit(solution)/shard_map/ppermute | solution.py:177
  167.2 2.2 %copy-start.5 = (bf16[64,8,16,256]{3,2,1,0:T(8,128)(2,1)S(1)}, bf16[64,8,16,256]{3,2,1,0:T(8,128)(2,1)}, u32[]{:S(2)}) copy-start(bf16[64,8,16,256]{3,2,1,0:T(8,128)(2,1)} %copy-done.2) | copy-start | bytes 12582916
  193.7 17.9 %all-to-all-start.7 = ((bf16[16,2,48,256]{3,2,1,0:T(8,128)(2,1)}), bf16[16,2,48,256]{3,2,1,0:T(8,128)(2,1)S(1)}, u32[]{:S(2)}, u32[]{:S(2)}) async-start(bf16[16,2,48,256]{3,2,1,0:T(8,128)(2,1)} %bitcast.191), calls=%async_computation.7 | async-start | bytes 1572864 | tf_op jit(solution)/shard_map/all_to_all | solution.py:140

commit v11 on v9

--- a/solution.py
+++ b/solution.py
@@ -149,7 +149,8 @@
 
 def expand_rows(u_tiles, z_real, z_imag):
     both = jnp.stack([jnp.stack([z_real, -z_imag]), jnp.stack([z_imag, z_real])])
-    return jnp.einsum("jcrit,ocivjr->iovt", u_tiles, both, preferred_element_type=jnp.float32)
+    product = jnp.einsum("jcrit,ocivjr->iovt", u_tiles, both, preferred_element_type=jnp.float32)
+    return product.astype(jnp.bfloat16)
 
 
 def adjoint_local(u_tiles, v_tiles, mask, minus):
@@ -172,8 +173,8 @@
     half = partial.shape[0] // 2
     mine = lax.dynamic_slice_in_dim(partial, place * half, half, 0)
     other = lax.dynamic_slice_in_dim(partial, (1 - place) * half, half, 0)
-    got = lax.ppermute(other.astype(jnp.bfloat16), "src", perm=[(0, 1), (1, 0)])
-    return (mine.astype(jnp.bfloat16).astype(jnp.float32) + got.astype(jnp.float32)).astype(jnp.bfloat16)
+    got = lax.ppermute(other, "src", perm=[(0, 1), (1, 0)])
+    return (mine.astype(jnp.float32) + got.astype(jnp.float32)).astype(jnp.bfloat16)
 
 
 def tile_major(x):

time: 217 us -> 217 us (level)
    unnamed x32 -> x30, local copies, waits for them, and re-layouts: 16.2 us -> 16.2 us
where the time goes in v11:
time: 217 us; the launch traced here: 215 us
  blocking collectives  70.5 us (32%)
  Pallas kernels  36.3 us (17%)
  waiting for transfers between devices  27.6 us (13%)
  matrix products  25.5 us (12%)
  starting transfers between devices  21.8 us (10%)
  local copies, waits for them, and re-layouts  21.5 us (10%)
  other arithmetic  10.6 us (5%)
    all_to_all x2, blocking collectives, exchange_back(): got = lax.all_to_all(flat, 'freq', split_axis=0, concat_axis=0, tiled=True)  31 us
    all_to_all x2, blocking collectives, exchange(): lax.all_to_all(pieces, 'freq', split_axis=0, concat_axis=0, tiled=True)  26.5 us
    pallas_call x2, Pallas kernels, window_gather(): pl.pallas_call(gather_kernel, grid=(blocks, points // rows), in_specs=[pl...  22.4 us
    all_to_all x2, waiting for transfers between devices, exchange_back(): got = lax.all_to_all(flat, 'freq', split_axis=0, concat_axis=0, tiled=True)  19.7 us
    unnamed x30, local copies, waits for them, and re-layouts  16.2 us
    pallas_call x4, Pallas kernels, window(): pl.pallas_call(window_kernel, grid=(blocks,), in_specs=[pl.BlockSpec((siz...  13.8 us
    all_gather x2, blocking collectives, per_device(): minus_all = lax.all_gather(minus, 'src', axis=0, tiled=True)  13.1 us
    all_to_all x2, starting transfers between devices, exchange(): lax.all_to_all(pieces, 'freq', split_axis=0, concat_axis=0, tiled=True)  8.61 us
  transfers between devices with their start and end apart: 6, of which 4 were waited for; matrix products, arithmetic and copies ran while one was open for 2% of the time, Pallas kernels for 10%

profile of v11, /device:TPU:0, one launch (start us, length us, event | category | flops | bytes accessed | tf_op | source)
XLA Modules:
  0.0 214.8 jit_solution(9580717968920226094)
XLA Ops:
  0.6 0.8 copy.111
  1.5 1.5 copy.180
  3.0 0.2 copy.254
  3.3 0.6 copy-done
  3.9 3.6 %copy.183 = bf16[128,8,8,256]{3,2,1,0:T(8,128)(2,1)} copy(bf16[128,8,8,256]{3,1,2,0:T(8,128)(2,1)S(1)} %bitcast.175) | data formatting | bytes 8388608
  7.5 1.4 copy.182
  9.0 3.4 %fusion.1 = bf16[2,8,48,16,32]{2,4,1,0,3:T(8,128)(2,1)S(1)} fusion(pred[8,16,32]{2,0,1:T(8,128)(4,1)S(1)} %iota_compare_fusion, bf16[8,2,32,16,256,1]{4,3,2,1,0,5:T(8,128)(2,1)S(1)} %bitcast.177, bf16[1,16,2,48,256]{4,3,2,0,1:T(8,128)(2,1)S(1)} %maximum_bitcast_fusion.13, bf16[1,16,2,48,256]{4,3,2,0,1:T(8,128)(2,1)S(1)} %bitcast.186), kind=kOutput, calls=%fused_computation.7 | convolution fusion | flops 406585344 | bytes 6557696 | tf_op jit(solution)/shard_map/icrjt,ojcvt->oivjr/dot_general | solution.py:145
  12.4 1.3 slice_negate_fusion.7
  13.7 2.5 %maximum_bitcast_fusion = (bf16[1,2,8,48,16,32]{3,5,2,1,4,0:T(8,128)(2,1)S(1)}, bf16[1,2,8,48,16,32]{3,5,2,1,4,0:T(8,128)(2,1)S(1)}) fusion(bf16[1,8,48,16,32]{2,4,1,0,3:T(8,128)(2,1)S(1)} %get-tuple-element.11, bf16[1,8,48,16,32]{2,4,1,0,3:T(8,128)(2,1)} %get-tuple-element.13, bf16[1,8,48,16,32]{2,4,1,0,3:T(8,128)(2,1)S(1)} %get-tuple-element.12), kind=kLoop, calls=%fused_computation.34 | loop fusion | flops 786432 | bytes 2752512 | tf_op jit(solution)/shard_map/stack | solution.py:151
  16.2 0.3 copy-done.6
  16.5 2.3 %fusion.41 = bf16[8,2,48,256]{3,2,0,1:T(8,128)(2,1)S(1)} fusion(bf16[16,2,32,8,256,1]{4,3,2,1,0,5:T(8,128)(2,1)S(1)} %bitcast.183, bf16[1,2,8,48,16,32]{3,5,2,1,4,0:T(8,128)(2,1)S(1)} %get-tuple-element.21, bf16[1,2,8,48,16,32]{3,5,2,1,4,0:T(8,128)(2,1)S(1)} %get-tuple-element.20), kind=kOutput, calls=%fused_computation.53 | convolution fusion | flops 403439616 | bytes 6160384 | tf_op jit(solution)/shard_map/jcrit,ocivjr->iovt/dot_general | solution.py:152
  18.8 3.0 %collective-permute-start = (bf16[4,2,48,256]{3,2,1,0:T(8,128)(2,1)S(1)}, bf16[4,2,48,256]{3,2,1,0:T(8,128)(2,1)S(1)}, u32[]{:S(2)}, u32[]{:S(2)}) collective-permute-start(bf16[4,2,48,256]{3,2,1,0:T(8,128)(2,1)S(1)} %constant_dynamic-slice_fusion.1), channel_id=1, source_target_pairs={{0,2},{2,0},{1,3},{3,1},{4,6},{6,4},{5,7},{7,5},{8,10},{10,8},{9,1... | collective-permute-start | bytes 589832 | tf_op jit(solution)/shard_map/ppermute | solution.py:176
  22.1 0.6 reduce-window.6
  22.7 0.2 slice_reduce_fusion
  23.0 3.7 %collective-permute-done = bf16[4,2,48,256]{3,2,1,0:T(8,128)(2,1)S(1)} collective-permute-done((bf16[4,2,48,256]{3,2,1,0:T(8,128)(2,1)S(1)}, bf16[4,2,48,256]{3,2,1,0:T(8,128)(2,1)S(1)}, u32[]{:S(2)}, u32[]{:S(2)}) %collective-permute-start) | collective-permute-done | bytes 196640 | tf_op jit(solution)/shard_map/ppermute | solution.py:176
  26.7 0.7 add_convert_fusion.1
  27.4 5.1 %all-to-all-start = ((bf16[4,2,48,256]{3,2,1,0:T(8,128)(2,1)}), bf16[4,2,48,256]{3,2,1,0:T(8,128)(2,1)S(1)}, u32[]{:S(2)}, u32[]{:S(2)}) async-start(bf16[4,2,48,256]{3,2,1,0:T(8,128)(2,1)} %add_convert_fusion.1), calls=%async_computation | async-start | bytes 393216 | tf_op jit(solution)/shard_map/all_to_all | solution.py:132
  32.6 0.6 copy.256
  33.2 0.7 copy_bitcast_fusion.5.table_ref
  33.9 5.3 %shard_map.78.matrix_ref = bf16[64,1,48,256]{3,2,1,0:T(8,128)(2,1)} custom-call(bf16[64,256]{1,0:T(8,128)(2,1)} %copy_bitcast_fusion.5.table_ref, s32[1,48,256]{2,1,0:T(8,128)} %bitcast.205), custom_call_target="tpu_custom_call" | custom-call | tf_op jit(solution)/shard_map/pallas_call | solution.py:49
  39.2 0.7 copy-done.10
  39.9 2.3 %shard_map.79 = bf16[4,1,2,48,256]{4,3,2,1,0:T(8,128)(2,1)} custom-call(bf16[64,1,48,256]{3,2,1,0:T(8,128)(2,1)} %shard_map.78.matrix_ref, bf16[4,1,2,48,256]{4,3,2,1,0:T(8,128)(2,1)} %bitcast.201), custom_call_target="tpu_custom_call" | custom-call | tf_op jit(solution)/shard_map/pallas_call | solution.py:85
  42.1 5.1 %all-to-all-start.1 = ((bf16[4,2,48,256]{3,2,1,0:T(8,128)(2,1)}), bf16[4,2,48,256]{3,2,1,0:T(8,128)(2,1)S(1)}, u32[]{:S(2)}, u32[]{:S(2)}) async-start(bf16[4,2,48,256]{3,2,1,0:T(8,128)(2,1)} %bitcast.202), calls=%async_computation.1 | async-start | bytes 393216 | tf_op jit(solution)/shard_map/all_to_all | solution.py:138
  47.2 6.2 %all-to-all-done.1 = bf16[4,2,48,256]{3,2,1,0:T(8,128)(2,1)S(1)} async-done(((bf16[4,2,48,256]{3,2,1,0:T(8,128)(2,1)}), bf16[4,2,48,256]{3,2,1,0:T(8,128)(2,1)S(1)}, u32[]{:S(2)}, u32[]{:S(2)}) %all-to-all-start.1) | async-done | bytes 196640 | tf_op jit(solution)/shard_map/all_to_all | solution.py:138
  53.4 6.5 %all_gather.6 = bf16[8,2,48,256]{3,2,1,0:T(8,128)(2,1)S(1)} all-gather(bf16[4,2,48,256]{3,2,1,0:T(8,128)(2,1)S(1)} %all-to-all-done.1), channel_id=1, replica_groups=mesh['groups'=2,'freq'=4,'src'=2,'vp'=2] {'src'}, dimensions={0}, use_global_device_ids=true | all-gather | bytes 589824 | tf_op jit(solution)/shard_map/all_gather | solution.py:215
  60.0 3.7 %fusion.24 = bf16[2,8,48,16,32]{2,4,3,0,1:T(8,128)(2,1)S(1)} fusion(pred[8,16,32]{2,1,0:T(8,128)(4,1)S(1)} %copy.112, bf16[16,2,32,8,256,1]{4,3,2,1,0,5:T(8,128)(2,1)} %bitcast.181, bf16[1,8,2,48,256]{4,3,2,0,1:T(8,128)(2,1)S(1)} %maximum_bitcast_fusion.19, bf16[1,8,2,48,256]{4,3,2,0,1:T(8,128)(2,1)S(1)} %bitcast.196), kind=kOutput, calls=%fused_computation.32 | convolution fusion | flops 405012480 | bytes 5771264 | tf_op jit(solution)/shard_map/jcrit,oicvt->oivjr/dot_general | solution.py:159
  63.7 0.3 slice_negate_fusion.6
  64.0 0.9 maximum_bitcast_fusion.2
  64.9 1.3 copy-done.3
  66.2 3.5 %fusion.5 = bf16[16,2,48,256,1,1]{3,2,4,1,0,5:T(8,128)(2,1)S(1)} fusion(bf16[8,2,32,16,256,1]{4,3,2,1,0,5:T(8,128)(2,1)S(1)} %bitcast.178, bf16[1,2,8,48,16,32]{3,5,4,1,2,0:T(8,128)(2,1)S(1)} %get-tuple-element.19, bf16[1,2,8,48,16,32]{3,5,4,1,2,0:T(8,128)(2,1)S(1)} %get-tuple-element.18), kind=kOutput, calls=%fused_computation.12 | convolution fusion | flops 403439616 | bytes 6553600 | tf_op jit(solution)/shard_map/icrjt,ocivjr->jovt/dot_general | solution.py:163
  69.7 1.0 copy.122
  70.7 3.5 %all-to-all-start.2 = ((bf16[16,2,48,256]{3,2,1,0:T(8,128)(2,1)}), bf16[16,2,48,256]{3,2,1,0:T(8,128)(2,1)S(1)}, u32[]{:S(2)}, u32[]{:S(2)}) async-start(bf16[16,2,48,256]{3,2,1,0:T(8,128)(2,1)} %copy.122), calls=%async_computation.2 | async-start | bytes 1572864 | tf_op jit(solution)/shard_map/all_to_all | solution.py:132
  74.2 0.2 copy.181
  74.5 0.7 copy.255
  75.3 17.2 %shard_map.77.matrix_ref = bf16[64,4,48,256]{3,2,1,0:T(8,128)(2,1)} custom-call(bf16[64,256]{1,0:T(8,128)(2,1)} %copy_bitcast_fusion.5.table_ref, s32[4,48,256]{2,1,0:T(8,128)} %bitcast.198), custom_call_target="tpu_custom_call" | custom-call | tf_op jit(solution)/shard_map/pallas_call | solution.py:49
  92.4 0.9 copy-done.8
  93.3 4.6 %shard_map.80 = bf16[4,4,2,48,256]{4,3,2,1,0:T(8,128)(2,1)} custom-call(bf16[64,4,48,256]{3,2,1,0:T(8,128)(2,1)} %shard_map.77.matrix_ref, bf16[4,4,2,48,256]{4,3,2,1,0:T(8,128)(2,1)} %bitcast.190), custom_call_target="tpu_custom_call" | custom-call | tf_op jit(solution)/shard_map/pallas_call | solution.py:85
  98.0 20.9 %all_to_all.40 = bf16[16,2,48,256]{3,2,1,0:T(8,128)(2,1)S(1)} all-to-all(bf16[16,2,48,256]{3,2,1,0:T(8,128)(2,1)} %bitcast.193), channel_id=1, replica_groups=mesh['groups'=2,'freq'=4,'src'=2,'vp'=2] {'freq'}, dimensions={0} | all-to-all | bytes 1572864 | tf_op jit(solution)/shard_map/all_to_all | solution.py:138
  118.8 0.3 fusion.26
  119.3 1.7 copy-done.4
  121.0 3.3 %fusion = bf16[2,8,48,16,32]{2,4,1,0,3:T(8,128)(2,1)S(1)} fusion(pred[8,16,32]{2,0,1:T(8,128)(4,1)S(1)} %iota_compare_fusion, bf16[8,2,32,16,256,1]{4,3,2,1,0,5:T(8,128)(2,1)S(1)} %bitcast.179, bf16[1,16,2,48,256]{4,3,2,1,0:T(8,128)(2,1)S(1)} %maximum_bitcast_fusion.16, bf16[1,16,2,48,256]{4,3,2,1,0:T(8,128)(2,1)S(1)} %bitcast.189), kind=kOutput, calls=%fused_computation.5 | convolution fusion | flops 404226048 | bytes 6557696 | tf_op jit(solution)/shard_map/icrjt,ojcvt->oivjr/dot_general | solution.py:145
  124.3 0.3 slice_negate_fusion.5
  124.6 0.8 maximum_bitcast_fusion.4
  125.4 1.4 copy-done.7
  126.8 2.3 %fusion.46 = bf16[8,2,48,256]{3,2,0,1:T(8,128)(2,1)S(1)} fusion(bf16[16,2,32,8,256,1]{4,3,2,1,0,5:T(8,128)(2,1)S(1)} %bitcast.184, bf16[1,2,8,48,16,32]{3,5,2,1,4,0:T(8,128)(2,1)S(1)} %get-tuple-element.17, bf16[1,2,8,48,16,32]{3,5,2,1,4,0:T(8,128)(2,1)S(1)} %get-tuple-element.16), kind=kOutput, calls=%fused_computation.54 | convolution fusion | flops 403439616 | bytes 6160384 | tf_op jit(solution)/shard_map/jcrit,ocivjr->iovt/dot_general | solution.py:152
  129.1 1.6 collective-permute-start.1
  130.7 4.2 %collective-permute-done.1 = bf16[4,2,48,256]{3,2,1,0:T(8,128)(2,1)S(1)} collective-permute-done((bf16[4,2,48,256]{3,2,1,0:T(8,128)(2,1)S(1)}, bf16[4,2,48,256]{3,2,1,0:T(8,128)(2,1)S(1)}, u32[]{:S(2)}, u32[]{:S(2)}) %collective-permute-start.1) | collective-permute-done | bytes 196640 | tf_op jit(solution)/shard_map/ppermute | solution.py:176
  134.9 9.9 %all_to_all.41 = bf16[4,2,48,256]{3,2,1,0:T(8,128)(2,1)} all-to-all(bf16[4,2,48,256]{3,2,1,0:T(8,128)(2,1)S(1)} %add_convert_fusion), channel_id=1, replica_groups=mesh['groups'=2,'freq'=4,'src'=2,'vp'=2] {'freq'}, dimensions={0} | all-to-all | bytes 393216 | tf_op jit(solution)/shard_map/all_to_all | solution.py:132
  144.8 2.3 %shard_map.81 = bf16[4,1,2,48,256]{4,3,2,1,0:T(8,128)(2,1)} custom-call(bf16[64,1,48,256]{3,2,1,0:T(8,128)(2,1)} %shard_map.78.matrix_ref, bf16[4,1,2,48,256]{4,3,2,1,0:T(8,128)(2,1)} %bitcast.203), custom_call_target="tpu_custom_call" | custom-call | tf_op jit(solution)/shard_map/pallas_call | solution.py:85
  147.0 10.1 %all_to_all.42 = bf16[4,2,48,256]{3,2,1,0:T(8,128)(2,1)S(1)} all-to-all(bf16[4,2,48,256]{3,2,1,0:T(8,128)(2,1)} %bitcast.204), channel_id=1, replica_groups=mesh['groups'=2,'freq'=4,'src'=2,'vp'=2] {'freq'}, dimensions={0} | all-to-all | bytes 393216 | tf_op jit(solution)/shard_map/all_to_all | solution.py:138
  157.2 6.6 %all_gather.7 = bf16[8,2,48,256]{3,2,1,0:T(8,128)(2,1)S(1)} all-gather(bf16[4,2,48,256]{3,2,1,0:T(8,128)(2,1)S(1)} %all_to_all.42), channel_id=1, replica_groups=mesh['groups'=2,'freq'=4,'src'=2,'vp'=2] {'src'}, dimensions={0}, use_global_device_ids=true | all-gather | bytes 589824 | tf_op jit(solution)/shard_map/all_gather | solution.py:215
  163.8 3.7 %fusion.25 = bf16[2,8,48,16,32]{2,4,3,0,1:T(8,128)(2,1)S(1)} fusion(pred[8,16,32]{2,1,0:T(8,128)(4,1)S(1)} %copy.112, bf16[16,2,32,8,256,1]{4,3,2,1,0,5:T(8,128)(2,1)} %bitcast.182, bf16[1,8,2,48,256]{4,3,2,0,1:T(8,128)(2,1)S(1)} %maximum_bitcast_fusion.20, bf16[1,8,2,48,256]{4,3,2,0,1:T(8,128)(2,1)S(1)} %bitcast.195), kind=kOutput, calls=%fused_computation.33 | convolution fusion | flops 405012480 | bytes 5771264 | tf_op jit(solution)/shard_map/jcrit,oicvt->oivjr/dot_general | solution.py:159
  167.5 0.3 slice_negate_fusion.4
  167.8 0.9 maximum_bitcast_fusion.6
  168.6 1.3 copy-done.5
  169.9 3.5 %fusion.2 = bf16[16,2,48,256,1,1]{3,2,4,1,0,5:T(8,128)(2,1)S(1)} fusion(bf16[8,2,32,16,256,1]{4,3,2,1,0,5:T(8,128)(2,1)S(1)} %bitcast.180, bf16[1,2,8,48,16,32]{3,5,4,1,2,0:T(8,128)(2,1)S(1)} %get-tuple-element.15, bf16[1,2,8,48,16,32]{3,5,4,1,2,0:T(8,128)(2,1)S(1)} %get-tuple-element.14), kind=kOutput, calls=%fused_computation.8 | convolution fusion | flops 403439616 | bytes 6553600 | tf_op jit(solution)/shard_map/icrjt,ocivjr->jovt/dot_general | solution.py:163
  173.6 16.6 %all_to_all.43 = bf16[16,2,48,256]{3,2,1,0:T(8,128)(2,1)} all-to-all(bf16[16,2,48,256]{3,2,1,0:T(8,128)(2,1)S(1)} %copy.131), channel_id=1, replica_groups=mesh['groups'=2,'freq'=4,'src'=2,'vp'=2] {'freq'}, dimensions={0} | all-to-all | bytes 1572864 | tf_op jit(solution)/shard_map/all_to_all | solution.py:132
  190.2 4.7 %shard_map.82 = bf16[4,4,2,48,256]{4,3,2,1,0:T(8,128)(2,1)} custom-call(bf16[64,4,48,256]{3,2,1,0:T(8,128)(2,1)} %shard_map.77.matrix_ref, bf16[4,4,2,48,256]{4,3,2,1,0:T(8,128)(2,1)} %bitcast.192), custom_call_target="tpu_custom_call" | custom-call | tf_op jit(solution)/shard_map/pallas_call | solution.py:85
  194.9 3.5 %all-to-all-start.7 = ((bf16[16,2,48,256]{3,2,1,0:T(8,128)(2,1)}), bf16[16,2,48,256]{3,2,1,0:T(8,128)(2,1)S(1)}, u32[]{:S(2)}, u32[]{:S(2)}) async-start(bf16[16,2,48,256]{3,2,1,0:T(8,128)(2,1)} %bitcast.191), calls=%async_computation.7 | async-start | bytes 1572864 | tf_op jit(solution)/shard_map/all_to_all | solution.py:138
  198.5 0.8 broadcast_in_dim_reshape.7
  199.3 13.5 %all-to-all-done.7 = bf16[16,2,48,256]{3,2,1,0:T(8,128)(2,1)S(1)} async-done(((bf16[16,2,48,256]{3,2,1,0:T(8,128)(2,1)}), bf16[16,2,48,256]{3,2,1,0:T(8,128)(2,1)S(1)}, u32[]{:S(2)}, u32[]{:S(2)}) %all-to-all-start.7) | async-done | bytes 786464 | tf_op jit(solution)/shard_map/all_to_all | solution.py:138
  212.8 0.3 fusion.51
  213.1 0.4 copy.132
  213.6 1.2 broadcast_in_dim_reshape.6
  (48 shorter events, 1.4 us)
Async XLA Ops:
  1.5 2.4 %copy-start = (bf16[1,16,2,32,2048]{4,3,2,1,0:T(8,128)(2,1)S(1)}, bf16[1,16,2,32,2048]{4,3,2,1,0:T(8,128)(2,1)}, u32[]{:S(2)}) copy-start(bf16[1,16,2,32,2048]{4,3,2,1,0:T(8,128)(2,1)} %param.7) | copy-start | bytes 12582916
  3.9 3.6 %copy-start.1 = (bf16[1,8,2,32,4096]{4,3,2,1,0:T(8,128)(2,1)S(1)}, bf16[1,8,2,32,4096]{4,3,2,1,0:T(8,128)(2,1)}, u32[]{:S(2)}) copy-start(bf16[1,8,2,32,4096]{4,3,2,1,0:T(8,128)(2,1)} %param.8) | copy-start | bytes 12582916
  8.9 3.5 %copy-start.2 = (bf16[64,8,16,256]{3,2,1,0:T(8,128)(2,1)}, bf16[64,8,16,256]{3,2,1,0:T(8,128)(2,1)S(1)}, u32[]{:S(2)}) copy-start(bf16[64,8,16,256]{3,2,1,0:T(8,128)(2,1)S(1)} %copy.182) | copy-start | bytes 12582916
  13.7 2.8 %copy-start.6 = (bf16[128,8,8,256]{3,2,1,0:T(8,128)(2,1)S(1)}, bf16[128,8,8,256]{3,2,1,0:T(8,128)(2,1)}, u32[]{:S(2)}) copy-start(bf16[128,8,8,256]{3,2,1,0:T(8,128)(2,1)} %copy.183) | copy-start | bytes 12582916
  16.5 6.4 %copy-start.11 = (s32[48,1024]{1,0:T(8,128)S(1)}, s32[48,1024]{1,0:T(8,128)}, u32[]{:S(2)}) copy-start(s32[48,1024]{1,0:T(8,128)} %param.10) | copy-start | bytes 589828
  18.8 7.9 %collective-permute-start = (bf16[4,2,48,256]{3,2,1,0:T(8,128)(2,1)S(1)}, bf16[4,2,48,256]{3,2,1,0:T(8,128)(2,1)S(1)}, u32[]{:S(2)}, u32[]{:S(2)}) collective-permute-start(bf16[4,2,48,256]{3,2,1,0:T(8,128)(2,1)S(1)} %constant_dynamic-slice_fusion.1), channel_id=1, source_target_pairs={{0,2},{2,0},{1,3},{3,1},{4,6},{6,4},{5,7},{7,5},{8,10},{10,8},{9,1... | collective-permute-start | bytes 589832 | tf_op jit(solution)/shard_map/ppermute | solution.py:176
  27.4 11.8 %all-to-all-start = ((bf16[4,2,48,256]{3,2,1,0:T(8,128)(2,1)}), bf16[4,2,48,256]{3,2,1,0:T(8,128)(2,1)S(1)}, u32[]{:S(2)}, u32[]{:S(2)}) async-start(bf16[4,2,48,256]{3,2,1,0:T(8,128)(2,1)} %add_convert_fusion.1), calls=%async_computation | async-start | bytes 393216 | tf_op jit(solution)/shard_map/all_to_all | solution.py:132
  39.2 0.7 copy-start.10
  42.1 11.3 %all-to-all-start.1 = ((bf16[4,2,48,256]{3,2,1,0:T(8,128)(2,1)}), bf16[4,2,48,256]{3,2,1,0:T(8,128)(2,1)S(1)}, u32[]{:S(2)}, u32[]{:S(2)}) async-start(bf16[4,2,48,256]{3,2,1,0:T(8,128)(2,1)} %bitcast.202), calls=%async_computation.1 | async-start | bytes 393216 | tf_op jit(solution)/shard_map/all_to_all | solution.py:138
  64.0 2.2 %copy-start.3 = (bf16[64,8,16,256]{3,2,1,0:T(8,128)(2,1)S(1)}, bf16[64,8,16,256]{3,2,1,0:T(8,128)(2,1)}, u32[]{:S(2)}) copy-start(bf16[64,8,16,256]{3,2,1,0:T(8,128)(2,1)} %copy-done.2) | copy-start | bytes 12582916
  69.7 4.5 %copy-start.9 = (s32[48,4096]{1,0:T(8,128)S(1)}, s32[48,4096]{1,0:T(8,128)}, u32[]{:S(2)}) copy-start(s32[48,4096]{1,0:T(8,128)} %param.11) | copy-start | bytes 2359300
  70.7 21.7 %all-to-all-start.2 = ((bf16[16,2,48,256]{3,2,1,0:T(8,128)(2,1)}), bf16[16,2,48,256]{3,2,1,0:T(8,128)(2,1)S(1)}, u32[]{:S(2)}, u32[]{:S(2)}) async-start(bf16[16,2,48,256]{3,2,1,0:T(8,128)(2,1)} %copy.122), calls=%async_computation.2 | async-start | bytes 1572864 | tf_op jit(solution)/shard_map/all_to_all | solution.py:132
  92.4 0.9 copy-start.8
  118.8 2.2 %copy-start.4 = (bf16[64,8,16,256]{3,2,1,0:T(8,128)(2,1)S(1)}, bf16[64,8,16,256]{3,2,1,0:T(8,128)(2,1)}, u32[]{:S(2)}) copy-start(bf16[64,8,16,256]{3,2,1,0:T(8,128)(2,1)} %copy-done.2) | copy-start | bytes 12582916
  124.6 2.2 %copy-start.7 = (bf16[128,8,8,256]{3,2,1,0:T(8,128)(2,1)S(1)}, bf16[128,8,8,256]{3,2,1,0:T(8,128)(2,1)}, u32[]{:S(2)}) copy-start(bf16[128,8,8,256]{3,2,1,0:T(8,128)(2,1)} %copy.183) | copy-start | bytes 12582916
  129.1 5.7 %collective-permute-start.1 = (bf16[4,2,48,256]{3,2,1,0:T(8,128)(2,1)S(1)}, bf16[4,2,48,256]{3,2,1,0:T(8,128)(2,1)S(1)}, u32[]{:S(2)}, u32[]{:S(2)}) collective-permute-start(bf16[4,2,48,256]{3,2,1,0:T(8,128)(2,1)S(1)} %constant_dynamic-slice_fusion), channel_id=1, source_target_pairs={{0,2},{2,0},{1,3},{3,1},{4,6},{6,4},{5,7},{7,5},{8,10},{10,8},{9,1... | collective-permute-start | bytes 589832 | tf_op jit(solution)/shard_map/ppermute | solution.py:176
  167.7 2.2 %copy-start.5 = (bf16[64,8,16,256]{3,2,1,0:T(8,128)(2,1)S(1)}, bf16[64,8,16,256]{3,2,1,0:T(8,128)(2,1)}, u32[]{:S(2)}) copy-start(bf16[64,8,16,256]{3,2,1,0:T(8,128)(2,1)} %copy-done.2) | copy-start | bytes 12582916
  194.9 17.9 %all-to-all-start.7 = ((bf16[16,2,48,256]{3,2,1,0:T(8,128)(2,1)}), bf16[16,2,48,256]{3,2,1,0:T(8,128)(2,1)S(1)}, u32[]{:S(2)}, u32[]{:S(2)}) async-start(bf16[16,2,48,256]{3,2,1,0:T(8,128)(2,1)} %bitcast.191), calls=%async_computation.7 | async-start | bytes 1572864 | tf_op jit(solution)/shard_map/all_to_all | solution.py:138

commit v12 on v9

--- a/solution.py
+++ b/solution.py
@@ -141,14 +141,14 @@
 
 def coefficients(v_tiles, mask, plus):
     turned = jnp.stack([plus[:, 1], -plus[:, 0]], axis=1)
-    both = jnp.stack([plus, turned])
+    both = jnp.stack([plus, turned, -turned])
     z = jnp.einsum("icrjt,ojcvt->oivjr", v_tiles, both, preferred_element_type=jnp.float32)
     z = jnp.where(mask[None], z, 0.0).astype(jnp.bfloat16)
-    return z[0], z[1]
-
-
-def expand_rows(u_tiles, z_real, z_imag):
-    both = jnp.stack([jnp.stack([z_real, -z_imag]), jnp.stack([z_imag, z_real])])
+    return z[0], z[1], z[2]
+
+
+def expand_rows(u_tiles, z_real, z_imag, z_minus):
+    both = jnp.stack([jnp.stack([z_real, z_minus]), jnp.stack([z_imag, z_real])])
     return jnp.einsum("jcrit,ocivjr->iovt", u_tiles, both, preferred_element_type=jnp.float32)
 
 
@@ -205,8 +205,8 @@
     plus = direct
     minus = None
     for sweep in range(ITERS):
-        z_real, z_imag = coefficients(v_tiles, mask, plus)
-        partial_terms = expand_rows(u_tiles, z_real, z_imag)
+        z_real, z_imag, z_minus = coefficients(v_tiles, mask, plus)
+        partial_terms = expand_rows(u_tiles, z_real, z_imag, z_minus)
         summed = reduce_src(partial_terms)
         traces = exchange(summed, parts)
         windowed = window(traces, rec_picked)

time: 217 us -> 218 us (level)
  no operation moved by 1% of the time
where the time goes in v12:
time: 218 us; the launch traced here: 215 us
  blocking collectives  70.5 us (32%)
  Pallas kernels  36.3 us (17%)
  waiting for transfers between devices  26.9 us (12%)
  matrix products  25.8 us (12%)
  local copies, waits for them, and re-layouts  23.5 us (11%)
  starting transfers between devices  21.8 us (10%)
  other arithmetic  9.26 us (4%)
    all_to_all x2, blocking collectives, exchange_back(): got = lax.all_to_all(flat, 'freq', split_axis=0, concat_axis=0, tiled=True)  31 us
    all_to_all x2, blocking collectives, exchange(): lax.all_to_all(pieces, 'freq', split_axis=0, concat_axis=0, tiled=True)  26.5 us
    pallas_call x2, Pallas kernels, window_gather(): pl.pallas_call(gather_kernel, grid=(blocks, points // rows), in_specs=[pl...  22.5 us
    all_to_all x2, waiting for transfers between devices, exchange_back(): got = lax.all_to_all(flat, 'freq', split_axis=0, concat_axis=0, tiled=True)  19 us
    unnamed x32, local copies, waits for them, and re-layouts  16.3 us
    pallas_call x4, Pallas kernels, window(): pl.pallas_call(window_kernel, grid=(blocks,), in_specs=[pl.BlockSpec((siz...  13.8 us
    all_gather x2, blocking collectives, per_device(): minus_all = lax.all_gather(minus, 'src', axis=0, tiled=True)  13.1 us
    all_to_all x2, starting transfers between devices, exchange(): lax.all_to_all(pieces, 'freq', split_axis=0, concat_axis=0, tiled=True)  8.62 us
  transfers between devices with their start and end apart: 6, of which 4 were waited for; matrix products, arithmetic and copies ran while one was open for 2% of the time, Pallas kernels for 10%

profile of v12, /device:TPU:0, one launch (start us, length us, event | category | flops | bytes accessed | tf_op | source)
XLA Modules:
  0.0 215.1 jit_solution(4492637501140982957)
XLA Ops:
  0.6 0.8 copy.129
  1.5 1.5 copy.208
  3.0 0.2 copy.288
  3.3 0.6 copy-done
  3.9 3.6 %copy.211 = bf16[128,8,8,256]{3,2,1,0:T(8,128)(2,1)} copy(bf16[128,8,8,256]{3,1,2,0:T(8,128)(2,1)S(1)} %bitcast.186) | data formatting | bytes 8388608
  7.5 1.4 copy.210
  9.0 3.5 %fusion.1 = bf16[3,8,48,16,32]{2,4,1,0,3:T(8,128)(2,1)S(1)} fusion(pred[8,16,32]{2,0,1:T(8,128)(4,1)S(1)} %iota_compare_fusion, bf16[8,2,32,16,256,1]{4,3,2,1,0,5:T(8,128)(2,1)S(1)} %bitcast.188, bf16[1,16,2,48,256]{4,3,2,0,1:T(8,128)(2,1)S(1)} %maximum_negate_fusion, bf16[1,16,2,48,256]{4,3,1,2,0:T(8,128)(2,1)S(1)} %bitcast.199, ...), kind=kOutput, calls=%fused_computation.3 | convolution fusion | flops 612630528 | bytes 7737344 | tf_op jit(solution)/shard_map/icrjt,ojcvt->oivjr/dot_general | solution.py:145
  12.5 1.5 fusion.70
  14.0 2.5 %maximum_bitcast_fusion.3 = (bf16[1,2,8,48,16,32]{3,5,2,1,4,0:T(8,128)(2,1)S(1)}, bf16[1,2,8,48,16,32]{3,5,2,1,4,0:T(8,128)(2,1)S(1)}) fusion(bf16[1,8,48,16,32]{2,4,1,0,3:T(8,128)(2,1)S(1)} %get-tuple-element.5, bf16[1,8,48,16,32]{2,4,1,0,3:T(8,128)(2,1)} %get-tuple-element.7, bf16[1,8,48,16,32]{2,4,1,0,3:T(8,128)(2,1)S(1)} %get-tuple-element.6), kind=kLoop, calls=%fused_computation.41 | loop fusion | flops 786432 | bytes 2752512 | tf_op jit(solution)/shard_map/stack | solution.py:151
  16.5 0.3 copy-done.6
  16.9 2.3 %fusion.43 = bf16[8,2,48,256]{3,2,0,1:T(8,128)(2,1)S(1)} fusion(bf16[16,2,32,8,256,1]{4,3,2,1,0,5:T(8,128)(2,1)S(1)} %bitcast.194, bf16[1,2,8,48,16,32]{3,5,2,1,4,0:T(8,128)(2,1)S(1)} %get-tuple-element.21, bf16[1,2,8,48,16,32]{3,5,2,1,4,0:T(8,128)(2,1)S(1)} %get-tuple-element.20), kind=kOutput, calls=%fused_computation.55 | convolution fusion | flops 403439616 | bytes 6160384 | tf_op jit(solution)/shard_map/jcrit,ocivjr->iovt/dot_general | solution.py:152
  19.2 3.0 %collective-permute-start = (bf16[4,2,48,256]{3,2,1,0:T(8,128)(2,1)S(1)}, bf16[4,2,48,256]{3,2,1,0:T(8,128)(2,1)S(1)}, u32[]{:S(2)}, u32[]{:S(2)}) collective-permute-start(bf16[4,2,48,256]{3,2,1,0:T(8,128)(2,1)S(1)} %copy.279), channel_id=1, source_target_pairs={{0,2},{2,0},{1,3},{3,1},{4,6},{6,4},{5,7},{7,5},{8,10},{10,8},{9,1... | collective-permute-start | bytes 589832 | tf_op jit(solution)/shard_map/ppermute | solution.py:175
  22.5 0.6 reduce-window.6
  23.1 0.2 slice_reduce_fusion
  23.4 3.7 %collective-permute-done = bf16[4,2,48,256]{3,2,1,0:T(8,128)(2,1)S(1)} collective-permute-done((bf16[4,2,48,256]{3,2,1,0:T(8,128)(2,1)S(1)}, bf16[4,2,48,256]{3,2,1,0:T(8,128)(2,1)S(1)}, u32[]{:S(2)}, u32[]{:S(2)}) %collective-permute-start) | collective-permute-done | bytes 196640 | tf_op jit(solution)/shard_map/ppermute | solution.py:175
  27.1 0.7 add_convert_fusion.1
  27.8 5.1 %all-to-all-start = ((bf16[4,2,48,256]{3,2,1,0:T(8,128)(2,1)}), bf16[4,2,48,256]{3,2,1,0:T(8,128)(2,1)S(1)}, u32[]{:S(2)}, u32[]{:S(2)}) async-start(bf16[4,2,48,256]{3,2,1,0:T(8,128)(2,1)} %add_convert_fusion.1), calls=%async_computation | async-start | bytes 393216 | tf_op jit(solution)/shard_map/all_to_all | solution.py:132
  33.0 0.6 copy.290
  33.6 0.7 copy_bitcast_fusion.5.table_ref
  34.3 5.3 %shard_map.78.matrix_ref = bf16[64,1,48,256]{3,2,1,0:T(8,128)(2,1)} custom-call(bf16[64,256]{1,0:T(8,128)(2,1)} %copy_bitcast_fusion.5.table_ref, s32[1,48,256]{2,1,0:T(8,128)} %bitcast.216), custom_call_target="tpu_custom_call" | custom-call | tf_op jit(solution)/shard_map/pallas_call | solution.py:49
  39.6 0.7 copy-done.10
  40.3 2.3 %shard_map.79 = bf16[4,1,2,48,256]{4,3,2,1,0:T(8,128)(2,1)} custom-call(bf16[64,1,48,256]{3,2,1,0:T(8,128)(2,1)} %shard_map.78.matrix_ref, bf16[4,1,2,48,256]{4,3,2,1,0:T(8,128)(2,1)} %bitcast.212), custom_call_target="tpu_custom_call" | custom-call | tf_op jit(solution)/shard_map/pallas_call | solution.py:85
  42.5 5.1 %all-to-all-start.1 = ((bf16[4,2,48,256]{3,2,1,0:T(8,128)(2,1)}), bf16[4,2,48,256]{3,2,1,0:T(8,128)(2,1)S(1)}, u32[]{:S(2)}, u32[]{:S(2)}) async-start(bf16[4,2,48,256]{3,2,1,0:T(8,128)(2,1)} %bitcast.213), calls=%async_computation.1 | async-start | bytes 393216 | tf_op jit(solution)/shard_map/all_to_all | solution.py:138
  47.6 6.2 %all-to-all-done.1 = bf16[4,2,48,256]{3,2,1,0:T(8,128)(2,1)S(1)} async-done(((bf16[4,2,48,256]{3,2,1,0:T(8,128)(2,1)}), bf16[4,2,48,256]{3,2,1,0:T(8,128)(2,1)S(1)}, u32[]{:S(2)}, u32[]{:S(2)}) %all-to-all-start.1) | async-done | bytes 196640 | tf_op jit(solution)/shard_map/all_to_all | solution.py:138
  53.9 6.5 %all_gather.6 = bf16[8,2,48,256]{3,2,1,0:T(8,128)(2,1)S(1)} all-gather(bf16[4,2,48,256]{3,2,1,0:T(8,128)(2,1)S(1)} %all-to-all-done.1), channel_id=1, replica_groups=mesh['groups'=2,'freq'=4,'src'=2,'vp'=2] {'src'}, dimensions={0}, use_global_device_ids=true | all-gather | bytes 589824 | tf_op jit(solution)/shard_map/all_gather | solution.py:214
  60.5 3.7 %fusion.29 = bf16[2,8,48,16,32]{2,4,3,0,1:T(8,128)(2,1)S(1)} fusion(pred[8,16,32]{2,1,0:T(8,128)(4,1)S(1)} %copy.130, bf16[16,2,32,8,256,1]{4,3,2,1,0,5:T(8,128)(2,1)} %bitcast.192, bf16[1,8,2,48,256]{4,3,2,0,1:T(8,128)(2,1)S(1)} %maximum_bitcast_fusion.19, bf16[1,8,2,48,256]{4,3,2,0,1:T(8,128)(2,1)S(1)} %bitcast.207), kind=kOutput, calls=%fused_computation.39 | convolution fusion | flops 405012480 | bytes 5771264 | tf_op jit(solution)/shard_map/jcrit,oicvt->oivjr/dot_general | solution.py:158
  64.1 0.3 slice_negate_fusion.5
  64.4 0.9 maximum_bitcast_fusion.5
  65.3 1.3 copy-done.3
  66.6 3.5 %fusion.5 = bf16[16,2,48,256,1,1]{3,2,4,1,0,5:T(8,128)(2,1)S(1)} fusion(bf16[8,2,32,16,256,1]{4,3,2,1,0,5:T(8,128)(2,1)S(1)} %bitcast.189, bf16[1,2,8,48,16,32]{3,5,4,1,2,0:T(8,128)(2,1)S(1)} %get-tuple-element.19, bf16[1,2,8,48,16,32]{3,5,4,1,2,0:T(8,128)(2,1)S(1)} %get-tuple-element.18), kind=kOutput, calls=%fused_computation.12 | convolution fusion | flops 403439616 | bytes 6553600 | tf_op jit(solution)/shard_map/icrjt,ocivjr->jovt/dot_general | solution.py:162
  70.2 1.0 copy.143
  71.1 3.5 %all-to-all-start.2 = ((bf16[16,2,48,256]{3,2,1,0:T(8,128)(2,1)}), bf16[16,2,48,256]{3,2,1,0:T(8,128)(2,1)S(1)}, u32[]{:S(2)}, u32[]{:S(2)}) async-start(bf16[16,2,48,256]{3,2,1,0:T(8,128)(2,1)} %copy.143), calls=%async_computation.2 | async-start | bytes 1572864 | tf_op jit(solution)/shard_map/all_to_all | solution.py:132
  74.6 0.2 copy.209
  75.0 0.7 copy.289
  75.7 17.2 %shard_map.77.matrix_ref = bf16[64,4,48,256]{3,2,1,0:T(8,128)(2,1)} custom-call(bf16[64,256]{1,0:T(8,128)(2,1)} %copy_bitcast_fusion.5.table_ref, s32[4,48,256]{2,1,0:T(8,128)} %bitcast.209), custom_call_target="tpu_custom_call" | custom-call | tf_op jit(solution)/shard_map/pallas_call | solution.py:49
  92.9 0.9 copy-done.8
  93.8 4.7 %shard_map.80 = bf16[4,4,2,48,256]{4,3,2,1,0:T(8,128)(2,1)} custom-call(bf16[64,4,48,256]{3,2,1,0:T(8,128)(2,1)} %shard_map.77.matrix_ref, bf16[4,4,2,48,256]{4,3,2,1,0:T(8,128)(2,1)} %bitcast.201), custom_call_target="tpu_custom_call" | custom-call | tf_op jit(solution)/shard_map/pallas_call | solution.py:85
  98.4 20.8 %all_to_all.40 = bf16[16,2,48,256]{3,2,1,0:T(8,128)(2,1)S(1)} all-to-all(bf16[16,2,48,256]{3,2,1,0:T(8,128)(2,1)} %bitcast.204), channel_id=1, replica_groups=mesh['groups'=2,'freq'=4,'src'=2,'vp'=2] {'freq'}, dimensions={0} | all-to-all | bytes 1572864 | tf_op jit(solution)/shard_map/all_to_all | solution.py:138
  119.3 0.3 fusion.37
  119.9 1.9 copy-done.4
  121.8 3.4 %fusion = bf16[3,8,48,16,32]{2,4,1,0,3:T(8,128)(2,1)S(1)} fusion(pred[8,16,32]{2,0,1:T(8,128)(4,1)S(1)} %iota_compare_fusion, bf16[8,2,32,16,256,1]{4,3,2,1,0,5:T(8,128)(2,1)S(1)} %bitcast.190, bf16[1,16,2,48,256]{4,3,1,2,0:T(8,128)(2,1)S(1)} %maximum_negate_fusion.1, bf16[1,16,2,48,256]{4,3,1,2,0:T(8,128)(2,1)S(1)} %maximum_bitcast_fusion.16, ...), kind=kOutput, calls=%fused_computation.1 | convolution fusion | flops 607518720 | bytes 7737344 | tf_op jit(solution)/shard_map/icrjt,ojcvt->oivjr/dot_general | solution.py:145
  125.2 0.5 fusion.69
  125.8 0.8 maximum_bitcast_fusion.7
  126.6 1.4 copy-done.7
  128.0 2.3 %fusion.48 = bf16[8,2,48,256]{3,2,0,1:T(8,128)(2,1)S(1)} fusion(bf16[16,2,32,8,256,1]{4,3,2,1,0,5:T(8,128)(2,1)S(1)} %bitcast.195, bf16[1,2,8,48,16,32]{3,5,2,1,4,0:T(8,128)(2,1)S(1)} %get-tuple-element.17, bf16[1,2,8,48,16,32]{3,5,2,1,4,0:T(8,128)(2,1)S(1)} %get-tuple-element.16), kind=kOutput, calls=%fused_computation.56 | convolution fusion | flops 403439616 | bytes 6160384 | tf_op jit(solution)/shard_map/jcrit,ocivjr->iovt/dot_general | solution.py:152
  130.3 1.6 collective-permute-start.1
  131.9 4.2 %collective-permute-done.1 = bf16[4,2,48,256]{3,2,1,0:T(8,128)(2,1)S(1)} collective-permute-done((bf16[4,2,48,256]{3,2,1,0:T(8,128)(2,1)S(1)}, bf16[4,2,48,256]{3,2,1,0:T(8,128)(2,1)S(1)}, u32[]{:S(2)}, u32[]{:S(2)}) %collective-permute-start.1) | collective-permute-done | bytes 196640 | tf_op jit(solution)/shard_map/ppermute | solution.py:175
  136.1 9.9 %all_to_all.41 = bf16[4,2,48,256]{3,2,1,0:T(8,128)(2,1)} all-to-all(bf16[4,2,48,256]{3,2,1,0:T(8,128)(2,1)S(1)} %add_convert_fusion), channel_id=1, replica_groups=mesh['groups'=2,'freq'=4,'src'=2,'vp'=2] {'freq'}, dimensions={0} | all-to-all | bytes 393216 | tf_op jit(solution)/shard_map/all_to_all | solution.py:132
  146.0 2.3 %shard_map.81 = bf16[4,1,2,48,256]{4,3,2,1,0:T(8,128)(2,1)} custom-call(bf16[64,1,48,256]{3,2,1,0:T(8,128)(2,1)} %shard_map.78.matrix_ref, bf16[4,1,2,48,256]{4,3,2,1,0:T(8,128)(2,1)} %bitcast.214), custom_call_target="tpu_custom_call" | custom-call | tf_op jit(solution)/shard_map/pallas_call | solution.py:85
  148.2 10.1 %all_to_all.42 = bf16[4,2,48,256]{3,2,1,0:T(8,128)(2,1)S(1)} all-to-all(bf16[4,2,48,256]{3,2,1,0:T(8,128)(2,1)} %bitcast.215), channel_id=1, replica_groups=mesh['groups'=2,'freq'=4,'src'=2,'vp'=2] {'freq'}, dimensions={0} | all-to-all | bytes 393216 | tf_op jit(solution)/shard_map/all_to_all | solution.py:138
  158.4 6.6 %all_gather.7 = bf16[8,2,48,256]{3,2,1,0:T(8,128)(2,1)S(1)} all-gather(bf16[4,2,48,256]{3,2,1,0:T(8,128)(2,1)S(1)} %all_to_all.42), channel_id=1, replica_groups=mesh['groups'=2,'freq'=4,'src'=2,'vp'=2] {'src'}, dimensions={0}, use_global_device_ids=true | all-gather | bytes 589824 | tf_op jit(solution)/shard_map/all_gather | solution.py:214
  165.0 3.7 %fusion.30 = bf16[2,8,48,16,32]{2,4,3,0,1:T(8,128)(2,1)S(1)} fusion(pred[8,16,32]{2,1,0:T(8,128)(4,1)S(1)} %copy.130, bf16[16,2,32,8,256,1]{4,3,2,1,0,5:T(8,128)(2,1)} %bitcast.193, bf16[1,8,2,48,256]{4,3,2,0,1:T(8,128)(2,1)S(1)} %maximum_bitcast_fusion.20, bf16[1,8,2,48,256]{4,3,2,0,1:T(8,128)(2,1)S(1)} %bitcast.206), kind=kOutput, calls=%fused_computation.40 | convolution fusion | flops 405012480 | bytes 5771264 | tf_op jit(solution)/shard_map/jcrit,oicvt->oivjr/dot_general | solution.py:158
  168.7 0.3 slice_negate_fusion.4
  169.0 0.9 maximum_bitcast_fusion.9
  169.9 1.3 copy-done.5
  171.1 3.5 %fusion.2 = bf16[16,2,48,256,1,1]{3,2,4,1,0,5:T(8,128)(2,1)S(1)} fusion(bf16[8,2,32,16,256,1]{4,3,2,1,0,5:T(8,128)(2,1)S(1)} %bitcast.191, bf16[1,2,8,48,16,32]{3,5,4,1,2,0:T(8,128)(2,1)S(1)} %get-tuple-element.15, bf16[1,2,8,48,16,32]{3,5,4,1,2,0:T(8,128)(2,1)S(1)} %get-tuple-element.14), kind=kOutput, calls=%fused_computation.8 | convolution fusion | flops 403439616 | bytes 6553600 | tf_op jit(solution)/shard_map/icrjt,ocivjr->jovt/dot_general | solution.py:162
  174.8 16.6 %all_to_all.43 = bf16[16,2,48,256]{3,2,1,0:T(8,128)(2,1)} all-to-all(bf16[16,2,48,256]{3,2,1,0:T(8,128)(2,1)S(1)} %copy.154), channel_id=1, replica_groups=mesh['groups'=2,'freq'=4,'src'=2,'vp'=2] {'freq'}, dimensions={0} | all-to-all | bytes 1572864 | tf_op jit(solution)/shard_map/all_to_all | solution.py:132
  191.4 4.7 %shard_map.82 = bf16[4,4,2,48,256]{4,3,2,1,0:T(8,128)(2,1)} custom-call(bf16[64,4,48,256]{3,2,1,0:T(8,128)(2,1)} %shard_map.77.matrix_ref, bf16[4,4,2,48,256]{4,3,2,1,0:T(8,128)(2,1)} %bitcast.203), custom_call_target="tpu_custom_call" | custom-call | tf_op jit(solution)/shard_map/pallas_call | solution.py:85
  196.1 3.5 %all-to-all-start.7 = ((bf16[16,2,48,256]{3,2,1,0:T(8,128)(2,1)}), bf16[16,2,48,256]{3,2,1,0:T(8,128)(2,1)S(1)}, u32[]{:S(2)}, u32[]{:S(2)}) async-start(bf16[16,2,48,256]{3,2,1,0:T(8,128)(2,1)} %bitcast.202), calls=%async_computation.7 | async-start | bytes 1572864 | tf_op jit(solution)/shard_map/all_to_all | solution.py:138
  199.7 0.8 broadcast_in_dim_reshape.7
  200.5 12.8 %all-to-all-done.7 = bf16[16,2,48,256]{3,2,1,0:T(8,128)(2,1)S(1)} async-done(((bf16[16,2,48,256]{3,2,1,0:T(8,128)(2,1)}), bf16[16,2,48,256]{3,2,1,0:T(8,128)(2,1)S(1)}, u32[]{:S(2)}, u32[]{:S(2)}) %all-to-all-start.7) | async-done | bytes 786464 | tf_op jit(solution)/shard_map/all_to_all | solution.py:138
  213.3 0.3 fusion.53
  213.6 0.2 copy.156
  213.9 1.2 broadcast_in_dim_reshape.6
  (51 shorter events, 1.7 us)
Async XLA Ops:
  1.5 2.4 %copy-start = (bf16[1,16,2,32,2048]{4,3,2,1,0:T(8,128)(2,1)S(1)}, bf16[1,16,2,32,2048]{4,3,2,1,0:T(8,128)(2,1)}, u32[]{:S(2)}) copy-start(bf16[1,16,2,32,2048]{4,3,2,1,0:T(8,128)(2,1)} %param.7) | copy-start | bytes 12582916
  3.9 3.6 %copy-start.1 = (bf16[1,8,2,32,4096]{4,3,2,1,0:T(8,128)(2,1)S(1)}, bf16[1,8,2,32,4096]{4,3,2,1,0:T(8,128)(2,1)}, u32[]{:S(2)}) copy-start(bf16[1,8,2,32,4096]{4,3,2,1,0:T(8,128)(2,1)} %param.8) | copy-start | bytes 12582916
  8.9 3.6 %copy-start.2 = (bf16[64,8,16,256]{3,2,1,0:T(8,128)(2,1)}, bf16[64,8,16,256]{3,2,1,0:T(8,128)(2,1)S(1)}, u32[]{:S(2)}) copy-start(bf16[64,8,16,256]{3,2,1,0:T(8,128)(2,1)S(1)} %copy.210) | copy-start | bytes 12582916
  14.0 2.8 %copy-start.6 = (bf16[128,8,8,256]{3,2,1,0:T(8,128)(2,1)S(1)}, bf16[128,8,8,256]{3,2,1,0:T(8,128)(2,1)}, u32[]{:S(2)}) copy-start(bf16[128,8,8,256]{3,2,1,0:T(8,128)(2,1)} %copy.211) | copy-start | bytes 12582916
  16.9 6.5 %copy-start.11 = (s32[48,1024]{1,0:T(8,128)S(1)}, s32[48,1024]{1,0:T(8,128)}, u32[]{:S(2)}) copy-start(s32[48,1024]{1,0:T(8,128)} %param.10) | copy-start | bytes 589828
  19.2 7.9 %collective-permute-start = (bf16[4,2,48,256]{3,2,1,0:T(8,128)(2,1)S(1)}, bf16[4,2,48,256]{3,2,1,0:T(8,128)(2,1)S(1)}, u32[]{:S(2)}, u32[]{:S(2)}) collective-permute-start(bf16[4,2,48,256]{3,2,1,0:T(8,128)(2,1)S(1)} %copy.279), channel_id=1, source_target_pairs={{0,2},{2,0},{1,3},{3,1},{4,6},{6,4},{5,7},{7,5},{8,10},{10,8},{9,1... | collective-permute-start | bytes 589832 | tf_op jit(solution)/shard_map/ppermute | solution.py:175
  27.8 11.8 %all-to-all-start = ((bf16[4,2,48,256]{3,2,1,0:T(8,128)(2,1)}), bf16[4,2,48,256]{3,2,1,0:T(8,128)(2,1)S(1)}, u32[]{:S(2)}, u32[]{:S(2)}) async-start(bf16[4,2,48,256]{3,2,1,0:T(8,128)(2,1)} %add_convert_fusion.1), calls=%async_computation | async-start | bytes 393216 | tf_op jit(solution)/shard_map/all_to_all | solution.py:132
  39.6 0.7 copy-start.10
  42.5 11.3 %all-to-all-start.1 = ((bf16[4,2,48,256]{3,2,1,0:T(8,128)(2,1)}), bf16[4,2,48,256]{3,2,1,0:T(8,128)(2,1)S(1)}, u32[]{:S(2)}, u32[]{:S(2)}) async-start(bf16[4,2,48,256]{3,2,1,0:T(8,128)(2,1)} %bitcast.213), calls=%async_computation.1 | async-start | bytes 393216 | tf_op jit(solution)/shard_map/all_to_all | solution.py:138
  64.4 2.2 %copy-start.3 = (bf16[64,8,16,256]{3,2,1,0:T(8,128)(2,1)S(1)}, bf16[64,8,16,256]{3,2,1,0:T(8,128)(2,1)}, u32[]{:S(2)}) copy-start(bf16[64,8,16,256]{3,2,1,0:T(8,128)(2,1)} %copy-done.2) | copy-start | bytes 12582916
  70.1 4.5 %copy-start.9 = (s32[48,4096]{1,0:T(8,128)S(1)}, s32[48,4096]{1,0:T(8,128)}, u32[]{:S(2)}) copy-start(s32[48,4096]{1,0:T(8,128)} %param.11) | copy-start | bytes 2359300
  71.1 21.8 %all-to-all-start.2 = ((bf16[16,2,48,256]{3,2,1,0:T(8,128)(2,1)}), bf16[16,2,48,256]{3,2,1,0:T(8,128)(2,1)S(1)}, u32[]{:S(2)}, u32[]{:S(2)}) async-start(bf16[16,2,48,256]{3,2,1,0:T(8,128)(2,1)} %copy.143), calls=%async_computation.2 | async-start | bytes 1572864 | tf_op jit(solution)/shard_map/all_to_all | solution.py:132
  92.9 0.9 copy-start.8
  119.6 2.2 %copy-start.4 = (bf16[64,8,16,256]{3,2,1,0:T(8,128)(2,1)S(1)}, bf16[64,8,16,256]{3,2,1,0:T(8,128)(2,1)}, u32[]{:S(2)}) copy-start(bf16[64,8,16,256]{3,2,1,0:T(8,128)(2,1)} %copy-done.2) | copy-start | bytes 12582916
  125.8 2.2 %copy-start.7 = (bf16[128,8,8,256]{3,2,1,0:T(8,128)(2,1)S(1)}, bf16[128,8,8,256]{3,2,1,0:T(8,128)(2,1)}, u32[]{:S(2)}) copy-start(bf16[128,8,8,256]{3,2,1,0:T(8,128)(2,1)} %copy.211) | copy-start | bytes 12582916
  130.3 5.7 %collective-permute-start.1 = (bf16[4,2,48,256]{3,2,1,0:T(8,128)(2,1)S(1)}, bf16[4,2,48,256]{3,2,1,0:T(8,128)(2,1)S(1)}, u32[]{:S(2)}, u32[]{:S(2)}) collective-permute-start(bf16[4,2,48,256]{3,2,1,0:T(8,128)(2,1)S(1)} %copy.278), channel_id=1, source_target_pairs={{0,2},{2,0},{1,3},{3,1},{4,6},{6,4},{5,7},{7,5},{8,10},{10,8},{9,1... | collective-permute-start | bytes 589832 | tf_op jit(solution)/shard_map/ppermute | solution.py:175
  169.0 2.2 %copy-start.5 = (bf16[64,8,16,256]{3,2,1,0:T(8,128)(2,1)S(1)}, bf16[64,8,16,256]{3,2,1,0:T(8,128)(2,1)}, u32[]{:S(2)}) copy-start(bf16[64,8,16,256]{3,2,1,0:T(8,128)(2,1)} %copy-done.2) | copy-start | bytes 12582916
  196.1 17.2 %all-to-all-start.7 = ((bf16[16,2,48,256]{3,2,1,0:T(8,128)(2,1)}), bf16[16,2,48,256]{3,2,1,0:T(8,128)(2,1)S(1)}, u32[]{:S(2)}, u32[]{:S(2)}) async-start(bf16[16,2,48,256]{3,2,1,0:T(8,128)(2,1)} %bitcast.202), calls=%async_computation.7 | async-start | bytes 1572864 | tf_op jit(solution)/shard_map/all_to_all | solution.py:138

commit v13 on v10

--- a/solution.py
+++ b/solution.py
@@ -151,7 +151,8 @@
 
 def expand_rows(u_tiles, z_real, z_imag):
     both = jnp.stack([jnp.stack([z_real, -z_imag]), jnp.stack([z_imag, z_real])])
-    return jnp.einsum("jcrit,ocivjr->iovt", u_tiles, both, preferred_element_type=jnp.float32)
+    product = jnp.einsum("jcrit,ocivjr->iovt", u_tiles, both, preferred_element_type=jnp.float32)
+    return product.astype(jnp.bfloat16)
 
 
 def adjoint_local(u_tiles, v_tiles, mask, minus):
@@ -174,8 +175,8 @@
     half = partial.shape[0] // 2
     mine = lax.dynamic_slice_in_dim(partial, place * half, half, 0)
     other = lax.dynamic_slice_in_dim(partial, (1 - place) * half, half, 0)
-    got = lax.ppermute(other.astype(jnp.bfloat16), "src", perm=[(0, 1), (1, 0)])
-    return (mine.astype(jnp.bfloat16).astype(jnp.float32) + got.astype(jnp.float32)).astype(jnp.bfloat16)
+    got = lax.ppermute(other, "src", perm=[(0, 1), (1, 0)])
+    return (mine.astype(jnp.float32) + got.astype(jnp.float32)).astype(jnp.bfloat16)
 
 
 def tile_major(x):

time: 216 us -> 215 us (level)
    unnamed x32 -> x30, local copies, waits for them, and re-layouts: 16.2 us -> 16.2 us
where the time goes in v13:
time: 215 us; the launch traced here: 213 us
  blocking collectives  70.5 us (33%)
  Pallas kernels  35.1 us (16%)
  waiting for transfers between devices  26.9 us (13%)
  matrix products  25.5 us (12%)
  starting transfers between devices  21.8 us (10%)
  local copies, waits for them, and re-layouts  21.5 us (10%)
  other arithmetic  10.6 us (5%)
    all_to_all x2, blocking collectives, exchange_back(): got = lax.all_to_all(flat, 'freq', split_axis=0, concat_axis=0, tiled=True)  31 us
    all_to_all x2, blocking collectives, exchange(): lax.all_to_all(pieces, 'freq', split_axis=0, concat_axis=0, tiled=True)  26.5 us
    pallas_call x2, Pallas kernels, window_gather(): pl.pallas_call(gather_kernel, grid=(blocks, points // rows), in_specs=[pl...  22.4 us
    all_to_all x2, waiting for transfers between devices, exchange_back(): got = lax.all_to_all(flat, 'freq', split_axis=0, concat_axis=0, tiled=True)  19 us
    unnamed x30, local copies, waits for them, and re-layouts  16.2 us
    all_gather x2, blocking collectives, per_device(): minus_all = lax.all_gather(minus, 'src', axis=0, tiled=True)  13.1 us
    pallas_call x4, Pallas kernels, window(): pl.pallas_call(window_kernel, grid=(blocks // step,), in_specs=[pl.BlockS...  12.6 us
    all_to_all x2, starting transfers between devices, exchange(): lax.all_to_all(pieces, 'freq', split_axis=0, concat_axis=0, tiled=True)  8.61 us
  transfers between devices with their start and end apart: 6, of which 4 were waited for; matrix products, arithmetic and copies ran while one was open for 2% of the time, Pallas kernels for 11%

profile of v13, /device:TPU:0, one launch (start us, length us, event | category | flops | bytes accessed | tf_op | source)
XLA Modules:
  0.0 212.9 jit_solution(5700005252491462364)
XLA Ops:
  0.6 0.8 copy.111
  1.5 1.5 copy.180
  3.0 0.2 copy.254
  3.3 0.6 copy-done
  3.9 3.6 %copy.183 = bf16[128,8,8,256]{3,2,1,0:T(8,128)(2,1)} copy(bf16[128,8,8,256]{3,1,2,0:T(8,128)(2,1)S(1)} %bitcast.175) | data formatting | bytes 8388608
  7.5 1.4 copy.182
  9.0 3.4 %fusion.1 = bf16[2,8,48,16,32]{2,4,1,0,3:T(8,128)(2,1)S(1)} fusion(pred[8,16,32]{2,0,1:T(8,128)(4,1)S(1)} %iota_compare_fusion, bf16[8,2,32,16,256,1]{4,3,2,1,0,5:T(8,128)(2,1)S(1)} %bitcast.177, bf16[1,16,2,48,256]{4,3,2,0,1:T(8,128)(2,1)S(1)} %maximum_bitcast_fusion.13, bf16[1,16,2,48,256]{4,3,2,0,1:T(8,128)(2,1)S(1)} %bitcast.186), kind=kOutput, calls=%fused_computation.7 | convolution fusion | flops 406585344 | bytes 6557696 | tf_op jit(solution)/shard_map/icrjt,ojcvt->oivjr/dot_general | solution.py:147
  12.4 1.3 slice_negate_fusion.7
  13.7 2.5 %maximum_bitcast_fusion = (bf16[1,2,8,48,16,32]{3,5,2,1,4,0:T(8,128)(2,1)S(1)}, bf16[1,2,8,48,16,32]{3,5,2,1,4,0:T(8,128)(2,1)S(1)}) fusion(bf16[1,8,48,16,32]{2,4,1,0,3:T(8,128)(2,1)S(1)} %get-tuple-element.11, bf16[1,8,48,16,32]{2,4,1,0,3:T(8,128)(2,1)} %get-tuple-element.13, bf16[1,8,48,16,32]{2,4,1,0,3:T(8,128)(2,1)S(1)} %get-tuple-element.12), kind=kLoop, calls=%fused_computation.34 | loop fusion | flops 786432 | bytes 2752512 | tf_op jit(solution)/shard_map/stack | solution.py:153
  16.2 0.3 copy-done.6
  16.5 2.3 %fusion.41 = bf16[8,2,48,256]{3,2,0,1:T(8,128)(2,1)S(1)} fusion(bf16[16,2,32,8,256,1]{4,3,2,1,0,5:T(8,128)(2,1)S(1)} %bitcast.183, bf16[1,2,8,48,16,32]{3,5,2,1,4,0:T(8,128)(2,1)S(1)} %get-tuple-element.21, bf16[1,2,8,48,16,32]{3,5,2,1,4,0:T(8,128)(2,1)S(1)} %get-tuple-element.20), kind=kOutput, calls=%fused_computation.53 | convolution fusion | flops 403439616 | bytes 6160384 | tf_op jit(solution)/shard_map/jcrit,ocivjr->iovt/dot_general | solution.py:154
  18.8 3.0 %collective-permute-start = (bf16[4,2,48,256]{3,2,1,0:T(8,128)(2,1)S(1)}, bf16[4,2,48,256]{3,2,1,0:T(8,128)(2,1)S(1)}, u32[]{:S(2)}, u32[]{:S(2)}) collective-permute-start(bf16[4,2,48,256]{3,2,1,0:T(8,128)(2,1)S(1)} %constant_dynamic-slice_fusion.1), channel_id=1, source_target_pairs={{0,2},{2,0},{1,3},{3,1},{4,6},{6,4},{5,7},{7,5},{8,10},{10,8},{9,1... | collective-permute-start | bytes 589832 | tf_op jit(solution)/shard_map/ppermute | solution.py:178
  22.1 0.6 reduce-window.6
  22.7 0.2 slice_reduce_fusion
  23.0 3.7 %collective-permute-done = bf16[4,2,48,256]{3,2,1,0:T(8,128)(2,1)S(1)} collective-permute-done((bf16[4,2,48,256]{3,2,1,0:T(8,128)(2,1)S(1)}, bf16[4,2,48,256]{3,2,1,0:T(8,128)(2,1)S(1)}, u32[]{:S(2)}, u32[]{:S(2)}) %collective-permute-start) | collective-permute-done | bytes 196640 | tf_op jit(solution)/shard_map/ppermute | solution.py:178
  26.7 0.7 add_convert_fusion.1
  27.4 5.1 %all-to-all-start = ((bf16[4,2,48,256]{3,2,1,0:T(8,128)(2,1)}), bf16[4,2,48,256]{3,2,1,0:T(8,128)(2,1)S(1)}, u32[]{:S(2)}, u32[]{:S(2)}) async-start(bf16[4,2,48,256]{3,2,1,0:T(8,128)(2,1)} %add_convert_fusion.1), calls=%async_computation | async-start | bytes 393216 | tf_op jit(solution)/shard_map/all_to_all | solution.py:134
  32.6 0.6 copy.256
  33.2 0.7 copy_bitcast_fusion.5.table_ref
  33.9 5.3 %shard_map.78.matrix_ref = bf16[64,1,48,256]{3,2,1,0:T(8,128)(2,1)} custom-call(bf16[64,256]{1,0:T(8,128)(2,1)} %copy_bitcast_fusion.5.table_ref, s32[1,48,256]{2,1,0:T(8,128)} %bitcast.205), custom_call_target="tpu_custom_call" | custom-call | tf_op jit(solution)/shard_map/pallas_call | solution.py:49
  39.2 0.7 copy-done.10
  39.9 2.3 %shard_map.79 = bf16[4,1,2,48,256]{4,3,2,1,0:T(8,128)(2,1)} custom-call(bf16[64,1,48,256]{3,2,1,0:T(8,128)(2,1)} %shard_map.78.matrix_ref, bf16[4,1,2,48,256]{4,3,2,1,0:T(8,128)(2,1)} %bitcast.201), custom_call_target="tpu_custom_call" | custom-call | tf_op jit(solution)/shard_map/pallas_call | solution.py:87
  42.1 5.1 %all-to-all-start.1 = ((bf16[4,2,48,256]{3,2,1,0:T(8,128)(2,1)}), bf16[4,2,48,256]{3,2,1,0:T(8,128)(2,1)S(1)}, u32[]{:S(2)}, u32[]{:S(2)}) async-start(bf16[4,2,48,256]{3,2,1,0:T(8,128)(2,1)} %bitcast.202), calls=%async_computation.1 | async-start | bytes 393216 | tf_op jit(solution)/shard_map/all_to_all | solution.py:140
  47.2 6.2 %all-to-all-done.1 = bf16[4,2,48,256]{3,2,1,0:T(8,128)(2,1)S(1)} async-done(((bf16[4,2,48,256]{3,2,1,0:T(8,128)(2,1)}), bf16[4,2,48,256]{3,2,1,0:T(8,128)(2,1)S(1)}, u32[]{:S(2)}, u32[]{:S(2)}) %all-to-all-start.1) | async-done | bytes 196640 | tf_op jit(solution)/shard_map/all_to_all | solution.py:140
  53.4 6.5 %all_gather.6 = bf16[8,2,48,256]{3,2,1,0:T(8,128)(2,1)S(1)} all-gather(bf16[4,2,48,256]{3,2,1,0:T(8,128)(2,1)S(1)} %all-to-all-done.1), channel_id=1, replica_groups=mesh['groups'=2,'freq'=4,'src'=2,'vp'=2] {'src'}, dimensions={0}, use_global_device_ids=true | all-gather | bytes 589824 | tf_op jit(solution)/shard_map/all_gather | solution.py:217
  60.0 3.7 %fusion.24 = bf16[2,8,48,16,32]{2,4,3,0,1:T(8,128)(2,1)S(1)} fusion(pred[8,16,32]{2,1,0:T(8,128)(4,1)S(1)} %copy.112, bf16[16,2,32,8,256,1]{4,3,2,1,0,5:T(8,128)(2,1)} %bitcast.181, bf16[1,8,2,48,256]{4,3,2,0,1:T(8,128)(2,1)S(1)} %maximum_bitcast_fusion.19, bf16[1,8,2,48,256]{4,3,2,0,1:T(8,128)(2,1)S(1)} %bitcast.196), kind=kOutput, calls=%fused_computation.32 | convolution fusion | flops 405012480 | bytes 5771264 | tf_op jit(solution)/shard_map/jcrit,oicvt->oivjr/dot_general | solution.py:161
  63.7 0.3 slice_negate_fusion.6
  64.0 0.9 maximum_bitcast_fusion.2
  64.9 1.3 copy-done.3
  66.2 3.5 %fusion.5 = bf16[16,2,48,256,1,1]{3,2,4,1,0,5:T(8,128)(2,1)S(1)} fusion(bf16[8,2,32,16,256,1]{4,3,2,1,0,5:T(8,128)(2,1)S(1)} %bitcast.178, bf16[1,2,8,48,16,32]{3,5,4,1,2,0:T(8,128)(2,1)S(1)} %get-tuple-element.19, bf16[1,2,8,48,16,32]{3,5,4,1,2,0:T(8,128)(2,1)S(1)} %get-tuple-element.18), kind=kOutput, calls=%fused_computation.12 | convolution fusion | flops 403439616 | bytes 6553600 | tf_op jit(solution)/shard_map/icrjt,ocivjr->jovt/dot_general | solution.py:165
  69.7 1.0 copy.122
  70.7 3.5 %all-to-all-start.2 = ((bf16[16,2,48,256]{3,2,1,0:T(8,128)(2,1)}), bf16[16,2,48,256]{3,2,1,0:T(8,128)(2,1)S(1)}, u32[]{:S(2)}, u32[]{:S(2)}) async-start(bf16[16,2,48,256]{3,2,1,0:T(8,128)(2,1)} %copy.122), calls=%async_computation.2 | async-start | bytes 1572864 | tf_op jit(solution)/shard_map/all_to_all | solution.py:134
  74.2 0.2 copy.181
  74.5 0.7 copy.255
  75.3 17.2 %shard_map.77.matrix_ref = bf16[64,4,48,256]{3,2,1,0:T(8,128)(2,1)} custom-call(bf16[64,256]{1,0:T(8,128)(2,1)} %copy_bitcast_fusion.5.table_ref, s32[4,48,256]{2,1,0:T(8,128)} %bitcast.198), custom_call_target="tpu_custom_call" | custom-call | tf_op jit(solution)/shard_map/pallas_call | solution.py:49
  92.4 0.9 copy-done.8
  93.3 4.0 %shard_map.80 = bf16[4,4,2,48,256]{4,3,2,1,0:T(8,128)(2,1)} custom-call(bf16[64,4,48,256]{3,2,1,0:T(8,128)(2,1)} %shard_map.77.matrix_ref, bf16[4,4,2,48,256]{4,3,2,1,0:T(8,128)(2,1)} %bitcast.190), custom_call_target="tpu_custom_call" | custom-call | tf_op jit(solution)/shard_map/pallas_call | solution.py:87
  97.4 20.9 %all_to_all.40 = bf16[16,2,48,256]{3,2,1,0:T(8,128)(2,1)S(1)} all-to-all(bf16[16,2,48,256]{3,2,1,0:T(8,128)(2,1)} %bitcast.193), channel_id=1, replica_groups=mesh['groups'=2,'freq'=4,'src'=2,'vp'=2] {'freq'}, dimensions={0} | all-to-all | bytes 1572864 | tf_op jit(solution)/shard_map/all_to_all | solution.py:140
  118.2 0.3 fusion.26
  118.7 1.7 copy-done.4
  120.4 3.3 %fusion = bf16[2,8,48,16,32]{2,4,1,0,3:T(8,128)(2,1)S(1)} fusion(pred[8,16,32]{2,0,1:T(8,128)(4,1)S(1)} %iota_compare_fusion, bf16[8,2,32,16,256,1]{4,3,2,1,0,5:T(8,128)(2,1)S(1)} %bitcast.179, bf16[1,16,2,48,256]{4,3,2,1,0:T(8,128)(2,1)S(1)} %maximum_bitcast_fusion.16, bf16[1,16,2,48,256]{4,3,2,1,0:T(8,128)(2,1)S(1)} %bitcast.189), kind=kOutput, calls=%fused_computation.5 | convolution fusion | flops 404226048 | bytes 6557696 | tf_op jit(solution)/shard_map/icrjt,ojcvt->oivjr/dot_general | solution.py:147
  123.7 0.3 slice_negate_fusion.5
  124.0 0.8 maximum_bitcast_fusion.4
  124.8 1.4 copy-done.7
  126.2 2.3 %fusion.46 = bf16[8,2,48,256]{3,2,0,1:T(8,128)(2,1)S(1)} fusion(bf16[16,2,32,8,256,1]{4,3,2,1,0,5:T(8,128)(2,1)S(1)} %bitcast.184, bf16[1,2,8,48,16,32]{3,5,2,1,4,0:T(8,128)(2,1)S(1)} %get-tuple-element.17, bf16[1,2,8,48,16,32]{3,5,2,1,4,0:T(8,128)(2,1)S(1)} %get-tuple-element.16), kind=kOutput, calls=%fused_computation.54 | convolution fusion | flops 403439616 | bytes 6160384 | tf_op jit(solution)/shard_map/jcrit,ocivjr->iovt/dot_general | solution.py:154
  128.5 1.6 collective-permute-start.1
  130.1 4.2 %collective-permute-done.1 = bf16[4,2,48,256]{3,2,1,0:T(8,128)(2,1)S(1)} collective-permute-done((bf16[4,2,48,256]{3,2,1,0:T(8,128)(2,1)S(1)}, bf16[4,2,48,256]{3,2,1,0:T(8,128)(2,1)S(1)}, u32[]{:S(2)}, u32[]{:S(2)}) %collective-permute-start.1) | collective-permute-done | bytes 196640 | tf_op jit(solution)/shard_map/ppermute | solution.py:178
  134.3 9.9 %all_to_all.41 = bf16[4,2,48,256]{3,2,1,0:T(8,128)(2,1)} all-to-all(bf16[4,2,48,256]{3,2,1,0:T(8,128)(2,1)S(1)} %add_convert_fusion), channel_id=1, replica_groups=mesh['groups'=2,'freq'=4,'src'=2,'vp'=2] {'freq'}, dimensions={0} | all-to-all | bytes 393216 | tf_op jit(solution)/shard_map/all_to_all | solution.py:134
  144.2 2.3 %shard_map.81 = bf16[4,1,2,48,256]{4,3,2,1,0:T(8,128)(2,1)} custom-call(bf16[64,1,48,256]{3,2,1,0:T(8,128)(2,1)} %shard_map.78.matrix_ref, bf16[4,1,2,48,256]{4,3,2,1,0:T(8,128)(2,1)} %bitcast.203), custom_call_target="tpu_custom_call" | custom-call | tf_op jit(solution)/shard_map/pallas_call | solution.py:87
  146.4 10.1 %all_to_all.42 = bf16[4,2,48,256]{3,2,1,0:T(8,128)(2,1)S(1)} all-to-all(bf16[4,2,48,256]{3,2,1,0:T(8,128)(2,1)} %bitcast.204), channel_id=1, replica_groups=mesh['groups'=2,'freq'=4,'src'=2,'vp'=2] {'freq'}, dimensions={0} | all-to-all | bytes 393216 | tf_op jit(solution)/shard_map/all_to_all | solution.py:140
  156.6 6.6 %all_gather.7 = bf16[8,2,48,256]{3,2,1,0:T(8,128)(2,1)S(1)} all-gather(bf16[4,2,48,256]{3,2,1,0:T(8,128)(2,1)S(1)} %all_to_all.42), channel_id=1, replica_groups=mesh['groups'=2,'freq'=4,'src'=2,'vp'=2] {'src'}, dimensions={0}, use_global_device_ids=true | all-gather | bytes 589824 | tf_op jit(solution)/shard_map/all_gather | solution.py:217
  163.2 3.7 %fusion.25 = bf16[2,8,48,16,32]{2,4,3,0,1:T(8,128)(2,1)S(1)} fusion(pred[8,16,32]{2,1,0:T(8,128)(4,1)S(1)} %copy.112, bf16[16,2,32,8,256,1]{4,3,2,1,0,5:T(8,128)(2,1)} %bitcast.182, bf16[1,8,2,48,256]{4,3,2,0,1:T(8,128)(2,1)S(1)} %maximum_bitcast_fusion.20, bf16[1,8,2,48,256]{4,3,2,0,1:T(8,128)(2,1)S(1)} %bitcast.195), kind=kOutput, calls=%fused_computation.33 | convolution fusion | flops 405012480 | bytes 5771264 | tf_op jit(solution)/shard_map/jcrit,oicvt->oivjr/dot_general | solution.py:161
  166.9 0.3 slice_negate_fusion.4
  167.2 0.9 maximum_bitcast_fusion.6
  168.0 1.3 copy-done.5
  169.3 3.5 %fusion.2 = bf16[16,2,48,256,1,1]{3,2,4,1,0,5:T(8,128)(2,1)S(1)} fusion(bf16[8,2,32,16,256,1]{4,3,2,1,0,5:T(8,128)(2,1)S(1)} %bitcast.180, bf16[1,2,8,48,16,32]{3,5,4,1,2,0:T(8,128)(2,1)S(1)} %get-tuple-element.15, bf16[1,2,8,48,16,32]{3,5,4,1,2,0:T(8,128)(2,1)S(1)} %get-tuple-element.14), kind=kOutput, calls=%fused_computation.8 | convolution fusion | flops 403439616 | bytes 6553600 | tf_op jit(solution)/shard_map/icrjt,ocivjr->jovt/dot_general | solution.py:165
  173.0 16.6 %all_to_all.43 = bf16[16,2,48,256]{3,2,1,0:T(8,128)(2,1)} all-to-all(bf16[16,2,48,256]{3,2,1,0:T(8,128)(2,1)S(1)} %copy.131), channel_id=1, replica_groups=mesh['groups'=2,'freq'=4,'src'=2,'vp'=2] {'freq'}, dimensions={0} | all-to-all | bytes 1572864 | tf_op jit(solution)/shard_map/all_to_all | solution.py:134
  189.6 4.1 %shard_map.82 = bf16[4,4,2,48,256]{4,3,2,1,0:T(8,128)(2,1)} custom-call(bf16[64,4,48,256]{3,2,1,0:T(8,128)(2,1)} %shard_map.77.matrix_ref, bf16[4,4,2,48,256]{4,3,2,1,0:T(8,128)(2,1)} %bitcast.192), custom_call_target="tpu_custom_call" | custom-call | tf_op jit(solution)/shard_map/pallas_call | solution.py:87
  193.7 3.5 %all-to-all-start.7 = ((bf16[16,2,48,256]{3,2,1,0:T(8,128)(2,1)}), bf16[16,2,48,256]{3,2,1,0:T(8,128)(2,1)S(1)}, u32[]{:S(2)}, u32[]{:S(2)}) async-start(bf16[16,2,48,256]{3,2,1,0:T(8,128)(2,1)} %bitcast.191), calls=%async_computation.7 | async-start | bytes 1572864 | tf_op jit(solution)/shard_map/all_to_all | solution.py:140
  197.3 0.8 broadcast_in_dim_reshape.7
  198.1 12.8 %all-to-all-done.7 = bf16[16,2,48,256]{3,2,1,0:T(8,128)(2,1)S(1)} async-done(((bf16[16,2,48,256]{3,2,1,0:T(8,128)(2,1)}), bf16[16,2,48,256]{3,2,1,0:T(8,128)(2,1)S(1)}, u32[]{:S(2)}, u32[]{:S(2)}) %all-to-all-start.7) | async-done | bytes 786464 | tf_op jit(solution)/shard_map/all_to_all | solution.py:140
  210.9 0.3 fusion.51
  211.2 0.4 copy.132
  211.7 1.2 broadcast_in_dim_reshape.6
  (48 shorter events, 1.4 us)
Async XLA Ops:
  1.5 2.4 %copy-start = (bf16[1,16,2,32,2048]{4,3,2,1,0:T(8,128)(2,1)S(1)}, bf16[1,16,2,32,2048]{4,3,2,1,0:T(8,128)(2,1)}, u32[]{:S(2)}) copy-start(bf16[1,16,2,32,2048]{4,3,2,1,0:T(8,128)(2,1)} %param.7) | copy-start | bytes 12582916
  3.9 3.6 %copy-start.1 = (bf16[1,8,2,32,4096]{4,3,2,1,0:T(8,128)(2,1)S(1)}, bf16[1,8,2,32,4096]{4,3,2,1,0:T(8,128)(2,1)}, u32[]{:S(2)}) copy-start(bf16[1,8,2,32,4096]{4,3,2,1,0:T(8,128)(2,1)} %param.8) | copy-start | bytes 12582916
  8.9 3.5 %copy-start.2 = (bf16[64,8,16,256]{3,2,1,0:T(8,128)(2,1)}, bf16[64,8,16,256]{3,2,1,0:T(8,128)(2,1)S(1)}, u32[]{:S(2)}) copy-start(bf16[64,8,16,256]{3,2,1,0:T(8,128)(2,1)S(1)} %copy.182) | copy-start | bytes 12582916
  13.7 2.8 %copy-start.6 = (bf16[128,8,8,256]{3,2,1,0:T(8,128)(2,1)S(1)}, bf16[128,8,8,256]{3,2,1,0:T(8,128)(2,1)}, u32[]{:S(2)}) copy-start(bf16[128,8,8,256]{3,2,1,0:T(8,128)(2,1)} %copy.183) | copy-start | bytes 12582916
  16.5 6.4 %copy-start.11 = (s32[48,1024]{1,0:T(8,128)S(1)}, s32[48,1024]{1,0:T(8,128)}, u32[]{:S(2)}) copy-start(s32[48,1024]{1,0:T(8,128)} %param.10) | copy-start | bytes 589828
  18.8 7.9 %collective-permute-start = (bf16[4,2,48,256]{3,2,1,0:T(8,128)(2,1)S(1)}, bf16[4,2,48,256]{3,2,1,0:T(8,128)(2,1)S(1)}, u32[]{:S(2)}, u32[]{:S(2)}) collective-permute-start(bf16[4,2,48,256]{3,2,1,0:T(8,128)(2,1)S(1)} %constant_dynamic-slice_fusion.1), channel_id=1, source_target_pairs={{0,2},{2,0},{1,3},{3,1},{4,6},{6,4},{5,7},{7,5},{8,10},{10,8},{9,1... | collective-permute-start | bytes 589832 | tf_op jit(solution)/shard_map/ppermute | solution.py:178
  27.4 11.8 %all-to-all-start = ((bf16[4,2,48,256]{3,2,1,0:T(8,128)(2,1)}), bf16[4,2,48,256]{3,2,1,0:T(8,128)(2,1)S(1)}, u32[]{:S(2)}, u32[]{:S(2)}) async-start(bf16[4,2,48,256]{3,2,1,0:T(8,128)(2,1)} %add_convert_fusion.1), calls=%async_computation | async-start | bytes 393216 | tf_op jit(solution)/shard_map/all_to_all | solution.py:134
  39.2 0.7 copy-start.10
  42.1 11.3 %all-to-all-start.1 = ((bf16[4,2,48,256]{3,2,1,0:T(8,128)(2,1)}), bf16[4,2,48,256]{3,2,1,0:T(8,128)(2,1)S(1)}, u32[]{:S(2)}, u32[]{:S(2)}) async-start(bf16[4,2,48,256]{3,2,1,0:T(8,128)(2,1)} %bitcast.202), calls=%async_computation.1 | async-start | bytes 393216 | tf_op jit(solution)/shard_map/all_to_all | solution.py:140
  64.0 2.2 %copy-start.3 = (bf16[64,8,16,256]{3,2,1,0:T(8,128)(2,1)S(1)}, bf16[64,8,16,256]{3,2,1,0:T(8,128)(2,1)}, u32[]{:S(2)}) copy-start(bf16[64,8,16,256]{3,2,1,0:T(8,128)(2,1)} %copy-done.2) | copy-start | bytes 12582916
  69.7 4.5 %copy-start.9 = (s32[48,4096]{1,0:T(8,128)S(1)}, s32[48,4096]{1,0:T(8,128)}, u32[]{:S(2)}) copy-start(s32[48,4096]{1,0:T(8,128)} %param.11) | copy-start | bytes 2359300
  70.7 21.7 %all-to-all-start.2 = ((bf16[16,2,48,256]{3,2,1,0:T(8,128)(2,1)}), bf16[16,2,48,256]{3,2,1,0:T(8,128)(2,1)S(1)}, u32[]{:S(2)}, u32[]{:S(2)}) async-start(bf16[16,2,48,256]{3,2,1,0:T(8,128)(2,1)} %copy.122), calls=%async_computation.2 | async-start | bytes 1572864 | tf_op jit(solution)/shard_map/all_to_all | solution.py:134
  92.4 0.9 copy-start.8
  118.2 2.2 %copy-start.4 = (bf16[64,8,16,256]{3,2,1,0:T(8,128)(2,1)S(1)}, bf16[64,8,16,256]{3,2,1,0:T(8,128)(2,1)}, u32[]{:S(2)}) copy-start(bf16[64,8,16,256]{3,2,1,0:T(8,128)(2,1)} %copy-done.2) | copy-start | bytes 12582916
  124.0 2.2 %copy-start.7 = (bf16[128,8,8,256]{3,2,1,0:T(8,128)(2,1)S(1)}, bf16[128,8,8,256]{3,2,1,0:T(8,128)(2,1)}, u32[]{:S(2)}) copy-start(bf16[128,8,8,256]{3,2,1,0:T(8,128)(2,1)} %copy.183) | copy-start | bytes 12582916
  128.5 5.7 %collective-permute-start.1 = (bf16[4,2,48,256]{3,2,1,0:T(8,128)(2,1)S(1)}, bf16[4,2,48,256]{3,2,1,0:T(8,128)(2,1)S(1)}, u32[]{:S(2)}, u32[]{:S(2)}) collective-permute-start(bf16[4,2,48,256]{3,2,1,0:T(8,128)(2,1)S(1)} %constant_dynamic-slice_fusion), channel_id=1, source_target_pairs={{0,2},{2,0},{1,3},{3,1},{4,6},{6,4},{5,7},{7,5},{8,10},{10,8},{9,1... | collective-permute-start | bytes 589832 | tf_op jit(solution)/shard_map/ppermute | solution.py:178
  167.1 2.2 %copy-start.5 = (bf16[64,8,16,256]{3,2,1,0:T(8,128)(2,1)S(1)}, bf16[64,8,16,256]{3,2,1,0:T(8,128)(2,1)}, u32[]{:S(2)}) copy-start(bf16[64,8,16,256]{3,2,1,0:T(8,128)(2,1)} %copy-done.2) | copy-start | bytes 12582916
  193.7 17.2 %all-to-all-start.7 = ((bf16[16,2,48,256]{3,2,1,0:T(8,128)(2,1)}), bf16[16,2,48,256]{3,2,1,0:T(8,128)(2,1)S(1)}, u32[]{:S(2)}, u32[]{:S(2)}) async-start(bf16[16,2,48,256]{3,2,1,0:T(8,128)(2,1)} %bitcast.191), calls=%async_computation.7 | async-start | bytes 1572864 | tf_op jit(solution)/shard_map/all_to_all | solution.py:140

commit v14 on v13

--- a/solution.py
+++ b/solution.py
@@ -45,7 +45,7 @@
     table = jnp.cumsum(terms.reshape(NT, size), axis=0)
     stacked = table.astype(jnp.bfloat16).T
     blocks, points, width = onset.shape
-    rows = 8
+    rows = 16 if points % 16 == 0 else 8
     return pl.pallas_call(
         gather_kernel,
         grid=(blocks, points // rows),

time: 215 us -> 214 us (level)
  waiting for transfers between devices: 26.9 us -> 30.8 us
  Pallas kernels: 35.1 us -> 31.4 us
    pallas_call x2, Pallas kernels: 22.4 us -> 18.8 us  [window_gather(): pl.pallas_call(gather_kernel, grid=(blocks, points // rows), in_specs=[pl...]
    all_to_all x2, waiting for transfers between devices: 19 us -> 21.4 us  [exchange_back(): got = lax.all_to_all(flat, 'freq', split_axis=0, concat_axis=0, tiled=True)]
  transfers between devices with their start and end apart: 6 -> 6, of which waited for: 4 -> 6; matrix products, arithmetic and copies ran while one was open for 2% -> 2% of each run, Pallas kernels for 11% -> 9%
where the time goes in v14:
time: 214 us; the launch traced here: 213 us
  blocking collectives  71 us (33%)
  Pallas kernels  31.4 us (15%)
  waiting for transfers between devices  30.8 us (14%)
  matrix products  25.5 us (12%)
  local copies, waits for them, and re-layouts  21.5 us (10%)
  starting transfers between devices  21.4 us (10%)
  other arithmetic  10.6 us (5%)
    all_to_all x2, blocking collectives, exchange_back(): got = lax.all_to_all(flat, 'freq', split_axis=0, concat_axis=0, tiled=True)  30.8 us
    all_to_all x2, blocking collectives, exchange(): lax.all_to_all(pieces, 'freq', split_axis=0, concat_axis=0, tiled=True)  27 us
    all_to_all x2, waiting for transfers between devices, exchange_back(): got = lax.all_to_all(flat, 'freq', split_axis=0, concat_axis=0, tiled=True)  21.4 us
    pallas_call x2, Pallas kernels, window_gather(): pl.pallas_call(gather_kernel, grid=(blocks, points // rows), in_specs=[pl...  18.8 us
    unnamed x30, local copies, waits for them, and re-layouts  16.2 us
    all_gather x2, blocking collectives, per_device(): minus_all = lax.all_gather(minus, 'src', axis=0, tiled=True)  13.1 us
    pallas_call x4, Pallas kernels, window(): pl.pallas_call(window_kernel, grid=(blocks // step,), in_specs=[pl.BlockS...  12.6 us
    all_to_all x2, starting transfers between devices, exchange(): lax.all_to_all(pieces, 'freq', split_axis=0, concat_axis=0, tiled=True)  8.61 us
  transfers between devices with their start and end apart: 6, of which 6 were waited for; matrix products, arithmetic and copies ran while one was open for 2% of the time, Pallas kernels for 9%

profile of v14, /device:TPU:0, one launch (start us, length us, event | category | flops | bytes accessed | tf_op | source)
XLA Modules:
  0.0 213.2 jit_solution(1845749888835458581)
XLA Ops:
  0.6 0.8 copy.111
  1.5 1.5 copy.180
  3.3 0.6 copy-done
  3.9 3.6 %copy.183 = bf16[128,8,8,256]{3,2,1,0:T(8,128)(2,1)} copy(bf16[128,8,8,256]{3,1,2,0:T(8,128)(2,1)S(1)} %bitcast.175) | data formatting | bytes 8388608
  7.5 1.4 copy.182
  9.0 3.4 %fusion.1 = bf16[2,8,48,16,32]{2,4,1,0,3:T(8,128)(2,1)S(1)} fusion(pred[8,16,32]{2,0,1:T(8,128)(4,1)S(1)} %iota_compare_fusion, bf16[8,2,32,16,256,1]{4,3,2,1,0,5:T(8,128)(2,1)S(1)} %bitcast.177, bf16[1,16,2,48,256]{4,3,2,0,1:T(8,128)(2,1)S(1)} %maximum_bitcast_fusion.13, bf16[1,16,2,48,256]{4,3,2,0,1:T(8,128)(2,1)S(1)} %bitcast.186), kind=kOutput, calls=%fused_computation.7 | convolution fusion | flops 406585344 | bytes 6557696 | tf_op jit(solution)/shard_map/icrjt,ojcvt->oivjr/dot_general | solution.py:147
  12.4 1.3 slice_negate_fusion.7
  13.7 2.5 %maximum_bitcast_fusion = (bf16[1,2,8,48,16,32]{3,5,2,1,4,0:T(8,128)(2,1)S(1)}, bf16[1,2,8,48,16,32]{3,5,2,1,4,0:T(8,128)(2,1)S(1)}) fusion(bf16[1,8,48,16,32]{2,4,1,0,3:T(8,128)(2,1)S(1)} %get-tuple-element.11, bf16[1,8,48,16,32]{2,4,1,0,3:T(8,128)(2,1)} %get-tuple-element.13, bf16[1,8,48,16,32]{2,4,1,0,3:T(8,128)(2,1)S(1)} %get-tuple-element.12), kind=kLoop, calls=%fused_computation.34 | loop fusion | flops 786432 | bytes 2752512 | tf_op jit(solution)/shard_map/stack | solution.py:153
  16.2 0.3 copy-done.6
  16.5 2.3 %fusion.41 = bf16[8,2,48,256]{3,2,0,1:T(8,128)(2,1)S(1)} fusion(bf16[16,2,32,8,256,1]{4,3,2,1,0,5:T(8,128)(2,1)S(1)} %bitcast.183, bf16[1,2,8,48,16,32]{3,5,2,1,4,0:T(8,128)(2,1)S(1)} %get-tuple-element.21, bf16[1,2,8,48,16,32]{3,5,2,1,4,0:T(8,128)(2,1)S(1)} %get-tuple-element.20), kind=kOutput, calls=%fused_computation.53 | convolution fusion | flops 403439616 | bytes 6160384 | tf_op jit(solution)/shard_map/jcrit,ocivjr->iovt/dot_general | solution.py:154
  18.8 3.0 %collective-permute-start = (bf16[4,2,48,256]{3,2,1,0:T(8,128)(2,1)S(1)}, bf16[4,2,48,256]{3,2,1,0:T(8,128)(2,1)S(1)}, u32[]{:S(2)}, u32[]{:S(2)}) collective-permute-start(bf16[4,2,48,256]{3,2,1,0:T(8,128)(2,1)S(1)} %constant_dynamic-slice_fusion.1), channel_id=1, source_target_pairs={{0,2},{2,0},{1,3},{3,1},{4,6},{6,4},{5,7},{7,5},{8,10},{10,8},{9,1... | collective-permute-start | bytes 589832 | tf_op jit(solution)/shard_map/ppermute | solution.py:178
  22.1 0.6 reduce-window.6
  23.0 3.7 %collective-permute-done = bf16[4,2,48,256]{3,2,1,0:T(8,128)(2,1)S(1)} collective-permute-done((bf16[4,2,48,256]{3,2,1,0:T(8,128)(2,1)S(1)}, bf16[4,2,48,256]{3,2,1,0:T(8,128)(2,1)S(1)}, u32[]{:S(2)}, u32[]{:S(2)}) %collective-permute-start) | collective-permute-done | bytes 196640 | tf_op jit(solution)/shard_map/ppermute | solution.py:178
  26.7 0.7 add_convert_fusion.1
  27.4 5.1 %all-to-all-start = ((bf16[4,2,48,256]{3,2,1,0:T(8,128)(2,1)}), bf16[4,2,48,256]{3,2,1,0:T(8,128)(2,1)S(1)}, u32[]{:S(2)}, u32[]{:S(2)}) async-start(bf16[4,2,48,256]{3,2,1,0:T(8,128)(2,1)} %add_convert_fusion.1), calls=%async_computation | async-start | bytes 393216 | tf_op jit(solution)/shard_map/all_to_all | solution.py:134
  32.6 0.6 copy.256
  33.2 0.7 copy_bitcast_fusion.5.table_ref
  33.9 4.7 %shard_map.78.matrix_ref = bf16[64,1,48,256]{3,2,1,0:T(8,128)(2,1)} custom-call(bf16[64,256]{1,0:T(8,128)(2,1)} %copy_bitcast_fusion.5.table_ref, s32[1,48,256]{2,1,0:T(8,128)} %bitcast.205), custom_call_target="tpu_custom_call" | custom-call | tf_op jit(solution)/shard_map/pallas_call | solution.py:49
  38.6 0.4 all-to-all-done
  39.0 0.7 copy-done.10
  39.7 2.3 %shard_map.79 = bf16[4,1,2,48,256]{4,3,2,1,0:T(8,128)(2,1)} custom-call(bf16[64,1,48,256]{3,2,1,0:T(8,128)(2,1)} %shard_map.78.matrix_ref, bf16[4,1,2,48,256]{4,3,2,1,0:T(8,128)(2,1)} %bitcast.201), custom_call_target="tpu_custom_call" | custom-call | tf_op jit(solution)/shard_map/pallas_call | solution.py:87
  41.9 4.7 %all-to-all-start.1 = ((bf16[4,2,48,256]{3,2,1,0:T(8,128)(2,1)}), bf16[4,2,48,256]{3,2,1,0:T(8,128)(2,1)S(1)}, u32[]{:S(2)}, u32[]{:S(2)}) async-start(bf16[4,2,48,256]{3,2,1,0:T(8,128)(2,1)} %bitcast.202), calls=%async_computation.1 | async-start | bytes 393216 | tf_op jit(solution)/shard_map/all_to_all | solution.py:140
  46.7 6.2 %all-to-all-done.1 = bf16[4,2,48,256]{3,2,1,0:T(8,128)(2,1)S(1)} async-done(((bf16[4,2,48,256]{3,2,1,0:T(8,128)(2,1)}), bf16[4,2,48,256]{3,2,1,0:T(8,128)(2,1)S(1)}, u32[]{:S(2)}, u32[]{:S(2)}) %all-to-all-start.1) | async-done | bytes 196640 | tf_op jit(solution)/shard_map/all_to_all | solution.py:140
  52.9 6.5 %all_gather.6 = bf16[8,2,48,256]{3,2,1,0:T(8,128)(2,1)S(1)} all-gather(bf16[4,2,48,256]{3,2,1,0:T(8,128)(2,1)S(1)} %all-to-all-done.1), channel_id=1, replica_groups=mesh['groups'=2,'freq'=4,'src'=2,'vp'=2] {'src'}, dimensions={0}, use_global_device_ids=true | all-gather | bytes 589824 | tf_op jit(solution)/shard_map/all_gather | solution.py:217
  59.5 3.7 %fusion.24 = bf16[2,8,48,16,32]{2,4,3,0,1:T(8,128)(2,1)S(1)} fusion(pred[8,16,32]{2,1,0:T(8,128)(4,1)S(1)} %copy.112, bf16[16,2,32,8,256,1]{4,3,2,1,0,5:T(8,128)(2,1)} %bitcast.181, bf16[1,8,2,48,256]{4,3,2,0,1:T(8,128)(2,1)S(1)} %maximum_bitcast_fusion.19, bf16[1,8,2,48,256]{4,3,2,0,1:T(8,128)(2,1)S(1)} %bitcast.196), kind=kOutput, calls=%fused_computation.32 | convolution fusion | flops 405012480 | bytes 5771264 | tf_op jit(solution)/shard_map/jcrit,oicvt->oivjr/dot_general | solution.py:161
  63.2 0.3 slice_negate_fusion.6
  63.5 0.9 maximum_bitcast_fusion.2
  64.3 1.3 copy-done.3
  65.6 3.5 %fusion.5 = bf16[16,2,48,256,1,1]{3,2,4,1,0,5:T(8,128)(2,1)S(1)} fusion(bf16[8,2,32,16,256,1]{4,3,2,1,0,5:T(8,128)(2,1)S(1)} %bitcast.178, bf16[1,2,8,48,16,32]{3,5,4,1,2,0:T(8,128)(2,1)S(1)} %get-tuple-element.19, bf16[1,2,8,48,16,32]{3,5,4,1,2,0:T(8,128)(2,1)S(1)} %get-tuple-element.18), kind=kOutput, calls=%fused_computation.12 | convolution fusion | flops 403439616 | bytes 6553600 | tf_op jit(solution)/shard_map/icrjt,ocivjr->jovt/dot_general | solution.py:165
  69.2 1.0 copy.122
  70.2 3.5 %all-to-all-start.2 = ((bf16[16,2,48,256]{3,2,1,0:T(8,128)(2,1)}), bf16[16,2,48,256]{3,2,1,0:T(8,128)(2,1)S(1)}, u32[]{:S(2)}, u32[]{:S(2)}) async-start(bf16[16,2,48,256]{3,2,1,0:T(8,128)(2,1)} %copy.122), calls=%async_computation.2 | async-start | bytes 1572864 | tf_op jit(solution)/shard_map/all_to_all | solution.py:134
  73.7 0.2 copy.181
  74.0 0.7 copy.255
  74.7 14.1 %shard_map.77.matrix_ref = bf16[64,4,48,256]{3,2,1,0:T(8,128)(2,1)} custom-call(bf16[64,256]{1,0:T(8,128)(2,1)} %copy_bitcast_fusion.5.table_ref, s32[4,48,256]{2,1,0:T(8,128)} %bitcast.198), custom_call_target="tpu_custom_call" | custom-call | tf_op jit(solution)/shard_map/pallas_call | solution.py:49
  88.8 1.2 all-to-all-done.2
  90.0 0.9 copy-done.8
  90.9 4.0 %shard_map.80 = bf16[4,4,2,48,256]{4,3,2,1,0:T(8,128)(2,1)} custom-call(bf16[64,4,48,256]{3,2,1,0:T(8,128)(2,1)} %shard_map.77.matrix_ref, bf16[4,4,2,48,256]{4,3,2,1,0:T(8,128)(2,1)} %bitcast.190), custom_call_target="tpu_custom_call" | custom-call | tf_op jit(solution)/shard_map/pallas_call | solution.py:87
  94.9 20.7 %all_to_all.40 = bf16[16,2,48,256]{3,2,1,0:T(8,128)(2,1)S(1)} all-to-all(bf16[16,2,48,256]{3,2,1,0:T(8,128)(2,1)} %bitcast.193), channel_id=1, replica_groups=mesh['groups'=2,'freq'=4,'src'=2,'vp'=2] {'freq'}, dimensions={0} | all-to-all | bytes 1572864 | tf_op jit(solution)/shard_map/all_to_all | solution.py:140
  115.6 0.3 fusion.26
  116.1 1.7 copy-done.4
  117.8 3.3 %fusion = bf16[2,8,48,16,32]{2,4,1,0,3:T(8,128)(2,1)S(1)} fusion(pred[8,16,32]{2,0,1:T(8,128)(4,1)S(1)} %iota_compare_fusion, bf16[8,2,32,16,256,1]{4,3,2,1,0,5:T(8,128)(2,1)S(1)} %bitcast.179, bf16[1,16,2,48,256]{4,3,2,1,0:T(8,128)(2,1)S(1)} %maximum_bitcast_fusion.16, bf16[1,16,2,48,256]{4,3,2,1,0:T(8,128)(2,1)S(1)} %bitcast.189), kind=kOutput, calls=%fused_computation.5 | convolution fusion | flops 404226048 | bytes 6557696 | tf_op jit(solution)/shard_map/icrjt,ojcvt->oivjr/dot_general | solution.py:147
  121.2 0.3 slice_negate_fusion.5
  121.4 0.8 maximum_bitcast_fusion.4
  122.3 1.4 copy-done.7
  123.6 2.3 %fusion.46 = bf16[8,2,48,256]{3,2,0,1:T(8,128)(2,1)S(1)} fusion(bf16[16,2,32,8,256,1]{4,3,2,1,0,5:T(8,128)(2,1)S(1)} %bitcast.184, bf16[1,2,8,48,16,32]{3,5,2,1,4,0:T(8,128)(2,1)S(1)} %get-tuple-element.17, bf16[1,2,8,48,16,32]{3,5,2,1,4,0:T(8,128)(2,1)S(1)} %get-tuple-element.16), kind=kOutput, calls=%fused_computation.54 | convolution fusion | flops 403439616 | bytes 6160384 | tf_op jit(solution)/shard_map/jcrit,ocivjr->iovt/dot_general | solution.py:154
  125.9 1.6 collective-permute-start.1
  127.5 4.2 %collective-permute-done.1 = bf16[4,2,48,256]{3,2,1,0:T(8,128)(2,1)S(1)} collective-permute-done((bf16[4,2,48,256]{3,2,1,0:T(8,128)(2,1)S(1)}, bf16[4,2,48,256]{3,2,1,0:T(8,128)(2,1)S(1)}, u32[]{:S(2)}, u32[]{:S(2)}) %collective-permute-start.1) | collective-permute-done | bytes 196640 | tf_op jit(solution)/shard_map/ppermute | solution.py:178
  131.7 9.9 %all_to_all.41 = bf16[4,2,48,256]{3,2,1,0:T(8,128)(2,1)} all-to-all(bf16[4,2,48,256]{3,2,1,0:T(8,128)(2,1)S(1)} %add_convert_fusion), channel_id=1, replica_groups=mesh['groups'=2,'freq'=4,'src'=2,'vp'=2] {'freq'}, dimensions={0} | all-to-all | bytes 393216 | tf_op jit(solution)/shard_map/all_to_all | solution.py:134
  141.6 2.3 %shard_map.81 = bf16[4,1,2,48,256]{4,3,2,1,0:T(8,128)(2,1)} custom-call(bf16[64,1,48,256]{3,2,1,0:T(8,128)(2,1)} %shard_map.78.matrix_ref, bf16[4,1,2,48,256]{4,3,2,1,0:T(8,128)(2,1)} %bitcast.203), custom_call_target="tpu_custom_call" | custom-call | tf_op jit(solution)/shard_map/pallas_call | solution.py:87
  143.8 10.1 %all_to_all.42 = bf16[4,2,48,256]{3,2,1,0:T(8,128)(2,1)S(1)} all-to-all(bf16[4,2,48,256]{3,2,1,0:T(8,128)(2,1)} %bitcast.204), channel_id=1, replica_groups=mesh['groups'=2,'freq'=4,'src'=2,'vp'=2] {'freq'}, dimensions={0} | all-to-all | bytes 393216 | tf_op jit(solution)/shard_map/all_to_all | solution.py:140
  154.0 6.6 %all_gather.7 = bf16[8,2,48,256]{3,2,1,0:T(8,128)(2,1)S(1)} all-gather(bf16[4,2,48,256]{3,2,1,0:T(8,128)(2,1)S(1)} %all_to_all.42), channel_id=1, replica_groups=mesh['groups'=2,'freq'=4,'src'=2,'vp'=2] {'src'}, dimensions={0}, use_global_device_ids=true | all-gather | bytes 589824 | tf_op jit(solution)/shard_map/all_gather | solution.py:217
  160.6 3.7 %fusion.25 = bf16[2,8,48,16,32]{2,4,3,0,1:T(8,128)(2,1)S(1)} fusion(pred[8,16,32]{2,1,0:T(8,128)(4,1)S(1)} %copy.112, bf16[16,2,32,8,256,1]{4,3,2,1,0,5:T(8,128)(2,1)} %bitcast.182, bf16[1,8,2,48,256]{4,3,2,0,1:T(8,128)(2,1)S(1)} %maximum_bitcast_fusion.20, bf16[1,8,2,48,256]{4,3,2,0,1:T(8,128)(2,1)S(1)} %bitcast.195), kind=kOutput, calls=%fused_computation.33 | convolution fusion | flops 405012480 | bytes 5771264 | tf_op jit(solution)/shard_map/jcrit,oicvt->oivjr/dot_general | solution.py:161
  164.3 0.3 slice_negate_fusion.4
  164.6 0.9 maximum_bitcast_fusion.6
  165.5 1.3 copy-done.5
  166.8 3.5 %fusion.2 = bf16[16,2,48,256,1,1]{3,2,4,1,0,5:T(8,128)(2,1)S(1)} fusion(bf16[8,2,32,16,256,1]{4,3,2,1,0,5:T(8,128)(2,1)S(1)} %bitcast.180, bf16[1,2,8,48,16,32]{3,5,4,1,2,0:T(8,128)(2,1)S(1)} %get-tuple-element.15, bf16[1,2,8,48,16,32]{3,5,4,1,2,0:T(8,128)(2,1)S(1)} %get-tuple-element.14), kind=kOutput, calls=%fused_computation.8 | convolution fusion | flops 403439616 | bytes 6553600 | tf_op jit(solution)/shard_map/icrjt,ocivjr->jovt/dot_general | solution.py:165
  170.4 17.2 %all_to_all.43 = bf16[16,2,48,256]{3,2,1,0:T(8,128)(2,1)} all-to-all(bf16[16,2,48,256]{3,2,1,0:T(8,128)(2,1)S(1)} %copy.131), channel_id=1, replica_groups=mesh['groups'=2,'freq'=4,'src'=2,'vp'=2] {'freq'}, dimensions={0} | all-to-all | bytes 1572864 | tf_op jit(solution)/shard_map/all_to_all | solution.py:134
  187.6 4.1 %shard_map.82 = bf16[4,4,2,48,256]{4,3,2,1,0:T(8,128)(2,1)} custom-call(bf16[64,4,48,256]{3,2,1,0:T(8,128)(2,1)} %shard_map.77.matrix_ref, bf16[4,4,2,48,256]{4,3,2,1,0:T(8,128)(2,1)} %bitcast.192), custom_call_target="tpu_custom_call" | custom-call | tf_op jit(solution)/shard_map/pallas_call | solution.py:87
  191.6 3.5 %all-to-all-start.7 = ((bf16[16,2,48,256]{3,2,1,0:T(8,128)(2,1)}), bf16[16,2,48,256]{3,2,1,0:T(8,128)(2,1)S(1)}, u32[]{:S(2)}, u32[]{:S(2)}) async-start(bf16[16,2,48,256]{3,2,1,0:T(8,128)(2,1)} %bitcast.191), calls=%async_computation.7 | async-start | bytes 1572864 | tf_op jit(solution)/shard_map/all_to_all | solution.py:140
  195.3 0.8 broadcast_in_dim_reshape.7
  196.1 15.1 %all-to-all-done.7 = bf16[16,2,48,256]{3,2,1,0:T(8,128)(2,1)S(1)} async-done(((bf16[16,2,48,256]{3,2,1,0:T(8,128)(2,1)}), bf16[16,2,48,256]{3,2,1,0:T(8,128)(2,1)S(1)}, u32[]{:S(2)}, u32[]{:S(2)}) %all-to-all-start.7) | async-done | bytes 786464 | tf_op jit(solution)/shard_map/all_to_all | solution.py:140
  211.2 0.3 fusion.51
  211.6 0.4 copy.132
  212.0 1.2 broadcast_in_dim_reshape.6
  (48 shorter events, 1.8 us)
Async XLA Ops:
  1.5 2.4 %copy-start = (bf16[1,16,2,32,2048]{4,3,2,1,0:T(8,128)(2,1)S(1)}, bf16[1,16,2,32,2048]{4,3,2,1,0:T(8,128)(2,1)}, u32[]{:S(2)}) copy-start(bf16[1,16,2,32,2048]{4,3,2,1,0:T(8,128)(2,1)} %param.7) | copy-start | bytes 12582916
  3.9 3.6 %copy-start.1 = (bf16[1,8,2,32,4096]{4,3,2,1,0:T(8,128)(2,1)S(1)}, bf16[1,8,2,32,4096]{4,3,2,1,0:T(8,128)(2,1)}, u32[]{:S(2)}) copy-start(bf16[1,8,2,32,4096]{4,3,2,1,0:T(8,128)(2,1)} %param.8) | copy-start | bytes 12582916
  8.9 3.5 %copy-start.2 = (bf16[64,8,16,256]{3,2,1,0:T(8,128)(2,1)}, bf16[64,8,16,256]{3,2,1,0:T(8,128)(2,1)S(1)}, u32[]{:S(2)}) copy-start(bf16[64,8,16,256]{3,2,1,0:T(8,128)(2,1)S(1)} %copy.182) | copy-start | bytes 12582916
  13.7 2.8 %copy-start.6 = (bf16[128,8,8,256]{3,2,1,0:T(8,128)(2,1)S(1)}, bf16[128,8,8,256]{3,2,1,0:T(8,128)(2,1)}, u32[]{:S(2)}) copy-start(bf16[128,8,8,256]{3,2,1,0:T(8,128)(2,1)} %copy.183) | copy-start | bytes 12582916
  16.5 6.4 %copy-start.11 = (s32[48,1024]{1,0:T(8,128)S(1)}, s32[48,1024]{1,0:T(8,128)}, u32[]{:S(2)}) copy-start(s32[48,1024]{1,0:T(8,128)} %param.10) | copy-start | bytes 589828
  18.8 7.9 %collective-permute-start = (bf16[4,2,48,256]{3,2,1,0:T(8,128)(2,1)S(1)}, bf16[4,2,48,256]{3,2,1,0:T(8,128)(2,1)S(1)}, u32[]{:S(2)}, u32[]{:S(2)}) collective-permute-start(bf16[4,2,48,256]{3,2,1,0:T(8,128)(2,1)S(1)} %constant_dynamic-slice_fusion.1), channel_id=1, source_target_pairs={{0,2},{2,0},{1,3},{3,1},{4,6},{6,4},{5,7},{7,5},{8,10},{10,8},{9,1... | collective-permute-start | bytes 589832 | tf_op jit(solution)/shard_map/ppermute | solution.py:178
  27.4 11.6 %all-to-all-start = ((bf16[4,2,48,256]{3,2,1,0:T(8,128)(2,1)}), bf16[4,2,48,256]{3,2,1,0:T(8,128)(2,1)S(1)}, u32[]{:S(2)}, u32[]{:S(2)}) async-start(bf16[4,2,48,256]{3,2,1,0:T(8,128)(2,1)} %add_convert_fusion.1), calls=%async_computation | async-start | bytes 393216 | tf_op jit(solution)/shard_map/all_to_all | solution.py:134
  39.0 0.7 copy-start.10
  41.9 11.0 %all-to-all-start.1 = ((bf16[4,2,48,256]{3,2,1,0:T(8,128)(2,1)}), bf16[4,2,48,256]{3,2,1,0:T(8,128)(2,1)S(1)}, u32[]{:S(2)}, u32[]{:S(2)}) async-start(bf16[4,2,48,256]{3,2,1,0:T(8,128)(2,1)} %bitcast.202), calls=%async_computation.1 | async-start | bytes 393216 | tf_op jit(solution)/shard_map/all_to_all | solution.py:140
  63.4 2.2 %copy-start.3 = (bf16[64,8,16,256]{3,2,1,0:T(8,128)(2,1)S(1)}, bf16[64,8,16,256]{3,2,1,0:T(8,128)(2,1)}, u32[]{:S(2)}) copy-start(bf16[64,8,16,256]{3,2,1,0:T(8,128)(2,1)} %copy-done.2) | copy-start | bytes 12582916
  69.1 4.5 %copy-start.9 = (s32[48,4096]{1,0:T(8,128)S(1)}, s32[48,4096]{1,0:T(8,128)}, u32[]{:S(2)}) copy-start(s32[48,4096]{1,0:T(8,128)} %param.11) | copy-start | bytes 2359300
  70.2 19.8 %all-to-all-start.2 = ((bf16[16,2,48,256]{3,2,1,0:T(8,128)(2,1)}), bf16[16,2,48,256]{3,2,1,0:T(8,128)(2,1)S(1)}, u32[]{:S(2)}, u32[]{:S(2)}) async-start(bf16[16,2,48,256]{3,2,1,0:T(8,128)(2,1)} %copy.122), calls=%async_computation.2 | async-start | bytes 1572864 | tf_op jit(solution)/shard_map/all_to_all | solution.py:134
  90.0 0.9 copy-start.8
  115.6 2.2 %copy-start.4 = (bf16[64,8,16,256]{3,2,1,0:T(8,128)(2,1)S(1)}, bf16[64,8,16,256]{3,2,1,0:T(8,128)(2,1)}, u32[]{:S(2)}) copy-start(bf16[64,8,16,256]{3,2,1,0:T(8,128)(2,1)} %copy-done.2) | copy-start | bytes 12582916
  121.4 2.2 %copy-start.7 = (bf16[128,8,8,256]{3,2,1,0:T(8,128)(2,1)S(1)}, bf16[128,8,8,256]{3,2,1,0:T(8,128)(2,1)}, u32[]{:S(2)}) copy-start(bf16[128,8,8,256]{3,2,1,0:T(8,128)(2,1)} %copy.183) | copy-start | bytes 12582916
  125.9 5.7 %collective-permute-start.1 = (bf16[4,2,48,256]{3,2,1,0:T(8,128)(2,1)S(1)}, bf16[4,2,48,256]{3,2,1,0:T(8,128)(2,1)S(1)}, u32[]{:S(2)}, u32[]{:S(2)}) collective-permute-start(bf16[4,2,48,256]{3,2,1,0:T(8,128)(2,1)S(1)} %constant_dynamic-slice_fusion), channel_id=1, source_target_pairs={{0,2},{2,0},{1,3},{3,1},{4,6},{6,4},{5,7},{7,5},{8,10},{10,8},{9,1... | collective-permute-start | bytes 589832 | tf_op jit(solution)/shard_map/ppermute | solution.py:178
  164.6 2.2 %copy-start.5 = (bf16[64,8,16,256]{3,2,1,0:T(8,128)(2,1)S(1)}, bf16[64,8,16,256]{3,2,1,0:T(8,128)(2,1)}, u32[]{:S(2)}) copy-start(bf16[64,8,16,256]{3,2,1,0:T(8,128)(2,1)} %copy-done.2) | copy-start | bytes 12582916
  191.6 19.6 %all-to-all-start.7 = ((bf16[16,2,48,256]{3,2,1,0:T(8,128)(2,1)}), bf16[16,2,48,256]{3,2,1,0:T(8,128)(2,1)S(1)}, u32[]{:S(2)}, u32[]{:S(2)}) async-start(bf16[16,2,48,256]{3,2,1,0:T(8,128)(2,1)} %bitcast.191), calls=%async_computation.7 | async-start | bytes 1572864 | tf_op jit(solution)/shard_map/all_to_all | solution.py:140

commit v15 on v14

--- a/solution.py
+++ b/solution.py
@@ -45,7 +45,7 @@
     table = jnp.cumsum(terms.reshape(NT, size), axis=0)
     stacked = table.astype(jnp.bfloat16).T
     blocks, points, width = onset.shape
-    rows = 16 if points % 16 == 0 else 8
+    rows = 24 if points % 24 == 0 else 8
     return pl.pallas_call(
         gather_kernel,
         grid=(blocks, points // rows),

time: 214 us -> 214 us (level)
  no operation moved by 1% of the time
where the time goes in v15:
time: 214 us; the launch traced here: 213 us
  blocking collectives  71 us (33%)
  Pallas kernels  31.5 us (15%)
  waiting for transfers between devices  30.8 us (14%)
  matrix products  25.5 us (12%)
  local copies, waits for them, and re-layouts  21.5 us (10%)
  starting transfers between devices  21.4 us (10%)
  other arithmetic  10.6 us (5%)
    all_to_all x2, blocking collectives, exchange_back(): got = lax.all_to_all(flat, 'freq', split_axis=0, concat_axis=0, tiled=True)  30.9 us
    all_to_all x2, blocking collectives, exchange(): lax.all_to_all(pieces, 'freq', split_axis=0, concat_axis=0, tiled=True)  27.1 us
    all_to_all x2, waiting for transfers between devices, exchange_back(): got = lax.all_to_all(flat, 'freq', split_axis=0, concat_axis=0, tiled=True)  21.4 us
    pallas_call x2, Pallas kernels, window_gather(): pl.pallas_call(gather_kernel, grid=(blocks, points // rows), in_specs=[pl...  18.8 us
    unnamed x30, local copies, waits for them, and re-layouts  16.2 us
    all_gather x2, blocking collectives, per_device(): minus_all = lax.all_gather(minus, 'src', axis=0, tiled=True)  13.1 us
    pallas_call x4, Pallas kernels, window(): pl.pallas_call(window_kernel, grid=(blocks // step,), in_specs=[pl.BlockS...  12.6 us
    all_to_all x2, starting transfers between devices, exchange(): lax.all_to_all(pieces, 'freq', split_axis=0, concat_axis=0, tiled=True)  8.61 us
  transfers between devices with their start and end apart: 6, of which 6 were waited for; matrix products, arithmetic and copies ran while one was open for 2% of the time, Pallas kernels for 9%

profile of v15, /device:TPU:0, one launch (start us, length us, event | category | flops | bytes accessed | tf_op | source)
XLA Modules:
  0.0 213.4 jit_solution(6674038711010677226)
XLA Ops:
  0.6 0.8 copy.111
  1.5 1.5 copy.180
  3.3 0.6 copy-done
  3.9 3.6 %copy.183 = bf16[128,8,8,256]{3,2,1,0:T(8,128)(2,1)} copy(bf16[128,8,8,256]{3,1,2,0:T(8,128)(2,1)S(1)} %bitcast.175) | data formatting | bytes 8388608
  7.5 1.4 copy.182
  9.0 3.4 %fusion.1 = bf16[2,8,48,16,32]{2,4,1,0,3:T(8,128)(2,1)S(1)} fusion(pred[8,16,32]{2,0,1:T(8,128)(4,1)S(1)} %iota_compare_fusion, bf16[8,2,32,16,256,1]{4,3,2,1,0,5:T(8,128)(2,1)S(1)} %bitcast.177, bf16[1,16,2,48,256]{4,3,2,0,1:T(8,128)(2,1)S(1)} %maximum_bitcast_fusion.13, bf16[1,16,2,48,256]{4,3,2,0,1:T(8,128)(2,1)S(1)} %bitcast.186), kind=kOutput, calls=%fused_computation.7 | convolution fusion | flops 406585344 | bytes 6557696 | tf_op jit(solution)/shard_map/icrjt,ojcvt->oivjr/dot_general | solution.py:147
  12.4 1.3 slice_negate_fusion.7
  13.7 2.5 %maximum_bitcast_fusion = (bf16[1,2,8,48,16,32]{3,5,2,1,4,0:T(8,128)(2,1)S(1)}, bf16[1,2,8,48,16,32]{3,5,2,1,4,0:T(8,128)(2,1)S(1)}) fusion(bf16[1,8,48,16,32]{2,4,1,0,3:T(8,128)(2,1)S(1)} %get-tuple-element.11, bf16[1,8,48,16,32]{2,4,1,0,3:T(8,128)(2,1)} %get-tuple-element.13, bf16[1,8,48,16,32]{2,4,1,0,3:T(8,128)(2,1)S(1)} %get-tuple-element.12), kind=kLoop, calls=%fused_computation.34 | loop fusion | flops 786432 | bytes 2752512 | tf_op jit(solution)/shard_map/stack | solution.py:153
  16.2 0.3 copy-done.6
  16.5 2.3 %fusion.41 = bf16[8,2,48,256]{3,2,0,1:T(8,128)(2,1)S(1)} fusion(bf16[16,2,32,8,256,1]{4,3,2,1,0,5:T(8,128)(2,1)S(1)} %bitcast.183, bf16[1,2,8,48,16,32]{3,5,2,1,4,0:T(8,128)(2,1)S(1)} %get-tuple-element.21, bf16[1,2,8,48,16,32]{3,5,2,1,4,0:T(8,128)(2,1)S(1)} %get-tuple-element.20), kind=kOutput, calls=%fused_computation.53 | convolution fusion | flops 403439616 | bytes 6160384 | tf_op jit(solution)/shard_map/jcrit,ocivjr->iovt/dot_general | solution.py:154
  18.8 3.0 %collective-permute-start = (bf16[4,2,48,256]{3,2,1,0:T(8,128)(2,1)S(1)}, bf16[4,2,48,256]{3,2,1,0:T(8,128)(2,1)S(1)}, u32[]{:S(2)}, u32[]{:S(2)}) collective-permute-start(bf16[4,2,48,256]{3,2,1,0:T(8,128)(2,1)S(1)} %constant_dynamic-slice_fusion.1), channel_id=1, source_target_pairs={{0,2},{2,0},{1,3},{3,1},{4,6},{6,4},{5,7},{7,5},{8,10},{10,8},{9,1... | collective-permute-start | bytes 589832 | tf_op jit(solution)/shard_map/ppermute | solution.py:178
  22.1 0.6 reduce-window.6
  23.0 3.7 %collective-permute-done = bf16[4,2,48,256]{3,2,1,0:T(8,128)(2,1)S(1)} collective-permute-done((bf16[4,2,48,256]{3,2,1,0:T(8,128)(2,1)S(1)}, bf16[4,2,48,256]{3,2,1,0:T(8,128)(2,1)S(1)}, u32[]{:S(2)}, u32[]{:S(2)}) %collective-permute-start) | collective-permute-done | bytes 196640 | tf_op jit(solution)/shard_map/ppermute | solution.py:178
  26.7 0.7 add_convert_fusion.1
  27.4 5.1 %all-to-all-start = ((bf16[4,2,48,256]{3,2,1,0:T(8,128)(2,1)}), bf16[4,2,48,256]{3,2,1,0:T(8,128)(2,1)S(1)}, u32[]{:S(2)}, u32[]{:S(2)}) async-start(bf16[4,2,48,256]{3,2,1,0:T(8,128)(2,1)} %add_convert_fusion.1), calls=%async_computation | async-start | bytes 393216 | tf_op jit(solution)/shard_map/all_to_all | solution.py:134
  32.6 0.6 copy.256
  33.2 0.7 copy_bitcast_fusion.5.table_ref
  33.9 4.8 %shard_map.78.matrix_ref = bf16[64,1,48,256]{3,2,1,0:T(8,128)(2,1)} custom-call(bf16[64,256]{1,0:T(8,128)(2,1)} %copy_bitcast_fusion.5.table_ref, s32[1,48,256]{2,1,0:T(8,128)} %bitcast.205), custom_call_target="tpu_custom_call" | custom-call | tf_op jit(solution)/shard_map/pallas_call | solution.py:49
  38.7 0.3 all-to-all-done
  39.0 0.7 copy-done.10
  39.7 2.3 %shard_map.79 = bf16[4,1,2,48,256]{4,3,2,1,0:T(8,128)(2,1)} custom-call(bf16[64,1,48,256]{3,2,1,0:T(8,128)(2,1)} %shard_map.78.matrix_ref, bf16[4,1,2,48,256]{4,3,2,1,0:T(8,128)(2,1)} %bitcast.201), custom_call_target="tpu_custom_call" | custom-call | tf_op jit(solution)/shard_map/pallas_call | solution.py:87
  41.9 4.8 %all-to-all-start.1 = ((bf16[4,2,48,256]{3,2,1,0:T(8,128)(2,1)}), bf16[4,2,48,256]{3,2,1,0:T(8,128)(2,1)S(1)}, u32[]{:S(2)}, u32[]{:S(2)}) async-start(bf16[4,2,48,256]{3,2,1,0:T(8,128)(2,1)} %bitcast.202), calls=%async_computation.1 | async-start | bytes 393216 | tf_op jit(solution)/shard_map/all_to_all | solution.py:140
  46.7 6.2 %all-to-all-done.1 = bf16[4,2,48,256]{3,2,1,0:T(8,128)(2,1)S(1)} async-done(((bf16[4,2,48,256]{3,2,1,0:T(8,128)(2,1)}), bf16[4,2,48,256]{3,2,1,0:T(8,128)(2,1)S(1)}, u32[]{:S(2)}, u32[]{:S(2)}) %all-to-all-start.1) | async-done | bytes 196640 | tf_op jit(solution)/shard_map/all_to_all | solution.py:140
  52.9 6.5 %all_gather.6 = bf16[8,2,48,256]{3,2,1,0:T(8,128)(2,1)S(1)} all-gather(bf16[4,2,48,256]{3,2,1,0:T(8,128)(2,1)S(1)} %all-to-all-done.1), channel_id=1, replica_groups=mesh['groups'=2,'freq'=4,'src'=2,'vp'=2] {'src'}, dimensions={0}, use_global_device_ids=true | all-gather | bytes 589824 | tf_op jit(solution)/shard_map/all_gather | solution.py:217
  59.5 3.7 %fusion.24 = bf16[2,8,48,16,32]{2,4,3,0,1:T(8,128)(2,1)S(1)} fusion(pred[8,16,32]{2,1,0:T(8,128)(4,1)S(1)} %copy.112, bf16[16,2,32,8,256,1]{4,3,2,1,0,5:T(8,128)(2,1)} %bitcast.181, bf16[1,8,2,48,256]{4,3,2,0,1:T(8,128)(2,1)S(1)} %maximum_bitcast_fusion.19, bf16[1,8,2,48,256]{4,3,2,0,1:T(8,128)(2,1)S(1)} %bitcast.196), kind=kOutput, calls=%fused_computation.32 | convolution fusion | flops 405012480 | bytes 5771264 | tf_op jit(solution)/shard_map/jcrit,oicvt->oivjr/dot_general | solution.py:161
  63.2 0.3 slice_negate_fusion.6
  63.5 0.9 maximum_bitcast_fusion.2
  64.4 1.3 copy-done.3
  65.7 3.5 %fusion.5 = bf16[16,2,48,256,1,1]{3,2,4,1,0,5:T(8,128)(2,1)S(1)} fusion(bf16[8,2,32,16,256,1]{4,3,2,1,0,5:T(8,128)(2,1)S(1)} %bitcast.178, bf16[1,2,8,48,16,32]{3,5,4,1,2,0:T(8,128)(2,1)S(1)} %get-tuple-element.19, bf16[1,2,8,48,16,32]{3,5,4,1,2,0:T(8,128)(2,1)S(1)} %get-tuple-element.18), kind=kOutput, calls=%fused_computation.12 | convolution fusion | flops 403439616 | bytes 6553600 | tf_op jit(solution)/shard_map/icrjt,ocivjr->jovt/dot_general | solution.py:165
  69.2 1.0 copy.122
  70.2 3.5 %all-to-all-start.2 = ((bf16[16,2,48,256]{3,2,1,0:T(8,128)(2,1)}), bf16[16,2,48,256]{3,2,1,0:T(8,128)(2,1)S(1)}, u32[]{:S(2)}, u32[]{:S(2)}) async-start(bf16[16,2,48,256]{3,2,1,0:T(8,128)(2,1)} %copy.122), calls=%async_computation.2 | async-start | bytes 1572864 | tf_op jit(solution)/shard_map/all_to_all | solution.py:134
  73.7 0.2 copy.181
  74.0 0.7 copy.255
  74.8 14.1 %shard_map.77.matrix_ref = bf16[64,4,48,256]{3,2,1,0:T(8,128)(2,1)} custom-call(bf16[64,256]{1,0:T(8,128)(2,1)} %copy_bitcast_fusion.5.table_ref, s32[4,48,256]{2,1,0:T(8,128)} %bitcast.198), custom_call_target="tpu_custom_call" | custom-call | tf_op jit(solution)/shard_map/pallas_call | solution.py:49
  88.8 1.2 all-to-all-done.2
  90.1 0.9 copy-done.8
  90.9 4.0 %shard_map.80 = bf16[4,4,2,48,256]{4,3,2,1,0:T(8,128)(2,1)} custom-call(bf16[64,4,48,256]{3,2,1,0:T(8,128)(2,1)} %shard_map.77.matrix_ref, bf16[4,4,2,48,256]{4,3,2,1,0:T(8,128)(2,1)} %bitcast.190), custom_call_target="tpu_custom_call" | custom-call | tf_op jit(solution)/shard_map/pallas_call | solution.py:87
  95.0 20.7 %all_to_all.40 = bf16[16,2,48,256]{3,2,1,0:T(8,128)(2,1)S(1)} all-to-all(bf16[16,2,48,256]{3,2,1,0:T(8,128)(2,1)} %bitcast.193), channel_id=1, replica_groups=mesh['groups'=2,'freq'=4,'src'=2,'vp'=2] {'freq'}, dimensions={0} | all-to-all | bytes 1572864 | tf_op jit(solution)/shard_map/all_to_all | solution.py:140
  115.7 0.3 fusion.26
  116.2 1.7 copy-done.4
  117.9 3.3 %fusion = bf16[2,8,48,16,32]{2,4,1,0,3:T(8,128)(2,1)S(1)} fusion(pred[8,16,32]{2,0,1:T(8,128)(4,1)S(1)} %iota_compare_fusion, bf16[8,2,32,16,256,1]{4,3,2,1,0,5:T(8,128)(2,1)S(1)} %bitcast.179, bf16[1,16,2,48,256]{4,3,2,1,0:T(8,128)(2,1)S(1)} %maximum_bitcast_fusion.16, bf16[1,16,2,48,256]{4,3,2,1,0:T(8,128)(2,1)S(1)} %bitcast.189), kind=kOutput, calls=%fused_computation.5 | convolution fusion | flops 404226048 | bytes 6557696 | tf_op jit(solution)/shard_map/icrjt,ojcvt->oivjr/dot_general | solution.py:147
  121.2 0.3 slice_negate_fusion.5
  121.5 0.8 maximum_bitcast_fusion.4
  122.3 1.4 copy-done.7
  123.7 2.3 %fusion.46 = bf16[8,2,48,256]{3,2,0,1:T(8,128)(2,1)S(1)} fusion(bf16[16,2,32,8,256,1]{4,3,2,1,0,5:T(8,128)(2,1)S(1)} %bitcast.184, bf16[1,2,8,48,16,32]{3,5,2,1,4,0:T(8,128)(2,1)S(1)} %get-tuple-element.17, bf16[1,2,8,48,16,32]{3,5,2,1,4,0:T(8,128)(2,1)S(1)} %get-tuple-element.16), kind=kOutput, calls=%fused_computation.54 | convolution fusion | flops 403439616 | bytes 6160384 | tf_op jit(solution)/shard_map/jcrit,ocivjr->iovt/dot_general | solution.py:154
  126.0 1.5 collective-permute-start.1
  127.5 4.2 %collective-permute-done.1 = bf16[4,2,48,256]{3,2,1,0:T(8,128)(2,1)S(1)} collective-permute-done((bf16[4,2,48,256]{3,2,1,0:T(8,128)(2,1)S(1)}, bf16[4,2,48,256]{3,2,1,0:T(8,128)(2,1)S(1)}, u32[]{:S(2)}, u32[]{:S(2)}) %collective-permute-start.1) | collective-permute-done | bytes 196640 | tf_op jit(solution)/shard_map/ppermute | solution.py:178
  131.8 9.9 %all_to_all.41 = bf16[4,2,48,256]{3,2,1,0:T(8,128)(2,1)} all-to-all(bf16[4,2,48,256]{3,2,1,0:T(8,128)(2,1)S(1)} %add_convert_fusion), channel_id=1, replica_groups=mesh['groups'=2,'freq'=4,'src'=2,'vp'=2] {'freq'}, dimensions={0} | all-to-all | bytes 393216 | tf_op jit(solution)/shard_map/all_to_all | solution.py:134
  141.7 2.3 %shard_map.81 = bf16[4,1,2,48,256]{4,3,2,1,0:T(8,128)(2,1)} custom-call(bf16[64,1,48,256]{3,2,1,0:T(8,128)(2,1)} %shard_map.78.matrix_ref, bf16[4,1,2,48,256]{4,3,2,1,0:T(8,128)(2,1)} %bitcast.203), custom_call_target="tpu_custom_call" | custom-call | tf_op jit(solution)/shard_map/pallas_call | solution.py:87
  143.9 10.1 %all_to_all.42 = bf16[4,2,48,256]{3,2,1,0:T(8,128)(2,1)S(1)} all-to-all(bf16[4,2,48,256]{3,2,1,0:T(8,128)(2,1)} %bitcast.204), channel_id=1, replica_groups=mesh['groups'=2,'freq'=4,'src'=2,'vp'=2] {'freq'}, dimensions={0} | all-to-all | bytes 393216 | tf_op jit(solution)/shard_map/all_to_all | solution.py:140
  154.0 6.6 %all_gather.7 = bf16[8,2,48,256]{3,2,1,0:T(8,128)(2,1)S(1)} all-gather(bf16[4,2,48,256]{3,2,1,0:T(8,128)(2,1)S(1)} %all_to_all.42), channel_id=1, replica_groups=mesh['groups'=2,'freq'=4,'src'=2,'vp'=2] {'src'}, dimensions={0}, use_global_device_ids=true | all-gather | bytes 589824 | tf_op jit(solution)/shard_map/all_gather | solution.py:217
  160.7 3.7 %fusion.25 = bf16[2,8,48,16,32]{2,4,3,0,1:T(8,128)(2,1)S(1)} fusion(pred[8,16,32]{2,1,0:T(8,128)(4,1)S(1)} %copy.112, bf16[16,2,32,8,256,1]{4,3,2,1,0,5:T(8,128)(2,1)} %bitcast.182, bf16[1,8,2,48,256]{4,3,2,0,1:T(8,128)(2,1)S(1)} %maximum_bitcast_fusion.20, bf16[1,8,2,48,256]{4,3,2,0,1:T(8,128)(2,1)S(1)} %bitcast.195), kind=kOutput, calls=%fused_computation.33 | convolution fusion | flops 405012480 | bytes 5771264 | tf_op jit(solution)/shard_map/jcrit,oicvt->oivjr/dot_general | solution.py:161
  164.4 0.3 slice_negate_fusion.4
  164.6 0.9 maximum_bitcast_fusion.6
  165.5 1.3 copy-done.5
  166.8 3.5 %fusion.2 = bf16[16,2,48,256,1,1]{3,2,4,1,0,5:T(8,128)(2,1)S(1)} fusion(bf16[8,2,32,16,256,1]{4,3,2,1,0,5:T(8,128)(2,1)S(1)} %bitcast.180, bf16[1,2,8,48,16,32]{3,5,4,1,2,0:T(8,128)(2,1)S(1)} %get-tuple-element.15, bf16[1,2,8,48,16,32]{3,5,4,1,2,0:T(8,128)(2,1)S(1)} %get-tuple-element.14), kind=kOutput, calls=%fused_computation.8 | convolution fusion | flops 403439616 | bytes 6553600 | tf_op jit(solution)/shard_map/icrjt,ocivjr->jovt/dot_general | solution.py:165
  170.5 17.2 %all_to_all.43 = bf16[16,2,48,256]{3,2,1,0:T(8,128)(2,1)} all-to-all(bf16[16,2,48,256]{3,2,1,0:T(8,128)(2,1)S(1)} %copy.131), channel_id=1, replica_groups=mesh['groups'=2,'freq'=4,'src'=2,'vp'=2] {'freq'}, dimensions={0} | all-to-all | bytes 1572864 | tf_op jit(solution)/shard_map/all_to_all | solution.py:134
  187.7 4.1 %shard_map.82 = bf16[4,4,2,48,256]{4,3,2,1,0:T(8,128)(2,1)} custom-call(bf16[64,4,48,256]{3,2,1,0:T(8,128)(2,1)} %shard_map.77.matrix_ref, bf16[4,4,2,48,256]{4,3,2,1,0:T(8,128)(2,1)} %bitcast.192), custom_call_target="tpu_custom_call" | custom-call | tf_op jit(solution)/shard_map/pallas_call | solution.py:87
  191.7 3.5 %all-to-all-start.7 = ((bf16[16,2,48,256]{3,2,1,0:T(8,128)(2,1)}), bf16[16,2,48,256]{3,2,1,0:T(8,128)(2,1)S(1)}, u32[]{:S(2)}, u32[]{:S(2)}) async-start(bf16[16,2,48,256]{3,2,1,0:T(8,128)(2,1)} %bitcast.191), calls=%async_computation.7 | async-start | bytes 1572864 | tf_op jit(solution)/shard_map/all_to_all | solution.py:140
  195.4 0.8 broadcast_in_dim_reshape.7
  196.2 15.2 %all-to-all-done.7 = bf16[16,2,48,256]{3,2,1,0:T(8,128)(2,1)S(1)} async-done(((bf16[16,2,48,256]{3,2,1,0:T(8,128)(2,1)}), bf16[16,2,48,256]{3,2,1,0:T(8,128)(2,1)S(1)}, u32[]{:S(2)}, u32[]{:S(2)}) %all-to-all-start.7) | async-done | bytes 786464 | tf_op jit(solution)/shard_map/all_to_all | solution.py:140
  211.4 0.3 fusion.51
  211.7 0.4 copy.132
  212.1 1.2 broadcast_in_dim_reshape.6
  (48 shorter events, 1.8 us)
Async XLA Ops:
  1.5 2.4 %copy-start = (bf16[1,16,2,32,2048]{4,3,2,1,0:T(8,128)(2,1)S(1)}, bf16[1,16,2,32,2048]{4,3,2,1,0:T(8,128)(2,1)}, u32[]{:S(2)}) copy-start(bf16[1,16,2,32,2048]{4,3,2,1,0:T(8,128)(2,1)} %param.7) | copy-start | bytes 12582916
  3.9 3.6 %copy-start.1 = (bf16[1,8,2,32,4096]{4,3,2,1,0:T(8,128)(2,1)S(1)}, bf16[1,8,2,32,4096]{4,3,2,1,0:T(8,128)(2,1)}, u32[]{:S(2)}) copy-start(bf16[1,8,2,32,4096]{4,3,2,1,0:T(8,128)(2,1)} %param.8) | copy-start | bytes 12582916
  8.9 3.5 %copy-start.2 = (bf16[64,8,16,256]{3,2,1,0:T(8,128)(2,1)}, bf16[64,8,16,256]{3,2,1,0:T(8,128)(2,1)S(1)}, u32[]{:S(2)}) copy-start(bf16[64,8,16,256]{3,2,1,0:T(8,128)(2,1)S(1)} %copy.182) | copy-start | bytes 12582916
  13.7 2.8 %copy-start.6 = (bf16[128,8,8,256]{3,2,1,0:T(8,128)(2,1)S(1)}, bf16[128,8,8,256]{3,2,1,0:T(8,128)(2,1)}, u32[]{:S(2)}) copy-start(bf16[128,8,8,256]{3,2,1,0:T(8,128)(2,1)} %copy.183) | copy-start | bytes 12582916
  16.5 6.4 %copy-start.11 = (s32[48,1024]{1,0:T(8,128)S(1)}, s32[48,1024]{1,0:T(8,128)}, u32[]{:S(2)}) copy-start(s32[48,1024]{1,0:T(8,128)} %param.10) | copy-start | bytes 589828
  18.8 7.9 %collective-permute-start = (bf16[4,2,48,256]{3,2,1,0:T(8,128)(2,1)S(1)}, bf16[4,2,48,256]{3,2,1,0:T(8,128)(2,1)S(1)}, u32[]{:S(2)}, u32[]{:S(2)}) collective-permute-start(bf16[4,2,48,256]{3,2,1,0:T(8,128)(2,1)S(1)} %constant_dynamic-slice_fusion.1), channel_id=1, source_target_pairs={{0,2},{2,0},{1,3},{3,1},{4,6},{6,4},{5,7},{7,5},{8,10},{10,8},{9,1... | collective-permute-start | bytes 589832 | tf_op jit(solution)/shard_map/ppermute | solution.py:178
  27.4 11.6 %all-to-all-start = ((bf16[4,2,48,256]{3,2,1,0:T(8,128)(2,1)}), bf16[4,2,48,256]{3,2,1,0:T(8,128)(2,1)S(1)}, u32[]{:S(2)}, u32[]{:S(2)}) async-start(bf16[4,2,48,256]{3,2,1,0:T(8,128)(2,1)} %add_convert_fusion.1), calls=%async_computation | async-start | bytes 393216 | tf_op jit(solution)/shard_map/all_to_all | solution.py:134
  39.0 0.7 copy-start.10
  41.9 11.0 %all-to-all-start.1 = ((bf16[4,2,48,256]{3,2,1,0:T(8,128)(2,1)}), bf16[4,2,48,256]{3,2,1,0:T(8,128)(2,1)S(1)}, u32[]{:S(2)}, u32[]{:S(2)}) async-start(bf16[4,2,48,256]{3,2,1,0:T(8,128)(2,1)} %bitcast.202), calls=%async_computation.1 | async-start | bytes 393216 | tf_op jit(solution)/shard_map/all_to_all | solution.py:140
  63.5 2.2 %copy-start.3 = (bf16[64,8,16,256]{3,2,1,0:T(8,128)(2,1)S(1)}, bf16[64,8,16,256]{3,2,1,0:T(8,128)(2,1)}, u32[]{:S(2)}) copy-start(bf16[64,8,16,256]{3,2,1,0:T(8,128)(2,1)} %copy-done.2) | copy-start | bytes 12582916
  69.2 4.5 %copy-start.9 = (s32[48,4096]{1,0:T(8,128)S(1)}, s32[48,4096]{1,0:T(8,128)}, u32[]{:S(2)}) copy-start(s32[48,4096]{1,0:T(8,128)} %param.11) | copy-start | bytes 2359300
  70.2 19.8 %all-to-all-start.2 = ((bf16[16,2,48,256]{3,2,1,0:T(8,128)(2,1)}), bf16[16,2,48,256]{3,2,1,0:T(8,128)(2,1)S(1)}, u32[]{:S(2)}, u32[]{:S(2)}) async-start(bf16[16,2,48,256]{3,2,1,0:T(8,128)(2,1)} %copy.122), calls=%async_computation.2 | async-start | bytes 1572864 | tf_op jit(solution)/shard_map/all_to_all | solution.py:134
  90.1 0.9 copy-start.8
  115.7 2.2 %copy-start.4 = (bf16[64,8,16,256]{3,2,1,0:T(8,128)(2,1)S(1)}, bf16[64,8,16,256]{3,2,1,0:T(8,128)(2,1)}, u32[]{:S(2)}) copy-start(bf16[64,8,16,256]{3,2,1,0:T(8,128)(2,1)} %copy-done.2) | copy-start | bytes 12582916
  121.5 2.2 %copy-start.7 = (bf16[128,8,8,256]{3,2,1,0:T(8,128)(2,1)S(1)}, bf16[128,8,8,256]{3,2,1,0:T(8,128)(2,1)}, u32[]{:S(2)}) copy-start(bf16[128,8,8,256]{3,2,1,0:T(8,128)(2,1)} %copy.183) | copy-start | bytes 12582916
  126.0 5.7 %collective-permute-start.1 = (bf16[4,2,48,256]{3,2,1,0:T(8,128)(2,1)S(1)}, bf16[4,2,48,256]{3,2,1,0:T(8,128)(2,1)S(1)}, u32[]{:S(2)}, u32[]{:S(2)}) collective-permute-start(bf16[4,2,48,256]{3,2,1,0:T(8,128)(2,1)S(1)} %constant_dynamic-slice_fusion), channel_id=1, source_target_pairs={{0,2},{2,0},{1,3},{3,1},{4,6},{6,4},{5,7},{7,5},{8,10},{10,8},{9,1... | collective-permute-start | bytes 589832 | tf_op jit(solution)/shard_map/ppermute | solution.py:178
  164.6 2.2 %copy-start.5 = (bf16[64,8,16,256]{3,2,1,0:T(8,128)(2,1)S(1)}, bf16[64,8,16,256]{3,2,1,0:T(8,128)(2,1)}, u32[]{:S(2)}) copy-start(bf16[64,8,16,256]{3,2,1,0:T(8,128)(2,1)} %copy-done.2) | copy-start | bytes 12582916
  191.7 19.6 %all-to-all-start.7 = ((bf16[16,2,48,256]{3,2,1,0:T(8,128)(2,1)}), bf16[16,2,48,256]{3,2,1,0:T(8,128)(2,1)S(1)}, u32[]{:S(2)}, u32[]{:S(2)}) async-start(bf16[16,2,48,256]{3,2,1,0:T(8,128)(2,1)} %bitcast.191), calls=%async_computation.7 | async-start | bytes 1572864 | tf_op jit(solution)/shard_map/all_to_all | solution.py:140
